TPU v7x, 32 devices: a whole 2x2x4 slice. The times are simulated.
32 devices in a mesh: seq: 8 (over z, y), tp: 4 (over x, core).
Axes of the slice: x: 2, y: 2, z: 4, core: 2. Of those that a mesh axis runs over, the one named last changes fastest.
Arguments:
- new_query: bfloat16 [8, 3584], P('seq', 'tp'), may hold values from -360 to 360
- new_key: bfloat16 [8, 512], P('seq', 'tp'), may hold values from -6 to 6
- new_value: bfloat16 [8, 512], P('seq', 'tp'), may hold values from -6 to 6
- cache_keys: bfloat16 [8, 4096, 512], P('seq', None, 'tp'), may hold values from -6 to 6
- cache_values: bfloat16 [8, 4096, 512], P('seq', None, 'tp'), may hold values from -6 to 6
- cache_length: int32 [8], P('seq'), may hold values from 1 to 4096, 16384 in all
- dealing: int32 [8], replicated, may hold values from 0 to 7, each once
- out_weight: bfloat16 [3584, 3584], P('tp', 'seq'), may hold values from -0.09375 to 0.09375
- stretch_query: bfloat16 [3, 256, 3584], P(None, 'seq', 'tp'), may hold values from -360 to 360
- stretch_key: bfloat16 [3, 256, 512], P(None, 'seq', 'tp'), may hold values from -6 to 6
- stretch_value: bfloat16 [3, 256, 512], P(None, 'seq', 'tp'), may hold values from -6 to 6
- prior_keys: bfloat16 [3, 8192, 512], P(None, 'seq', 'tp'), may hold values from -6 to 6
- prior_values: bfloat16 [3, 8192, 512], P(None, 'seq', 'tp'), may hold values from -6 to 6
- stretch_start: int32 [3], replicated, may hold values from 1 to 8192, 16384 in all
Outputs:
- decode_mixed: bfloat16 [8, 3584], P('tp', 'seq')
- stretch_out: bfloat16 [3, 256, 3584], P(None, 'seq', 'tp')
Inputs may be any that keep to these rules, and one draw needn't show every extreme that they name: dealing[a] is the cache slot of the decode request that arrives a-th; every slot appears once. `cache_length`: cached positions in use of each decode slot; one slot is full. `stretch_start`: cached positions of each stretch's request that precede the stretch; one request's cache is full.
All inputs are finite; a program needn't handle non-finite values. No bound on the sum of `cache_length` on one device may be relied on, other than what follows from the above.
Results may differ from a plain program's by a relative error of at most 0.0051.
Values may be sent and summed in bfloat16 or wider, within the bound.
No kernel may reach another device: no remote copies, remote signals or barrier semaphores. Data moves between devices by JAX's collectives and lax.ppermute only.
A program may use at most 64 MiB of HBM per device.

v0:
```python
import math

import jax
import jax.numpy as jnp
from jax import lax
from jax.sharding import PartitionSpec as P

NEG_FILL = -1e30


def partial_attend(queries, keys, values, visible):
    factor = 1.0 / math.sqrt(queries.shape[-1])
    scores = jnp.dot(queries, keys.T, preferred_element_type=jnp.float32) * factor
    scores = jnp.where(visible, scores, NEG_FILL)
    row_top = jnp.max(scores, axis=1)
    weights = jnp.where(visible, jnp.exp(scores - row_top[:, None]), 0.0)
    weight_sum = jnp.sum(weights, axis=1)
    numerator = jnp.dot(weights.astype(jnp.bfloat16), values, preferred_element_type=jnp.float32)
    return (row_top, weight_sum, numerator)


def body(
    new_query,
    new_key,
    new_value,
    cache_keys,
    cache_values,
    cache_length,
    dealing,
    out_weight,
    stretch_query,
    stretch_key,
    stretch_value,
    prior_keys,
    prior_values,
    stretch_start,
):
    head_size = cache_keys.shape[2]
    group_size = new_query.shape[1] // head_size
    local_dec = new_query.shape[0]
    seq_rank = lax.axis_index("seq")
    seq_count = lax.axis_size("seq")
    total_dec = local_dec * seq_count
    every_query, every_key, every_value = (
        lax.all_gather(new_query, "seq", axis=0, tiled=True),
        lax.all_gather(new_key, "seq", axis=0, tiled=True),
        lax.all_gather(new_value, "seq", axis=0, tiled=True),
    )
    slot_ids = seq_rank * local_dec + jnp.arange(local_dec, dtype=jnp.int32)
    arrival_ids = jnp.arange(total_dec, dtype=jnp.int32)
    sources = jnp.sum(
        jnp.where(dealing[None, :] == slot_ids[:, None], arrival_ids[None, :], 0), axis=1
    )
    home_query = jnp.take(every_query, sources, axis=0)
    home_key = jnp.take(every_key, sources, axis=0)
    home_value = jnp.take(every_value, sources, axis=0)
    cache_span = cache_keys.shape[1]
    cache_pos = jnp.arange(cache_span, dtype=jnp.int32)

    def decode_slot(query_row, own_key, own_value, cached_keys, cached_values, length):
        key_all = jnp.concatenate([cached_keys, own_key[None, :]], axis=0)
        value_all = jnp.concatenate([cached_values, own_value[None, :]], axis=0)
        visible = jnp.concatenate([cache_pos < length, jnp.ones((1,), dtype=jnp.bool_)])
        visible = jnp.broadcast_to(visible[None, :], (group_size, cache_span + 1))
        row_top, weight_sum, numerator = partial_attend(
            query_row.reshape(group_size, head_size), key_all, value_all, visible
        )
        return (
            (numerator / weight_sum[:, None]).astype(jnp.bfloat16).reshape(group_size * head_size)
        )

    home_out = jax.vmap(decode_slot)(
        home_query, home_key, home_value, cache_keys, cache_values, cache_length
    )
    stored_terms = jnp.dot(
        lax.all_gather(home_out, "seq", axis=0, tiled=True),
        out_weight,
        preferred_element_type=jnp.float32,
    )
    arrival_terms = jnp.take(stored_terms, dealing, axis=0)
    decode_mixed = lax.psum_scatter(arrival_terms, "tp", scatter_dimension=0, tiled=True).astype(
        jnp.bfloat16
    )
    stretch_count, local_tok, _ = stretch_query.shape
    stretch_len = local_tok * seq_count
    prior_span = prior_keys.shape[1]
    row_count = stretch_len * group_size
    every_stretch_key, every_stretch_value = (
        lax.all_gather(stretch_key, "seq", axis=1, tiled=True),
        lax.all_gather(stretch_value, "seq", axis=1, tiled=True),
    )
    gathered_query = lax.all_gather(stretch_query, "seq", axis=1, tiled=True)
    prior_pos = seq_rank * prior_span + jnp.arange(prior_span, dtype=jnp.int32)
    peak_list, total_list, numer_list = ([], [], [])
    for stretch_index in range(stretch_count):
        queries_all = gathered_query[stretch_index].reshape(row_count, head_size)
        prior_visible = jnp.broadcast_to(
            (prior_pos < stretch_start[stretch_index])[None, :], (row_count, prior_span)
        )

        def work_part():
            return partial_attend(
                queries_all, prior_keys[stretch_index], prior_values[stretch_index], prior_visible
            )

        def skip_part():
            return (
                jnp.full((row_count,), NEG_FILL, jnp.float32),
                jnp.zeros((row_count,), jnp.float32),
                jnp.zeros((row_count, head_size), jnp.float32),
            )

        pieces = lax.cond(
            seq_rank * prior_span < stretch_start[stretch_index], work_part, skip_part
        )
        peak_list.append(pieces[0].reshape(stretch_len, group_size))
        total_list.append(pieces[1].reshape(stretch_len, group_size))
        numer_list.append(pieces[2].reshape(stretch_len, group_size, head_size))
    part_top = jnp.stack(peak_list)
    part_sum = jnp.stack(total_list)
    part_num = jnp.stack(numer_list)
    peak_all = lax.pmax(part_top, "seq")
    factor = jnp.exp(part_top - peak_all)
    got_sum, got_num = (
        lax.psum_scatter(part_sum * factor, "seq", scatter_dimension=1, tiled=True),
        lax.psum_scatter(part_num * factor[..., None], "seq", scatter_dimension=1, tiled=True),
    )
    got_top = lax.dynamic_slice_in_dim(peak_all, seq_rank * local_tok, local_tok, 1)
    local_rows = local_tok * group_size
    stretch_pos = jnp.arange(stretch_len, dtype=jnp.int32)
    own_token = seq_rank * local_tok + jnp.arange(local_rows, dtype=jnp.int32) // group_size
    causal = stretch_pos[None, :] <= own_token[:, None]
    self_tops, self_totals, self_numers = ([], [], [])
    for stretch_index in range(stretch_count):
        local_queries = stretch_query[stretch_index].reshape(local_rows, head_size)
        pieces = partial_attend(
            local_queries,
            every_stretch_key[stretch_index],
            every_stretch_value[stretch_index],
            causal,
        )
        self_tops.append(pieces[0].reshape(local_tok, group_size))
        self_totals.append(pieces[1].reshape(local_tok, group_size))
        self_numers.append(pieces[2].reshape(local_tok, group_size, head_size))
    self_top = jnp.stack(self_tops)
    final_top = jnp.maximum(got_top, self_top)
    first_factor = jnp.exp(got_top - final_top)
    second_factor = jnp.exp(self_top - final_top)
    got_sum = got_sum * first_factor + jnp.stack(self_totals) * second_factor
    got_num = got_num * first_factor[..., None] + jnp.stack(self_numers) * second_factor[..., None]
    stretch_out = (
        (got_num / got_sum[..., None])
        .astype(jnp.bfloat16)
        .reshape(stretch_count, local_tok, group_size * head_size)
    )
    return (decode_mixed, stretch_out)


def solution(mesh):
    return jax.shard_map(
        body,
        mesh=mesh,
        in_specs=(
            P("seq", "tp"),
            P("seq", "tp"),
            P("seq", "tp"),
            P("seq", None, "tp"),
            P("seq", None, "tp"),
            P("seq"),
            P(),
            P("tp", "seq"),
            P(None, "seq", "tp"),
            P(None, "seq", "tp"),
            P(None, "seq", "tp"),
            P(None, "seq", "tp"),
            P(None, "seq", "tp"),
            P(),
        ),
        out_specs=(P("tp", "seq"), P(None, "seq", "tp")),
        check_vma=False,
    )
```

profile of v0, /device:TPU:0, one launch (start us, length us, event | category | flops | bytes accessed | tf_op | source)
XLA Modules:
  0.0 355.2 jit_solution(8637244430150871322)
XLA Ops:
  11.4 43.9 %all-gather.6.cloned.1.call-done = bf16[3,256,896]{2,1,0:T(8,128)(2,1)} async-done(((bf16[3,32,896]{2,1,0:T(8,128)(2,1)}), bf16[3,256,896]{2,1,0:T(8,128)(2,1)}) %all-gather.6.cloned.1.call-update) | async-done | bytes 1376272 | tf_op jit(solution)/shard_map/all_gather | solution.py:92
  55.3 21.5 %conditional.3 = (f32[1,256,7,128]{3,1,2,0:T(8,128)S(1)}, f32[1,256,7]{1,2,0:T(8,128)S(1)}, f32[1,256,7]{1,2,0:T(8,128)S(1)}) conditional(s32[]{:T(128)} %convert_element_type.44, () %tuple.51, (bf16[3,1024,128]{2,1,0:T(8,128)(2,1)}, bf16[3,256,896]{2,1,0:T(8,128)(2,1)}, s32[1024]{0:T(1024)S(1)}, bf16[3,1024,128]{2,1,0:T(8,128)(2,1)}, s32[]{:T(128)}) %tuple.52), branch_computations={%region_4.6_spmd, %region_5.9_spmd} | conditional | flops 956036608 | bytes 33706012 | solution.py:113
  59.6 3.8 %fusion.2 = (f32[1792]{0:T(1024)S(1)}, bf16[1792,1024]{1,0:T(8,128)(2,1)}) fusion(f32[1792,1024]{1,0:T(8,128)S(1)} %get-tuple-element.123, f32[1792]{0:T(1024)S(1)} %get-tuple-element.122, pred[1024]{0:T(1024)(128)(4,1)S(1)} %broadcast_compare_fusion), kind=kLoop, calls=%fused_computation.5 | loop fusion | flops 11008256 | bytes 11025408 | tf_op jit(solution)/shard_map/cond/branch_1_fun/reduce_sum | solution.py:17
  63.5 6.4 %reshape.159 = bf16[256,7,1024]{2,1,0:T(8,128)(2,1)} reshape(bf16[1792,1024]{1,0:T(8,128)(2,1)} %get-tuple-element.121) | data formatting | bytes 7340032 | tf_op jit(solution)/shard_map/reshape.122
  69.9 6.3 %fusion.5 = f32[1,256,7,128]{3,1,2,0:T(8,128)S(1)} fusion(bf16[256,7,1024]{2,1,0:T(8,128)(2,1)} %reshape.159, bf16[3,1024,128]{2,1,0:T(8,128)(2,1)} %get-tuple-element.37), kind=kOutput, calls=%fused_computation.8 | convolution fusion | flops 469762048 | bytes 5373952 | tf_op jit(solution)/shard_map/cond/branch_1_fun/dot_general | solution.py:18
  77.4 21.5 %conditional.4 = (f32[1,256,7,128]{3,1,2,0:T(8,128)S(1)}, f32[1,256,7]{1,2,0:T(8,128)S(1)}, f32[1,256,7]{1,2,0:T(8,128)S(1)}) conditional(s32[]{:T(128)} %convert_element_type.45, () %tuple.53, (bf16[3,1024,128]{2,1,0:T(8,128)(2,1)}, bf16[3,256,896]{2,1,0:T(8,128)(2,1)}, s32[1024]{0:T(1024)S(1)}, bf16[3,1024,128]{2,1,0:T(8,128)(2,1)}, ...), branch_computations={%region_8.10_spmd, %region_9.13_spmd} | conditional | flops 956036608 | bytes 33706012 | solution.py:113
  79.6 2.2 fusion.13
  81.8 3.9 %fusion.15 = (f32[1792]{0:T(1024)S(1)}, bf16[1792,1024]{1,0:T(8,128)(2,1)}) fusion(f32[1792,1024]{1,0:T(8,128)S(1)} %get-tuple-element.127, f32[1792]{0:T(1024)S(1)} %get-tuple-element.126, pred[1024]{0:T(1024)(128)(4,1)S(1)} %broadcast_compare_fusion.1), kind=kLoop, calls=%fused_computation.19 | loop fusion | flops 11008256 | bytes 11025408 | tf_op jit(solution)/shard_map/cond/branch_1_fun/reduce_sum | solution.py:17
  85.6 6.4 %reshape.160 = bf16[256,7,1024]{2,1,0:T(8,128)(2,1)} reshape(bf16[1792,1024]{1,0:T(8,128)(2,1)} %get-tuple-element.125) | data formatting | bytes 7340032 | tf_op jit(solution)/shard_map/reshape.125
  92.1 6.3 %fusion.18 = f32[1,256,7,128]{3,1,2,0:T(8,128)S(1)} fusion(bf16[256,7,1024]{2,1,0:T(8,128)(2,1)} %reshape.160, bf16[3,1024,128]{2,1,0:T(8,128)(2,1)} %get-tuple-element.41), kind=kOutput, calls=%fused_computation.22 | convolution fusion | flops 469762048 | bytes 5373952 | tf_op jit(solution)/shard_map/cond/branch_1_fun/dot_general | solution.py:18
  99.6 23.7 %conditional.5 = (f32[1,256,7,128]{3,1,2,0:T(8,128)}, f32[1,256,7]{1,2,0:T(8,128)}, f32[1,256,7]{1,2,0:T(8,128)S(1)}) conditional(s32[]{:T(128)} %convert_element_type.46, () %tuple.55, (bf16[3,1024,128]{2,1,0:T(8,128)(2,1)}, bf16[3,256,896]{2,1,0:T(8,128)(2,1)}, s32[1024]{0:T(1024)S(1)}, bf16[3,1024,128]{2,1,0:T(8,128)(2,1)}, s32[]{:T(128)}) %tuple.56), branch_computations={%region_12.14_spmd, %region_13.17_spmd} | conditional | flops 956036608 | bytes 33710136 | solution.py:113
  102.4 2.2 fusion.26
  104.6 3.8 %fusion.28 = (f32[1792]{0:T(1024)S(1)}, bf16[1792,1024]{1,0:T(8,128)(2,1)}) fusion(f32[1792,1024]{1,0:T(8,128)S(1)} %get-tuple-element.131, f32[1792]{0:T(1024)S(1)} %get-tuple-element.130, pred[1024]{0:T(1024)(128)(4,1)S(1)} %copy-done.7), kind=kLoop, calls=%fused_computation.33 | loop fusion | flops 11008256 | bytes 11025408 | tf_op jit(solution)/shard_map/cond/branch_1_fun/reduce_sum | solution.py:17
  108.4 6.4 %reshape.161 = bf16[256,7,1024]{2,1,0:T(8,128)(2,1)} reshape(bf16[1792,1024]{1,0:T(8,128)(2,1)} %get-tuple-element.129) | data formatting | bytes 7340032 | tf_op jit(solution)/shard_map/reshape.128
  114.9 7.2 %fusion.31 = f32[1,256,7,128]{3,1,2,0:T(8,128)} fusion(bf16[256,7,1024]{2,1,0:T(8,128)(2,1)} %reshape.161, bf16[3,1024,128]{2,1,0:T(8,128)(2,1)} %get-tuple-element.45), kind=kOutput, calls=%fused_computation.36 | convolution fusion | flops 469762048 | bytes 5373952 | tf_op jit(solution)/shard_map/cond/branch_1_fun/dot_general | solution.py:18
  124.6 34.1 %pmax.7 = f32[3,256,7]{1,2,0:T(8,128)S(1)} all-reduce(f32[3,256,7]{1,2,0:T(8,128)} %constant_dynamic-update-slice_fusion), channel_id=1, replica_groups=mesh['seq'=8,'tp'=4] {'seq'}, use_global_device_ids=true, to_apply=%region_16.18 | all-reduce | flops 5376 | bytes 43008 | tf_op jit(solution)/shard_map/pmax | solution.py:122
  162.5 3.0 maximum_multiply_fusion
  165.9 30.6 %all_gather.26 = bf16[3,256,128]{2,1,0:T(8,128)(2,1)S(1)} all-gather(bf16[3,32,128]{2,1,0:T(8,128)(2,1)S(1)} %copy-done.5), channel_id=1, replica_groups=mesh['seq'=8,'tp'=4] {'seq'}, dimensions={1}, use_global_device_ids=true | all-gather | bytes 221184 | tf_op jit(solution)/shard_map/all_gather | solution.py:89
  201.6 16.2 %all-gather.1 = bf16[8,1,128]{2,1,0:T(2,128)(2,1)S(1)} all-gather(bf16[1,1,128]{2,1,0:T(2,128)(2,1)S(1)} %bitcast.128), channel_id=1, replica_groups=mesh['seq'=8,'tp'=4] {'seq'}, dimensions={0}, use_global_device_ids=true | all-gather | bytes 2304 | tf_op jit(solution)/shard_map/all_gather | solution.py:46
  218.5 18.1 %all-gather.2 = bf16[8,1,128]{2,1,0:T(2,128)(2,1)S(1)} all-gather(bf16[1,1,128]{2,1,0:T(2,128)(2,1)S(1)} %bitcast.129), channel_id=1, replica_groups=mesh['seq'=8,'tp'=4] {'seq'}, dimensions={0}, use_global_device_ids=true | all-gather | bytes 2304 | tf_op jit(solution)/shard_map/all_gather | solution.py:47
  236.6 30.7 %all-gather = bf16[8,1,896]{2,1,0:T(2,128)(2,1)S(1)} all-gather(bf16[1,1,896]{2,1,0:T(2,128)(2,1)S(1)} %bitcast.125), channel_id=1, replica_groups=mesh['seq'=8,'tp'=4] {'seq'}, dimensions={0}, use_global_device_ids=true | all-gather | bytes 16128 | tf_op jit(solution)/shard_map/all_gather | solution.py:45
  271.0 30.4 %all-gather.3 = bf16[8,1,896]{2,1,0:T(2,128)(2,1)S(1)} all-gather(bf16[1,1,896]{2,1,0:T(2,128)(2,1)S(1)} %reshape.252), channel_id=1, replica_groups=mesh['seq'=8,'tp'=4] {'seq'}, dimensions={0}, use_global_device_ids=true | all-gather | bytes 16128 | tf_op jit(solution)/shard_map/all_gather | solution.py:76
  303.7 10.1 %all-reduce = bf16[8,448]{1,0:T(8,128)(2,1)S(1)} all-reduce(f32[8,448]{1,0:T(8,128)S(1)} %broadcast_select_fusion), channel_id=2, replica_groups=mesh['seq'=8,'tp'=4] {'tp'}, use_global_device_ids=true, to_apply=%region_3.5.clone | all-reduce | flops 3584 | bytes 21504
  313.9 30.6 %all_gather.27 = bf16[3,256,128]{2,1,0:T(8,128)(2,1)S(1)} all-gather(bf16[3,32,128]{2,1,0:T(8,128)(2,1)S(1)} %copy-done.6), channel_id=1, replica_groups=mesh['seq'=8,'tp'=4] {'seq'}, dimensions={1}, use_global_device_ids=true | all-gather | bytes 221184 | tf_op jit(solution)/shard_map/all_gather | solution.py:90
  (114 shorter events, 32.8 us)
Async XLA Ops:
  7.2 294.3 %copy-start = (bf16[896,448]{0,1:T(8,128)(2,1)S(1)}, bf16[896,448]{0,1:T(8,128)(2,1)}, u32[]{:S(2)}) copy-start(bf16[896,448]{0,1:T(8,128)(2,1)} %param.29) | copy-start | bytes 2408452
  7.2 48.1 %all-gather.6.cloned.1.call-start = ((), (), s32[]{:S(2)}) async-start(), calls=%async_computation.2 | async-start | bytes 1548288 | tf_op jit(solution)/shard_map/all_gather | solution.py:92
  7.9 337.7 %reduce-scatter.7.cloned.1.call-start = ((), (), s32[]{:S(2)}) async-start(), calls=%async_computation.4 | async-start | bytes 147456
  76.8 0.6 copy-start.3
  98.9 0.6 copy-start.4
  98.9 0.6 copy-start.2
  102.3 2.2 copy-start.7
  162.4 3.2 copy-start.1
  162.4 184.2 %reduce-scatter.5.cloned.1.call-start = ((), (), s32[]{:S(2)}) async-start(), calls=%async_computation.3 | async-start | bytes 3096576 | tf_op jit(solution)/shard_map/reduce_scatter | solution.py:126
  162.4 3.4 copy-start.5
  165.5 33.5 %copy-start.11 = (s32[8]{0:T(128)S(1)}, s32[8]{0:T(128)}, u32[]{:S(2)}) copy-start(s32[8]{0:T(128)} %param.28) | copy-start | bytes 100
  165.5 36.1 %copy-start.9 = (bf16[1,128]{1,0:T(2,128)(2,1)S(1)}, bf16[1,128]{1,0:T(2,128)(2,1)}, u32[]{:S(2)}) copy-start(bf16[1,128]{1,0:T(2,128)(2,1)} %param.23) | copy-start | bytes 772
  165.5 53.0 %copy-start.10 = (bf16[1,128]{1,0:T(2,128)(2,1)S(1)}, bf16[1,128]{1,0:T(2,128)(2,1)}, u32[]{:S(2)}) copy-start(bf16[1,128]{1,0:T(2,128)(2,1)} %param.24) | copy-start | bytes 772
  165.5 71.1 %copy-start.8 = (bf16[1,896]{1,0:T(2,128)(2,1)S(1)}, bf16[1,896]{1,0:T(2,128)(2,1)}, u32[]{:S(2)}) copy-start(bf16[1,896]{1,0:T(2,128)(2,1)} %param.22) | copy-start | bytes 5380
  165.6 136.8 %copy-start.12 = (u32[32]{0:T(128)S(1)}, u32[32]{0:T(128)}, u32[]{:S(2)}) copy-start(u32[32]{0:T(128)} %constant.174) | copy-start | bytes 388
  165.7 148.2 %copy-start.6 = (bf16[3,32,128]{2,1,0:T(8,128)(2,1)S(1)}, bf16[3,32,128]{2,1,0:T(8,128)(2,1)}, u32[]{:S(2)}) copy-start(bf16[3,32,128]{2,1,0:T(8,128)(2,1)} %param.32) | copy-start | bytes 73732
Sparse Core Ops, SparseCore 0:
  10.2 45.0 all-gather.5
  162.5 58.1 reduce-scatter.6
  224.3 70.5 reduce-scatter.4
where the time goes:
time: 357 us; the launch traced here: 355 us
  blocking collectives  201 us (56%)
  waiting for transfers between devices  44.6 us (12%)
  local copies, waits for them, and re-layouts  37.3 us (10%)
  matrix products  31.3 us (9%)
  other arithmetic  21.5 us (6%)
  between operations  19.3 us (5%)
    all_gather x1, waiting for transfers between devices, body(): gathered_query = lax.all_gather(stretch_query, 'seq', axis=1, tiled=True)  43.9 us
    pmax x1, blocking collectives, body(): peak_all = lax.pmax(part_top, 'seq')  34.1 us
    all_gather x1, blocking collectives, body(): lax.all_gather(new_query, 'seq', axis=0, tiled=True)  30.7 us
    all_gather x1, blocking collectives, body(): lax.all_gather(stretch_key, 'seq', axis=1, tiled=True)  30.6 us
    all_gather x1, blocking collectives, body(): lax.all_gather(stretch_value, 'seq', axis=1, tiled=True)  30.6 us
    all_gather x1, blocking collectives, body(): lax.all_gather(home_out, 'seq', axis=0, tiled=True)  30.4 us
    dot_general x7, matrix products, partial_attend(): jnp.dot(weights.astype(jnp.bfloat16), values, preferred_element_type=jnp....  21.8 us
    another operation x6, local copies, waits for them, and re-layouts  19.5 us
  transfers between devices with their start and end apart: 3, of which 1 were waited for; matrix products, arithmetic and copies ran while one was open for 4% of the time, Pallas kernels for 0%

commit v1 on v0

--- a/solution.py
+++ b/solution.py
@@ -41,11 +41,22 @@
     seq_rank = lax.axis_index("seq")
     seq_count = lax.axis_size("seq")
     total_dec = local_dec * seq_count
-    every_query, every_key, every_value = (
-        lax.all_gather(new_query, "seq", axis=0, tiled=True),
-        lax.all_gather(new_key, "seq", axis=0, tiled=True),
-        lax.all_gather(new_value, "seq", axis=0, tiled=True),
-    )
+    stretch_count, local_tok, query_width = stretch_query.shape
+    key_width = stretch_key.shape[2]
+    stretch_rows = stretch_count * local_tok
+
+    stretch_pack = jnp.concatenate([stretch_query, stretch_key, stretch_value], axis=2).reshape(
+        stretch_rows, query_width + 2 * key_width
+    )
+    decode_pack = jnp.concatenate([new_query, new_key, new_value], axis=1)
+    gathered = lax.all_gather(
+        jnp.concatenate([stretch_pack, decode_pack], axis=0), "seq", axis=0, tiled=False
+    )
+
+    decode_part = gathered[:, stretch_rows:, :].reshape(total_dec, query_width + 2 * key_width)
+    every_query = decode_part[:, :query_width]
+    every_key = decode_part[:, query_width : query_width + key_width]
+    every_value = decode_part[:, query_width + key_width :]
     slot_ids = seq_rank * local_dec + jnp.arange(local_dec, dtype=jnp.int32)
     arrival_ids = jnp.arange(total_dec, dtype=jnp.int32)
     sources = jnp.sum(
@@ -72,28 +83,17 @@
     home_out = jax.vmap(decode_slot)(
         home_query, home_key, home_value, cache_keys, cache_values, cache_length
     )
-    stored_terms = jnp.dot(
-        lax.all_gather(home_out, "seq", axis=0, tiled=True),
-        out_weight,
-        preferred_element_type=jnp.float32,
-    )
-    arrival_terms = jnp.take(stored_terms, dealing, axis=0)
-    decode_mixed = lax.psum_scatter(arrival_terms, "tp", scatter_dimension=0, tiled=True).astype(
-        jnp.bfloat16
-    )
-    stretch_count, local_tok, _ = stretch_query.shape
-    stretch_len = local_tok * seq_count
+
     prior_span = prior_keys.shape[1]
-    row_count = stretch_len * group_size
-    every_stretch_key, every_stretch_value = (
-        lax.all_gather(stretch_key, "seq", axis=1, tiled=True),
-        lax.all_gather(stretch_value, "seq", axis=1, tiled=True),
-    )
-    gathered_query = lax.all_gather(stretch_query, "seq", axis=1, tiled=True)
+    rows_per_src = local_tok * group_size
+    row_count = seq_count * rows_per_src
     prior_pos = seq_rank * prior_span + jnp.arange(prior_span, dtype=jnp.int32)
-    peak_list, total_list, numer_list = ([], [], [])
+    stretch_part = gathered[:, :stretch_rows, :].reshape(
+        seq_count, stretch_count, local_tok, query_width + 2 * key_width
+    )
+    numer_list, total_list, peak_list = ([], [], [])
     for stretch_index in range(stretch_count):
-        queries_all = gathered_query[stretch_index].reshape(row_count, head_size)
+        queries_all = stretch_part[:, stretch_index, :, :query_width].reshape(row_count, head_size)
         prior_visible = jnp.broadcast_to(
             (prior_pos < stretch_start[stretch_index])[None, :], (row_count, prior_span)
         )
@@ -113,19 +113,44 @@
         pieces = lax.cond(
             seq_rank * prior_span < stretch_start[stretch_index], work_part, skip_part
         )
-        peak_list.append(pieces[0].reshape(stretch_len, group_size))
-        total_list.append(pieces[1].reshape(stretch_len, group_size))
-        numer_list.append(pieces[2].reshape(stretch_len, group_size, head_size))
-    part_top = jnp.stack(peak_list)
-    part_sum = jnp.stack(total_list)
-    part_num = jnp.stack(numer_list)
-    peak_all = lax.pmax(part_top, "seq")
-    factor = jnp.exp(part_top - peak_all)
-    got_sum, got_num = (
-        lax.psum_scatter(part_sum * factor, "seq", scatter_dimension=1, tiled=True),
-        lax.psum_scatter(part_num * factor[..., None], "seq", scatter_dimension=1, tiled=True),
-    )
-    got_top = lax.dynamic_slice_in_dim(peak_all, seq_rank * local_tok, local_tok, 1)
+        peak_list.append(pieces[0].reshape(seq_count, rows_per_src))
+        total_list.append(pieces[1].reshape(seq_count, rows_per_src))
+        numer_list.append(pieces[2].reshape(seq_count, rows_per_src * head_size))
+
+    dec_width = local_dec * group_size * head_size
+    payload = jnp.concatenate(
+        numer_list
+        + total_list
+        + peak_list
+        + [
+            jnp.broadcast_to(
+                home_out.reshape(1, dec_width).astype(jnp.float32), (seq_count, dec_width)
+            )
+        ],
+        axis=1,
+    )
+    received = lax.all_to_all(payload, "seq", 0, 0, tiled=True)
+    numer_width = stretch_count * rows_per_src * head_size
+    got_num = received[:, :numer_width].reshape(seq_count, stretch_count, local_tok, group_size, head_size)
+    got_sum = received[:, numer_width : numer_width + stretch_count * rows_per_src].reshape(
+        seq_count, stretch_count, local_tok, group_size
+    )
+    got_top = received[
+        :, numer_width + stretch_count * rows_per_src : numer_width + 2 * stretch_count * rows_per_src
+    ].reshape(seq_count, stretch_count, local_tok, group_size)
+    all_out = (
+        received[:, numer_width + 2 * stretch_count * rows_per_src :]
+        .reshape(total_dec, group_size * head_size)
+        .astype(jnp.bfloat16)
+    )
+
+    arrival_out = jnp.take(all_out, dealing, axis=0)
+    arrival_terms = jnp.dot(arrival_out, out_weight, preferred_element_type=jnp.float32)
+    decode_mixed = lax.psum_scatter(arrival_terms, "tp", scatter_dimension=0, tiled=True).astype(
+        jnp.bfloat16
+    )
+
+    stretch_len = local_tok * seq_count
     local_rows = local_tok * group_size
     stretch_pos = jnp.arange(stretch_len, dtype=jnp.int32)
     own_token = seq_rank * local_tok + jnp.arange(local_rows, dtype=jnp.int32) // group_size
@@ -133,23 +158,28 @@
     self_tops, self_totals, self_numers = ([], [], [])
     for stretch_index in range(stretch_count):
         local_queries = stretch_query[stretch_index].reshape(local_rows, head_size)
-        pieces = partial_attend(
-            local_queries,
-            every_stretch_key[stretch_index],
-            every_stretch_value[stretch_index],
-            causal,
-        )
+        keys_all = stretch_part[:, stretch_index, :, query_width : query_width + key_width].reshape(
+            stretch_len, key_width
+        )
+        values_all = stretch_part[:, stretch_index, :, query_width + key_width :].reshape(
+            stretch_len, key_width
+        )
+        pieces = partial_attend(local_queries, keys_all, values_all, causal)
         self_tops.append(pieces[0].reshape(local_tok, group_size))
         self_totals.append(pieces[1].reshape(local_tok, group_size))
         self_numers.append(pieces[2].reshape(local_tok, group_size, head_size))
     self_top = jnp.stack(self_tops)
-    final_top = jnp.maximum(got_top, self_top)
-    first_factor = jnp.exp(got_top - final_top)
-    second_factor = jnp.exp(self_top - final_top)
-    got_sum = got_sum * first_factor + jnp.stack(self_totals) * second_factor
-    got_num = got_num * first_factor[..., None] + jnp.stack(self_numers) * second_factor[..., None]
+    self_sum = jnp.stack(self_totals)
+    self_num = jnp.stack(self_numers)
+    final_top = jnp.maximum(jnp.max(got_top, axis=0), self_top)
+    part_factor = jnp.exp(got_top - final_top[None])
+    self_factor = jnp.exp(self_top - final_top)
+    total_sum = jnp.sum(got_sum * part_factor, axis=0) + self_sum * self_factor
+    total_num = (
+        jnp.sum(got_num * part_factor[..., None], axis=0) + self_num * self_factor[..., None]
+    )
     stretch_out = (
-        (got_num / got_sum[..., None])
+        (total_num / total_sum[..., None])
         .astype(jnp.bfloat16)
         .reshape(stretch_count, local_tok, group_size * head_size)
     )

time: 357 us -> 219 us (0.61)
  blocking collectives: 201 us -> 10.2 us
  waiting for transfers between devices: 44.6 us -> 101 us
  matrix products: 31.3 us -> 24.3 us
  starting transfers between devices: 0.12 us -> 4.45 us
    all_gather x6 -> x0, blocking collectives: 157 us -> none  [the longest x1 30.7 us: body(): lax.all_gather(new_query, 'seq', axis=0, tiled=True)]
    all_to_all x0 -> x1, waiting for transfers between devices: none -> 58 us  [body(): received = lax.all_to_all(payload, 'seq', 0, 0, tiled=True)]
    pmax x1 -> x0, blocking collectives: 34.1 us -> none  [body(): peak_all = lax.pmax(part_top, 'seq')]
    another operation x22 -> x12, local copies, waits for them, and re-layouts: 24 us -> 1.88 us  [the longest x3 1.36 us: body(): stretch_part[:, stretch_index, :, :query_width]]
    unnamed x34 -> x30, local copies, waits for them, and re-layouts: 5.72 us -> 15.6 us
    dot_general x7, matrix products: 21.8 us -> 14.9 us  [partial_attend(): jnp.dot(weights.astype(jnp.bfloat16), values, preferred_element_type=jnp....]
    all_to_all x0 -> x1, local copies, waits for them, and re-layouts: none -> 5.36 us  [body(): received = lax.all_to_all(payload, 'seq', 0, 0, tiled=True)]
    reshape x0 -> x10, local copies, waits for them, and re-layouts: none -> 4.77 us  [the longest x3 4.04 us: body(): numer_list.append(pieces[2].reshape(seq_count, rows_per_src * head_size))]
  transfers between devices with their start and end apart: 3 -> 2, of which waited for: 1 -> 2; matrix products, arithmetic and copies ran while one was open for 4% -> 3% of each run, Pallas kernels for 0% -> 0%
where the time goes in v1:
time: 219 us; the launch traced here: 218 us
  waiting for transfers between devices  101 us (46%)
  local copies, waits for them, and re-layouts  38 us (17%)
  matrix products  24.3 us (11%)
  other arithmetic  19.9 us (9%)
  between operations  19.7 us (9%)
  blocking collectives  10.2 us (5%)
  starting transfers between devices  4.45 us (2%)
    all_to_all x1, waiting for transfers between devices, body(): received = lax.all_to_all(payload, 'seq', 0, 0, tiled=True)  58 us
    all_gather x1, waiting for transfers between devices, body(): lax.all_gather(jnp.concatenate([stretch_pack, decode_pack], axis=0), 'seq...  43 us
    unnamed x30, local copies, waits for them, and re-layouts  15.6 us
    dot_general x7, matrix products, partial_attend(): jnp.dot(weights.astype(jnp.bfloat16), values, preferred_element_type=jnp....  14.9 us
    unnamed x1, blocking collectives  10.2 us
    dot_general x7, matrix products, partial_attend(): jnp.dot(queries, keys.T, preferred_element_type=jnp.float32) * factor  9.1 us
    reduce_sum x5, other arithmetic, partial_attend(): weight_sum = jnp.sum(weights, axis=1)  9.02 us
    all_to_all x1, local copies, waits for them, and re-layouts, body(): received = lax.all_to_all(payload, 'seq', 0, 0, tiled=True)  5.36 us
  transfers between devices with their start and end apart: 2, of which 2 were waited for; matrix products, arithmetic and copies ran while one was open for 3% of the time, Pallas kernels for 0%

profile of v1, /device:TPU:0, one launch (start us, length us, event | category | flops | bytes accessed | tf_op | source)
XLA Modules:
  0.0 217.8 jit_solution(518809278993771897)
XLA Ops:
  17.0 43.0 %all-gather.4.cloned.1.call-done = bf16[8,97,1152]{2,1,0:T(8,128)(2,1)} async-done(((bf16[1,97,1152]{2,1,0:T(8,128)(2,1)}), bf16[8,97,1152]{2,1,0:T(8,128)(2,1)}) %all-gather.4.cloned.1.call-update) | async-done | bytes 1787920 | tf_op jit(solution)/shard_map/all_gather | solution.py:52
  60.0 1.6 slice.137
  62.6 11.8 %conditional.3 = (f32[8,224]{1,0:T(8,128)S(1)}, f32[8,224]{1,0:T(8,128)S(1)}, f32[8,28672]{1,0:T(8,128)S(1)}) conditional(s32[]{:T(128)} %convert_element_type.54, () %tuple.51, (bf16[3,1024,128]{2,1,0:T(8,128)(2,1)}, bf16[8,3,32,1152]{3,2,1,0:T(8,128)(2,1)S(1)}, s32[1024]{0:T(1024)S(1)}, bf16[3,1024,128]{2,1,0:T(8,128)(2,1)}, s32[]{:T(128)}) %tuple.103), branch_computations={%region_0.1_spmd, %region_1.0_spmd} | conditional | flops 963376640 | bytes 27656220 | solution.py:113
  63.8 2.2 %fusion = (f32[1792]{0:T(1024)S(1)}, f32[1792,1024]{0,1:T(8,128)S(1)}) fusion(pred[1024]{0:T(1024)(128)(4,1)S(1)} %broadcast_compare_fusion, bf16[1792,128]{1,0:T(8,128)(2,1)S(1)} %reshape_squeeze.48, bf16[3,1024,128]{2,1,0:T(8,128)(2,1)} %get-tuple-element.36), kind=kOutput, calls=%fused_computation.3 | convolution fusion | flops 475265280 | bytes 8069120 | tf_op jit(solution)/shard_map/cond/branch_1_fun/dot_general | solution.py:13
  65.9 2.6 %fusion.2 = f32[1792]{0:T(1024)S(1)} fusion(f32[1792,1024]{0,1:T(8,128)S(1)} %get-tuple-element.113, f32[1792]{0:T(1024)S(1)} %get-tuple-element.112, pred[1024]{0:T(1024)(128)(4,1)S(1)} %broadcast_compare_fusion), kind=kLoop, calls=%fused_computation.5 | loop fusion | flops 9173248 | bytes 7355392 | tf_op jit(solution)/shard_map/cond/branch_1_fun/reduce_sum | solution.py:17
  68.6 4.2 %fusion.3 = f32[1792,128]{1,0:T(8,128)} fusion(f32[1792,1024]{0,1:T(8,128)S(1)} %get-tuple-element.113, f32[1792]{0:T(1024)S(1)} %get-tuple-element.112, pred[1024]{0:T(1024)(128)(4,1)S(1)} %broadcast_compare_fusion, bf16[3,1024,128]{2,1,0:T(8,128)(2,1)} %get-tuple-element.37), kind=kOutput, calls=%fused_computation.6 | convolution fusion | flops 478937088 | bytes 8527872 | tf_op jit(solution)/shard_map/cond/branch_1_fun/dot_general | solution.py:18
  75.9 1.7 fusion.99
  78.4 11.7 %conditional.4 = (f32[8,224]{1,0:T(8,128)S(1)}, f32[8,224]{1,0:T(8,128)S(1)}, f32[8,28672]{1,0:T(8,128)S(1)}) conditional(s32[]{:T(128)} %convert_element_type.55, () %tuple.53, (bf16[3,1024,128]{2,1,0:T(8,128)(2,1)}, bf16[8,3,32,1152]{3,2,1,0:T(8,128)(2,1)S(1)}, s32[1024]{0:T(1024)S(1)}, bf16[3,1024,128]{2,1,0:T(8,128)(2,1)}, s32[]{:T(128)}) %tuple.104), branch_computations={%region_4.5_spmd, %region_5.8_spmd} | conditional | flops 963376640 | bytes 27656220 | solution.py:113
  79.5 2.2 %fusion.14 = (f32[1792]{0:T(1024)S(1)}, f32[1792,1024]{0,1:T(8,128)S(1)}) fusion(pred[1024]{0:T(1024)(128)(4,1)S(1)} %broadcast_compare_fusion.1, bf16[1792,128]{1,0:T(8,128)(2,1)S(1)} %reshape_squeeze.49, bf16[3,1024,128]{2,1,0:T(8,128)(2,1)} %get-tuple-element.40), kind=kOutput, calls=%fused_computation.19 | convolution fusion | flops 475265280 | bytes 8069120 | tf_op jit(solution)/shard_map/cond/branch_1_fun/dot_general | solution.py:13
  81.7 2.6 %fusion.16 = f32[1792]{0:T(1024)S(1)} fusion(f32[1792,1024]{0,1:T(8,128)S(1)} %get-tuple-element.115, f32[1792]{0:T(1024)S(1)} %get-tuple-element.114, pred[1024]{0:T(1024)(128)(4,1)S(1)} %broadcast_compare_fusion.1), kind=kLoop, calls=%fused_computation.21 | loop fusion | flops 9173248 | bytes 7355392 | tf_op jit(solution)/shard_map/cond/branch_1_fun/reduce_sum | solution.py:17
  84.3 4.2 %fusion.17 = f32[1792,128]{1,0:T(8,128)} fusion(f32[1792,1024]{0,1:T(8,128)S(1)} %get-tuple-element.115, f32[1792]{0:T(1024)S(1)} %get-tuple-element.114, pred[1024]{0:T(1024)(128)(4,1)S(1)} %broadcast_compare_fusion.1, bf16[3,1024,128]{2,1,0:T(8,128)(2,1)} %get-tuple-element.41), kind=kOutput, calls=%fused_computation.22 | convolution fusion | flops 478937088 | bytes 8527872 | tf_op jit(solution)/shard_map/cond/branch_1_fun/dot_general | solution.py:18
  91.1 11.9 %conditional.5 = (f32[8,224]{1,0:T(8,128)S(1)}, f32[8,224]{1,0:T(8,128)S(1)}, f32[8,28672]{1,0:T(8,128)S(1)}) conditional(s32[]{:T(128)} %convert_element_type.56, () %tuple.55, (bf16[3,1024,128]{2,1,0:T(8,128)(2,1)}, bf16[8,3,32,1152]{3,2,1,0:T(8,128)(2,1)S(1)}, s32[1024]{0:T(1024)S(1)}, bf16[3,1024,128]{2,1,0:T(8,128)(2,1)}, s32[]{:T(128)}) %tuple.105), branch_computations={%region_8.9_spmd, %region_9.12_spmd} | conditional | flops 963376640 | bytes 27656220 | solution.py:113
  92.2 2.2 %fusion.28 = (f32[1792]{0:T(1024)S(1)}, f32[1792,1024]{0,1:T(8,128)S(1)}) fusion(pred[1024]{0:T(1024)(128)(4,1)S(1)} %broadcast_compare_fusion.2, bf16[1792,128]{1,0:T(8,128)(2,1)S(1)} %reshape_squeeze.50, bf16[3,1024,128]{2,1,0:T(8,128)(2,1)} %get-tuple-element.44), kind=kOutput, calls=%fused_computation.35 | convolution fusion | flops 475265280 | bytes 8069120 | tf_op jit(solution)/shard_map/cond/branch_1_fun/dot_general | solution.py:13
  94.4 2.6 %fusion.30 = f32[1792]{0:T(1024)S(1)} fusion(f32[1792,1024]{0,1:T(8,128)S(1)} %get-tuple-element.117, f32[1792]{0:T(1024)S(1)} %get-tuple-element.116, pred[1024]{0:T(1024)(128)(4,1)S(1)} %broadcast_compare_fusion.2), kind=kLoop, calls=%fused_computation.37 | loop fusion | flops 9173248 | bytes 7355392 | tf_op jit(solution)/shard_map/cond/branch_1_fun/reduce_sum | solution.py:17
  97.1 4.2 %fusion.31 = f32[1792,128]{1,0:T(8,128)} fusion(f32[1792,1024]{0,1:T(8,128)S(1)} %get-tuple-element.117, f32[1792]{0:T(1024)S(1)} %get-tuple-element.116, pred[1024]{0:T(1024)(128)(4,1)S(1)} %broadcast_compare_fusion.2, bf16[3,1024,128]{2,1,0:T(8,128)(2,1)} %get-tuple-element.45), kind=kOutput, calls=%fused_computation.38 | convolution fusion | flops 478937088 | bytes 8527872 | tf_op jit(solution)/shard_map/cond/branch_1_fun/dot_general | solution.py:18
  104.0 1.7 fusion.52
  114.1 1.5 dynamic-update-slice.14
  115.7 5.4 %all_to_all.8 = f32[8,1,88256]{2,1,0:T(1,128)} reshape(f32[8,88256]{1,0:T(8,128)} %dynamic-update-slice.14) | data formatting | bytes 5648384 | tf_op jit(solution)/shard_map/all_to_all | solution.py:132
  121.0 4.4 %all-to-all-start = ((f32[8,1,88256]{2,1,0:T(1,128)}), f32[8,1,88256]{2,1,0:T(1,128)}, u32[]{:S(2)}, u32[]{:S(2)}) async-start(f32[8,1,88256]{2,1,0:T(1,128)} %all_to_all.8), calls=%async_computation | async-start | bytes 5652480 | tf_op jit(solution)/shard_map/all_to_all | solution.py:132
  130.5 58.0 %all-to-all-done = f32[8,1,88256]{2,1,0:T(1,128)} async-done(((f32[8,1,88256]{2,1,0:T(1,128)}), f32[8,1,88256]{2,1,0:T(1,128)}, u32[]{:S(2)}, u32[]{:S(2)}) %all-to-all-start) | async-done | bytes 2824224 | tf_op jit(solution)/shard_map/all_to_all | solution.py:132
  188.5 2.0 copy.74
  190.6 1.5 copy-done.1
  193.1 10.2 %all-reduce = bf16[8,448]{1,0:T(8,128)(2,1)S(1)} all-reduce(f32[8,448]{1,0:T(8,128)S(1)} %fusion.80), channel_id=3, replica_groups=mesh['seq'=8,'tp'=4] {'tp'}, use_global_device_ids=true, to_apply=%region_15.17.clone | all-reduce | flops 3584 | bytes 21504
  206.8 2.7 %fusion.43 = f32[86016]{0:T(1024)S(1)} fusion(f32[8,86016]{1,0:T(8,128)S(1)} %bitcast.119, f32[8,88256]{1,0:T(8,128)} %bitcast.118), kind=kLoop, calls=%fused_computation.53 | loop fusion | flops 1290240 | bytes 5849088 | tf_op jit(solution)/shard_map/reduce_sum | solution.py:179
  (118 shorter events, 37.0 us)
Async XLA Ops:
  7.2 185.6 %copy-start = (bf16[896,448]{0,1:T(8,128)(2,1)S(1)}, bf16[896,448]{0,1:T(8,128)(2,1)}, u32[]{:S(2)}) copy-start(bf16[896,448]{0,1:T(8,128)(2,1)} %param.29) | copy-start | bytes 2408452
  7.2 52.8 %all-gather.4.cloned.1.call-start = ((), (), s32[]{:S(2)}) async-start(), calls=%async_computation.1 | async-start | bytes 2156544 | tf_op jit(solution)/shard_map/all_gather | solution.py:52
  17.0 60.7 %copy-start.4 = (pred[4097]{0:T(1024)(128)(4,1)}, pred[4097]{0:T(1024)(128)(4,1)S(1)}, u32[]{:S(2)}) copy-start(pred[4097]{0:T(1024)(128)(4,1)S(1)} %add_reduce_fusion) | copy-start | bytes 12295
  77.6 0.8 copy-start.5
  77.6 0.8 copy-start.3
  104.0 21.5 %copy-start.2 = (bf16[3,32,896]{2,1,0:T(8,128)(2,1)S(1)}, bf16[3,32,896]{2,1,0:T(8,128)(2,1)}, u32[]{:S(2)}) copy-start(bf16[3,32,896]{2,1,0:T(8,128)(2,1)} %param.30) | copy-start | bytes 516100
  104.0 21.8 %copy-start.7 = (u32[32]{0:T(128)S(1)}, u32[32]{0:T(128)}, u32[]{:S(2)}) copy-start(u32[32]{0:T(128)} %constant.170) | copy-start | bytes 388
  104.0 23.1 %copy-start.6 = (s32[8]{0:T(128)S(1)}, s32[8]{0:T(128)}, u32[]{:S(2)}) copy-start(s32[8]{0:T(128)} %param.28) | copy-start | bytes 100
  121.0 67.5 %all-to-all-start = ((f32[8,1,88256]{2,1,0:T(1,128)}), f32[8,1,88256]{2,1,0:T(1,128)}, u32[]{:S(2)}, u32[]{:S(2)}) async-start(f32[8,1,88256]{2,1,0:T(1,128)} %all_to_all.8), calls=%async_computation | async-start | bytes 5652480 | tf_op jit(solution)/shard_map/all_to_all | solution.py:132
  190.5 1.6 copy-start.1
Sparse Core Ops, SparseCore 0:
  10.2 49.7 all-gather.3

commit v2 on v1

--- a/solution.py
+++ b/solution.py
@@ -91,58 +91,70 @@
     stretch_part = gathered[:, :stretch_rows, :].reshape(
         seq_count, stretch_count, local_tok, query_width + 2 * key_width
     )
-    numer_list, total_list, peak_list = ([], [], [])
-    for stretch_index in range(stretch_count):
-        queries_all = stretch_part[:, stretch_index, :, :query_width].reshape(row_count, head_size)
-        prior_visible = jnp.broadcast_to(
-            (prior_pos < stretch_start[stretch_index])[None, :], (row_count, prior_span)
-        )
-
-        def work_part():
-            return partial_attend(
-                queries_all, prior_keys[stretch_index], prior_values[stretch_index], prior_visible
-            )
-
-        def skip_part():
-            return (
-                jnp.full((row_count,), NEG_FILL, jnp.float32),
-                jnp.zeros((row_count,), jnp.float32),
-                jnp.zeros((row_count, head_size), jnp.float32),
-            )
-
-        pieces = lax.cond(
-            seq_rank * prior_span < stretch_start[stretch_index], work_part, skip_part
-        )
-        peak_list.append(pieces[0].reshape(seq_count, rows_per_src))
-        total_list.append(pieces[1].reshape(seq_count, rows_per_src))
-        numer_list.append(pieces[2].reshape(seq_count, rows_per_src * head_size))
-
-    dec_width = local_dec * group_size * head_size
+    queries_all = (
+        stretch_part[:, :, :, :query_width]
+        .transpose(1, 0, 2, 3)
+        .reshape(stretch_count, row_count, head_size)
+    )
+    factor = 1.0 / math.sqrt(head_size)
+    scores = (
+        jnp.einsum("crd,cpd->crp", queries_all, prior_keys, preferred_element_type=jnp.float32)
+        * factor
+    )
+    prior_visible = (prior_pos[None, :] < stretch_start[:, None])[:, None, :]
+    scores = jnp.where(prior_visible, scores, NEG_FILL)
+    part_top = jnp.max(scores, axis=2)
+    weights = jnp.where(prior_visible, jnp.exp(scores - part_top[..., None]), 0.0)
+    part_sum = jnp.sum(weights, axis=2)
+    part_num = jnp.einsum(
+        "crp,cpd->crd", weights.astype(jnp.bfloat16), prior_values,
+        preferred_element_type=jnp.float32,
+    )
+    safe_sum = jnp.maximum(part_sum, 1.0)
+    part_out = (part_num / safe_sum[..., None]).astype(jnp.bfloat16)
+    part_lse = part_top + jnp.log(safe_sum)
+    lse_hi = lax.reduce_precision(part_lse, exponent_bits=8, mantissa_bits=7)
+    lse_rest = part_lse - lse_hi
+    lse_mid = lax.reduce_precision(lse_rest, exponent_bits=8, mantissa_bits=7)
+    lse_lo = lse_rest - lse_mid
+    stat_count = 3 * stretch_count * rows_per_src
+    stat_rows = -(-stat_count // head_size)
+    stats = (
+        jnp.stack([lse_hi, lse_mid, lse_lo])
+        .reshape(3, stretch_count, seq_count, rows_per_src)
+        .transpose(2, 0, 1, 3)
+        .reshape(seq_count, stat_count)
+    )
+    stats = jnp.pad(stats, ((0, 0), (0, stat_rows * head_size - stat_count))).astype(jnp.bfloat16)
+
+    dec_rows = local_dec * group_size
+    out_rows = stretch_count * rows_per_src
     payload = jnp.concatenate(
-        numer_list
-        + total_list
-        + peak_list
-        + [
+        [
+            part_out.reshape(stretch_count, seq_count, rows_per_src, head_size)
+            .transpose(1, 0, 2, 3)
+            .reshape(seq_count, out_rows, head_size),
+            stats.reshape(seq_count, stat_rows, head_size),
             jnp.broadcast_to(
-                home_out.reshape(1, dec_width).astype(jnp.float32), (seq_count, dec_width)
-            )
+                home_out.reshape(1, dec_rows, head_size), (seq_count, dec_rows, head_size)
+            ),
         ],
         axis=1,
     )
     received = lax.all_to_all(payload, "seq", 0, 0, tiled=True)
-    numer_width = stretch_count * rows_per_src * head_size
-    got_num = received[:, :numer_width].reshape(seq_count, stretch_count, local_tok, group_size, head_size)
-    got_sum = received[:, numer_width : numer_width + stretch_count * rows_per_src].reshape(
-        seq_count, stretch_count, local_tok, group_size
-    )
-    got_top = received[
-        :, numer_width + stretch_count * rows_per_src : numer_width + 2 * stretch_count * rows_per_src
-    ].reshape(seq_count, stretch_count, local_tok, group_size)
-    all_out = (
-        received[:, numer_width + 2 * stretch_count * rows_per_src :]
-        .reshape(total_dec, group_size * head_size)
-        .astype(jnp.bfloat16)
-    )
+    got_out = (
+        received[:, :out_rows, :]
+        .reshape(seq_count, stretch_count, local_tok, group_size, head_size)
+        .astype(jnp.float32)
+    )
+    got_stats = (
+        received[:, out_rows : out_rows + stat_rows, :]
+        .reshape(seq_count, stat_rows * head_size)[:, :stat_count]
+        .astype(jnp.float32)
+        .reshape(seq_count, 3, stretch_count, local_tok, group_size)
+    )
+    got_lse = (got_stats[:, 0] + got_stats[:, 1]) + got_stats[:, 2]
+    all_out = received[:, out_rows + stat_rows :, :].reshape(total_dec, group_size * head_size)
 
     arrival_out = jnp.take(all_out, dealing, axis=0)
     arrival_terms = jnp.dot(arrival_out, out_weight, preferred_element_type=jnp.float32)
@@ -171,12 +183,12 @@
     self_top = jnp.stack(self_tops)
     self_sum = jnp.stack(self_totals)
     self_num = jnp.stack(self_numers)
-    final_top = jnp.maximum(jnp.max(got_top, axis=0), self_top)
-    part_factor = jnp.exp(got_top - final_top[None])
+    final_top = jnp.maximum(jnp.max(got_lse, axis=0), self_top + jnp.log(self_sum))
+    part_factor = jnp.exp(got_lse - final_top[None])
     self_factor = jnp.exp(self_top - final_top)
-    total_sum = jnp.sum(got_sum * part_factor, axis=0) + self_sum * self_factor
+    total_sum = jnp.sum(part_factor, axis=0) + self_sum * self_factor
     total_num = (
-        jnp.sum(got_num * part_factor[..., None], axis=0) + self_num * self_factor[..., None]
+        jnp.sum(got_out * part_factor[..., None], axis=0) + self_num * self_factor[..., None]
     )
     stretch_out = (
         (total_num / total_sum[..., None])

time: 219 us -> 159 us (0.73)
  waiting for transfers between devices: 101 us -> 72 us
  local copies, waits for them, and re-layouts: 38 us -> 17.2 us
  matrix products: 24.3 us -> 17.5 us
    all_to_all x1, waiting for transfers between devices: 58 us -> 29.1 us  [body(): received = lax.all_to_all(payload, 'seq', 0, 0, tiled=True)]
    unnamed x30 -> x26, local copies, waits for them, and re-layouts: 15.6 us -> 2.16 us
    dot_general x7 -> x4, matrix products: 14.9 us -> 2.02 us  [partial_attend(): jnp.dot(weights.astype(jnp.bfloat16), values, preferred_element_type=jnp....]
    dot_general x0 -> x2, matrix products: none -> 12.6 us  [the longest x1 7.85 us: body(): jnp.einsum('crp,cpd->crd', weights.astype(jnp.bfloat16), prior_values, pr...]
    reduce_sum x5 -> x2, other arithmetic: 9.02 us -> 0.59 us  [partial_attend(): weight_sum = jnp.sum(weights, axis=1)]
    dot_general x7 -> x4, matrix products: 9.1 us -> 2.56 us  [partial_attend(): jnp.dot(queries, keys.T, preferred_element_type=jnp.float32) * factor]
    all_to_all x1 -> x0, local copies, waits for them, and re-layouts: 5.36 us -> none  [body(): received = lax.all_to_all(payload, 'seq', 0, 0, tiled=True)]
    reduce_sum x2 -> x3, other arithmetic: 3.6 us -> 8.9 us  [the longest x1 6.82 us: body(): part_sum = jnp.sum(weights, axis=2)]
  transfers between devices with their start and end apart: 2 -> 2, of which waited for: 2 -> 2; matrix products, arithmetic and copies ran while one was open for 3% -> 5% of each run, Pallas kernels for 0% -> 0%
where the time goes in v2:
time: 159 us; the launch traced here: 158 us
  waiting for transfers between devices  72 us (45%)
  other arithmetic  18.8 us (12%)
  between operations  17.8 us (11%)
  matrix products  17.5 us (11%)
  local copies, waits for them, and re-layouts  17.2 us (11%)
  blocking collectives  10.2 us (6%)
  starting transfers between devices  4.31 us (3%)
    all_gather x1, waiting for transfers between devices, body(): lax.all_gather(jnp.concatenate([stretch_pack, decode_pack], axis=0), 'seq...  42.9 us
    all_to_all x1, waiting for transfers between devices, body(): received = lax.all_to_all(payload, 'seq', 0, 0, tiled=True)  29.1 us
    unnamed x1, blocking collectives  10.2 us
    dot_general x1, matrix products, body(): jnp.einsum('crp,cpd->crd', weights.astype(jnp.bfloat16), prior_values, pr...  7.85 us
    reduce_sum x1, other arithmetic, body(): part_sum = jnp.sum(weights, axis=2)  6.82 us
    dot_general x1, matrix products, body(): jnp.einsum('crd,cpd->crp', queries_all, prior_keys, preferred_element_typ...  4.77 us
    all_to_all x1, starting transfers between devices, body(): received = lax.all_to_all(payload, 'seq', 0, 0, tiled=True)  4.27 us
    reshape x1, local copies, waits for them, and re-layouts, body(): queries_all = stretch_part[:, :, :, :query_width].transpose(1, 0, 2, 3).r...  3.79 us
  transfers between devices with their start and end apart: 2, of which 2 were waited for; matrix products, arithmetic and copies ran while one was open for 5% of the time, Pallas kernels for 0%

profile of v2, /device:TPU:0, one launch (start us, length us, event | category | flops | bytes accessed | tf_op | source)
XLA Modules:
  0.0 157.8 jit_solution(1808221792266303195)
XLA Ops:
  7.2 1.0 pad_maximum_fusion.1
  8.3 1.4 maximum_bitcast_fusion.4
  10.4 1.3 compare_select_fusion
  14.3 1.1 compare_and_fusion
  16.2 0.9 fusion.63
  17.1 42.9 %all-gather.4.cloned.1.call-done = bf16[8,97,1152]{2,1,0:T(8,128)(2,1)} async-done(((bf16[1,97,1152]{2,1,0:T(8,128)(2,1)}), bf16[8,97,1152]{2,1,0:T(8,128)(2,1)}) %all-gather.4.cloned.1.call-update) | async-done | bytes 1787920 | tf_op jit(solution)/shard_map/all_gather | solution.py:52
  60.0 0.9 slice.106
  61.5 1.6 %slice.104 = bf16[8,96,1152]{2,1,0:T(8,128)(2,1)S(1)} slice(bf16[8,97,1152]{2,1,0:T(8,128)(2,1)} %all-gather.4.cloned.1.call-done), slice={[0:8], [0:96], [0:1152]} | slice | bytes 3538944 | tf_op jit(solution)/shard_map/slice | solution.py:91
  63.3 1.2 copy.117
  64.5 3.8 %reshape.502 = bf16[3,1792,128]{2,1,0:T(8,128)(2,1)} reshape(bf16[3,8,32,896]{3,2,1,0:T(8,128)(2,1)} %copy.117) | data formatting | bytes 2752512 | tf_op jit(solution)/shard_map/reshape | solution.py:97
  68.3 4.8 %fusion = (f32[3,1792]{1,0:T(4,128)S(1)}, f32[3,1792,1024]{1,2,0:T(8,128)S(1)}) fusion(pred[3,1024]{1,0:T(4,128)(4,1)S(1)} %broadcast_compare_fusion, bf16[3,1792,128]{2,1,0:T(8,128)(2,1)} %reshape.502, bf16[3,1024,128]{2,1,0:T(8,128)(2,1)S(1)} %copy-done.2), kind=kOutput, calls=%fused_computation.3 | convolution fusion | flops 1425795840 | bytes 24207360 | tf_op jit(solution)/shard_map/crd,cpd->crp/dot_general | solution.py:101
  73.1 6.8 %fusion.1 = f32[3,1792]{1,0:T(4,128)S(1)} fusion(f32[3,1792,1024]{1,2,0:T(8,128)S(1)} %get-tuple-element.56, f32[3,1792]{1,0:T(4,128)S(1)} %get-tuple-element.55, pred[3,1024]{1,0:T(4,128)(4,1)S(1)} %broadcast_compare_fusion), kind=kLoop, calls=%fused_computation.4 | loop fusion | flops 27519744 | bytes 22066176 | tf_op jit(solution)/shard_map/reduce_sum | solution.py:108
  79.9 7.8 %divide_convert_fusion = bf16[3,1792,128]{2,1,0:T(8,128)(2,1)S(1)} fusion(bf16[3,1024,128]{2,1,0:T(8,128)(2,1)S(1)} %copy-done.5, f32[3,1792,1024]{1,2,0:T(8,128)S(1)} %get-tuple-element.56, f32[3,1792]{1,0:T(4,128)S(1)} %get-tuple-element.55, pred[3,1024]{1,0:T(4,128)(4,1)S(1)} %broadcast_compare_fusion, f32[3,1792]{1,0:T(4,128)S(1)} %get-tuple-element.44), kind=kOutput, calls=%fused_computation.11 | convolution fusion | flops 1438187520 | bytes 24228864 | tf_op jit(solution)/shard_map/crp,cpd->crd/dot_general | solution.py:109
  87.8 1.2 copy.119
  89.3 0.8 fusion.51
  90.1 1.7 %fusion.65 = (f32[7]{0:T(128)S(1)}, f32[7,4097]{1,0:T(8,128)S(1)}) fusion(bf16[1,1,128]{2,1,0:T(2,128)(2,1)S(1)} %get-tuple-element.63, bf16[1,4096,128]{2,1,0:T(8,128)(2,1)} %param.19, bf16[896]{0:T(1024)(128)(2,1)S(1)} %fusion.48, pred[4097]{0:T(1024)(128)(4,1)S(1)} %copy-done.3), kind=kOutput, calls=%fused_computation.129 | convolution fusion | flops 9525518 | bytes 1169465 | tf_op jit(solution)/shard_map/vmap()/dot_general | solution.py:13
  92.0 1.5 fusion.15
  93.6 1.2 pad_maximum_fusion
  94.8 4.3 %all-to-all-start = ((bf16[8,695,128]{2,1,0:T(8,128)(2,1)}), bf16[8,695,128]{2,1,0:T(8,128)(2,1)}, u32[]{:S(2)}, u32[]{:S(2)}) async-start(bf16[8,695,128]{2,1,0:T(8,128)(2,1)} %pad_maximum_fusion), calls=%async_computation | async-start | bytes 2850816 | tf_op jit(solution)/shard_map/all_to_all | solution.py:144
  103.6 29.1 %all-to-all-done = bf16[8,695,128]{2,1,0:T(8,128)(2,1)} async-done(((bf16[8,695,128]{2,1,0:T(8,128)(2,1)}), bf16[8,695,128]{2,1,0:T(8,128)(2,1)}, u32[]{:S(2)}, u32[]{:S(2)}) %all-to-all-start) | async-done | bytes 1423392 | tf_op jit(solution)/shard_map/all_to_all | solution.py:144
  132.8 0.8 slice_bitcast_fusion.1
  133.5 1.1 reshape.558
  136.9 10.2 %all-reduce.1 = bf16[8,448]{1,0:T(8,128)(2,1)S(1)} all-reduce(f32[8,448]{1,0:T(8,128)S(1)} %fusion.44), channel_id=3, replica_groups=mesh['seq'=8,'tp'=4] {'tp'}, use_global_device_ids=true, to_apply=%region_5.7.clone | all-reduce | flops 3584 | bytes 21504
  147.1 2.0 %multiply_reduce_fusion = f32[672,128]{1,0:T(8,128)S(1)} fusion(bf16[8,695,128]{2,1,0:T(8,128)(2,1)} %all-to-all-done, f32[8,672]{1,0:T(8,128)S(1)} %subtract_exponential_fusion.1), kind=kLoop, calls=%fused_computation.10 | loop fusion | flops 1978368 | bytes 1741824 | tf_op jit(solution)/shard_map/reduce_sum | solution.py:191
  (89 shorter events, 10.6 us)
Async XLA Ops:
  7.2 129.4 %copy-start = (bf16[896,448]{0,1:T(8,128)(2,1)S(1)}, bf16[896,448]{0,1:T(8,128)(2,1)}, u32[]{:S(2)}) copy-start(bf16[896,448]{0,1:T(8,128)(2,1)} %param.23) | copy-start | bytes 2408452
  7.2 52.8 %all-gather.4.cloned.1.call-start = ((), (), s32[]{:S(2)}) async-start(), calls=%async_computation.1 | async-start | bytes 2156544 | tf_op jit(solution)/shard_map/all_gather | solution.py:52
  63.3 5.0 %copy-start.2 = (bf16[3,1024,128]{2,1,0:T(8,128)(2,1)S(1)}, bf16[3,1024,128]{2,1,0:T(8,128)(2,1)}, u32[]{:S(2)}) copy-start(bf16[3,1024,128]{2,1,0:T(8,128)(2,1)} %param.27) | copy-start | bytes 2359300
  73.0 6.9 %copy-start.5 = (bf16[3,1024,128]{2,1,0:T(8,128)(2,1)S(1)}, bf16[3,1024,128]{2,1,0:T(8,128)(2,1)}, u32[]{:S(2)}) copy-start(bf16[3,1024,128]{2,1,0:T(8,128)(2,1)} %param.28) | copy-start | bytes 2359300
  87.8 2.3 %copy-start.3 = (pred[4097]{0:T(1024)(128)(4,1)S(1)}, pred[4097]{0:T(1024)(128)(4,1)}, u32[]{:S(2)}) copy-start(pred[4097]{0:T(1024)(128)(4,1)} %add_reduce_fusion) | copy-start | bytes 12295
  89.2 4.4 %copy-start.1 = (bf16[3,8,224,128]{3,2,0,1:T(8,128)(2,1)S(1)}, bf16[3,8,224,128]{3,2,0,1:T(8,128)(2,1)}, u32[]{:S(2)}) copy-start(bf16[3,8,224,128]{3,2,0,1:T(8,128)(2,1)} %copy.119) | copy-start | bytes 4128772
  93.6 5.8 %copy-start.6 = (u32[32]{0:T(128)S(1)}, u32[32]{0:T(128)}, u32[]{:S(2)}) copy-start(u32[32]{0:T(128)} %constant.139) | copy-start | bytes 388
  94.8 37.9 %all-to-all-start = ((bf16[8,695,128]{2,1,0:T(8,128)(2,1)}), bf16[8,695,128]{2,1,0:T(8,128)(2,1)}, u32[]{:S(2)}, u32[]{:S(2)}) async-start(bf16[8,695,128]{2,1,0:T(8,128)(2,1)} %pad_maximum_fusion), calls=%async_computation | async-start | bytes 2850816 | tf_op jit(solution)/shard_map/all_to_all | solution.py:144
  103.3 33.3 %copy-start.4 = (pred[8]{0:T(512)(128)(4,1)S(1)}, pred[8]{0:T(512)(128)(4,1)}, u32[]{:S(2)}) copy-start(pred[8]{0:T(512)(128)(4,1)} %compare_and_fusion) | copy-start | bytes 28
Sparse Core Ops, SparseCore 0:
  10.2 49.7 all-gather.3

commit v3 on v2

--- a/solution.py
+++ b/solution.py
@@ -1,8 +1,11 @@
+import functools
 import math
 
 import jax
 import jax.numpy as jnp
 from jax import lax
+from jax.experimental import pallas as pl
+from jax.experimental.pallas import tpu as pltpu
 from jax.sharding import PartitionSpec as P
 
 NEG_FILL = -1e30
@@ -17,6 +20,49 @@
     weight_sum = jnp.sum(weights, axis=1)
     numerator = jnp.dot(weights.astype(jnp.bfloat16), values, preferred_element_type=jnp.float32)
     return (row_top, weight_sum, numerator)
+
+
+def _prefill_kernel(limit_ref, q_ref, k_ref, v_ref, o_ref, lse_ref, *, group_size, head_size):
+    c = pl.program_id(0)
+    limit = limit_ref[c]
+    keys = k_ref[0]
+    values = v_ref[0]
+    factor = 1.0 / math.sqrt(head_size)
+    col = lax.broadcasted_iota(jnp.int32, (1, keys.shape[0]), 1)
+    visible = col < limit
+    for h in range(group_size):
+        q = q_ref[0, :, h * head_size:(h + 1) * head_size]
+        s = lax.dot_general(q, keys, (((1,), (1,)), ((), ())), preferred_element_type=jnp.float32) * factor
+        s = jnp.where(visible, s, NEG_FILL)
+        m = jnp.max(s, axis=1, keepdims=True)
+        w = jnp.where(visible, jnp.exp(s - m), 0.0)
+        l = jnp.sum(w, axis=1, keepdims=True)
+        num = jnp.dot(w.astype(jnp.bfloat16), values, preferred_element_type=jnp.float32)
+        safe = jnp.maximum(l, 1.0)
+        o_ref[0, :, h * head_size:(h + 1) * head_size] = (num / safe).astype(o_ref.dtype)
+        lse_ref[0, :, h:h + 1] = m + jnp.log(safe)
+
+def prefill_partial(limits, queries, keys, values, group_size):
+    n, t, qw = queries.shape
+    p, hd = keys.shape[1], keys.shape[2]
+    kern = functools.partial(_prefill_kernel, group_size=group_size, head_size=hd)
+    return pl.pallas_call(
+        kern,
+        grid_spec=pltpu.PrefetchScalarGridSpec(
+            num_scalar_prefetch=1,
+            grid=(n,),
+            in_specs=[
+                pl.BlockSpec((1, t, qw), lambda c, lim: (c, 0, 0)),
+                pl.BlockSpec((1, p, hd), lambda c, lim: (c, 0, 0)),
+                pl.BlockSpec((1, p, hd), lambda c, lim: (c, 0, 0)),
+            ],
+            out_specs=[
+                pl.BlockSpec((1, t, qw), lambda c, lim: (c, 0, 0)),
+                pl.BlockSpec((1, t, group_size), lambda c, lim: (c, 0, 0)),
+            ],
+        ),
+        out_shape=[jax.ShapeDtypeStruct((n, t, qw), jnp.bfloat16), jax.ShapeDtypeStruct((n, t, group_size), jnp.float32)],
+    )(limits, queries, keys, values)
 
 
 def body(
@@ -94,25 +140,12 @@
     queries_all = (
         stretch_part[:, :, :, :query_width]
         .transpose(1, 0, 2, 3)
-        .reshape(stretch_count, row_count, head_size)
-    )
-    factor = 1.0 / math.sqrt(head_size)
-    scores = (
-        jnp.einsum("crd,cpd->crp", queries_all, prior_keys, preferred_element_type=jnp.float32)
-        * factor
-    )
-    prior_visible = (prior_pos[None, :] < stretch_start[:, None])[:, None, :]
-    scores = jnp.where(prior_visible, scores, NEG_FILL)
-    part_top = jnp.max(scores, axis=2)
-    weights = jnp.where(prior_visible, jnp.exp(scores - part_top[..., None]), 0.0)
-    part_sum = jnp.sum(weights, axis=2)
-    part_num = jnp.einsum(
-        "crp,cpd->crd", weights.astype(jnp.bfloat16), prior_values,
-        preferred_element_type=jnp.float32,
-    )
-    safe_sum = jnp.maximum(part_sum, 1.0)
-    part_out = (part_num / safe_sum[..., None]).astype(jnp.bfloat16)
-    part_lse = part_top + jnp.log(safe_sum)
+        .reshape(stretch_count, seq_count * local_tok, query_width)
+    )
+    limits = jnp.clip(stretch_start - seq_rank * prior_span, 0, prior_span).astype(jnp.int32)
+    part_out, part_lse = prefill_partial(limits, queries_all, prior_keys, prior_values, group_size)
+    part_out = part_out.reshape(stretch_count, row_count, head_size)
+    part_lse = part_lse.reshape(stretch_count, row_count)
     lse_hi = lax.reduce_precision(part_lse, exponent_bits=8, mantissa_bits=7)
     lse_rest = part_lse - lse_hi
     lse_mid = lax.reduce_precision(lse_rest, exponent_bits=8, mantissa_bits=7)

time: 159 us -> 152 us (0.956)
  Pallas kernels: 0 us -> 13.7 us
  matrix products: 17.5 us -> 3.83 us
  other arithmetic: 18.8 us -> 10.5 us
    pallas_call x0 -> x1, Pallas kernels: none -> 13.7 us  [prefill_partial(): pl.pallas_call(kern, grid_spec=pltpu.PrefetchScalarGridSpec(num_scalar_pr...]
    dot_general x2 -> x0, matrix products: 12.6 us -> none  [the longest x1 7.85 us: body(): jnp.einsum('crp,cpd->crd', weights.astype(jnp.bfloat16), prior_values, pr...]
    reduce_sum x1 -> x0, other arithmetic: 6.82 us -> none  [body(): part_sum = jnp.sum(weights, axis=2)]
    another operation x3 -> x5, local copies, waits for them, and re-layouts: 0.14 us -> 6.49 us  [the longest x2 6.35 us: body(): part_out.reshape(stretch_count, seq_count, rows_per_src, head_size)]
    reshape x2 -> x1, local copies, waits for them, and re-layouts: 4.96 us -> 0.22 us  [body(): part_lse = part_lse.reshape(stretch_count, row_count)]
where the time goes in v3:
time: 152 us; the launch traced here: 151 us
  waiting for transfers between devices  72.7 us (48%)
  local copies, waits for them, and re-layouts  18.1 us (12%)
  between operations  17.8 us (12%)
  Pallas kernels  13.7 us (9%)
  other arithmetic  10.5 us (7%)
  blocking collectives  10.2 us (7%)
  starting transfers between devices  4.44 us (3%)
  matrix products  3.83 us (3%)
    all_gather x1, waiting for transfers between devices, body(): lax.all_gather(jnp.concatenate([stretch_pack, decode_pack], axis=0), 'seq...  43.6 us
    all_to_all x1, waiting for transfers between devices, body(): received = lax.all_to_all(payload, 'seq', 0, 0, tiled=True)  29.2 us
    pallas_call x1, Pallas kernels, prefill_partial(): pl.pallas_call(kern, grid_spec=pltpu.PrefetchScalarGridSpec(num_scalar_pr...  13.7 us
    unnamed x1, blocking collectives  10.2 us
    another operation x2, local copies, waits for them, and re-layouts, body(): part_out.reshape(stretch_count, seq_count, rows_per_src, head_size)  6.35 us
    all_to_all x1, starting transfers between devices, body(): received = lax.all_to_all(payload, 'seq', 0, 0, tiled=True)  4.4 us
  transfers between devices with their start and end apart: 2, of which 2 were waited for; matrix products, arithmetic and copies ran while one was open for 5% of the time, Pallas kernels for 0%

profile of v3, /device:TPU:0, one launch (start us, length us, event | category | flops | bytes accessed | tf_op | source)
XLA Modules:
  0.0 151.3 jit_solution(2865907027549735325)
XLA Ops:
  7.2 1.0 pad_maximum_fusion.1
  8.3 1.4 maximum_bitcast_fusion.4
  10.4 1.3 compare_select_fusion
  13.7 0.7 compare_and_fusion
  14.4 1.1 subtract_clamp_fusion.limit_ref
  15.5 0.9 fusion.52
  16.4 43.6 %all-gather.4.cloned.1.call-done = bf16[8,97,1152]{2,1,0:T(8,128)(2,1)} async-done(((bf16[1,97,1152]{2,1,0:T(8,128)(2,1)}), bf16[8,97,1152]{2,1,0:T(8,128)(2,1)}) %all-gather.4.cloned.1.call-update) | async-done | bytes 1787920 | tf_op jit(solution)/shard_map/all_gather | solution.py:98
  60.0 0.9 slice.106
  61.0 1.6 %slice.104 = bf16[8,96,1152]{2,1,0:T(8,128)(2,1)S(1)} slice(bf16[8,97,1152]{2,1,0:T(8,128)(2,1)} %all-gather.4.cloned.1.call-done), slice={[0:8], [0:96], [0:1152]} | slice | bytes 3538944 | tf_op jit(solution)/shard_map/slice | solution.py:137
  62.7 1.2 copy.112
  63.9 13.7 %shard_map.149 = (bf16[3,256,896]{2,1,0:T(8,128)(2,1)}, f32[3,256,7]{2,1,0:T(8,128)}) custom-call(s32[3]{0:T(128)} %subtract_clamp_fusion.limit_ref, bf16[3,256,896]{2,1,0:T(8,128)(2,1)} %bitcast.102, bf16[3,1024,128]{2,1,0:T(8,128)(2,1)} %k_ref.1, bf16[3,1024,128]{2,1,0:T(8,128)(2,1)} %v_ref.1), custom_call_target="tpu_custom_call" | custom-call | tf_op jit(solution)/shard_map/pallas_call | solution.py:49
  77.6 3.8 %reshape_reshape.3 = bf16[3,8,224,128]{3,2,1,0:T(8,128)(2,1)} reshape(bf16[3,256,896]{2,1,0:T(8,128)(2,1)} %get-tuple-element.5) | data formatting | bytes 2752512 | tf_op jit(solution)/shard_map/reshape;reshape | solution.py:167
  81.4 2.6 %copy.113 = bf16[3,8,224,128]{3,2,0,1:T(8,128)(2,1)} copy(bf16[3,8,224,128]{3,2,1,0:T(8,128)(2,1)} %reshape_reshape.3) | data formatting | bytes 2752512 | tf_op jit(solution)/shard_map/reshape;reshape | solution.py:167
  84.5 1.9 %fusion.54 = (f32[7]{0:T(128)S(1)}, f32[7,4097]{1,0:T(8,128)S(1)}) fusion(bf16[1,1,128]{2,1,0:T(2,128)(2,1)S(1)} %get-tuple-element.63, bf16[1,4096,128]{2,1,0:T(8,128)(2,1)} %param.19, bf16[896]{0:T(1024)(128)(2,1)S(1)} %fusion.40, pred[4097]{0:T(1024)(128)(4,1)S(1)} %add_reduce_fusion), kind=kOutput, calls=%fused_computation.115 | convolution fusion | flops 9525518 | bytes 1169465 | tf_op jit(solution)/shard_map/vmap()/dot_general | solution.py:16
  86.9 1.2 pad_maximum_fusion
  88.1 4.4 %all-to-all-start = ((bf16[8,695,128]{2,1,0:T(8,128)(2,1)}), bf16[8,695,128]{2,1,0:T(8,128)(2,1)}, u32[]{:S(2)}, u32[]{:S(2)}) async-start(bf16[8,695,128]{2,1,0:T(8,128)(2,1)} %pad_maximum_fusion), calls=%async_computation | async-start | bytes 2850816 | tf_op jit(solution)/shard_map/all_to_all | solution.py:177
  97.1 29.2 %all-to-all-done = bf16[8,695,128]{2,1,0:T(8,128)(2,1)} async-done(((bf16[8,695,128]{2,1,0:T(8,128)(2,1)}), bf16[8,695,128]{2,1,0:T(8,128)(2,1)}, u32[]{:S(2)}, u32[]{:S(2)}) %all-to-all-start) | async-done | bytes 1423392 | tf_op jit(solution)/shard_map/all_to_all | solution.py:177
  126.2 0.8 slice_bitcast_fusion.1
  127.0 1.1 reshape.505
  128.7 0.7 slice_bitcast_fusion.2
  130.3 10.2 %all-reduce.1 = bf16[8,448]{1,0:T(8,128)(2,1)S(1)} all-reduce(f32[8,448]{1,0:T(8,128)S(1)} %fusion.36), channel_id=3, replica_groups=mesh['seq'=8,'tp'=4] {'tp'}, use_global_device_ids=true, to_apply=%region_3.5.clone | all-reduce | flops 3584 | bytes 21504
  140.5 2.0 %multiply_reduce_fusion = f32[672,128]{1,0:T(8,128)S(1)} fusion(bf16[8,695,128]{2,1,0:T(8,128)(2,1)} %all-to-all-done, f32[8,672]{1,0:T(8,128)S(1)} %subtract_exponential_fusion.1), kind=kLoop, calls=%fused_computation.3 | loop fusion | flops 1978368 | bytes 1741824 | tf_op jit(solution)/shard_map/reduce_sum | solution.py:224
  143.1 0.6 dynamic-slice_convert_fusion
  143.7 0.7 fusion.16
  (81 shorter events, 7.0 us)
Async XLA Ops:
  7.2 122.8 %copy-start = (bf16[896,448]{0,1:T(8,128)(2,1)S(1)}, bf16[896,448]{0,1:T(8,128)(2,1)}, u32[]{:S(2)}) copy-start(bf16[896,448]{0,1:T(8,128)(2,1)} %param.23) | copy-start | bytes 2408452
  7.2 52.8 %all-gather.4.cloned.1.call-start = ((), (), s32[]{:S(2)}) async-start(), calls=%async_computation.1 | async-start | bytes 2156544 | tf_op jit(solution)/shard_map/all_gather | solution.py:98
  81.4 2.6 %copy-start.2 = (f32[3,256,7]{2,1,0:T(8,128)S(1)}, f32[3,256,7]{2,1,0:T(8,128)}, u32[]{:S(2)}) copy-start(f32[3,256,7]{2,1,0:T(8,128)} %get-tuple-element.6) | copy-start | bytes 64516
  84.4 2.2 %copy-start.3 = (bf16[1,4096,128]{2,1,0:T(8,128)(2,1)S(1)}, bf16[1,4096,128]{2,1,0:T(8,128)(2,1)}, u32[]{:S(2)}) copy-start(bf16[1,4096,128]{2,1,0:T(8,128)(2,1)} %param.20) | copy-start | bytes 3145732
  84.5 2.4 %copy-start.1 = (bf16[3,8,224,128]{3,2,0,1:T(8,128)(2,1)S(1)}, bf16[3,8,224,128]{3,2,0,1:T(8,128)(2,1)}, u32[]{:S(2)}) copy-start(bf16[3,8,224,128]{3,2,0,1:T(8,128)(2,1)} %copy.113) | copy-start | bytes 4128772
  88.1 4.7 %copy-start.4 = (u32[32]{0:T(128)S(1)}, u32[32]{0:T(128)}, u32[]{:S(2)}) copy-start(u32[32]{0:T(128)} %constant.136) | copy-start | bytes 388
  88.1 38.1 %all-to-all-start = ((bf16[8,695,128]{2,1,0:T(8,128)(2,1)}), bf16[8,695,128]{2,1,0:T(8,128)(2,1)}, u32[]{:S(2)}, u32[]{:S(2)}) async-start(bf16[8,695,128]{2,1,0:T(8,128)(2,1)} %pad_maximum_fusion), calls=%async_computation | async-start | bytes 2850816 | tf_op jit(solution)/shard_map/all_to_all | solution.py:177
Sparse Core Ops, SparseCore 0:
  10.2 49.7 all-gather.3

commit v4 on v3

--- a/solution.py
+++ b/solution.py
@@ -95,8 +95,9 @@
         stretch_rows, query_width + 2 * key_width
     )
     decode_pack = jnp.concatenate([new_query, new_key, new_value], axis=1)
-    gathered = lax.all_gather(
-        jnp.concatenate([stretch_pack, decode_pack], axis=0), "seq", axis=0, tiled=False
+    pack = jnp.concatenate([stretch_pack, decode_pack], axis=0)
+    gathered = lax.all_to_all(
+        jnp.broadcast_to(pack[None], (seq_count,) + pack.shape), "seq", 0, 0, tiled=True
     )
 
     decode_part = gathered[:, stretch_rows:, :].reshape(total_dec, query_width + 2 * key_width)

time: 152 us -> 142 us (0.934)
  between operations: 17.8 us -> 4.38 us
  waiting for transfers between devices: 72.7 us -> 61.7 us
  starting transfers between devices: 4.44 us -> 11.2 us
  other arithmetic: 10.5 us -> 14.6 us
  local copies, waits for them, and re-layouts: 18.1 us -> 21.9 us
    all_gather x1 -> x0, waiting for transfers between devices: 43.6 us -> none  [body(): lax.all_gather(jnp.concatenate([stretch_pack, decode_pack], axis=0), 'seq...]
    all_to_all x0 -> x1, waiting for transfers between devices: none -> 38.1 us  [body(): lax.all_to_all(jnp.broadcast_to(pack[None], (seq_count,) + pack.shape), '...]
    all_to_all x0 -> x1, starting transfers between devices: none -> 7.41 us  [body(): lax.all_to_all(jnp.broadcast_to(pack[None], (seq_count,) + pack.shape), '...]
    all_to_all x1, waiting for transfers between devices: 29.2 us -> 23.6 us  [body(): received = lax.all_to_all(payload, 'seq', 0, 0, tiled=True)]
    another operation x2, local copies, waits for them, and re-layouts: 6.35 us -> 2.97 us  [body(): part_out.reshape(stretch_count, seq_count, rows_per_src, head_size)]
    unnamed x22 -> x42, local copies, waits for them, and re-layouts: 2.15 us -> 3.23 us
  transfers between devices with their start and end apart: 2 -> 2, of which waited for: 2 -> 2; matrix products, arithmetic and copies ran while one was open for 5% -> 9% of each run, Pallas kernels for 0% -> 0%
where the time goes in v4:
time: 142 us; the launch traced here: 141 us
  waiting for transfers between devices  61.7 us (43%)
  local copies, waits for them, and re-layouts  21.9 us (15%)
  other arithmetic  14.6 us (10%)
  Pallas kernels  13.7 us (10%)
  starting transfers between devices  11.2 us (8%)
  blocking collectives  10.2 us (7%)
  between operations  4.38 us (3%)
  matrix products  3.68 us (3%)
    all_to_all x1, waiting for transfers between devices, body(): lax.all_to_all(jnp.broadcast_to(pack[None], (seq_count,) + pack.shape), '...  38.1 us
    all_to_all x1, waiting for transfers between devices, body(): received = lax.all_to_all(payload, 'seq', 0, 0, tiled=True)  23.6 us
    pallas_call x1, Pallas kernels, prefill_partial(): pl.pallas_call(kern, grid_spec=pltpu.PrefetchScalarGridSpec(num_scalar_pr...  13.7 us
    unnamed x1, blocking collectives  10.2 us
    all_to_all x1, starting transfers between devices, body(): lax.all_to_all(jnp.broadcast_to(pack[None], (seq_count,) + pack.shape), '...  7.41 us
    all_to_all x1, starting transfers between devices, body(): received = lax.all_to_all(payload, 'seq', 0, 0, tiled=True)  3.78 us
    unnamed x42, local copies, waits for them, and re-layouts  3.23 us
    another operation x2, local copies, waits for them, and re-layouts, body(): part_out.reshape(stretch_count, seq_count, rows_per_src, head_size)  2.97 us
  transfers between devices with their start and end apart: 2, of which 2 were waited for; matrix products, arithmetic and copies ran while one was open for 9% of the time, Pallas kernels for 0%

profile of v4, /device:TPU:0, one launch (start us, length us, event | category | flops | bytes accessed | tf_op | source)
XLA Modules:
  0.0 141.3 jit_solution(11537524810740433931)
XLA Ops:
  0.6 1.0 pad_maximum_fusion.1
  2.4 1.4 %broadcast_in_dim.94 = bf16[8,97,1152]{2,1,0:T(8,128)(2,1)} broadcast(bf16[97,1152]{1,0:T(8,128)(2,1)S(1)} %maximum_maximum_fusion), dimensions={1,2} | broadcast | bytes 2011392 | tf_op jit(solution)/shard_map/broadcast_in_dim | solution.py:100
  3.9 7.4 %all-to-all-start = ((bf16[8,97,1152]{2,1,0:T(8,128)(2,1)}), bf16[8,97,1152]{2,1,0:T(8,128)(2,1)S(1)}, u32[]{:S(2)}, u32[]{:S(2)}) async-start(bf16[8,97,1152]{2,1,0:T(8,128)(2,1)} %broadcast_in_dim.94), calls=%async_computation | async-start | bytes 3833856 | tf_op jit(solution)/shard_map/all_to_all | solution.py:99
  17.6 38.1 %all-to-all-done = bf16[8,97,1152]{2,1,0:T(8,128)(2,1)S(1)} async-done(((bf16[8,97,1152]{2,1,0:T(8,128)(2,1)}), bf16[8,97,1152]{2,1,0:T(8,128)(2,1)S(1)}, u32[]{:S(2)}, u32[]{:S(2)}) %all-to-all-start) | async-done | bytes 1787936 | tf_op jit(solution)/shard_map/all_to_all | solution.py:99
  57.1 1.4 copy.87
  58.7 13.7 %shard_map.149 = (bf16[3,256,896]{2,1,0:T(8,128)(2,1)}, f32[3,256,7]{2,1,0:T(8,128)}) custom-call(s32[3]{0:T(128)} %subtract_clamp_fusion.limit_ref, bf16[3,256,896]{2,1,0:T(8,128)(2,1)} %bitcast.100, bf16[3,1024,128]{2,1,0:T(8,128)(2,1)} %k_ref.1, bf16[3,1024,128]{2,1,0:T(8,128)(2,1)} %v_ref.1), custom_call_target="tpu_custom_call" | custom-call | tf_op jit(solution)/shard_map/pallas_call | solution.py:49
  72.4 2.9 %reshape_reshape.3 = bf16[3,8,224,128]{3,2,1,0:T(8,128)(2,1)S(1)} reshape(bf16[3,256,896]{2,1,0:T(8,128)(2,1)} %get-tuple-element.5) | data formatting | bytes 2752512 | tf_op jit(solution)/shard_map/reshape;reshape | solution.py:168
  75.4 1.3 reshape.452
  76.9 0.7 fusion.40
  78.3 1.7 %fusion.54 = (f32[7]{0:T(128)S(1)}, f32[7,4097]{1,0:T(8,128)S(1)}) fusion(bf16[1,1,128]{2,1,0:T(2,128)(2,1)S(1)} %get-tuple-element.63, bf16[1,4096,128]{2,1,0:T(8,128)(2,1)} %param.19, bf16[896]{0:T(1024)(128)(2,1)S(1)} %fusion.40, pred[4097]{0:T(1024)(128)(4,1)} %add_reduce_fusion), kind=kOutput, calls=%fused_computation.115 | convolution fusion | flops 9525518 | bytes 1169465 | tf_op jit(solution)/shard_map/vmap()/dot_general | solution.py:16
  80.6 1.2 pad_maximum_fusion
  81.8 3.8 %all-to-all-start.1 = ((bf16[8,695,128]{2,1,0:T(8,128)(2,1)}), bf16[8,695,128]{2,1,0:T(8,128)(2,1)S(1)}, u32[]{:S(2)}, u32[]{:S(2)}) async-start(bf16[8,695,128]{2,1,0:T(8,128)(2,1)} %pad_maximum_fusion), calls=%async_computation.1 | async-start | bytes 2850816 | tf_op jit(solution)/shard_map/all_to_all | solution.py:178
  87.2 1.1 fusion.51
  89.4 1.0 fusion.22
  96.1 23.6 %all-to-all-done.1 = bf16[8,695,128]{2,1,0:T(8,128)(2,1)S(1)} async-done(((bf16[8,695,128]{2,1,0:T(8,128)(2,1)}), bf16[8,695,128]{2,1,0:T(8,128)(2,1)S(1)}, u32[]{:S(2)}, u32[]{:S(2)}) %all-to-all-start.1) | async-done | bytes 1423392 | tf_op jit(solution)/shard_map/all_to_all | solution.py:178
  120.3 1.9 %reshape.506 = f32[8,3,3,32,7]{4,3,2,1,0:T(8,128)S(1)} reshape(f32[8,2016]{1,0:T(8,128)} %slice_convert_fusion) | data formatting | bytes 129024 | tf_op jit(solution)/shard_map/reshape | solution.py:188
  122.2 0.9 fusion.50
  123.1 0.8 add_maximum_fusion
  124.1 1.2 add.83
  125.3 1.1 fusion.13
  127.4 10.2 %all-reduce.1 = bf16[8,448]{1,0:T(8,128)(2,1)S(1)} all-reduce(f32[8,448]{1,0:T(8,128)S(1)} %fusion.36), channel_id=2, replica_groups=mesh['seq'=8,'tp'=4] {'tp'}, use_global_device_ids=true, to_apply=%region_3.5.clone | all-reduce | flops 3584 | bytes 21504
  137.6 0.8 multiply_add_fusion
  138.5 0.9 multiply_reduce_fusion
  140.6 0.7 fusion.16
  (101 shorter events, 18.0 us)
Async XLA Ops:
  0.6 126.5 %copy-start = (bf16[896,448]{0,1:T(8,128)(2,1)S(1)}, bf16[896,448]{0,1:T(8,128)(2,1)}, u32[]{:S(2)}) copy-start(bf16[896,448]{0,1:T(8,128)(2,1)} %param.23) | copy-start | bytes 2408452
  3.9 8.1 %copy-start.10 = (s32[8]{0:T(128)S(1)}, s32[8]{0:T(128)}, u32[]{:S(2)}) copy-start(s32[8]{0:T(128)} %param.22) | copy-start | bytes 100
  3.9 12.5 %copy-start.13 = (s32[3]{0:T(128)S(1)}, s32[3]{0:T(128)}, u32[]{:S(2)}) copy-start(s32[3]{0:T(128)} %param.29) | copy-start | bytes 40
  3.9 13.0 %copy-start.2 = (bf16[3,32,896]{2,1,0:T(8,128)(2,1)S(1)}, bf16[3,32,896]{2,1,0:T(8,128)(2,1)}, u32[]{:S(2)}) copy-start(bf16[3,32,896]{2,1,0:T(8,128)(2,1)} %param.24) | copy-start | bytes 516100
  3.9 51.8 %all-to-all-start = ((bf16[8,97,1152]{2,1,0:T(8,128)(2,1)}), bf16[8,97,1152]{2,1,0:T(8,128)(2,1)S(1)}, u32[]{:S(2)}, u32[]{:S(2)}) async-start(bf16[8,97,1152]{2,1,0:T(8,128)(2,1)} %broadcast_in_dim.94), calls=%async_computation | async-start | bytes 3833856 | tf_op jit(solution)/shard_map/all_to_all | solution.py:99
  57.0 1.7 %copy-start.1 = (bf16[8,96,1152]{2,1,0:T(8,128)(2,1)}, bf16[8,96,1152]{2,1,0:T(8,128)(2,1)S(1)}, u32[]{:S(2)}) copy-start(bf16[8,96,1152]{2,1,0:T(8,128)(2,1)S(1)} %slice.104) | copy-start | bytes 5308420
  75.4 4.7 %copy-start.8 = (pred[4097]{0:T(1024)(128)(4,1)S(1)}, pred[4097]{0:T(1024)(128)(4,1)}, u32[]{:S(2)}) copy-start(pred[4097]{0:T(1024)(128)(4,1)} %add_reduce_fusion) | copy-start | bytes 12295
  75.4 4.9 %copy-start.12 = (bf16[1,4096,128]{2,1,0:T(8,128)(2,1)S(1)}, bf16[1,4096,128]{2,1,0:T(8,128)(2,1)}, u32[]{:S(2)}) copy-start(bf16[1,4096,128]{2,1,0:T(8,128)(2,1)} %param.20) | copy-start | bytes 3145732
  81.8 3.8 %copy-start.7 = (bf16[1,32,896]{2,1,0:T(8,128)(2,1)S(1)}, bf16[1,32,896]{2,1,0:T(8,128)(2,1)}, u32[]{:S(2)}) copy-start(bf16[1,32,896]{2,1,0:T(8,128)(2,1)} %get-tuple-element.45) | copy-start | bytes 172036
  81.8 3.9 %copy-start.6 = (bf16[1,32,896]{2,1,0:T(8,128)(2,1)S(1)}, bf16[1,32,896]{2,1,0:T(8,128)(2,1)}, u32[]{:S(2)}) copy-start(bf16[1,32,896]{2,1,0:T(8,128)(2,1)} %get-tuple-element.46) | copy-start | bytes 172036
  81.8 4.0 %copy-start.5 = (bf16[1,32,896]{2,1,0:T(8,128)(2,1)S(1)}, bf16[1,32,896]{2,1,0:T(8,128)(2,1)}, u32[]{:S(2)}) copy-start(bf16[1,32,896]{2,1,0:T(8,128)(2,1)} %get-tuple-element.47) | copy-start | bytes 172036
  81.8 4.1 %copy-start.14 = (u32[32]{0:T(128)S(1)}, u32[32]{0:T(128)}, u32[]{:S(2)}) copy-start(u32[32]{0:T(128)} %constant.136) | copy-start | bytes 388
  81.8 37.8 %all-to-all-start.1 = ((bf16[8,695,128]{2,1,0:T(8,128)(2,1)}), bf16[8,695,128]{2,1,0:T(8,128)(2,1)S(1)}, u32[]{:S(2)}, u32[]{:S(2)}) async-start(bf16[8,695,128]{2,1,0:T(8,128)(2,1)} %pad_maximum_fusion), calls=%async_computation.1 | async-start | bytes 2850816 | tf_op jit(solution)/shard_map/all_to_all | solution.py:178
  85.6 3.7 %copy-start.9 = (s32[224]{0:T(256)}, s32[224]{0:T(256)S(1)}, u32[]{:S(2)}) copy-start(s32[224]{0:T(256)S(1)} %fusion.42) | copy-start | bytes 2692
  122.2 4.9 %copy-start.11 = (pred[8]{0:T(512)(128)(4,1)S(1)}, pred[8]{0:T(512)(128)(4,1)}, u32[]{:S(2)}) copy-start(pred[8]{0:T(512)(128)(4,1)} %compare_and_fusion) | copy-start | bytes 28
  139.4 1.2 copy-start.3
  139.4 1.2 copy-start.4

commit v5 on v4

--- a/solution.py
+++ b/solution.py
@@ -22,29 +22,49 @@
     return (row_top, weight_sum, numerator)
 
 
-def _prefill_kernel(limit_ref, q_ref, k_ref, v_ref, o_ref, lse_ref, *, group_size, head_size):
+def _prefill_kernel(
+    info_ref, q_ref, k_ref, v_ref, sk_ref, sv_ref, o_ref, lse_ref, *, group_size, head_size
+):
     c = pl.program_id(0)
-    limit = limit_ref[c]
+    limit = info_ref[c]
+    key_offset = info_ref[info_ref.shape[0] - 1]
     keys = k_ref[0]
     values = v_ref[0]
+    own_keys = sk_ref[0]
+    own_values = sv_ref[0]
     factor = 1.0 / math.sqrt(head_size)
+    tokens = q_ref.shape[1]
     col = lax.broadcasted_iota(jnp.int32, (1, keys.shape[0]), 1)
     visible = col < limit
+    key_token = key_offset + lax.broadcasted_iota(jnp.int32, (tokens, own_keys.shape[0]), 1)
+    query_token = lax.broadcasted_iota(jnp.int32, (tokens, own_keys.shape[0]), 0)
+    causal = key_token <= query_token
+    dims = (((1,), (1,)), ((), ()))
     for h in range(group_size):
-        q = q_ref[0, :, h * head_size:(h + 1) * head_size]
-        s = lax.dot_general(q, keys, (((1,), (1,)), ((), ())), preferred_element_type=jnp.float32) * factor
+        q = q_ref[0, :, h * head_size : (h + 1) * head_size]
+        s = lax.dot_general(q, keys, dims, preferred_element_type=jnp.float32) * factor
         s = jnp.where(visible, s, NEG_FILL)
-        m = jnp.max(s, axis=1, keepdims=True)
+        s_own = lax.dot_general(q, own_keys, dims, preferred_element_type=jnp.float32) * factor
+        s_own = jnp.where(causal, s_own, NEG_FILL)
+        m = jnp.maximum(
+            jnp.max(s, axis=1, keepdims=True), jnp.max(s_own, axis=1, keepdims=True)
+        )
         w = jnp.where(visible, jnp.exp(s - m), 0.0)
-        l = jnp.sum(w, axis=1, keepdims=True)
+        w_own = jnp.where(causal, jnp.exp(s_own - m), 0.0)
+        l = jnp.sum(w, axis=1, keepdims=True) + jnp.sum(w_own, axis=1, keepdims=True)
         num = jnp.dot(w.astype(jnp.bfloat16), values, preferred_element_type=jnp.float32)
+        num = num + jnp.dot(
+            w_own.astype(jnp.bfloat16), own_values, preferred_element_type=jnp.float32
+        )
         safe = jnp.maximum(l, 1.0)
-        o_ref[0, :, h * head_size:(h + 1) * head_size] = (num / safe).astype(o_ref.dtype)
-        lse_ref[0, :, h:h + 1] = m + jnp.log(safe)
-
-def prefill_partial(limits, queries, keys, values, group_size):
+        o_ref[0, :, h * head_size : (h + 1) * head_size] = (num / safe).astype(o_ref.dtype)
+        lse_ref[0, :, h : h + 1] = m + jnp.log(safe)
+
+
+def prefill_partial(info, queries, keys, values, own_keys, own_values, group_size):
     n, t, qw = queries.shape
     p, hd = keys.shape[1], keys.shape[2]
+    own = own_keys.shape[1]
     kern = functools.partial(_prefill_kernel, group_size=group_size, head_size=hd)
     return pl.pallas_call(
         kern,
@@ -52,17 +72,22 @@
             num_scalar_prefetch=1,
             grid=(n,),
             in_specs=[
-                pl.BlockSpec((1, t, qw), lambda c, lim: (c, 0, 0)),
-                pl.BlockSpec((1, p, hd), lambda c, lim: (c, 0, 0)),
-                pl.BlockSpec((1, p, hd), lambda c, lim: (c, 0, 0)),
+                pl.BlockSpec((1, t, qw), lambda c, info: (c, 0, 0)),
+                pl.BlockSpec((1, p, hd), lambda c, info: (c, 0, 0)),
+                pl.BlockSpec((1, p, hd), lambda c, info: (c, 0, 0)),
+                pl.BlockSpec((1, own, hd), lambda c, info: (c, 0, 0)),
+                pl.BlockSpec((1, own, hd), lambda c, info: (c, 0, 0)),
             ],
             out_specs=[
-                pl.BlockSpec((1, t, qw), lambda c, lim: (c, 0, 0)),
-                pl.BlockSpec((1, t, group_size), lambda c, lim: (c, 0, 0)),
+                pl.BlockSpec((1, t, qw), lambda c, info: (c, 0, 0)),
+                pl.BlockSpec((1, t, group_size), lambda c, info: (c, 0, 0)),
             ],
         ),
-        out_shape=[jax.ShapeDtypeStruct((n, t, qw), jnp.bfloat16), jax.ShapeDtypeStruct((n, t, group_size), jnp.float32)],
-    )(limits, queries, keys, values)
+        out_shape=[
+            jax.ShapeDtypeStruct((n, t, qw), jnp.bfloat16),
+            jax.ShapeDtypeStruct((n, t, group_size), jnp.float32),
+        ],
+    )(info, queries, keys, values, own_keys, own_values)
 
 
 def body(
@@ -91,19 +116,20 @@
     key_width = stretch_key.shape[2]
     stretch_rows = stretch_count * local_tok
 
-    stretch_pack = jnp.concatenate([stretch_query, stretch_key, stretch_value], axis=2).reshape(
-        stretch_rows, query_width + 2 * key_width
-    )
-    decode_pack = jnp.concatenate([new_query, new_key, new_value], axis=1)
-    pack = jnp.concatenate([stretch_pack, decode_pack], axis=0)
+    decode_kv = jnp.concatenate([new_key, new_value], axis=1)
+    decode_kv = jnp.pad(decode_kv, ((0, 0), (0, query_width - 2 * key_width)))
+    pack = jnp.concatenate(
+        [stretch_query.reshape(stretch_rows, query_width), new_query, decode_kv], axis=0
+    )
     gathered = lax.all_to_all(
         jnp.broadcast_to(pack[None], (seq_count,) + pack.shape), "seq", 0, 0, tiled=True
     )
-
-    decode_part = gathered[:, stretch_rows:, :].reshape(total_dec, query_width + 2 * key_width)
-    every_query = decode_part[:, :query_width]
-    every_key = decode_part[:, query_width : query_width + key_width]
-    every_value = decode_part[:, query_width + key_width :]
+    every_query = gathered[:, stretch_rows : stretch_rows + local_dec, :].reshape(
+        total_dec, query_width
+    )
+    every_kv = gathered[:, stretch_rows + local_dec :, :].reshape(total_dec, query_width)
+    every_key = every_kv[:, :key_width]
+    every_value = every_kv[:, key_width : 2 * key_width]
     slot_ids = seq_rank * local_dec + jnp.arange(local_dec, dtype=jnp.int32)
     arrival_ids = jnp.arange(total_dec, dtype=jnp.int32)
     sources = jnp.sum(
@@ -135,16 +161,17 @@
     rows_per_src = local_tok * group_size
     row_count = seq_count * rows_per_src
     prior_pos = seq_rank * prior_span + jnp.arange(prior_span, dtype=jnp.int32)
-    stretch_part = gathered[:, :stretch_rows, :].reshape(
-        seq_count, stretch_count, local_tok, query_width + 2 * key_width
-    )
     queries_all = (
-        stretch_part[:, :, :, :query_width]
+        gathered[:, :stretch_rows, :]
+        .reshape(seq_count, stretch_count, local_tok, query_width)
         .transpose(1, 0, 2, 3)
         .reshape(stretch_count, seq_count * local_tok, query_width)
     )
     limits = jnp.clip(stretch_start - seq_rank * prior_span, 0, prior_span).astype(jnp.int32)
-    part_out, part_lse = prefill_partial(limits, queries_all, prior_keys, prior_values, group_size)
+    info = jnp.concatenate([limits, (seq_rank * local_tok).astype(jnp.int32)[None]])
+    part_out, part_lse = prefill_partial(
+        info, queries_all, prior_keys, prior_values, stretch_key, stretch_value, group_size
+    )
     part_out = part_out.reshape(stretch_count, row_count, head_size)
     part_lse = part_lse.reshape(stretch_count, row_count)
     lse_hi = lax.reduce_precision(part_lse, exponent_bits=8, mantissa_bits=7)
@@ -196,34 +223,10 @@
         jnp.bfloat16
     )
 
-    stretch_len = local_tok * seq_count
-    local_rows = local_tok * group_size
-    stretch_pos = jnp.arange(stretch_len, dtype=jnp.int32)
-    own_token = seq_rank * local_tok + jnp.arange(local_rows, dtype=jnp.int32) // group_size
-    causal = stretch_pos[None, :] <= own_token[:, None]
-    self_tops, self_totals, self_numers = ([], [], [])
-    for stretch_index in range(stretch_count):
-        local_queries = stretch_query[stretch_index].reshape(local_rows, head_size)
-        keys_all = stretch_part[:, stretch_index, :, query_width : query_width + key_width].reshape(
-            stretch_len, key_width
-        )
-        values_all = stretch_part[:, stretch_index, :, query_width + key_width :].reshape(
-            stretch_len, key_width
-        )
-        pieces = partial_attend(local_queries, keys_all, values_all, causal)
-        self_tops.append(pieces[0].reshape(local_tok, group_size))
-        self_totals.append(pieces[1].reshape(local_tok, group_size))
-        self_numers.append(pieces[2].reshape(local_tok, group_size, head_size))
-    self_top = jnp.stack(self_tops)
-    self_sum = jnp.stack(self_totals)
-    self_num = jnp.stack(self_numers)
-    final_top = jnp.maximum(jnp.max(got_lse, axis=0), self_top + jnp.log(self_sum))
+    final_top = jnp.max(got_lse, axis=0)
     part_factor = jnp.exp(got_lse - final_top[None])
-    self_factor = jnp.exp(self_top - final_top)
-    total_sum = jnp.sum(part_factor, axis=0) + self_sum * self_factor
-    total_num = (
-        jnp.sum(got_out * part_factor[..., None], axis=0) + self_num * self_factor[..., None]
-    )
+    total_sum = jnp.sum(part_factor, axis=0)
+    total_num = jnp.sum(got_out * part_factor[..., None], axis=0)
     stretch_out = (
         (total_num / total_sum[..., None])
         .astype(jnp.bfloat16)

time: 142 us -> 128 us (0.901)
  local copies, waits for them, and re-layouts: 21.9 us -> 12.6 us
  other arithmetic: 14.6 us -> 8.11 us
  matrix products: 3.68 us -> 1.14 us
  waiting for transfers between devices: 61.7 us -> 64.1 us
  Pallas kernels: 13.7 us -> 15.7 us
    all_to_all x1, waiting for transfers between devices: 23.6 us -> 32.8 us  [body(): received = lax.all_to_all(payload, 'seq', 0, 0, tiled=True)]
    all_to_all x1, waiting for transfers between devices: 38.1 us -> 31.3 us  [body(): lax.all_to_all(jnp.broadcast_to(pack[None], (seq_count,) + pack.shape), '...]
    another operation x16 -> x0, local copies, waits for them, and re-layouts: 2.97 us -> none  [the longest x3 1.36 us: body(): self_num = jnp.stack(self_numers)]
    slice x5 -> x2, local copies, waits for them, and re-layouts: 2.91 us -> 0.04 us  [the longest x1 0.04 us: body(): gathered[:, stretch_rows:stretch_rows + local_dec, :]]
    dot_general x4 -> x1, matrix products: 2.56 us -> 0.49 us  [partial_attend(): jnp.dot(queries, keys.T, preferred_element_type=jnp.float32) * factor]
    pallas_call x1, Pallas kernels: 13.7 us -> 15.7 us  [prefill_partial(): pl.pallas_call(kern, grid_spec=pltpu.PrefetchScalarGridSpec(num_scalar_pr...]
    transpose x2 -> x0, local copies, waits for them, and re-layouts: 1.52 us -> none  [body(): queries_all = stretch_part[:, :, :, :query_width].transpose(1, 0, 2, 3).r...]
    unnamed x42 -> x20, local copies, waits for them, and re-layouts: 3.23 us -> 1.71 us
  transfers between devices with their start and end apart: 2 -> 2, of which waited for: 2 -> 2; matrix products, arithmetic and copies ran while one was open for 9% -> 1% of each run, Pallas kernels for 0% -> 0%
where the time goes in v5:
time: 128 us; the launch traced here: 127 us
  waiting for transfers between devices  64.1 us (50%)
  Pallas kernels  15.7 us (12%)
  local copies, waits for them, and re-layouts  12.6 us (10%)
  starting transfers between devices  11.2 us (9%)
  blocking collectives  10.2 us (8%)
  other arithmetic  8.11 us (6%)
  between operations  4.14 us (3%)
    all_to_all x1, waiting for transfers between devices, body(): received = lax.all_to_all(payload, 'seq', 0, 0, tiled=True)  32.8 us
    all_to_all x1, waiting for transfers between devices, body(): lax.all_to_all(jnp.broadcast_to(pack[None], (seq_count,) + pack.shape), '...  31.3 us
    pallas_call x1, Pallas kernels, prefill_partial(): pl.pallas_call(kern, grid_spec=pltpu.PrefetchScalarGridSpec(num_scalar_pr...  15.7 us
    unnamed x1, blocking collectives  10.2 us
    all_to_all x1, starting transfers between devices, body(): lax.all_to_all(jnp.broadcast_to(pack[None], (seq_count,) + pack.shape), '...  7.41 us
    all_to_all x1, starting transfers between devices, body(): received = lax.all_to_all(payload, 'seq', 0, 0, tiled=True)  3.77 us
    another operation x2, local copies, waits for them, and re-layouts, body(): part_out.reshape(stretch_count, seq_count, rows_per_src, head_size)  2.98 us
  transfers between devices with their start and end apart: 2, of which 2 were waited for; matrix products, arithmetic and copies ran while one was open for 1% of the time, Pallas kernels for 0%

profile of v5, /device:TPU:0, one launch (start us, length us, event | category | flops | bytes accessed | tf_op | source)
XLA Modules:
  0.0 127.0 jit_solution(13647100570500675391)
XLA Ops:
  0.6 0.8 fusion.20
  1.4 1.0 pad_maximum_fusion.1
  2.4 1.3 broadcast_in_dim.81
  3.6 7.4 %all-to-all-start = ((bf16[8,98,896]{2,1,0:T(8,128)(2,1)}), bf16[8,98,896]{2,1,0:T(8,128)(2,1)S(1)}, u32[]{:S(2)}, u32[]{:S(2)}) async-start(bf16[8,98,896]{2,1,0:T(8,128)(2,1)} %broadcast_in_dim.81), calls=%async_computation | async-start | bytes 2981888 | tf_op jit(solution)/shard_map/all_to_all | solution.py:124
  11.0 0.6 compare_select_fusion.2
  15.0 31.3 %all-to-all-done = bf16[8,98,896]{2,1,0:T(8,128)(2,1)S(1)} async-done(((bf16[8,98,896]{2,1,0:T(8,128)(2,1)}), bf16[8,98,896]{2,1,0:T(8,128)(2,1)S(1)}, u32[]{:S(2)}, u32[]{:S(2)}) %all-to-all-start) | async-done | bytes 1404960 | tf_op jit(solution)/shard_map/all_to_all | solution.py:124
  46.5 1.2 copy.26
  47.7 15.7 %shard_map.149 = (bf16[3,256,896]{2,1,0:T(8,128)(2,1)}, f32[3,256,7]{2,1,0:T(8,128)}) custom-call(s32[4]{0:T(128)} %pad_add_fusion.info_ref, bf16[3,256,896]{2,1,0:T(8,128)(2,1)} %bitcast.66, bf16[3,1024,128]{2,1,0:T(8,128)(2,1)} %k_ref.1, bf16[3,1024,128]{2,1,0:T(8,128)(2,1)} %v_ref.1, bf16[3,32,128]{2,1,0:T(8,128)(2,1)} %sk_ref.1, bf16[3,32,128]{2,1,0:T(8,128)(2,1)} %sv_ref.1), custom_call_target="tpu_custom_call" | custom-call | tf_op jit(solution)/shard_map/pallas_call | solution.py:69
  63.4 1.2 reshape.211
  64.8 2.9 %reshape_reshape.3 = bf16[3,8,224,128]{3,2,1,0:T(8,128)(2,1)S(1)} reshape(bf16[3,256,896]{2,1,0:T(8,128)(2,1)} %get-tuple-element.5) | data formatting | bytes 2752512 | tf_op jit(solution)/shard_map/reshape;reshape | solution.py:195
  67.8 1.1 copy-done.2
  69.9 1.2 pad_maximum_fusion
  71.2 3.8 %all-to-all-start.1 = ((bf16[8,695,128]{2,1,0:T(8,128)(2,1)}), bf16[8,695,128]{2,1,0:T(8,128)(2,1)S(1)}, u32[]{:S(2)}, u32[]{:S(2)}) async-start(bf16[8,695,128]{2,1,0:T(8,128)(2,1)} %pad_maximum_fusion), calls=%async_computation.1 | async-start | bytes 2850816 | tf_op jit(solution)/shard_map/all_to_all | solution.py:205
  75.0 0.6 dynamic-slice.12
  76.2 32.8 %all-to-all-done.1 = bf16[8,695,128]{2,1,0:T(8,128)(2,1)S(1)} async-done(((bf16[8,695,128]{2,1,0:T(8,128)(2,1)}), bf16[8,695,128]{2,1,0:T(8,128)(2,1)S(1)}, u32[]{:S(2)}, u32[]{:S(2)}) %all-to-all-start.1) | async-done | bytes 1423392 | tf_op jit(solution)/shard_map/all_to_all | solution.py:205
  109.0 1.1 reshape.263
  110.1 0.9 fusion.29
  110.9 1.2 add.43
  112.1 1.1 fusion.7
  113.7 0.9 multiply_reduce_fusion
  114.7 0.6 gather_fusion
  115.6 10.2 %all-reduce.2 = bf16[8,448]{1,0:T(8,128)(2,1)S(1)} all-reduce(f32[8,448]{1,0:T(8,128)S(1)} %fusion.15), channel_id=2, replica_groups=mesh['seq'=8,'tp'=4] {'tp'}, use_global_device_ids=true, to_apply=%region_3.5.clone | all-reduce | flops 3584 | bytes 21504
  125.7 0.7 divide_convert_fusion
  126.5 0.6 dynamic-slice_convert_fusion
  (45 shorter events, 3.0 us)
Async XLA Ops:
  0.6 114.6 %copy-start = (bf16[896,448]{0,1:T(8,128)(2,1)S(1)}, bf16[896,448]{0,1:T(8,128)(2,1)}, u32[]{:S(2)}) copy-start(bf16[896,448]{0,1:T(8,128)(2,1)} %param.23) | copy-start | bytes 2408452
  3.6 7.4 %copy-start.1 = (s32[8]{0:T(128)S(1)}, s32[8]{0:T(128)}, u32[]{:S(2)}) copy-start(s32[8]{0:T(128)} %param.22) | copy-start | bytes 100
  3.6 10.7 %copy-start.4 = (s32[3]{0:T(128)S(1)}, s32[3]{0:T(128)}, u32[]{:S(2)}) copy-start(s32[3]{0:T(128)} %param.29) | copy-start | bytes 40
  3.6 42.7 %all-to-all-start = ((bf16[8,98,896]{2,1,0:T(8,128)(2,1)}), bf16[8,98,896]{2,1,0:T(8,128)(2,1)S(1)}, u32[]{:S(2)}, u32[]{:S(2)}) async-start(bf16[8,98,896]{2,1,0:T(8,128)(2,1)} %broadcast_in_dim.81), calls=%async_computation | async-start | bytes 2981888 | tf_op jit(solution)/shard_map/all_to_all | solution.py:124
  67.7 1.2 copy-start.2
  67.8 1.8 %copy-start.3 = (bf16[1,4096,128]{2,1,0:T(8,128)(2,1)S(1)}, bf16[1,4096,128]{2,1,0:T(8,128)(2,1)}, u32[]{:S(2)}) copy-start(bf16[1,4096,128]{2,1,0:T(8,128)(2,1)} %param.20) | copy-start | bytes 3145732
  71.2 3.8 %copy-start.5 = (u32[32]{0:T(128)S(1)}, u32[32]{0:T(128)}, u32[]{:S(2)}) copy-start(u32[32]{0:T(128)} %constant.130) | copy-start | bytes 388
  71.2 37.8 %all-to-all-start.1 = ((bf16[8,695,128]{2,1,0:T(8,128)(2,1)}), bf16[8,695,128]{2,1,0:T(8,128)(2,1)S(1)}, u32[]{:S(2)}, u32[]{:S(2)}) async-start(bf16[8,695,128]{2,1,0:T(8,128)(2,1)} %pad_maximum_fusion), calls=%async_computation.1 | async-start | bytes 2850816 | tf_op jit(solution)/shard_map/all_to_all | solution.py:205

commit v6 on v5

--- a/solution.py
+++ b/solution.py
@@ -156,6 +156,14 @@
     home_out = jax.vmap(decode_slot)(
         home_query, home_key, home_value, cache_keys, cache_values, cache_length
     )
+    all_out = lax.all_to_all(
+        jnp.broadcast_to(home_out[None], (seq_count,) + home_out.shape), "seq", 0, 0, tiled=True
+    ).reshape(total_dec, group_size * head_size)
+    arrival_out = jnp.take(all_out, dealing, axis=0)
+    arrival_terms = jnp.dot(arrival_out, out_weight, preferred_element_type=jnp.float32)
+    decode_mixed = lax.psum_scatter(arrival_terms, "tp", scatter_dimension=0, tiled=True).astype(
+        jnp.bfloat16
+    )
 
     prior_span = prior_keys.shape[1]
     rows_per_src = local_tok * group_size
@@ -196,9 +204,6 @@
             .transpose(1, 0, 2, 3)
             .reshape(seq_count, out_rows, head_size),
             stats.reshape(seq_count, stat_rows, head_size),
-            jnp.broadcast_to(
-                home_out.reshape(1, dec_rows, head_size), (seq_count, dec_rows, head_size)
-            ),
         ],
         axis=1,
     )
@@ -215,13 +220,6 @@
         .reshape(seq_count, 3, stretch_count, local_tok, group_size)
     )
     got_lse = (got_stats[:, 0] + got_stats[:, 1]) + got_stats[:, 2]
-    all_out = received[:, out_rows + stat_rows :, :].reshape(total_dec, group_size * head_size)
-
-    arrival_out = jnp.take(all_out, dealing, axis=0)
-    arrival_terms = jnp.dot(arrival_out, out_weight, preferred_element_type=jnp.float32)
-    decode_mixed = lax.psum_scatter(arrival_terms, "tp", scatter_dimension=0, tiled=True).astype(
-        jnp.bfloat16
-    )
 
     final_top = jnp.max(got_lse, axis=0)
     part_factor = jnp.exp(got_lse - final_top[None])

time: 128 us -> 123 us (0.961)
  waiting for transfers between devices: 64.1 us -> 49.4 us
  starting transfers between devices: 11.2 us -> 17.4 us
  local copies, waits for them, and re-layouts: 12.6 us -> 14 us
    all_to_all x1, waiting for transfers between devices: 32.8 us -> 18.6 us  [body(): received = lax.all_to_all(payload, 'seq', 0, 0, tiled=True)]
    all_to_all x0 -> x1, starting transfers between devices: none -> 3.94 us  [body(): lax.all_to_all(jnp.broadcast_to(home_out[None], (seq_count,) + home_out.s...]
    all_to_all x1, starting transfers between devices: 3.77 us -> 6.04 us  [body(): received = lax.all_to_all(payload, 'seq', 0, 0, tiled=True)]
    unnamed x20 -> x25, local copies, waits for them, and re-layouts: 1.71 us -> 2.63 us
  transfers between devices with their start and end apart: 2 -> 3, of which waited for: 2 -> 2; matrix products, arithmetic and copies ran while one was open for 1% -> 8% of each run, Pallas kernels for 0% -> 13%
where the time goes in v6:
time: 123 us; the launch traced here: 122 us
  waiting for transfers between devices  49.4 us (40%)
  starting transfers between devices  17.4 us (14%)
  Pallas kernels  15.7 us (13%)
  local copies, waits for them, and re-layouts  14 us (11%)
  blocking collectives  10.7 us (9%)
  other arithmetic  9.36 us (8%)
  between operations  4.15 us (3%)
    all_to_all x1, waiting for transfers between devices, body(): lax.all_to_all(jnp.broadcast_to(pack[None], (seq_count,) + pack.shape), '...  30.8 us
    all_to_all x1, waiting for transfers between devices, body(): received = lax.all_to_all(payload, 'seq', 0, 0, tiled=True)  18.6 us
    pallas_call x1, Pallas kernels, prefill_partial(): pl.pallas_call(kern, grid_spec=pltpu.PrefetchScalarGridSpec(num_scalar_pr...  15.7 us
    unnamed x1, blocking collectives  10.7 us
    all_to_all x1, starting transfers between devices, body(): lax.all_to_all(jnp.broadcast_to(pack[None], (seq_count,) + pack.shape), '...  7.41 us
    all_to_all x1, starting transfers between devices, body(): received = lax.all_to_all(payload, 'seq', 0, 0, tiled=True)  6.04 us
    all_to_all x1, starting transfers between devices, body(): lax.all_to_all(jnp.broadcast_to(home_out[None], (seq_count,) + home_out.s...  3.94 us
    another operation x2, local copies, waits for them, and re-layouts, body(): part_out.reshape(stretch_count, seq_count, rows_per_src, head_size)  2.97 us
  transfers between devices with their start and end apart: 3, of which 2 were waited for; matrix products, arithmetic and copies ran while one was open for 8% of the time, Pallas kernels for 13%

profile of v6, /device:TPU:0, one launch (start us, length us, event | category | flops | bytes accessed | tf_op | source)
XLA Modules:
  0.0 121.8 jit_solution(16151425327270515846)
XLA Ops:
  0.6 0.8 fusion.21
  1.4 1.0 pad_maximum_fusion.1
  2.4 1.3 %broadcast_in_dim.86 = bf16[8,98,896]{2,1,0:T(8,128)(2,1)} broadcast(bf16[98,896]{1,0:T(8,128)(2,1)S(1)} %pad_maximum_fusion.1), dimensions={1,2} | broadcast | bytes 1580544 | tf_op jit(solution)/shard_map/broadcast_in_dim | solution.py:125
  3.6 7.4 %all-to-all-start = ((bf16[8,98,896]{2,1,0:T(8,128)(2,1)}), bf16[8,98,896]{2,1,0:T(8,128)(2,1)S(1)}, u32[]{:S(2)}, u32[]{:S(2)}) async-start(bf16[8,98,896]{2,1,0:T(8,128)(2,1)} %broadcast_in_dim.86), calls=%async_computation | async-start | bytes 2981888 | tf_op jit(solution)/shard_map/all_to_all | solution.py:124
  11.7 1.1 compare_select_fusion.2
  15.5 30.8 %all-to-all-done = bf16[8,98,896]{2,1,0:T(8,128)(2,1)S(1)} async-done(((bf16[8,98,896]{2,1,0:T(8,128)(2,1)}), bf16[8,98,896]{2,1,0:T(8,128)(2,1)S(1)}, u32[]{:S(2)}, u32[]{:S(2)}) %all-to-all-start) | async-done | bytes 1404960 | tf_op jit(solution)/shard_map/all_to_all | solution.py:124
  46.4 1.2 copy.24
  49.8 0.7 reduce.12
  50.5 0.7 reshape.309
  51.2 3.9 %all-to-all-start.1 = ((bf16[8,2,448]{2,1,0:T(2,128)(2,1)}), bf16[8,2,448]{2,1,0:T(2,128)(2,1)}, u32[]{:S(2)}, u32[]{:S(2)}) async-start(bf16[8,2,448]{2,1,0:T(2,128)(2,1)} %reshape.309), calls=%async_computation.1 | async-start | bytes 32768 | tf_op jit(solution)/shard_map/all_to_all | solution.py:159
  55.2 15.7 %shard_map.149 = (bf16[3,256,896]{2,1,0:T(8,128)(2,1)}, f32[3,256,7]{2,1,0:T(8,128)}) custom-call(s32[4]{0:T(128)} %pad_add_fusion.info_ref, bf16[3,256,896]{2,1,0:T(8,128)(2,1)} %bitcast.65, bf16[3,1024,128]{2,1,0:T(8,128)(2,1)} %k_ref.1, bf16[3,1024,128]{2,1,0:T(8,128)(2,1)} %v_ref.1, bf16[3,32,128]{2,1,0:T(8,128)(2,1)} %sk_ref.1, bf16[3,32,128]{2,1,0:T(8,128)(2,1)} %sv_ref.1), custom_call_target="tpu_custom_call" | custom-call | tf_op jit(solution)/shard_map/pallas_call | solution.py:69
  70.9 2.9 %reshape_reshape.3 = bf16[3,8,224,128]{3,2,1,0:T(8,128)(2,1)S(1)} reshape(bf16[3,256,896]{2,1,0:T(8,128)(2,1)} %get-tuple-element.5) | data formatting | bytes 2752512 | tf_op jit(solution)/shard_map/reshape;reshape | solution.py:203
  73.8 1.2 reshape.220
  75.2 1.2 pad_maximum_fusion
  76.4 6.0 %all-to-all-start.2 = ((bf16[8,688,128]{2,1,0:T(8,128)(2,1)}), bf16[8,688,128]{2,1,0:T(8,128)(2,1)S(1)}, u32[]{:S(2)}, u32[]{:S(2)}) async-start(bf16[8,688,128]{2,1,0:T(8,128)(2,1)} %pad_maximum_fusion), calls=%async_computation.2 | async-start | bytes 2818048 | tf_op jit(solution)/shard_map/all_to_all | solution.py:210
  83.8 0.8 reshape.310
  85.5 10.7 %all-reduce.2 = bf16[8,448]{1,0:T(8,128)(2,1)S(1)} all-reduce(f32[8,448]{1,0:T(8,128)S(1)} %fusion.16), channel_id=2, replica_groups=mesh['seq'=8,'tp'=4] {'tp'}, use_global_device_ids=true, to_apply=%region_3.5.clone | all-reduce | flops 3584 | bytes 21504
  96.9 18.6 %all-to-all-done.2 = bf16[8,688,128]{2,1,0:T(8,128)(2,1)S(1)} async-done(((bf16[8,688,128]{2,1,0:T(8,128)(2,1)}), bf16[8,688,128]{2,1,0:T(8,128)(2,1)S(1)}, u32[]{:S(2)}, u32[]{:S(2)}) %all-to-all-start.2) | async-done | bytes 1409056 | tf_op jit(solution)/shard_map/all_to_all | solution.py:210
  115.5 1.1 reshape.267
  116.5 0.9 fusion.30
  117.6 1.1 fusion.8
  118.6 1.2 add.43
  119.9 0.9 multiply_reduce_fusion
  121.1 0.7 divide_convert_fusion
  (54 shorter events, 5.8 us)
Async XLA Ops:
  0.6 84.6 %copy-start = (bf16[896,448]{0,1:T(8,128)(2,1)S(1)}, bf16[896,448]{0,1:T(8,128)(2,1)}, u32[]{:S(2)}) copy-start(bf16[896,448]{0,1:T(8,128)(2,1)} %param.23) | copy-start | bytes 2408452
  3.6 8.1 %copy-start.2 = (s32[8]{0:T(128)S(1)}, s32[8]{0:T(128)}, u32[]{:S(2)}) copy-start(s32[8]{0:T(128)} %param.22) | copy-start | bytes 100
  3.6 11.3 %copy-start.6 = (s32[3]{0:T(128)S(1)}, s32[3]{0:T(128)}, u32[]{:S(2)}) copy-start(s32[3]{0:T(128)} %param.29) | copy-start | bytes 40
  3.6 42.7 %all-to-all-start = ((bf16[8,98,896]{2,1,0:T(8,128)(2,1)}), bf16[8,98,896]{2,1,0:T(8,128)(2,1)S(1)}, u32[]{:S(2)}, u32[]{:S(2)}) async-start(bf16[8,98,896]{2,1,0:T(8,128)(2,1)} %broadcast_in_dim.86), calls=%async_computation | async-start | bytes 2981888 | tf_op jit(solution)/shard_map/all_to_all | solution.py:124
  46.4 1.6 %copy-start.4 = (bf16[1,4096,128]{2,1,0:T(8,128)(2,1)S(1)}, bf16[1,4096,128]{2,1,0:T(8,128)(2,1)}, u32[]{:S(2)}) copy-start(bf16[1,4096,128]{2,1,0:T(8,128)(2,1)} %param.19) | copy-start | bytes 3145732
  47.6 1.3 %copy-start.5 = (bf16[1,4096,128]{2,1,0:T(8,128)(2,1)S(1)}, bf16[1,4096,128]{2,1,0:T(8,128)(2,1)}, u32[]{:S(2)}) copy-start(bf16[1,4096,128]{2,1,0:T(8,128)(2,1)} %param.20) | copy-start | bytes 3145732
  51.2 25.2 %all-to-all-start.1 = ((bf16[8,2,448]{2,1,0:T(2,128)(2,1)}), bf16[8,2,448]{2,1,0:T(2,128)(2,1)}, u32[]{:S(2)}, u32[]{:S(2)}) async-start(bf16[8,2,448]{2,1,0:T(2,128)(2,1)} %reshape.309), calls=%async_computation.1 | async-start | bytes 32768 | tf_op jit(solution)/shard_map/all_to_all | solution.py:159
  76.4 6.1 %copy-start.7 = (u32[32]{0:T(128)S(1)}, u32[32]{0:T(128)}, u32[]{:S(2)}) copy-start(u32[32]{0:T(128)} %constant.130) | copy-start | bytes 388
  76.4 7.3 %copy-start.1 = (s32[8]{0:T(128)S(1)}, s32[8]{0:T(128)}, u32[]{:S(2)}) copy-start(s32[8]{0:T(128)} %get-tuple-element.38) | copy-start | bytes 100
  76.4 7.3 %copy-start.3 = (s32[8]{0:T(128)S(1)}, s32[8]{0:T(128)}, u32[]{:S(2)}) copy-start(s32[8]{0:T(128)} %param.22) | copy-start | bytes 100
  76.4 39.0 %all-to-all-start.2 = ((bf16[8,688,128]{2,1,0:T(8,128)(2,1)}), bf16[8,688,128]{2,1,0:T(8,128)(2,1)S(1)}, u32[]{:S(2)}, u32[]{:S(2)}) async-start(bf16[8,688,128]{2,1,0:T(8,128)(2,1)} %pad_maximum_fusion), calls=%async_computation.2 | async-start | bytes 2818048 | tf_op jit(solution)/shard_map/all_to_all | solution.py:210

commit v7 on v6

--- a/solution.py
+++ b/solution.py
@@ -23,7 +23,7 @@
 
 
 def _prefill_kernel(
-    info_ref, q_ref, k_ref, v_ref, sk_ref, sv_ref, o_ref, lse_ref, *, group_size, head_size
+    info_ref, q_ref, k_ref, v_ref, sk_ref, sv_ref, o_ref, lse_ref, *, group_size, head_size, local_tok
 ):
     c = pl.program_id(0)
     limit = info_ref[c]
@@ -33,15 +33,17 @@
     own_keys = sk_ref[0]
     own_values = sv_ref[0]
     factor = 1.0 / math.sqrt(head_size)
-    tokens = q_ref.shape[1]
+    src_count, tok_block, _ = q_ref.shape
+    tokens = src_count * tok_block
     col = lax.broadcasted_iota(jnp.int32, (1, keys.shape[0]), 1)
     visible = col < limit
     key_token = key_offset + lax.broadcasted_iota(jnp.int32, (tokens, own_keys.shape[0]), 1)
-    query_token = lax.broadcasted_iota(jnp.int32, (tokens, own_keys.shape[0]), 0)
+    row = lax.broadcasted_iota(jnp.int32, (tokens, own_keys.shape[0]), 0)
+    query_token = (row // tok_block) * local_tok + row % tok_block
     causal = key_token <= query_token
     dims = (((1,), (1,)), ((), ()))
     for h in range(group_size):
-        q = q_ref[0, :, h * head_size : (h + 1) * head_size]
+        q = q_ref[:, :, h * head_size : (h + 1) * head_size].reshape(tokens, head_size)
         s = lax.dot_general(q, keys, dims, preferred_element_type=jnp.float32) * factor
         s = jnp.where(visible, s, NEG_FILL)
         s_own = lax.dot_general(q, own_keys, dims, preferred_element_type=jnp.float32) * factor
@@ -49,43 +51,53 @@
         m = jnp.maximum(
             jnp.max(s, axis=1, keepdims=True), jnp.max(s_own, axis=1, keepdims=True)
         )
-        w = jnp.where(visible, jnp.exp(s - m), 0.0)
-        w_own = jnp.where(causal, jnp.exp(s_own - m), 0.0)
+        w = jnp.exp(s - m)
+        w_own = jnp.exp(s_own - m)
+        empty = m < 0.5 * NEG_FILL
         l = jnp.sum(w, axis=1, keepdims=True) + jnp.sum(w_own, axis=1, keepdims=True)
         num = jnp.dot(w.astype(jnp.bfloat16), values, preferred_element_type=jnp.float32)
         num = num + jnp.dot(
             w_own.astype(jnp.bfloat16), own_values, preferred_element_type=jnp.float32
         )
+        l = jnp.where(empty, 0.0, l)
+        num = jnp.where(empty, 0.0, num)
         safe = jnp.maximum(l, 1.0)
-        o_ref[0, :, h * head_size : (h + 1) * head_size] = (num / safe).astype(o_ref.dtype)
+        o_ref[:, :, h * head_size : (h + 1) * head_size] = (
+            (num / safe).astype(o_ref.dtype).reshape(src_count, tok_block, head_size)
+        )
         lse_ref[0, :, h : h + 1] = m + jnp.log(safe)
 
 
-def prefill_partial(info, queries, keys, values, own_keys, own_values, group_size):
-    n, t, qw = queries.shape
-    p, hd = keys.shape[1], keys.shape[2]
+def prefill_partial(
+    info, queries, keys, values, own_keys, own_values, group_size, tok_block, local_tok, out_rows
+):
+    src_count, _, qw = queries.shape
+    n, p, hd = keys.shape
     own = own_keys.shape[1]
-    kern = functools.partial(_prefill_kernel, group_size=group_size, head_size=hd)
+    tokens = src_count * tok_block
+    kern = functools.partial(
+        _prefill_kernel, group_size=group_size, head_size=hd, local_tok=local_tok
+    )
     return pl.pallas_call(
         kern,
         grid_spec=pltpu.PrefetchScalarGridSpec(
             num_scalar_prefetch=1,
             grid=(n,),
             in_specs=[
-                pl.BlockSpec((1, t, qw), lambda c, info: (c, 0, 0)),
+                pl.BlockSpec((src_count, tok_block, qw), lambda c, info: (0, c, 0)),
                 pl.BlockSpec((1, p, hd), lambda c, info: (c, 0, 0)),
                 pl.BlockSpec((1, p, hd), lambda c, info: (c, 0, 0)),
                 pl.BlockSpec((1, own, hd), lambda c, info: (c, 0, 0)),
                 pl.BlockSpec((1, own, hd), lambda c, info: (c, 0, 0)),
             ],
             out_specs=[
-                pl.BlockSpec((1, t, qw), lambda c, info: (c, 0, 0)),
-                pl.BlockSpec((1, t, group_size), lambda c, info: (c, 0, 0)),
+                pl.BlockSpec((src_count, tok_block, qw), lambda c, info: (0, c, 0)),
+                pl.BlockSpec((1, tokens, group_size), lambda c, info: (c, 0, 0)),
             ],
         ),
         out_shape=[
-            jax.ShapeDtypeStruct((n, t, qw), jnp.bfloat16),
-            jax.ShapeDtypeStruct((n, t, group_size), jnp.float32),
+            jax.ShapeDtypeStruct((src_count, out_rows, qw), jnp.bfloat16),
+            jax.ShapeDtypeStruct((n, tokens, group_size), jnp.float32),
         ],
     )(info, queries, keys, values, own_keys, own_values)
 
@@ -166,65 +178,67 @@
     )
 
     prior_span = prior_keys.shape[1]
-    rows_per_src = local_tok * group_size
-    row_count = seq_count * rows_per_src
-    prior_pos = seq_rank * prior_span + jnp.arange(prior_span, dtype=jnp.int32)
-    queries_all = (
-        gathered[:, :stretch_rows, :]
-        .reshape(seq_count, stretch_count, local_tok, query_width)
-        .transpose(1, 0, 2, 3)
-        .reshape(stretch_count, seq_count * local_tok, query_width)
-    )
+    direct = local_tok % 16 == 0
+    stat_count = 3 * stretch_count * local_tok * group_size
+    stat_rows = -(-stat_count // query_width)
+    out_rows = stretch_rows
     limits = jnp.clip(stretch_start - seq_rank * prior_span, 0, prior_span).astype(jnp.int32)
     info = jnp.concatenate([limits, (seq_rank * local_tok).astype(jnp.int32)[None]])
-    part_out, part_lse = prefill_partial(
-        info, queries_all, prior_keys, prior_values, stretch_key, stretch_value, group_size
-    )
-    part_out = part_out.reshape(stretch_count, row_count, head_size)
-    part_lse = part_lse.reshape(stretch_count, row_count)
+    if direct:
+        payload, part_lse = prefill_partial(
+            info, gathered, prior_keys, prior_values, stretch_key, stretch_value, group_size,
+            local_tok, local_tok, out_rows + stat_rows,
+        )
+    else:
+        token_count = seq_count * local_tok
+        queries_all = (
+            gathered[:, :stretch_rows, :]
+            .reshape(seq_count, stretch_count, local_tok, query_width)
+            .transpose(1, 0, 2, 3)
+            .reshape(1, stretch_rows * seq_count, query_width)
+        )
+        flat_out, part_lse = prefill_partial(
+            info, queries_all, prior_keys, prior_values, stretch_key, stretch_value, group_size,
+            token_count, token_count, stretch_rows * seq_count,
+        )
+        payload = jnp.pad(
+            flat_out.reshape(stretch_count, seq_count, local_tok, query_width)
+            .transpose(1, 0, 2, 3)
+            .reshape(seq_count, out_rows, query_width),
+            ((0, 0), (0, stat_rows), (0, 0)),
+        )
+    part_lse = part_lse.reshape(stretch_count, seq_count, local_tok, group_size)
     lse_hi = lax.reduce_precision(part_lse, exponent_bits=8, mantissa_bits=7)
     lse_rest = part_lse - lse_hi
     lse_mid = lax.reduce_precision(lse_rest, exponent_bits=8, mantissa_bits=7)
     lse_lo = lse_rest - lse_mid
-    stat_count = 3 * stretch_count * rows_per_src
-    stat_rows = -(-stat_count // head_size)
     stats = (
         jnp.stack([lse_hi, lse_mid, lse_lo])
-        .reshape(3, stretch_count, seq_count, rows_per_src)
-        .transpose(2, 0, 1, 3)
+        .transpose(2, 0, 1, 3, 4)
         .reshape(seq_count, stat_count)
     )
-    stats = jnp.pad(stats, ((0, 0), (0, stat_rows * head_size - stat_count))).astype(jnp.bfloat16)
-
-    dec_rows = local_dec * group_size
-    out_rows = stretch_count * rows_per_src
-    payload = jnp.concatenate(
-        [
-            part_out.reshape(stretch_count, seq_count, rows_per_src, head_size)
-            .transpose(1, 0, 2, 3)
-            .reshape(seq_count, out_rows, head_size),
-            stats.reshape(seq_count, stat_rows, head_size),
-        ],
-        axis=1,
-    )
+    stats = jnp.pad(stats, ((0, 0), (0, stat_rows * query_width - stat_count)))
+    payload = lax.dynamic_update_slice(
+        payload,
+        stats.astype(jnp.bfloat16).reshape(seq_count, stat_rows, query_width),
+        (0, out_rows, 0),
+    )
+
     received = lax.all_to_all(payload, "seq", 0, 0, tiled=True)
-    got_out = (
-        received[:, :out_rows, :]
-        .reshape(seq_count, stretch_count, local_tok, group_size, head_size)
-        .astype(jnp.float32)
+    got_out = received[:, :out_rows, :].reshape(
+        seq_count, stretch_count, local_tok, group_size, head_size
     )
     got_stats = (
-        received[:, out_rows : out_rows + stat_rows, :]
-        .reshape(seq_count, stat_rows * head_size)[:, :stat_count]
+        received[:, out_rows:, :]
+        .reshape(seq_count, stat_rows * query_width)[:, :stat_count]
         .astype(jnp.float32)
         .reshape(seq_count, 3, stretch_count, local_tok, group_size)
     )
     got_lse = (got_stats[:, 0] + got_stats[:, 1]) + got_stats[:, 2]
-
     final_top = jnp.max(got_lse, axis=0)
     part_factor = jnp.exp(got_lse - final_top[None])
     total_sum = jnp.sum(part_factor, axis=0)
-    total_num = jnp.sum(got_out * part_factor[..., None], axis=0)
+    total_num = jnp.sum(got_out.astype(jnp.float32) * part_factor[..., None], axis=0)
     stretch_out = (
         (total_num / total_sum[..., None])
         .astype(jnp.bfloat16)

time: 123 us -> 129 us (1.049)
  local copies, waits for them, and re-layouts: 14 us -> 19.1 us
  waiting for transfers between devices: 49.4 us -> 52.4 us
  other arithmetic: 9.36 us -> 7.44 us
    mul x0 -> x2, local copies, waits for them, and re-layouts: none -> 4.96 us  [body(): got_out.astype(jnp.float32) * part_factor[..., None]]
    div x2, local copies, waits for them, and re-layouts: 0.23 us -> 3.5 us  [body(): total_num / total_sum[..., None]]
    another operation x2 -> x0, local copies, waits for them, and re-layouts: 2.97 us -> none  [body(): part_out.reshape(stretch_count, seq_count, rows_per_src, head_size)]
    all_to_all x1, waiting for transfers between devices: 18.6 us -> 21.1 us  [body(): received = lax.all_to_all(payload, 'seq', 0, 0, tiled=True)]
  transfers between devices with their start and end apart: 3 -> 3, of which waited for: 2 -> 2; matrix products, arithmetic and copies ran while one was open for 8% -> 5% of each run, Pallas kernels for 13% -> 12%
where the time goes in v7:
time: 129 us; the launch traced here: 128 us
  waiting for transfers between devices  52.4 us (41%)
  local copies, waits for them, and re-layouts  19.1 us (15%)
  starting transfers between devices  17.2 us (13%)
  Pallas kernels  15.7 us (12%)
  blocking collectives  10.9 us (8%)
  other arithmetic  7.44 us (6%)
  between operations  4.08 us (3%)
    all_to_all x1, waiting for transfers between devices, body(): lax.all_to_all(jnp.broadcast_to(pack[None], (seq_count,) + pack.shape), '...  31.3 us
    all_to_all x1, waiting for transfers between devices, body(): received = lax.all_to_all(payload, 'seq', 0, 0, tiled=True)  21.1 us
    pallas_call x1, Pallas kernels, prefill_partial(): pl.pallas_call(kern, grid_spec=pltpu.PrefetchScalarGridSpec(num_scalar_pr...  15.7 us
    unnamed x1, blocking collectives  10.9 us
    all_to_all x1, starting transfers between devices, body(): lax.all_to_all(jnp.broadcast_to(pack[None], (seq_count,) + pack.shape), '...  7.41 us
    all_to_all x1, starting transfers between devices, body(): received = lax.all_to_all(payload, 'seq', 0, 0, tiled=True)  6.13 us
    mul x2, local copies, waits for them, and re-layouts, body(): got_out.astype(jnp.float32) * part_factor[..., None]  4.96 us
    all_to_all x1, starting transfers between devices, body(): lax.all_to_all(jnp.broadcast_to(home_out[None], (seq_count,) + home_out.s...  3.64 us
  transfers between devices with their start and end apart: 3, of which 2 were waited for; matrix products, arithmetic and copies ran while one was open for 5% of the time, Pallas kernels for 12%

profile of v7, /device:TPU:0, one launch (start us, length us, event | category | flops | bytes accessed | tf_op | source)
XLA Modules:
  0.0 127.9 jit_solution(11511058410023720967)
XLA Ops:
  0.6 0.8 fusion.20
  1.4 1.0 pad_maximum_fusion
  2.4 1.3 broadcast_in_dim.86
  3.6 7.4 %all-to-all-start = ((bf16[8,98,896]{2,1,0:T(8,128)(2,1)}), bf16[8,98,896]{2,1,0:T(8,128)(2,1)S(1)}, u32[]{:S(2)}, u32[]{:S(2)}) async-start(bf16[8,98,896]{2,1,0:T(8,128)(2,1)} %broadcast_in_dim.86), calls=%async_computation | async-start | bytes 2981888 | tf_op jit(solution)/shard_map/all_to_all | solution.py:136
  15.0 31.3 %all-to-all-done.q_ref = bf16[8,98,896]{2,1,0:T(8,128)(2,1)S(1)} async-done(((bf16[8,98,896]{2,1,0:T(8,128)(2,1)}), bf16[8,98,896]{2,1,0:T(8,128)(2,1)S(1)}, u32[]{:S(2)}, u32[]{:S(2)}) %all-to-all-start) | async-done | bytes 1404960 | tf_op jit(solution)/shard_map/all_to_all | solution.py:136
  47.2 0.9 copy-done.6
  48.9 0.7 reduce.12
  49.6 0.7 reshape.286
  50.3 3.6 %all-to-all-start.1 = ((bf16[8,2,448]{2,1,0:T(2,128)(2,1)}), bf16[8,2,448]{2,1,0:T(2,128)(2,1)S(1)}, u32[]{:S(2)}, u32[]{:S(2)}) async-start(bf16[8,2,448]{2,1,0:T(2,128)(2,1)} %reshape.286), calls=%async_computation.1 | async-start | bytes 32768 | tf_op jit(solution)/shard_map/all_to_all | solution.py:171
  54.0 15.7 %shard_map.149 = (bf16[8,99,896]{2,1,0:T(8,128)(2,1)}, f32[3,256,7]{2,1,0:T(8,128)}) custom-call(s32[4]{0:T(128)} %pad_add_fusion.info_ref, bf16[8,98,896]{2,1,0:T(8,128)(2,1)} %copy-done.1, bf16[3,1024,128]{2,1,0:T(8,128)(2,1)} %k_ref.1, bf16[3,1024,128]{2,1,0:T(8,128)(2,1)} %v_ref.1, bf16[3,32,128]{2,1,0:T(8,128)(2,1)} %sk_ref.1, bf16[3,32,128]{2,1,0:T(8,128)(2,1)} %sv_ref.1), custom_call_target="tpu_custom_call" | custom-call | tf_op jit(solution)/shard_map/pallas_call | solution.py:81
  69.7 1.2 copy.21
  72.2 0.7 constant_dynamic-update-slice_fusion
  72.9 6.1 %all-to-all-start.2 = ((bf16[8,99,896]{2,1,0:T(8,128)(2,1)}), bf16[8,99,896]{2,1,0:T(8,128)(2,1)S(1)}, u32[]{:S(2)}, u32[]{:S(2)}) async-start(bf16[8,99,896]{2,1,0:T(8,128)(2,1)} %constant_dynamic-update-slice_fusion), calls=%async_computation.2 | async-start | bytes 2981888 | tf_op jit(solution)/shard_map/all_to_all | solution.py:227
  81.3 10.9 %all-reduce.2 = bf16[8,448]{1,0:T(8,128)(2,1)S(1)} all-reduce(f32[8,448]{1,0:T(8,128)S(1)} %fusion.15), channel_id=2, replica_groups=mesh['seq'=8,'tp'=4] {'tp'}, use_global_device_ids=true, to_apply=%region_3.5.clone | all-reduce | flops 3584 | bytes 21504
  92.8 21.1 %all-to-all-done.2 = bf16[8,99,896]{2,1,0:T(8,128)(2,1)S(1)} async-done(((bf16[8,99,896]{2,1,0:T(8,128)(2,1)}), bf16[8,99,896]{2,1,0:T(8,128)(2,1)S(1)}, u32[]{:S(2)}, u32[]{:S(2)}) %all-to-all-start.2) | async-done | bytes 1419296 | tf_op jit(solution)/shard_map/all_to_all | solution.py:227
  113.9 1.1 copy-done.2
  115.0 1.1 reshape.244
  116.2 0.8 fusion.30
  117.0 2.1 %mul.28 = f32[8,3,32,7,128]{4,3,2,1,0:T(8,128)} broadcast(f32[8,3,32,7]{3,2,1,0:T(8,128)S(1)} %get-tuple-element.30), dimensions={0,1,2,3} | broadcast | bytes 2774016 | tf_op jit(solution)/shard_map/mul | solution.py:241
  119.1 2.8 %mul.29 = f32[8,96,896]{2,1,0:T(8,128)S(1)} reshape(f32[8,3,32,7,128]{4,3,2,1,0:T(8,128)} %mul.28) | data formatting | bytes 5505024 | tf_op jit(solution)/shard_map/mul | solution.py:241
  121.9 1.7 %div.22 = f32[3,32,7,128]{3,2,1,0:T(8,128)} broadcast(f32[3,32,7]{2,1,0:T(8,128)} %get-tuple-element.29), dimensions={0,1,2} | broadcast | bytes 346752 | tf_op jit(solution)/shard_map/div | solution.py:243
  123.6 1.8 %div.23 = f32[3,32,896]{2,1,0:T(8,128)} reshape(f32[3,32,7,128]{3,2,1,0:T(8,128)} %div.22) | data formatting | bytes 688128 | tf_op jit(solution)/shard_map/div | solution.py:243
  125.4 1.7 %multiply_reduce_fusion = f32[96,896]{1,0:T(8,128)S(1)} fusion(f32[8,96,896]{2,1,0:T(8,128)S(1)} %mul.29, bf16[8,99,896]{2,1,0:T(8,128)(2,1)} %copy-done.2), kind=kLoop, calls=%fused_computation.3 | loop fusion | flops 1978368 | bytes 4472832 | tf_op jit(solution)/shard_map/reduce_sum | solution.py:241
  127.2 0.7 divide_convert_fusion
  (50 shorter events, 6.7 us)
Async XLA Ops:
  0.6 80.4 %copy-start = (bf16[896,448]{0,1:T(8,128)(2,1)S(1)}, bf16[896,448]{0,1:T(8,128)(2,1)}, u32[]{:S(2)}) copy-start(bf16[896,448]{0,1:T(8,128)(2,1)} %param.23) | copy-start | bytes 2408452
  3.6 7.4 %copy-start.4 = (s32[8]{0:T(128)S(1)}, s32[8]{0:T(128)}, u32[]{:S(2)}) copy-start(s32[8]{0:T(128)} %param.22) | copy-start | bytes 100
  3.6 10.8 %copy-start.7 = (s32[3]{0:T(128)S(1)}, s32[3]{0:T(128)}, u32[]{:S(2)}) copy-start(s32[3]{0:T(128)} %param.29) | copy-start | bytes 40
  3.6 42.8 %copy-start.5 = (bf16[1,4096,128]{2,1,0:T(8,128)(2,1)S(1)}, bf16[1,4096,128]{2,1,0:T(8,128)(2,1)}, u32[]{:S(2)}) copy-start(bf16[1,4096,128]{2,1,0:T(8,128)(2,1)} %param.19) | copy-start | bytes 3145732
  3.6 42.7 %all-to-all-start = ((bf16[8,98,896]{2,1,0:T(8,128)(2,1)}), bf16[8,98,896]{2,1,0:T(8,128)(2,1)S(1)}, u32[]{:S(2)}, u32[]{:S(2)}) async-start(bf16[8,98,896]{2,1,0:T(8,128)(2,1)} %broadcast_in_dim.86), calls=%async_computation | async-start | bytes 2981888 | tf_op jit(solution)/shard_map/all_to_all | solution.py:136
  46.3 2.1 %copy-start.1 = (bf16[8,98,896]{2,1,0:T(8,128)(2,1)}, bf16[8,98,896]{2,1,0:T(8,128)(2,1)S(1)}, u32[]{:S(2)}) copy-start(bf16[8,98,896]{2,1,0:T(8,128)(2,1)S(1)} %all-to-all-done.q_ref) | copy-start | bytes 4214788
  46.3 1.8 %copy-start.6 = (bf16[1,4096,128]{2,1,0:T(8,128)(2,1)S(1)}, bf16[1,4096,128]{2,1,0:T(8,128)(2,1)}, u32[]{:S(2)}) copy-start(bf16[1,4096,128]{2,1,0:T(8,128)(2,1)} %param.20) | copy-start | bytes 3145732
  50.3 22.6 %all-to-all-start.1 = ((bf16[8,2,448]{2,1,0:T(2,128)(2,1)}), bf16[8,2,448]{2,1,0:T(2,128)(2,1)S(1)}, u32[]{:S(2)}, u32[]{:S(2)}) async-start(bf16[8,2,448]{2,1,0:T(2,128)(2,1)} %reshape.286), calls=%async_computation.1 | async-start | bytes 32768 | tf_op jit(solution)/shard_map/all_to_all | solution.py:171
  72.9 6.1 %copy-start.8 = (u32[32]{0:T(128)S(1)}, u32[32]{0:T(128)}, u32[]{:S(2)}) copy-start(u32[32]{0:T(128)} %constant.132) | copy-start | bytes 388
  72.9 41.0 %all-to-all-start.2 = ((bf16[8,99,896]{2,1,0:T(8,128)(2,1)}), bf16[8,99,896]{2,1,0:T(8,128)(2,1)S(1)}, u32[]{:S(2)}, u32[]{:S(2)}) async-start(bf16[8,99,896]{2,1,0:T(8,128)(2,1)} %constant_dynamic-update-slice_fusion), calls=%async_computation.2 | async-start | bytes 2981888 | tf_op jit(solution)/shard_map/all_to_all | solution.py:227
  113.9 1.1 copy-start.2
  125.4 1.7 %copy-start.3 = (f32[3,32,896]{2,1,0:T(8,128)S(1)}, f32[3,32,896]{2,1,0:T(8,128)}, u32[]{:S(2)}) copy-start(f32[3,32,896]{2,1,0:T(8,128)} %div.23) | copy-start | bytes 1032196

commit v8 on v7

--- a/solution.py
+++ b/solution.py
@@ -102,6 +102,34 @@
     )(info, queries, keys, values, own_keys, own_values)
 
 
+def _combine_kernel(o_ref, lse_ref, out_ref, *, group_size, head_size):
+    stretch_count, local_tok, _ = out_ref.shape
+    for c in range(stretch_count):
+        lse = lse_ref[:, c]
+        top = jnp.max(lse, axis=0, keepdims=True)
+        weights = jnp.exp(lse - top)
+        total = jnp.sum(weights, axis=0)
+        for h in range(group_size):
+            part = o_ref[
+                :, c * local_tok : (c + 1) * local_tok, h * head_size : (h + 1) * head_size
+            ].astype(jnp.float32)
+            num = jnp.sum(part * weights[:, :, h : h + 1], axis=0)
+            out_ref[c, :, h * head_size : (h + 1) * head_size] = (
+                num / total[:, h : h + 1]
+            ).astype(out_ref.dtype)
+
+
+def combine_partials(received, lse, group_size, head_size):
+    _, stretch_count, local_tok, _ = lse.shape
+    kern = functools.partial(_combine_kernel, group_size=group_size, head_size=head_size)
+    return pl.pallas_call(
+        kern,
+        out_shape=jax.ShapeDtypeStruct(
+            (stretch_count, local_tok, group_size * head_size), jnp.bfloat16
+        ),
+    )(received, lse)
+
+
 def body(
     new_query,
     new_key,
@@ -225,9 +253,6 @@
     )
 
     received = lax.all_to_all(payload, "seq", 0, 0, tiled=True)
-    got_out = received[:, :out_rows, :].reshape(
-        seq_count, stretch_count, local_tok, group_size, head_size
-    )
     got_stats = (
         received[:, out_rows:, :]
         .reshape(seq_count, stat_rows * query_width)[:, :stat_count]
@@ -235,15 +260,7 @@
         .reshape(seq_count, 3, stretch_count, local_tok, group_size)
     )
     got_lse = (got_stats[:, 0] + got_stats[:, 1]) + got_stats[:, 2]
-    final_top = jnp.max(got_lse, axis=0)
-    part_factor = jnp.exp(got_lse - final_top[None])
-    total_sum = jnp.sum(part_factor, axis=0)
-    total_num = jnp.sum(got_out.astype(jnp.float32) * part_factor[..., None], axis=0)
-    stretch_out = (
-        (total_num / total_sum[..., None])
-        .astype(jnp.bfloat16)
-        .reshape(stretch_count, local_tok, group_size * head_size)
-    )
+    stretch_out = combine_partials(received, got_lse, group_size, head_size)
     return (decode_mixed, stretch_out)
 
 

time: 129 us -> 119 us (0.922)
  local copies, waits for them, and re-layouts: 19.1 us -> 9.5 us
  Pallas kernels: 15.7 us -> 18.8 us
  other arithmetic: 7.44 us -> 5.02 us
    mul x2 -> x0, local copies, waits for them, and re-layouts: 4.96 us -> none  [body(): got_out.astype(jnp.float32) * part_factor[..., None]]
    div x2 -> x0, local copies, waits for them, and re-layouts: 3.5 us -> none  [body(): total_num / total_sum[..., None]]
    pallas_call x0 -> x1, Pallas kernels: none -> 3.03 us  [combine_partials(): pl.pallas_call(kern, out_shape=jax.ShapeDtypeStruct((stretch_count, local...]
    reduce_sum x2 -> x0, other arithmetic: 2.47 us -> none  [the longest x1 1.71 us: body(): jnp.sum(got_out.astype(jnp.float32) * part_factor[..., None], axis=0)]
    unnamed x25 -> x23, local copies, waits for them, and re-layouts: 3.43 us -> 2.35 us
  transfers between devices with their start and end apart: 3 -> 3, of which waited for: 2 -> 2; matrix products, arithmetic and copies ran while one was open for 5% -> 6% of each run, Pallas kernels for 12% -> 13%
where the time goes in v8:
time: 119 us
  waiting for transfers between devices  52.3 us (44%)
  Pallas kernels  18.8 us (16%)
  starting transfers between devices  17.2 us (14%)
  blocking collectives  10.9 us (9%)
  local copies, waits for them, and re-layouts  9.5 us (8%)
  other arithmetic  5.02 us (4%)
  between operations  4.07 us (3%)
    all_to_all x1, waiting for transfers between devices, body(): lax.all_to_all(jnp.broadcast_to(pack[None], (seq_count,) + pack.shape), '...  31.2 us
    all_to_all x1, waiting for transfers between devices, body(): received = lax.all_to_all(payload, 'seq', 0, 0, tiled=True)  21.1 us
    pallas_call x1, Pallas kernels, prefill_partial(): pl.pallas_call(kern, grid_spec=pltpu.PrefetchScalarGridSpec(num_scalar_pr...  15.8 us
    unnamed x1, blocking collectives  10.9 us
    all_to_all x1, starting transfers between devices, body(): lax.all_to_all(jnp.broadcast_to(pack[None], (seq_count,) + pack.shape), '...  7.41 us
    all_to_all x1, starting transfers between devices, body(): received = lax.all_to_all(payload, 'seq', 0, 0, tiled=True)  6.13 us
    all_to_all x1, starting transfers between devices, body(): lax.all_to_all(jnp.broadcast_to(home_out[None], (seq_count,) + home_out.s...  3.64 us
    pallas_call x1, Pallas kernels, combine_partials(): pl.pallas_call(kern, out_shape=jax.ShapeDtypeStruct((stretch_count, local...  3.03 us
  transfers between devices with their start and end apart: 3, of which 2 were waited for; matrix products, arithmetic and copies ran while one was open for 6% of the time, Pallas kernels for 13%

profile of v8, /device:TPU:0, one launch (start us, length us, event | category | flops | bytes accessed | tf_op | source)
XLA Modules:
  0.0 118.9 jit_solution(368381383142924382)
XLA Ops:
  0.6 0.8 fusion.22
  1.4 1.0 pad_maximum_fusion
  2.4 1.3 %broadcast_in_dim.83 = bf16[8,98,896]{2,1,0:T(8,128)(2,1)} broadcast(bf16[98,896]{1,0:T(8,128)(2,1)S(1)} %pad_maximum_fusion), dimensions={1,2} | broadcast | bytes 1580544 | tf_op jit(solution)/shard_map/broadcast_in_dim | solution.py:165
  3.6 7.4 %all-to-all-start = ((bf16[8,98,896]{2,1,0:T(8,128)(2,1)}), bf16[8,98,896]{2,1,0:T(8,128)(2,1)S(1)}, u32[]{:S(2)}, u32[]{:S(2)}) async-start(bf16[8,98,896]{2,1,0:T(8,128)(2,1)} %broadcast_in_dim.83), calls=%async_computation | async-start | bytes 2981888 | tf_op jit(solution)/shard_map/all_to_all | solution.py:164
  11.7 0.6 compare_select_fusion.2
  14.4 0.6 pad_add_fusion.info_ref
  15.0 31.2 %all-to-all-done.q_ref = bf16[8,98,896]{2,1,0:T(8,128)(2,1)S(1)} async-done(((bf16[8,98,896]{2,1,0:T(8,128)(2,1)}), bf16[8,98,896]{2,1,0:T(8,128)(2,1)S(1)}, u32[]{:S(2)}, u32[]{:S(2)}) %all-to-all-start) | async-done | bytes 1404960 | tf_op jit(solution)/shard_map/all_to_all | solution.py:164
  47.2 0.9 copy-done.5
  48.9 0.7 reduce.10
  49.6 0.7 reshape.261
  50.3 3.6 %all-to-all-start.1 = ((bf16[8,2,448]{2,1,0:T(2,128)(2,1)}), bf16[8,2,448]{2,1,0:T(2,128)(2,1)S(1)}, u32[]{:S(2)}, u32[]{:S(2)}) async-start(bf16[8,2,448]{2,1,0:T(2,128)(2,1)} %reshape.261), calls=%async_computation.1 | async-start | bytes 32768 | tf_op jit(solution)/shard_map/all_to_all | solution.py:199
  54.0 15.8 %shard_map.149 = (bf16[8,99,896]{2,1,0:T(8,128)(2,1)}, f32[3,256,7]{2,1,0:T(8,128)}) custom-call(s32[4]{0:T(128)} %pad_add_fusion.info_ref, bf16[8,98,896]{2,1,0:T(8,128)(2,1)} %copy-done.1, bf16[3,1024,128]{2,1,0:T(8,128)(2,1)} %k_ref.1, bf16[3,1024,128]{2,1,0:T(8,128)(2,1)} %v_ref.1, bf16[3,32,128]{2,1,0:T(8,128)(2,1)} %sk_ref.1, bf16[3,32,128]{2,1,0:T(8,128)(2,1)} %sv_ref.1), custom_call_target="tpu_custom_call" | custom-call | tf_op jit(solution)/shard_map/pallas_call | solution.py:81
  69.7 1.2 %copy.28 = f32[1,3,8,32,7]{3,2,4,1,0:T(8,128)S(1)} copy(f32[1,3,8,32,7]{4,3,2,1,0:T(8,128)} %bitcast.65) | data formatting | bytes 43008 | tf_op jit(solution)/shard_map/reshape | solution.py:238
  71.6 0.6 reshape.173
  72.3 0.6 constant_dynamic-update-slice_fusion
  72.9 6.1 %all-to-all-start.2 = ((bf16[8,99,896]{2,1,0:T(8,128)(2,1)}), bf16[8,99,896]{2,1,0:T(8,128)(2,1)S(1)}, u32[]{:S(2)}, u32[]{:S(2)}) async-start(bf16[8,99,896]{2,1,0:T(8,128)(2,1)} %constant_dynamic-update-slice_fusion), calls=%async_computation.2 | async-start | bytes 2981888 | tf_op jit(solution)/shard_map/all_to_all | solution.py:255
  79.0 0.6 dynamic-slice.12
  80.4 0.6 gather_fusion
  81.3 10.9 %all-reduce.2 = bf16[8,448]{1,0:T(8,128)(2,1)S(1)} all-reduce(f32[8,448]{1,0:T(8,128)S(1)} %fusion.17), channel_id=2, replica_groups=mesh['seq'=8,'tp'=4] {'tp'}, use_global_device_ids=true, to_apply=%region_3.5.clone | all-reduce | flops 3584 | bytes 21504
  92.2 0.6 dynamic-slice_convert_fusion
  92.8 21.1 %all-to-all-done.2.o_ref = bf16[8,99,896]{2,1,0:T(8,128)(2,1)S(1)} async-done(((bf16[8,99,896]{2,1,0:T(8,128)(2,1)}), bf16[8,99,896]{2,1,0:T(8,128)(2,1)S(1)}, u32[]{:S(2)}, u32[]{:S(2)}) %all-to-all-start.2) | async-done | bytes 1419296 | tf_op jit(solution)/shard_map/all_to_all | solution.py:255
  114.0 1.1 reshape.219
  115.0 0.8 fusion.8.lse_ref
  115.9 3.0 %shard_map.150 = bf16[3,32,896]{2,1,0:T(8,128)(2,1)} custom-call(bf16[8,99,896]{2,1,0:T(8,128)(2,1)} %copy-done.2, f32[8,3,32,7]{3,2,1,0:T(8,128)} %fusion.8.lse_ref), custom_call_target="tpu_custom_call" | custom-call | tf_op jit(solution)/shard_map/pallas_call | solution.py:125
  (42 shorter events, 2.9 us)
Async XLA Ops:
  0.6 80.4 %copy-start = (bf16[896,448]{0,1:T(8,128)(2,1)S(1)}, bf16[896,448]{0,1:T(8,128)(2,1)}, u32[]{:S(2)}) copy-start(bf16[896,448]{0,1:T(8,128)(2,1)} %param.23) | copy-start | bytes 2408452
  3.6 8.1 %copy-start.3 = (s32[8]{0:T(128)S(1)}, s32[8]{0:T(128)}, u32[]{:S(2)}) copy-start(s32[8]{0:T(128)} %param.22) | copy-start | bytes 100
  3.6 10.8 %copy-start.6 = (s32[3]{0:T(128)S(1)}, s32[3]{0:T(128)}, u32[]{:S(2)}) copy-start(s32[3]{0:T(128)} %param.29) | copy-start | bytes 40
  3.6 42.8 %copy-start.4 = (bf16[1,4096,128]{2,1,0:T(8,128)(2,1)S(1)}, bf16[1,4096,128]{2,1,0:T(8,128)(2,1)}, u32[]{:S(2)}) copy-start(bf16[1,4096,128]{2,1,0:T(8,128)(2,1)} %param.19) | copy-start | bytes 3145732
  3.6 42.7 %all-to-all-start = ((bf16[8,98,896]{2,1,0:T(8,128)(2,1)}), bf16[8,98,896]{2,1,0:T(8,128)(2,1)S(1)}, u32[]{:S(2)}, u32[]{:S(2)}) async-start(bf16[8,98,896]{2,1,0:T(8,128)(2,1)} %broadcast_in_dim.83), calls=%async_computation | async-start | bytes 2981888 | tf_op jit(solution)/shard_map/all_to_all | solution.py:164
  46.3 2.1 %copy-start.1 = (bf16[8,98,896]{2,1,0:T(8,128)(2,1)}, bf16[8,98,896]{2,1,0:T(8,128)(2,1)S(1)}, u32[]{:S(2)}) copy-start(bf16[8,98,896]{2,1,0:T(8,128)(2,1)S(1)} %all-to-all-done.q_ref) | copy-start | bytes 4214788
  46.3 1.8 %copy-start.5 = (bf16[1,4096,128]{2,1,0:T(8,128)(2,1)S(1)}, bf16[1,4096,128]{2,1,0:T(8,128)(2,1)}, u32[]{:S(2)}) copy-start(bf16[1,4096,128]{2,1,0:T(8,128)(2,1)} %param.20) | copy-start | bytes 3145732
  50.3 22.6 %all-to-all-start.1 = ((bf16[8,2,448]{2,1,0:T(2,128)(2,1)}), bf16[8,2,448]{2,1,0:T(2,128)(2,1)S(1)}, u32[]{:S(2)}, u32[]{:S(2)}) async-start(bf16[8,2,448]{2,1,0:T(2,128)(2,1)} %reshape.261), calls=%async_computation.1 | async-start | bytes 32768 | tf_op jit(solution)/shard_map/all_to_all | solution.py:199
  72.9 6.1 %copy-start.7 = (u32[32]{0:T(128)S(1)}, u32[32]{0:T(128)}, u32[]{:S(2)}) copy-start(u32[32]{0:T(128)} %constant.132) | copy-start | bytes 388
  72.9 41.0 %all-to-all-start.2 = ((bf16[8,99,896]{2,1,0:T(8,128)(2,1)}), bf16[8,99,896]{2,1,0:T(8,128)(2,1)S(1)}, u32[]{:S(2)}, u32[]{:S(2)}) async-start(bf16[8,99,896]{2,1,0:T(8,128)(2,1)} %constant_dynamic-update-slice_fusion), calls=%async_computation.2 | async-start | bytes 2981888 | tf_op jit(solution)/shard_map/all_to_all | solution.py:255
  113.9 2.0 %copy-start.2 = (bf16[8,99,896]{2,1,0:T(8,128)(2,1)}, bf16[8,99,896]{2,1,0:T(8,128)(2,1)S(1)}, u32[]{:S(2)}) copy-start(bf16[8,99,896]{2,1,0:T(8,128)(2,1)S(1)} %all-to-all-done.2.o_ref) | copy-start | bytes 4257796

commit v9 on v8

--- a/solution.py
+++ b/solution.py
@@ -42,30 +42,43 @@
     query_token = (row // tok_block) * local_tok + row % tok_block
     causal = key_token <= query_token
     dims = (((1,), (1,)), ((), ()))
-    for h in range(group_size):
-        q = q_ref[:, :, h * head_size : (h + 1) * head_size].reshape(tokens, head_size)
-        s = lax.dot_general(q, keys, dims, preferred_element_type=jnp.float32) * factor
-        s = jnp.where(visible, s, NEG_FILL)
-        s_own = lax.dot_general(q, own_keys, dims, preferred_element_type=jnp.float32) * factor
-        s_own = jnp.where(causal, s_own, NEG_FILL)
-        m = jnp.maximum(
-            jnp.max(s, axis=1, keepdims=True), jnp.max(s_own, axis=1, keepdims=True)
-        )
-        w = jnp.exp(s - m)
-        w_own = jnp.exp(s_own - m)
-        empty = m < 0.5 * NEG_FILL
-        l = jnp.sum(w, axis=1, keepdims=True) + jnp.sum(w_own, axis=1, keepdims=True)
-        num = jnp.dot(w.astype(jnp.bfloat16), values, preferred_element_type=jnp.float32)
-        num = num + jnp.dot(
-            w_own.astype(jnp.bfloat16), own_values, preferred_element_type=jnp.float32
-        )
-        l = jnp.where(empty, 0.0, l)
-        num = jnp.where(empty, 0.0, num)
-        safe = jnp.maximum(l, 1.0)
-        o_ref[:, :, h * head_size : (h + 1) * head_size] = (
-            (num / safe).astype(o_ref.dtype).reshape(src_count, tok_block, head_size)
-        )
-        lse_ref[0, :, h : h + 1] = m + jnp.log(safe)
+
+    def heads(masked):
+        for h in range(group_size):
+            q = q_ref[:, :, h * head_size : (h + 1) * head_size].reshape(tokens, head_size)
+            s = lax.dot_general(q, keys, dims, preferred_element_type=jnp.float32) * factor
+            if masked:
+                s = jnp.where(visible, s, NEG_FILL)
+            s_own = lax.dot_general(q, own_keys, dims, preferred_element_type=jnp.float32) * factor
+            s_own = jnp.where(causal, s_own, NEG_FILL)
+            m = jnp.maximum(
+                jnp.max(s, axis=1, keepdims=True), jnp.max(s_own, axis=1, keepdims=True)
+            )
+            w = jnp.exp(s - m)
+            w_own = jnp.exp(s_own - m)
+            empty = m < 0.5 * NEG_FILL
+            l = jnp.sum(w, axis=1, keepdims=True) + jnp.sum(w_own, axis=1, keepdims=True)
+            num = jnp.dot(w.astype(jnp.bfloat16), values, preferred_element_type=jnp.float32)
+            num = num + jnp.dot(
+                w_own.astype(jnp.bfloat16), own_values, preferred_element_type=jnp.float32
+            )
+            l = jnp.where(empty, 0.0, l)
+            num = jnp.where(empty, 0.0, num)
+            safe = jnp.maximum(l, 1.0)
+            o_ref[:, :, h * head_size : (h + 1) * head_size] = (
+                (num / safe).astype(o_ref.dtype).reshape(src_count, tok_block, head_size)
+            )
+            lse_ref[0, :, h : h + 1] = m + jnp.log(safe)
+
+    whole_block = limit >= keys.shape[0]
+
+    @pl.when(whole_block)
+    def _():
+        heads(False)
+
+    @pl.when(jnp.logical_not(whole_block))
+    def _():
+        heads(True)
 
 
 def prefill_partial(

time: 119 us -> 120 us (level)
  transfers between devices with their start and end apart: 3 -> 3, of which waited for: 2 -> 2; matrix products, arithmetic and copies ran while one was open for 6% -> 6% of each run, Pallas kernels for 13% -> 14%
where the time goes in v9:
time: 120 us; the launch traced here: 119 us
  waiting for transfers between devices  52.3 us (44%)
  Pallas kernels  19.6 us (16%)
  starting transfers between devices  16.8 us (14%)
  blocking collectives  10.9 us (9%)
  local copies, waits for them, and re-layouts  9.5 us (8%)
  other arithmetic  5.02 us (4%)
  between operations  4.07 us (3%)
    all_to_all x1, waiting for transfers between devices, body(): lax.all_to_all(jnp.broadcast_to(pack[None], (seq_count,) + pack.shape), '...  31.2 us
    all_to_all x1, waiting for transfers between devices, body(): received = lax.all_to_all(payload, 'seq', 0, 0, tiled=True)  21.1 us
    pallas_call x1, Pallas kernels, prefill_partial(): pl.pallas_call(kern, grid_spec=pltpu.PrefetchScalarGridSpec(num_scalar_pr...  16.6 us
    unnamed x1, blocking collectives  10.9 us
    all_to_all x1, starting transfers between devices, body(): lax.all_to_all(jnp.broadcast_to(pack[None], (seq_count,) + pack.shape), '...  7.41 us
    all_to_all x1, starting transfers between devices, body(): received = lax.all_to_all(payload, 'seq', 0, 0, tiled=True)  5.8 us
    all_to_all x1, starting transfers between devices, body(): lax.all_to_all(jnp.broadcast_to(home_out[None], (seq_count,) + home_out.s...  3.64 us
    pallas_call x1, Pallas kernels, combine_partials(): pl.pallas_call(kern, out_shape=jax.ShapeDtypeStruct((stretch_count, local...  3.03 us
  transfers between devices with their start and end apart: 3, of which 2 were waited for; matrix products, arithmetic and copies ran while one was open for 6% of the time, Pallas kernels for 14%

profile of v9, /device:TPU:0, one launch (start us, length us, event | category | flops | bytes accessed | tf_op | source)
XLA Modules:
  0.0 119.4 jit_solution(16228279465899765867)
XLA Ops:
  0.6 0.8 fusion.22
  1.4 1.0 pad_maximum_fusion
  2.4 1.3 %broadcast_in_dim.83 = bf16[8,98,896]{2,1,0:T(8,128)(2,1)} broadcast(bf16[98,896]{1,0:T(8,128)(2,1)S(1)} %pad_maximum_fusion), dimensions={1,2} | broadcast | bytes 1580544 | tf_op jit(solution)/shard_map/broadcast_in_dim | solution.py:178
  3.6 7.4 %all-to-all-start = ((bf16[8,98,896]{2,1,0:T(8,128)(2,1)}), bf16[8,98,896]{2,1,0:T(8,128)(2,1)S(1)}, u32[]{:S(2)}, u32[]{:S(2)}) async-start(bf16[8,98,896]{2,1,0:T(8,128)(2,1)} %broadcast_in_dim.83), calls=%async_computation | async-start | bytes 2981888 | tf_op jit(solution)/shard_map/all_to_all | solution.py:177
  11.7 0.6 compare_select_fusion.2
  14.4 0.6 pad_add_fusion.info_ref
  15.0 31.2 %all-to-all-done.q_ref = bf16[8,98,896]{2,1,0:T(8,128)(2,1)S(1)} async-done(((bf16[8,98,896]{2,1,0:T(8,128)(2,1)}), bf16[8,98,896]{2,1,0:T(8,128)(2,1)S(1)}, u32[]{:S(2)}, u32[]{:S(2)}) %all-to-all-start) | async-done | bytes 1404960 | tf_op jit(solution)/shard_map/all_to_all | solution.py:177
  47.2 0.9 copy-done.5
  48.9 0.7 reduce.10
  49.6 0.7 reshape.261
  50.3 3.6 %all-to-all-start.1 = ((bf16[8,2,448]{2,1,0:T(2,128)(2,1)}), bf16[8,2,448]{2,1,0:T(2,128)(2,1)S(1)}, u32[]{:S(2)}, u32[]{:S(2)}) async-start(bf16[8,2,448]{2,1,0:T(2,128)(2,1)} %reshape.261), calls=%async_computation.1 | async-start | bytes 32768 | tf_op jit(solution)/shard_map/all_to_all | solution.py:212
  54.0 16.6 %shard_map.149 = (bf16[8,99,896]{2,1,0:T(8,128)(2,1)}, f32[3,256,7]{2,1,0:T(8,128)}) custom-call(s32[4]{0:T(128)} %pad_add_fusion.info_ref, bf16[8,98,896]{2,1,0:T(8,128)(2,1)} %copy-done.1, bf16[3,1024,128]{2,1,0:T(8,128)(2,1)} %k_ref.1, bf16[3,1024,128]{2,1,0:T(8,128)(2,1)} %v_ref.1, bf16[3,32,128]{2,1,0:T(8,128)(2,1)} %sk_ref.1, bf16[3,32,128]{2,1,0:T(8,128)(2,1)} %sv_ref.1), custom_call_target="tpu_custom_call" | custom-call | tf_op jit(solution)/shard_map/pallas_call | solution.py:94
  70.6 1.2 %copy.28 = f32[1,3,8,32,7]{3,2,4,1,0:T(8,128)S(1)} copy(f32[1,3,8,32,7]{4,3,2,1,0:T(8,128)} %bitcast.65) | data formatting | bytes 43008 | tf_op jit(solution)/shard_map/reshape | solution.py:251
  72.5 0.6 reshape.173
  73.1 0.6 constant_dynamic-update-slice_fusion
  73.8 5.8 %all-to-all-start.2 = ((bf16[8,99,896]{2,1,0:T(8,128)(2,1)}), bf16[8,99,896]{2,1,0:T(8,128)(2,1)S(1)}, u32[]{:S(2)}, u32[]{:S(2)}) async-start(bf16[8,99,896]{2,1,0:T(8,128)(2,1)} %constant_dynamic-update-slice_fusion), calls=%async_computation.2 | async-start | bytes 2981888 | tf_op jit(solution)/shard_map/all_to_all | solution.py:268
  79.6 0.6 dynamic-slice.12
  81.0 0.6 gather_fusion
  81.9 10.9 %all-reduce.2 = bf16[8,448]{1,0:T(8,128)(2,1)S(1)} all-reduce(f32[8,448]{1,0:T(8,128)S(1)} %fusion.17), channel_id=2, replica_groups=mesh['seq'=8,'tp'=4] {'tp'}, use_global_device_ids=true, to_apply=%region_3.5.clone | all-reduce | flops 3584 | bytes 21504
  92.8 0.6 dynamic-slice_convert_fusion
  93.3 21.1 %all-to-all-done.2.o_ref = bf16[8,99,896]{2,1,0:T(8,128)(2,1)S(1)} async-done(((bf16[8,99,896]{2,1,0:T(8,128)(2,1)}), bf16[8,99,896]{2,1,0:T(8,128)(2,1)S(1)}, u32[]{:S(2)}, u32[]{:S(2)}) %all-to-all-start.2) | async-done | bytes 1419296 | tf_op jit(solution)/shard_map/all_to_all | solution.py:268
  114.5 1.1 reshape.219
  115.6 0.8 fusion.8.lse_ref
  116.4 3.0 %shard_map.150 = bf16[3,32,896]{2,1,0:T(8,128)(2,1)} custom-call(bf16[8,99,896]{2,1,0:T(8,128)(2,1)} %copy-done.2, f32[8,3,32,7]{3,2,1,0:T(8,128)} %fusion.8.lse_ref), custom_call_target="tpu_custom_call" | custom-call | tf_op jit(solution)/shard_map/pallas_call | solution.py:138
  (42 shorter events, 2.9 us)
Async XLA Ops:
  0.6 80.9 %copy-start = (bf16[896,448]{0,1:T(8,128)(2,1)S(1)}, bf16[896,448]{0,1:T(8,128)(2,1)}, u32[]{:S(2)}) copy-start(bf16[896,448]{0,1:T(8,128)(2,1)} %param.23) | copy-start | bytes 2408452
  3.6 8.1 %copy-start.3 = (s32[8]{0:T(128)S(1)}, s32[8]{0:T(128)}, u32[]{:S(2)}) copy-start(s32[8]{0:T(128)} %param.22) | copy-start | bytes 100
  3.6 10.8 %copy-start.6 = (s32[3]{0:T(128)S(1)}, s32[3]{0:T(128)}, u32[]{:S(2)}) copy-start(s32[3]{0:T(128)} %param.29) | copy-start | bytes 40
  3.6 42.8 %copy-start.4 = (bf16[1,4096,128]{2,1,0:T(8,128)(2,1)S(1)}, bf16[1,4096,128]{2,1,0:T(8,128)(2,1)}, u32[]{:S(2)}) copy-start(bf16[1,4096,128]{2,1,0:T(8,128)(2,1)} %param.19) | copy-start | bytes 3145732
  3.6 42.7 %all-to-all-start = ((bf16[8,98,896]{2,1,0:T(8,128)(2,1)}), bf16[8,98,896]{2,1,0:T(8,128)(2,1)S(1)}, u32[]{:S(2)}, u32[]{:S(2)}) async-start(bf16[8,98,896]{2,1,0:T(8,128)(2,1)} %broadcast_in_dim.83), calls=%async_computation | async-start | bytes 2981888 | tf_op jit(solution)/shard_map/all_to_all | solution.py:177
  46.3 2.1 %copy-start.1 = (bf16[8,98,896]{2,1,0:T(8,128)(2,1)}, bf16[8,98,896]{2,1,0:T(8,128)(2,1)S(1)}, u32[]{:S(2)}) copy-start(bf16[8,98,896]{2,1,0:T(8,128)(2,1)S(1)} %all-to-all-done.q_ref) | copy-start | bytes 4214788
  46.3 1.8 %copy-start.5 = (bf16[1,4096,128]{2,1,0:T(8,128)(2,1)S(1)}, bf16[1,4096,128]{2,1,0:T(8,128)(2,1)}, u32[]{:S(2)}) copy-start(bf16[1,4096,128]{2,1,0:T(8,128)(2,1)} %param.20) | copy-start | bytes 3145732
  50.3 23.4 %all-to-all-start.1 = ((bf16[8,2,448]{2,1,0:T(2,128)(2,1)}), bf16[8,2,448]{2,1,0:T(2,128)(2,1)S(1)}, u32[]{:S(2)}, u32[]{:S(2)}) async-start(bf16[8,2,448]{2,1,0:T(2,128)(2,1)} %reshape.261), calls=%async_computation.1 | async-start | bytes 32768 | tf_op jit(solution)/shard_map/all_to_all | solution.py:212
  73.8 5.8 %copy-start.7 = (u32[32]{0:T(128)S(1)}, u32[32]{0:T(128)}, u32[]{:S(2)}) copy-start(u32[32]{0:T(128)} %constant.132) | copy-start | bytes 388
  73.8 40.7 %all-to-all-start.2 = ((bf16[8,99,896]{2,1,0:T(8,128)(2,1)}), bf16[8,99,896]{2,1,0:T(8,128)(2,1)S(1)}, u32[]{:S(2)}, u32[]{:S(2)}) async-start(bf16[8,99,896]{2,1,0:T(8,128)(2,1)} %constant_dynamic-update-slice_fusion), calls=%async_computation.2 | async-start | bytes 2981888 | tf_op jit(solution)/shard_map/all_to_all | solution.py:268
  114.4 2.0 %copy-start.2 = (bf16[8,99,896]{2,1,0:T(8,128)(2,1)}, bf16[8,99,896]{2,1,0:T(8,128)(2,1)S(1)}, u32[]{:S(2)}) copy-start(bf16[8,99,896]{2,1,0:T(8,128)(2,1)S(1)} %all-to-all-done.2.o_ref) | copy-start | bytes 4257796

commit v10 on v8

--- a/solution.py
+++ b/solution.py
@@ -130,6 +130,26 @@
     )(received, lse)
 
 
+def broadcast_over_seq(pack, seq_rank, seq_count):
+    if seq_count > 16 or seq_count % 2:
+        return lax.all_to_all(
+            jnp.broadcast_to(pack[None], (seq_count,) + pack.shape), "seq", 0, 0, tiled=True
+        )
+    half = seq_count // 2
+    partner = lax.ppermute(pack, "seq", [(i, (i + half) % seq_count) for i in range(seq_count)])
+    pair = jnp.stack([pack, partner])
+    pieces = [pair]
+    for shift in range(1, half):
+        perm = [(i, (i // half) * half + (i % half + shift) % half) for i in range(seq_count)]
+        pieces.append(lax.ppermute(pair, "seq", perm))
+    every = jnp.stack(pieces).reshape((2 * half,) + pack.shape)
+    sources = jnp.arange(seq_count, dtype=jnp.int32)
+    far = (sources // half) != (seq_rank // half)
+    near = jnp.where(far, (sources + half) % seq_count, sources)
+    shift_of = (seq_rank % half - near % half) % half
+    return jnp.take(every, shift_of * 2 + far.astype(jnp.int32), axis=0)
+
+
 def body(
     new_query,
     new_key,
@@ -161,9 +181,7 @@
     pack = jnp.concatenate(
         [stretch_query.reshape(stretch_rows, query_width), new_query, decode_kv], axis=0
     )
-    gathered = lax.all_to_all(
-        jnp.broadcast_to(pack[None], (seq_count,) + pack.shape), "seq", 0, 0, tiled=True
-    )
+    gathered = broadcast_over_seq(pack, seq_rank, seq_count)
     every_query = gathered[:, stretch_rows : stretch_rows + local_dec, :].reshape(
         total_dec, query_width
     )

time: 119 us -> 112 us (0.941)
  waiting for transfers between devices: 52.3 us -> 40 us
  other arithmetic: 5.02 us -> 8.4 us
  starting transfers between devices: 17.2 us -> 18.6 us
    all_to_all x1 -> x0, waiting for transfers between devices: 31.2 us -> none  [body(): lax.all_to_all(jnp.broadcast_to(pack[None], (seq_count,) + pack.shape), '...]
    ppermute x0 -> x4, waiting for transfers between devices: none -> 19.9 us  [the longest x3 14.5 us: broadcast_over_seq(): pieces.append(lax.ppermute(pair, 'seq', perm))]
    ppermute x0 -> x4, starting transfers between devices: none -> 7.81 us  [the longest x1 4.1 us: broadcast_over_seq(): lax.ppermute(pack, 'seq', [(i, (i + half) % seq_count) for i in range(seq...]
    all_to_all x1 -> x0, starting transfers between devices: 7.41 us -> none  [body(): lax.all_to_all(jnp.broadcast_to(pack[None], (seq_count,) + pack.shape), '...]
    gather x0 -> x1, local copies, waits for them, and re-layouts: none -> 1.87 us  [broadcast_over_seq(): return jnp.take(every, shift_of * 2 + far.astype(jnp.int32), axis=0)]
    select_n x0 -> x2, other arithmetic: none -> 1.71 us  [broadcast_over_seq(): return jnp.take(every, shift_of * 2 + far.astype(jnp.int32), axis=0)]
    broadcast_in_dim x1 -> x0, local copies, waits for them, and re-layouts: 1.26 us -> none  [body(): jnp.broadcast_to(pack[None], (seq_count,) + pack.shape)]
    another operation x1 -> x4, other arithmetic: 0.04 us -> 1.3 us  [the longest x1 0.96 us: broadcast_over_seq(): pair = jnp.stack([pack, partner])]
  transfers between devices with their start and end apart: 3 -> 6, of which waited for: 2 -> 5; matrix products, arithmetic and copies ran while one was open for 6% -> 7% of each run, Pallas kernels for 13% -> 14%
where the time goes in v10:
time: 112 us
  waiting for transfers between devices  40 us (36%)
  Pallas kernels  18.7 us (17%)
  starting transfers between devices  18.6 us (17%)
  blocking collectives  10.7 us (10%)
  local copies, waits for them, and re-layouts  10.1 us (9%)
  other arithmetic  8.4 us (8%)
  between operations  4.13 us (4%)
  matrix products  1.13 us (1%)
    all_to_all x1, waiting for transfers between devices, body(): received = lax.all_to_all(payload, 'seq', 0, 0, tiled=True)  20.1 us
    pallas_call x1, Pallas kernels, prefill_partial(): pl.pallas_call(kern, grid_spec=pltpu.PrefetchScalarGridSpec(num_scalar_pr...  15.7 us
    ppermute x3, waiting for transfers between devices, broadcast_over_seq(): pieces.append(lax.ppermute(pair, 'seq', perm))  14.5 us
    unnamed x1, blocking collectives  10.7 us
    all_to_all x1, starting transfers between devices, body(): received = lax.all_to_all(payload, 'seq', 0, 0, tiled=True)  6.13 us
    ppermute x1, waiting for transfers between devices, broadcast_over_seq(): lax.ppermute(pack, 'seq', [(i, (i + half) % seq_count) for i in range(seq...  5.35 us
    all_to_all x1, starting transfers between devices, body(): lax.all_to_all(jnp.broadcast_to(home_out[None], (seq_count,) + home_out.s...  4.66 us
    ppermute x1, starting transfers between devices, broadcast_over_seq(): lax.ppermute(pack, 'seq', [(i, (i + half) % seq_count) for i in range(seq...  4.1 us
  transfers between devices with their start and end apart: 6, of which 5 were waited for; matrix products, arithmetic and copies ran while one was open for 7% of the time, Pallas kernels for 14%

profile of v10, /device:TPU:0, one launch (start us, length us, event | category | flops | bytes accessed | tf_op | source)
XLA Modules:
  0.0 111.9 jit_solution(18250559630228474094)
XLA Ops:
  0.7 0.8 fusion.22
  1.4 1.0 fusion.44
  2.4 4.1 %collective-permute-start = (bf16[98,896]{1,0:T(8,128)(2,1)S(1)}, bf16[98,896]{1,0:T(8,128)(2,1)S(1)}, u32[]{:S(2)}, u32[]{:S(2)}) collective-permute-start(bf16[98,896]{1,0:T(8,128)(2,1)S(1)} %get-tuple-element.34), channel_id=1, source_target_pairs={{0,16},{4,20},{8,24},{12,28},{16,0},{20,4},{24,8},{28,12},{1,17},{... | collective-permute-start | bytes 526856 | tf_op jit(solution)/shard_map/ppermute | solution.py:139
  8.5 1.3 %compare_select_fusion.4 = (s32[8]{0:T(128)S(1)}, s32[]{:T(128)}) fusion(s32[8]{0:T(128)} %param.22, s32[]{:T(128)S(6)} %axis_index.15), kind=kLoop, calls=%fused_computation.55 | loop fusion | flops 47 | bytes 72 | tf_op jit(solution)/shard_map/jit(_take)/jit(_where)/select_n | solution.py:220
  9.8 5.3 %collective-permute-done = bf16[98,896]{1,0:T(8,128)(2,1)S(1)} collective-permute-done((bf16[98,896]{1,0:T(8,128)(2,1)S(1)}, bf16[98,896]{1,0:T(8,128)(2,1)S(1)}, u32[]{:S(2)}, u32[]{:S(2)}) %collective-permute-start) | collective-permute-done | bytes 175648 | tf_op jit(solution)/shard_map/ppermute | solution.py:139
  15.2 0.8 collective-permute-start.2
  16.0 1.5 %collective-permute-start.1 = (bf16[2,98,896]{2,1,0:T(8,128)(2,1)S(1)}, bf16[2,98,896]{2,1,0:T(8,128)(2,1)S(1)}, u32[]{:S(2)}, u32[]{:S(2)}) collective-permute-start(bf16[2,98,896]{2,1,0:T(8,128)(2,1)S(1)} %get-tuple-element.32), channel_id=1, source_target_pairs={{0,4},{4,8},{8,12},{12,0},{16,20},{20,24},{24,28},{28,16},{1,5},{5... | collective-permute-start | bytes 1053704 | tf_op jit(solution)/shard_map/ppermute | solution.py:144
  17.5 1.4 %collective-permute-start.3 = (bf16[2,98,896]{2,1,0:T(8,128)(2,1)S(1)}, bf16[2,98,896]{2,1,0:T(8,128)(2,1)S(1)}, u32[]{:S(2)}, u32[]{:S(2)}) collective-permute-start(bf16[2,98,896]{2,1,0:T(8,128)(2,1)S(1)} %get-tuple-element.32), channel_id=1, source_target_pairs={{0,12},{4,0},{8,4},{12,8},{16,28},{20,16},{24,20},{28,24},{1,13},{... | collective-permute-start | bytes 1053704 | tf_op jit(solution)/shard_map/ppermute | solution.py:144
  21.0 5.9 %collective-permute-done.2 = bf16[2,98,896]{2,1,0:T(8,128)(2,1)S(1)} collective-permute-done((bf16[2,98,896]{2,1,0:T(8,128)(2,1)S(1)}, bf16[2,98,896]{2,1,0:T(8,128)(2,1)S(1)}, u32[]{:S(2)}, u32[]{:S(2)}) %collective-permute-start.2) | collective-permute-done | bytes 351264 | tf_op jit(solution)/shard_map/ppermute | solution.py:144
  26.9 7.1 %collective-permute-done.1 = bf16[2,98,896]{2,1,0:T(8,128)(2,1)S(1)} collective-permute-done((bf16[2,98,896]{2,1,0:T(8,128)(2,1)S(1)}, bf16[2,98,896]{2,1,0:T(8,128)(2,1)S(1)}, u32[]{:S(2)}, u32[]{:S(2)}) %collective-permute-start.1) | collective-permute-done | bytes 351264 | tf_op jit(solution)/shard_map/ppermute | solution.py:144
  34.0 1.6 %collective-permute-done.3 = bf16[2,98,896]{2,1,0:T(8,128)(2,1)S(1)} collective-permute-done((bf16[2,98,896]{2,1,0:T(8,128)(2,1)S(1)}, bf16[2,98,896]{2,1,0:T(8,128)(2,1)S(1)}, u32[]{:S(2)}, u32[]{:S(2)}) %collective-permute-start.3) | collective-permute-done | bytes 351264 | tf_op jit(solution)/shard_map/ppermute | solution.py:144
  35.8 1.9 %gather_fusion = bf16[8,98,896]{2,1,0:T(8,128)(2,1)} fusion(bf16[8,98,896]{2,1,0:T(8,128)(2,1)S(1)} %bitcast.75, s32[1024]{0:T(1024)S(1)} %pad_clamp_fusion.1), kind=kCustom, calls=%fused_computation | custom fusion | bytes 2809888 | tf_op jit(solution)/shard_map/jit(_take)/gather | solution.py:150
  37.7 1.7 %broadcast_select_fusion.q_ref = bf16[8,98,896]{2,1,0:T(8,128)(2,1)S(1)} fusion(bf16[8,98,896]{2,1,0:T(8,128)(2,1)} %gather_fusion, pred[8]{0:T(512)(128)(4,1)S(1)} %get-tuple-element.44), kind=kLoop, calls=%fused_computation.5 | loop fusion | flops 702464 | bytes 2809864 | tf_op jit(solution)/shard_map/jit(_take)/select_n | solution.py:150
  40.3 0.9 copy-done.5
  42.0 0.7 reduce.10
  43.4 4.7 %all-to-all-start = ((bf16[8,2,448]{2,1,0:T(2,128)(2,1)}), bf16[8,2,448]{2,1,0:T(2,128)(2,1)S(1)}, u32[]{:S(2)}, u32[]{:S(2)}) async-start(bf16[8,2,448]{2,1,0:T(2,128)(2,1)} %reshape.446), calls=%async_computation | async-start | bytes 32768 | tf_op jit(solution)/shard_map/all_to_all | solution.py:217
  48.1 15.7 %shard_map.149 = (bf16[8,99,896]{2,1,0:T(8,128)(2,1)}, f32[3,256,7]{2,1,0:T(8,128)}) custom-call(s32[4]{0:T(128)} %pad_add_fusion.info_ref, bf16[8,98,896]{2,1,0:T(8,128)(2,1)} %copy-done.1, bf16[3,1024,128]{2,1,0:T(8,128)(2,1)} %k_ref.1, bf16[3,1024,128]{2,1,0:T(8,128)(2,1)} %v_ref.1, bf16[3,32,128]{2,1,0:T(8,128)(2,1)} %sk_ref.1, bf16[3,32,128]{2,1,0:T(8,128)(2,1)} %sv_ref.1), custom_call_target="tpu_custom_call" | custom-call | tf_op jit(solution)/shard_map/pallas_call | solution.py:81
  63.8 1.2 %copy.28 = f32[1,3,8,32,7]{3,2,4,1,0:T(8,128)S(1)} copy(f32[1,3,8,32,7]{4,3,2,1,0:T(8,128)} %bitcast.77) | data formatting | bytes 43008 | tf_op jit(solution)/shard_map/reshape | solution.py:256
  67.0 6.1 %all-to-all-start.1 = ((bf16[8,99,896]{2,1,0:T(8,128)(2,1)}), bf16[8,99,896]{2,1,0:T(8,128)(2,1)S(1)}, u32[]{:S(2)}, u32[]{:S(2)}) async-start(bf16[8,99,896]{2,1,0:T(8,128)(2,1)} %constant_dynamic-update-slice_fusion), calls=%async_computation.1 | async-start | bytes 2981888 | tf_op jit(solution)/shard_map/all_to_all | solution.py:273
  75.4 10.7 %all-reduce.2 = bf16[8,448]{1,0:T(8,128)(2,1)S(1)} all-reduce(f32[8,448]{1,0:T(8,128)S(1)} %fusion.17), channel_id=2, replica_groups=mesh['seq'=8,'tp'=4] {'tp'}, use_global_device_ids=true, to_apply=%region_3.5.clone | all-reduce | flops 3584 | bytes 21504
  86.7 20.1 %all-to-all-done.1.o_ref = bf16[8,99,896]{2,1,0:T(8,128)(2,1)S(1)} async-done(((bf16[8,99,896]{2,1,0:T(8,128)(2,1)}), bf16[8,99,896]{2,1,0:T(8,128)(2,1)S(1)}, u32[]{:S(2)}, u32[]{:S(2)}) %all-to-all-start.1) | async-done | bytes 1419296 | tf_op jit(solution)/shard_map/all_to_all | solution.py:273
  106.9 1.1 reshape.396
  108.0 0.8 fusion.8.lse_ref
  108.8 3.0 %shard_map.150 = bf16[3,32,896]{2,1,0:T(8,128)(2,1)} custom-call(bf16[8,99,896]{2,1,0:T(8,128)(2,1)} %copy-done.2, f32[8,3,32,7]{3,2,1,0:T(8,128)} %fusion.8.lse_ref), custom_call_target="tpu_custom_call" | custom-call | tf_op jit(solution)/shard_map/pallas_call | solution.py:125
  (52 shorter events, 8.4 us)
Async XLA Ops:
  0.6 74.4 %copy-start = (bf16[896,448]{0,1:T(8,128)(2,1)S(1)}, bf16[896,448]{0,1:T(8,128)(2,1)}, u32[]{:S(2)}) copy-start(bf16[896,448]{0,1:T(8,128)(2,1)} %param.23) | copy-start | bytes 2408452
  0.6 20.3 %copy-start.3 = (s32[8]{0:T(128)S(1)}, s32[8]{0:T(128)}, u32[]{:S(2)}) copy-start(s32[8]{0:T(128)} %param.22) | copy-start | bytes 100
  2.4 12.8 %collective-permute-start = (bf16[98,896]{1,0:T(8,128)(2,1)S(1)}, bf16[98,896]{1,0:T(8,128)(2,1)S(1)}, u32[]{:S(2)}, u32[]{:S(2)}) collective-permute-start(bf16[98,896]{1,0:T(8,128)(2,1)S(1)} %get-tuple-element.34), channel_id=1, source_target_pairs={{0,16},{4,20},{8,24},{12,28},{16,0},{20,4},{24,8},{28,12},{1,17},{... | collective-permute-start | bytes 526856 | tf_op jit(solution)/shard_map/ppermute | solution.py:139
  15.2 11.7 %collective-permute-start.2 = (bf16[2,98,896]{2,1,0:T(8,128)(2,1)S(1)}, bf16[2,98,896]{2,1,0:T(8,128)(2,1)S(1)}, u32[]{:S(2)}, u32[]{:S(2)}) collective-permute-start(bf16[2,98,896]{2,1,0:T(8,128)(2,1)S(1)} %get-tuple-element.32), channel_id=1, source_target_pairs={{0,8},{4,12},{8,0},{12,4},{16,24},{20,28},{24,16},{28,20},{1,9},{5... | collective-permute-start | bytes 1053704 | tf_op jit(solution)/shard_map/ppermute | solution.py:144
  16.0 17.9 %collective-permute-start.1 = (bf16[2,98,896]{2,1,0:T(8,128)(2,1)S(1)}, bf16[2,98,896]{2,1,0:T(8,128)(2,1)S(1)}, u32[]{:S(2)}, u32[]{:S(2)}) collective-permute-start(bf16[2,98,896]{2,1,0:T(8,128)(2,1)S(1)} %get-tuple-element.32), channel_id=1, source_target_pairs={{0,4},{4,8},{8,12},{12,0},{16,20},{20,24},{24,28},{28,16},{1,5},{5... | collective-permute-start | bytes 1053704 | tf_op jit(solution)/shard_map/ppermute | solution.py:144
  17.5 18.0 %collective-permute-start.3 = (bf16[2,98,896]{2,1,0:T(8,128)(2,1)S(1)}, bf16[2,98,896]{2,1,0:T(8,128)(2,1)S(1)}, u32[]{:S(2)}, u32[]{:S(2)}) collective-permute-start(bf16[2,98,896]{2,1,0:T(8,128)(2,1)S(1)} %get-tuple-element.32), channel_id=1, source_target_pairs={{0,12},{4,0},{8,4},{12,8},{16,28},{20,16},{24,20},{28,24},{1,13},{... | collective-permute-start | bytes 1053704 | tf_op jit(solution)/shard_map/ppermute | solution.py:144
  37.7 1.9 %copy-start.4 = (bf16[1,4096,128]{2,1,0:T(8,128)(2,1)S(1)}, bf16[1,4096,128]{2,1,0:T(8,128)(2,1)}, u32[]{:S(2)}) copy-start(bf16[1,4096,128]{2,1,0:T(8,128)(2,1)} %param.19) | copy-start | bytes 3145732
  39.4 2.1 %copy-start.1 = (bf16[8,98,896]{2,1,0:T(8,128)(2,1)}, bf16[8,98,896]{2,1,0:T(8,128)(2,1)S(1)}, u32[]{:S(2)}) copy-start(bf16[8,98,896]{2,1,0:T(8,128)(2,1)S(1)} %broadcast_select_fusion.q_ref) | copy-start | bytes 4214788
  39.4 1.8 %copy-start.5 = (bf16[1,4096,128]{2,1,0:T(8,128)(2,1)S(1)}, bf16[1,4096,128]{2,1,0:T(8,128)(2,1)}, u32[]{:S(2)}) copy-start(bf16[1,4096,128]{2,1,0:T(8,128)(2,1)} %param.20) | copy-start | bytes 3145732
  43.4 23.6 %all-to-all-start = ((bf16[8,2,448]{2,1,0:T(2,128)(2,1)}), bf16[8,2,448]{2,1,0:T(2,128)(2,1)S(1)}, u32[]{:S(2)}, u32[]{:S(2)}) async-start(bf16[8,2,448]{2,1,0:T(2,128)(2,1)} %reshape.446), calls=%async_computation | async-start | bytes 32768 | tf_op jit(solution)/shard_map/all_to_all | solution.py:217
  67.0 6.1 %copy-start.6 = (u32[32]{0:T(128)S(1)}, u32[32]{0:T(128)}, u32[]{:S(2)}) copy-start(u32[32]{0:T(128)} %constant.212) | copy-start | bytes 388
  67.0 39.9 %all-to-all-start.1 = ((bf16[8,99,896]{2,1,0:T(8,128)(2,1)}), bf16[8,99,896]{2,1,0:T(8,128)(2,1)S(1)}, u32[]{:S(2)}, u32[]{:S(2)}) async-start(bf16[8,99,896]{2,1,0:T(8,128)(2,1)} %constant_dynamic-update-slice_fusion), calls=%async_computation.1 | async-start | bytes 2981888 | tf_op jit(solution)/shard_map/all_to_all | solution.py:273
  106.9 2.0 %copy-start.2 = (bf16[8,99,896]{2,1,0:T(8,128)(2,1)}, bf16[8,99,896]{2,1,0:T(8,128)(2,1)S(1)}, u32[]{:S(2)}) copy-start(bf16[8,99,896]{2,1,0:T(8,128)(2,1)S(1)} %all-to-all-done.1.o_ref) | copy-start | bytes 4257796

commit v11 on v10

--- a/solution.py
+++ b/solution.py
@@ -214,9 +214,9 @@
     home_out = jax.vmap(decode_slot)(
         home_query, home_key, home_value, cache_keys, cache_values, cache_length
     )
-    all_out = lax.all_to_all(
-        jnp.broadcast_to(home_out[None], (seq_count,) + home_out.shape), "seq", 0, 0, tiled=True
-    ).reshape(total_dec, group_size * head_size)
+    all_out = broadcast_over_seq(home_out, seq_rank, seq_count).reshape(
+        total_dec, group_size * head_size
+    )
     arrival_out = jnp.take(all_out, dealing, axis=0)
     arrival_terms = jnp.dot(arrival_out, out_weight, preferred_element_type=jnp.float32)
     decode_mixed = lax.psum_scatter(arrival_terms, "tp", scatter_dimension=0, tiled=True).astype(

time: 112 us -> 122 us (1.089)
  waiting for transfers between devices: 40 us -> 50 us
    ppermute x1 -> x2, waiting for transfers between devices: 5.35 us -> 31.3 us  [broadcast_over_seq(): lax.ppermute(pack, 'seq', [(i, (i + half) % seq_count) for i in range(seq...]
    all_to_all x1, waiting for transfers between devices: 20.1 us -> 0.01 us  [body(): received = lax.all_to_all(payload, 'seq', 0, 0, tiled=True)]
    all_to_all x1 -> x0, starting transfers between devices: 4.66 us -> none  [body(): lax.all_to_all(jnp.broadcast_to(home_out[None], (seq_count,) + home_out.s...]
    ppermute x3 -> x6, waiting for transfers between devices: 14.5 us -> 18.6 us  [broadcast_over_seq(): pieces.append(lax.ppermute(pair, 'seq', perm))]
    ppermute x3 -> x6, starting transfers between devices: 3.71 us -> 6.76 us  [broadcast_over_seq(): pieces.append(lax.ppermute(pair, 'seq', perm))]
    ppermute x1 -> x2, starting transfers between devices: 4.1 us -> 7.07 us  [broadcast_over_seq(): lax.ppermute(pack, 'seq', [(i, (i + half) % seq_count) for i in range(seq...]
    unnamed x21 -> x17, local copies, waits for them, and re-layouts: 2.33 us -> 0.67 us
    all_to_all x1, starting transfers between devices: 6.13 us -> 4.79 us  [body(): received = lax.all_to_all(payload, 'seq', 0, 0, tiled=True)]
  transfers between devices with their start and end apart: 6 -> 9, of which waited for: 5 -> 8; matrix products, arithmetic and copies ran while one was open for 7% -> 6% of each run, Pallas kernels for 14% -> 0%
where the time goes in v11:
time: 122 us; the launch traced here: 121 us
  waiting for transfers between devices  50 us (41%)
  Pallas kernels  18.8 us (15%)
  starting transfers between devices  18.6 us (15%)
  blocking collectives  10.2 us (8%)
  local copies, waits for them, and re-layouts  9.49 us (8%)
  other arithmetic  8.85 us (7%)
  between operations  4.09 us (3%)
    ppermute x2, waiting for transfers between devices, broadcast_over_seq(): lax.ppermute(pack, 'seq', [(i, (i + half) % seq_count) for i in range(seq...  31.3 us
    ppermute x6, waiting for transfers between devices, broadcast_over_seq(): pieces.append(lax.ppermute(pair, 'seq', perm))  18.6 us
    pallas_call x1, Pallas kernels, prefill_partial(): pl.pallas_call(kern, grid_spec=pltpu.PrefetchScalarGridSpec(num_scalar_pr...  15.7 us
    unnamed x1, blocking collectives  10.2 us
    ppermute x2, starting transfers between devices, broadcast_over_seq(): lax.ppermute(pack, 'seq', [(i, (i + half) % seq_count) for i in range(seq...  7.07 us
    ppermute x6, starting transfers between devices, broadcast_over_seq(): pieces.append(lax.ppermute(pair, 'seq', perm))  6.76 us
    all_to_all x1, starting transfers between devices, body(): received = lax.all_to_all(payload, 'seq', 0, 0, tiled=True)  4.79 us
    pallas_call x1, Pallas kernels, combine_partials(): pl.pallas_call(kern, out_shape=jax.ShapeDtypeStruct((stretch_count, local...  3.03 us
  transfers between devices with their start and end apart: 9, of which 8 were waited for; matrix products, arithmetic and copies ran while one was open for 6% of the time, Pallas kernels for 0%

profile of v11, /device:TPU:0, one launch (start us, length us, event | category | flops | bytes accessed | tf_op | source)
XLA Modules:
  0.0 121.1 jit_solution(14412629622342823263)
XLA Ops:
  1.4 1.0 fusion.43
  2.4 4.1 %collective-permute-start = (bf16[98,896]{1,0:T(8,128)(2,1)S(1)}, bf16[98,896]{1,0:T(8,128)(2,1)S(1)}, u32[]{:S(2)}, u32[]{:S(2)}) collective-permute-start(bf16[98,896]{1,0:T(8,128)(2,1)S(1)} %get-tuple-element.34), channel_id=1, source_target_pairs={{0,16},{4,20},{8,24},{12,28},{16,0},{20,4},{24,8},{28,12},{1,17},{... | collective-permute-start | bytes 526856 | tf_op jit(solution)/shard_map/ppermute | solution.py:139
  9.2 6.0 %collective-permute-done = bf16[98,896]{1,0:T(8,128)(2,1)S(1)} collective-permute-done((bf16[98,896]{1,0:T(8,128)(2,1)S(1)}, bf16[98,896]{1,0:T(8,128)(2,1)S(1)}, u32[]{:S(2)}, u32[]{:S(2)}) %collective-permute-start) | collective-permute-done | bytes 175648 | tf_op jit(solution)/shard_map/ppermute | solution.py:139
  15.2 0.8 collective-permute-start.2
  16.0 1.5 %collective-permute-start.1 = (bf16[2,98,896]{2,1,0:T(8,128)(2,1)S(1)}, bf16[2,98,896]{2,1,0:T(8,128)(2,1)S(1)}, u32[]{:S(2)}, u32[]{:S(2)}) collective-permute-start(bf16[2,98,896]{2,1,0:T(8,128)(2,1)S(1)} %get-tuple-element.32), channel_id=1, source_target_pairs={{0,4},{4,8},{8,12},{12,0},{16,20},{20,24},{24,28},{28,16},{1,5},{5... | collective-permute-start | bytes 1053704 | tf_op jit(solution)/shard_map/ppermute | solution.py:144
  17.5 1.4 %collective-permute-start.3 = (bf16[2,98,896]{2,1,0:T(8,128)(2,1)S(1)}, bf16[2,98,896]{2,1,0:T(8,128)(2,1)S(1)}, u32[]{:S(2)}, u32[]{:S(2)}) collective-permute-start(bf16[2,98,896]{2,1,0:T(8,128)(2,1)S(1)} %get-tuple-element.32), channel_id=1, source_target_pairs={{0,12},{4,0},{8,4},{12,8},{16,28},{20,16},{24,20},{28,24},{1,13},{... | collective-permute-start | bytes 1053704 | tf_op jit(solution)/shard_map/ppermute | solution.py:144
  18.9 7.9 %collective-permute-done.2 = bf16[2,98,896]{2,1,0:T(8,128)(2,1)S(1)} collective-permute-done((bf16[2,98,896]{2,1,0:T(8,128)(2,1)S(1)}, bf16[2,98,896]{2,1,0:T(8,128)(2,1)S(1)}, u32[]{:S(2)}, u32[]{:S(2)}) %collective-permute-start.2) | collective-permute-done | bytes 351264 | tf_op jit(solution)/shard_map/ppermute | solution.py:144
  26.9 7.1 %collective-permute-done.1 = bf16[2,98,896]{2,1,0:T(8,128)(2,1)S(1)} collective-permute-done((bf16[2,98,896]{2,1,0:T(8,128)(2,1)S(1)}, bf16[2,98,896]{2,1,0:T(8,128)(2,1)S(1)}, u32[]{:S(2)}, u32[]{:S(2)}) %collective-permute-start.1) | collective-permute-done | bytes 351264 | tf_op jit(solution)/shard_map/ppermute | solution.py:144
  33.9 1.6 %collective-permute-done.3 = bf16[2,98,896]{2,1,0:T(8,128)(2,1)S(1)} collective-permute-done((bf16[2,98,896]{2,1,0:T(8,128)(2,1)S(1)}, bf16[2,98,896]{2,1,0:T(8,128)(2,1)S(1)}, u32[]{:S(2)}, u32[]{:S(2)}) %collective-permute-start.3) | collective-permute-done | bytes 351264 | tf_op jit(solution)/shard_map/ppermute | solution.py:144
  35.8 1.9 %gather_fusion = bf16[8,98,896]{2,1,0:T(8,128)(2,1)} fusion(bf16[8,98,896]{2,1,0:T(8,128)(2,1)S(1)} %bitcast.84, s32[1024]{0:T(1024)S(1)} %pad_clamp_fusion.1), kind=kCustom, calls=%fused_computation | custom fusion | bytes 2809888 | tf_op jit(solution)/shard_map/jit(_take)/gather | solution.py:150
  37.6 2.7 %broadcast_select_fusion.q_ref = bf16[8,98,896]{2,1,0:T(8,128)(2,1)} fusion(bf16[8,98,896]{2,1,0:T(8,128)(2,1)} %gather_fusion, pred[8]{0:T(512)(128)(4,1)S(1)} %get-tuple-element.44), kind=kLoop, calls=%fused_computation.6 | loop fusion | flops 702464 | bytes 2809864 | tf_op jit(solution)/shard_map/jit(_take)/select_n | solution.py:150
  40.4 15.7 %shard_map.149 = (bf16[8,99,896]{2,1,0:T(8,128)(2,1)}, f32[3,256,7]{2,1,0:T(8,128)}) custom-call(s32[4]{0:T(128)} %pad_add_fusion.info_ref, bf16[8,98,896]{2,1,0:T(8,128)(2,1)} %broadcast_select_fusion.q_ref, bf16[3,1024,128]{2,1,0:T(8,128)(2,1)} %k_ref.1, bf16[3,1024,128]{2,1,0:T(8,128)(2,1)} %v_ref.1, bf16[3,32,128]{2,1,0:T(8,128)(2,1)} %sk_ref.1, ...), custom_call_target="tpu_custom_call" | custom-call | tf_op jit(solution)/shard_map/pallas_call | solution.py:81
  56.1 1.2 copy.26
  59.3 4.8 %all-to-all-start = ((bf16[8,99,896]{2,1,0:T(8,128)(2,1)}), bf16[8,99,896]{2,1,0:T(8,128)(2,1)S(1)}, u32[]{:S(2)}, u32[]{:S(2)}) async-start(bf16[8,99,896]{2,1,0:T(8,128)(2,1)} %constant_dynamic-update-slice_fusion), calls=%async_computation | async-start | bytes 2981888 | tf_op jit(solution)/shard_map/all_to_all | solution.py:273
  66.8 1.0 fusion.45
  69.0 3.0 %collective-permute-start.4 = (bf16[1,896]{1,0:T(2,128)(2,1)S(1)}, bf16[1,896]{1,0:T(2,128)(2,1)S(1)}, u32[]{:S(2)}, u32[]{:S(2)}) collective-permute-start(bf16[1,896]{1,0:T(2,128)(2,1)S(1)} %bitcast.101), channel_id=1, source_target_pairs={{0,16},{4,20},{8,24},{12,28},{16,0},{20,4},{24,8},{28,12},{1,17},{... | collective-permute-start | bytes 5384 | tf_op jit(solution)/shard_map/ppermute | solution.py:139
  73.2 25.3 %collective-permute-done.4 = bf16[1,896]{1,0:T(2,128)(2,1)S(1)} collective-permute-done((bf16[1,896]{1,0:T(2,128)(2,1)S(1)}, bf16[1,896]{1,0:T(2,128)(2,1)S(1)}, u32[]{:S(2)}, u32[]{:S(2)}) %collective-permute-start.4) | collective-permute-done | bytes 1824 | tf_op jit(solution)/shard_map/ppermute | solution.py:139
  98.7 1.2 %collective-permute-start.5 = (bf16[2,1,896]{2,0,1:T(2,128)(2,1)S(1)}, bf16[2,1,896]{2,0,1:T(2,128)(2,1)S(1)}, u32[]{:S(2)}, u32[]{:S(2)}) collective-permute-start(bf16[2,1,896]{2,0,1:T(2,128)(2,1)S(1)} %pad_maximum_fusion.4), channel_id=1, source_target_pairs={{0,4},{4,8},{8,12},{12,0},{16,20},{20,24},{24,28},{28,16},{1,5},{5... | collective-permute-start | bytes 10760 | tf_op jit(solution)/shard_map/ppermute | solution.py:144
  99.9 1.7 %collective-permute-start.7 = (bf16[2,1,896]{2,0,1:T(2,128)(2,1)S(1)}, bf16[2,1,896]{2,0,1:T(2,128)(2,1)S(1)}, u32[]{:S(2)}, u32[]{:S(2)}) collective-permute-start(bf16[2,1,896]{2,0,1:T(2,128)(2,1)S(1)} %pad_maximum_fusion.4), channel_id=1, source_target_pairs={{0,12},{4,0},{8,4},{12,8},{16,28},{20,16},{24,20},{28,24},{1,13},{... | collective-permute-start | bytes 10760 | tf_op jit(solution)/shard_map/ppermute | solution.py:144
  102.2 1.0 collective-permute-done.5
  105.3 10.2 %all-reduce.2 = bf16[8,448]{1,0:T(8,128)(2,1)S(1)} all-reduce(f32[8,448]{1,0:T(8,128)S(1)} %fusion.16), channel_id=2, replica_groups=mesh['seq'=8,'tp'=4] {'tp'}, use_global_device_ids=true, to_apply=%region_3.5.clone | all-reduce | flops 3584 | bytes 21504
  116.1 1.1 reshape.410
  117.2 0.9 fusion.7.lse_ref
  118.1 3.0 %shard_map.150 = bf16[3,32,896]{2,1,0:T(8,128)(2,1)} custom-call(bf16[8,99,896]{2,1,0:T(8,128)(2,1)} %copy-done.1, f32[8,3,32,7]{3,2,1,0:T(8,128)} %fusion.7.lse_ref), custom_call_target="tpu_custom_call" | custom-call | tf_op jit(solution)/shard_map/pallas_call | solution.py:125
  (58 shorter events, 10.9 us)
Async XLA Ops:
  0.6 104.4 %copy-start = (bf16[896,448]{0,1:T(8,128)(2,1)S(1)}, bf16[896,448]{0,1:T(8,128)(2,1)}, u32[]{:S(2)}) copy-start(bf16[896,448]{0,1:T(8,128)(2,1)} %param.23) | copy-start | bytes 2408452
  2.4 12.8 %collective-permute-start = (bf16[98,896]{1,0:T(8,128)(2,1)S(1)}, bf16[98,896]{1,0:T(8,128)(2,1)S(1)}, u32[]{:S(2)}, u32[]{:S(2)}) collective-permute-start(bf16[98,896]{1,0:T(8,128)(2,1)S(1)} %get-tuple-element.34), channel_id=1, source_target_pairs={{0,16},{4,20},{8,24},{12,28},{16,0},{20,4},{24,8},{28,12},{1,17},{... | collective-permute-start | bytes 526856 | tf_op jit(solution)/shard_map/ppermute | solution.py:139
  15.2 11.7 %collective-permute-start.2 = (bf16[2,98,896]{2,1,0:T(8,128)(2,1)S(1)}, bf16[2,98,896]{2,1,0:T(8,128)(2,1)S(1)}, u32[]{:S(2)}, u32[]{:S(2)}) collective-permute-start(bf16[2,98,896]{2,1,0:T(8,128)(2,1)S(1)} %get-tuple-element.32), channel_id=1, source_target_pairs={{0,8},{4,12},{8,0},{12,4},{16,24},{20,28},{24,16},{28,20},{1,9},{5... | collective-permute-start | bytes 1053704 | tf_op jit(solution)/shard_map/ppermute | solution.py:144
  16.0 17.9 %collective-permute-start.1 = (bf16[2,98,896]{2,1,0:T(8,128)(2,1)S(1)}, bf16[2,98,896]{2,1,0:T(8,128)(2,1)S(1)}, u32[]{:S(2)}, u32[]{:S(2)}) collective-permute-start(bf16[2,98,896]{2,1,0:T(8,128)(2,1)S(1)} %get-tuple-element.32), channel_id=1, source_target_pairs={{0,4},{4,8},{8,12},{12,0},{16,20},{20,24},{24,28},{28,16},{1,5},{5... | collective-permute-start | bytes 1053704 | tf_op jit(solution)/shard_map/ppermute | solution.py:144
  17.5 18.0 %collective-permute-start.3 = (bf16[2,98,896]{2,1,0:T(8,128)(2,1)S(1)}, bf16[2,98,896]{2,1,0:T(8,128)(2,1)S(1)}, u32[]{:S(2)}, u32[]{:S(2)}) collective-permute-start(bf16[2,98,896]{2,1,0:T(8,128)(2,1)S(1)} %get-tuple-element.32), channel_id=1, source_target_pairs={{0,12},{4,0},{8,4},{12,8},{16,28},{20,16},{24,20},{28,24},{1,13},{... | collective-permute-start | bytes 1053704 | tf_op jit(solution)/shard_map/ppermute | solution.py:144
  59.3 4.8 %copy-start.2 = (s32[8]{0:T(128)S(1)}, s32[8]{0:T(128)}, u32[]{:S(2)}) copy-start(s32[8]{0:T(128)} %param.22) | copy-start | bytes 100
  59.3 8.6 %copy-start.3 = (bf16[1,4096,128]{2,1,0:T(8,128)(2,1)S(1)}, bf16[1,4096,128]{2,1,0:T(8,128)(2,1)}, u32[]{:S(2)}) copy-start(bf16[1,4096,128]{2,1,0:T(8,128)(2,1)} %param.19) | copy-start | bytes 3145732
  59.3 56.8 %all-to-all-start = ((bf16[8,99,896]{2,1,0:T(8,128)(2,1)}), bf16[8,99,896]{2,1,0:T(8,128)(2,1)S(1)}, u32[]{:S(2)}, u32[]{:S(2)}) async-start(bf16[8,99,896]{2,1,0:T(8,128)(2,1)} %constant_dynamic-update-slice_fusion), calls=%async_computation | async-start | bytes 2981888 | tf_op jit(solution)/shard_map/all_to_all | solution.py:273
  64.1 4.5 %copy-start.4 = (bf16[1,4096,128]{2,1,0:T(8,128)(2,1)S(1)}, bf16[1,4096,128]{2,1,0:T(8,128)(2,1)}, u32[]{:S(2)}) copy-start(bf16[1,4096,128]{2,1,0:T(8,128)(2,1)} %param.20) | copy-start | bytes 3145732
  67.9 4.1 %copy-start.5 = (u32[32]{0:T(128)S(1)}, u32[32]{0:T(128)}, u32[]{:S(2)}) copy-start(u32[32]{0:T(128)} %constant.239) | copy-start | bytes 388
  69.0 29.6 %collective-permute-start.4 = (bf16[1,896]{1,0:T(2,128)(2,1)S(1)}, bf16[1,896]{1,0:T(2,128)(2,1)S(1)}, u32[]{:S(2)}, u32[]{:S(2)}) collective-permute-start(bf16[1,896]{1,0:T(2,128)(2,1)S(1)} %bitcast.101), channel_id=1, source_target_pairs={{0,16},{4,20},{8,24},{12,28},{16,0},{20,4},{24,8},{28,12},{1,17},{... | collective-permute-start | bytes 5384 | tf_op jit(solution)/shard_map/ppermute | solution.py:139
  98.6 3.7 %collective-permute-start.6 = (bf16[2,1,896]{2,0,1:T(2,128)(2,1)S(1)}, bf16[2,1,896]{2,0,1:T(2,128)(2,1)S(1)}, u32[]{:S(2)}, u32[]{:S(2)}) collective-permute-start(bf16[2,1,896]{2,0,1:T(2,128)(2,1)S(1)} %pad_maximum_fusion.4), channel_id=1, source_target_pairs={{0,8},{4,12},{8,0},{12,4},{16,24},{20,28},{24,16},{28,20},{1,9},{5... | collective-permute-start | bytes 10760 | tf_op jit(solution)/shard_map/ppermute | solution.py:144
  98.7 4.6 %collective-permute-start.5 = (bf16[2,1,896]{2,0,1:T(2,128)(2,1)S(1)}, bf16[2,1,896]{2,0,1:T(2,128)(2,1)S(1)}, u32[]{:S(2)}, u32[]{:S(2)}) collective-permute-start(bf16[2,1,896]{2,0,1:T(2,128)(2,1)S(1)} %pad_maximum_fusion.4), channel_id=1, source_target_pairs={{0,4},{4,8},{8,12},{12,0},{16,20},{20,24},{24,28},{28,16},{1,5},{5... | collective-permute-start | bytes 10760 | tf_op jit(solution)/shard_map/ppermute | solution.py:144
  99.9 3.8 %collective-permute-start.7 = (bf16[2,1,896]{2,0,1:T(2,128)(2,1)S(1)}, bf16[2,1,896]{2,0,1:T(2,128)(2,1)S(1)}, u32[]{:S(2)}, u32[]{:S(2)}) collective-permute-start(bf16[2,1,896]{2,0,1:T(2,128)(2,1)S(1)} %pad_maximum_fusion.4), channel_id=1, source_target_pairs={{0,12},{4,0},{8,4},{12,8},{16,28},{20,16},{24,20},{28,24},{1,13},{... | collective-permute-start | bytes 10760 | tf_op jit(solution)/shard_map/ppermute | solution.py:144
  116.1 2.0 %copy-start.1 = (bf16[8,99,896]{2,1,0:T(8,128)(2,1)}, bf16[8,99,896]{2,1,0:T(8,128)(2,1)S(1)}, u32[]{:S(2)}) copy-start(bf16[8,99,896]{2,1,0:T(8,128)(2,1)S(1)} %all-to-all-done.o_ref) | copy-start | bytes 4257796

commit v12 on v10

--- a/solution.py
+++ b/solution.py
@@ -147,7 +147,7 @@
     far = (sources // half) != (seq_rank // half)
     near = jnp.where(far, (sources + half) % seq_count, sources)
     shift_of = (seq_rank % half - near % half) % half
-    return jnp.take(every, shift_of * 2 + far.astype(jnp.int32), axis=0)
+    return jnp.take(every, shift_of * 2 + far.astype(jnp.int32), axis=0, mode="clip")
 
 
 def body(

time: 112 us -> 113 us (level)
  matrix products: 1.13 us -> 2.98 us
  other arithmetic: 8.4 us -> 7.17 us
    dot_general x1, matrix products: 0.5 us -> 2.33 us  [partial_attend(): jnp.dot(queries, keys.T, preferred_element_type=jnp.float32) * factor]
    select_n x2 -> x0, other arithmetic: 1.71 us -> none  [broadcast_over_seq(): return jnp.take(every, shift_of * 2 + far.astype(jnp.int32), axis=0)]
    ppermute x1, waiting for transfers between devices: 5.35 us -> 6.7 us  [broadcast_over_seq(): lax.ppermute(pack, 'seq', [(i, (i + half) % seq_count) for i in range(seq...]
where the time goes in v12:
time: 113 us
  waiting for transfers between devices  40.7 us (36%)
  Pallas kernels  18.7 us (17%)
  starting transfers between devices  18.6 us (16%)
  blocking collectives  10.7 us (9%)
  local copies, waits for them, and re-layouts  9.57 us (8%)
  other arithmetic  7.17 us (6%)
  between operations  4.1 us (4%)
  matrix products  2.98 us (3%)
    all_to_all x1, waiting for transfers between devices, body(): received = lax.all_to_all(payload, 'seq', 0, 0, tiled=True)  20.1 us
    pallas_call x1, Pallas kernels, prefill_partial(): pl.pallas_call(kern, grid_spec=pltpu.PrefetchScalarGridSpec(num_scalar_pr...  15.7 us
    ppermute x3, waiting for transfers between devices, broadcast_over_seq(): pieces.append(lax.ppermute(pair, 'seq', perm))  13.9 us
    unnamed x1, blocking collectives  10.7 us
    ppermute x1, waiting for transfers between devices, broadcast_over_seq(): lax.ppermute(pack, 'seq', [(i, (i + half) % seq_count) for i in range(seq...  6.7 us
    all_to_all x1, starting transfers between devices, body(): received = lax.all_to_all(payload, 'seq', 0, 0, tiled=True)  6.13 us
    all_to_all x1, starting transfers between devices, body(): lax.all_to_all(jnp.broadcast_to(home_out[None], (seq_count,) + home_out.s...  4.66 us
    ppermute x1, starting transfers between devices, broadcast_over_seq(): lax.ppermute(pack, 'seq', [(i, (i + half) % seq_count) for i in range(seq...  4.1 us
  transfers between devices with their start and end apart: 6, of which 5 were waited for; matrix products, arithmetic and copies ran while one was open for 7% of the time, Pallas kernels for 14%

profile of v12, /device:TPU:0, one launch (start us, length us, event | category | flops | bytes accessed | tf_op | source)
XLA Modules:
  0.0 112.6 jit_solution(4883693955487819891)
XLA Ops:
  0.7 0.8 fusion.22
  1.4 1.0 fusion.38
  2.4 4.1 %collective-permute-start = (bf16[98,896]{1,0:T(8,128)(2,1)S(1)}, bf16[98,896]{1,0:T(8,128)(2,1)S(1)}, u32[]{:S(2)}, u32[]{:S(2)}) collective-permute-start(bf16[98,896]{1,0:T(8,128)(2,1)S(1)} %get-tuple-element.34), channel_id=1, source_target_pairs={{0,16},{4,20},{8,24},{12,28},{16,0},{20,4},{24,8},{28,12},{1,17},{... | collective-permute-start | bytes 526856 | tf_op jit(solution)/shard_map/ppermute | solution.py:139
  7.2 1.3 %compare_select_fusion.2 = (s32[8]{0:T(128)S(1)}, s32[]{:T(128)}) fusion(s32[8]{0:T(128)} %param.22, s32[]{:T(128)S(6)} %axis_index.15), kind=kLoop, calls=%fused_computation.52 | loop fusion | flops 47 | bytes 72 | tf_op jit(solution)/shard_map/jit(_take)/jit(_where)/select_n | solution.py:220
  8.5 6.7 %collective-permute-done = bf16[98,896]{1,0:T(8,128)(2,1)S(1)} collective-permute-done((bf16[98,896]{1,0:T(8,128)(2,1)S(1)}, bf16[98,896]{1,0:T(8,128)(2,1)S(1)}, u32[]{:S(2)}, u32[]{:S(2)}) %collective-permute-start) | collective-permute-done | bytes 175648 | tf_op jit(solution)/shard_map/ppermute | solution.py:139
  15.2 0.8 collective-permute-start.2
  16.0 1.5 %collective-permute-start.1 = (bf16[2,98,896]{2,1,0:T(8,128)(2,1)S(1)}, bf16[2,98,896]{2,1,0:T(8,128)(2,1)S(1)}, u32[]{:S(2)}, u32[]{:S(2)}) collective-permute-start(bf16[2,98,896]{2,1,0:T(8,128)(2,1)S(1)} %get-tuple-element.32), channel_id=1, source_target_pairs={{0,4},{4,8},{8,12},{12,0},{16,20},{20,24},{24,28},{28,16},{1,5},{5... | collective-permute-start | bytes 1053704 | tf_op jit(solution)/shard_map/ppermute | solution.py:144
  17.5 1.4 %collective-permute-start.3 = (bf16[2,98,896]{2,1,0:T(8,128)(2,1)S(1)}, bf16[2,98,896]{2,1,0:T(8,128)(2,1)S(1)}, u32[]{:S(2)}, u32[]{:S(2)}) collective-permute-start(bf16[2,98,896]{2,1,0:T(8,128)(2,1)S(1)} %get-tuple-element.32), channel_id=1, source_target_pairs={{0,12},{4,0},{8,4},{12,8},{16,28},{20,16},{24,20},{28,24},{1,13},{... | collective-permute-start | bytes 1053704 | tf_op jit(solution)/shard_map/ppermute | solution.py:144
  21.7 5.2 %collective-permute-done.2 = bf16[2,98,896]{2,1,0:T(8,128)(2,1)S(1)} collective-permute-done((bf16[2,98,896]{2,1,0:T(8,128)(2,1)S(1)}, bf16[2,98,896]{2,1,0:T(8,128)(2,1)S(1)}, u32[]{:S(2)}, u32[]{:S(2)}) %collective-permute-start.2) | collective-permute-done | bytes 351264 | tf_op jit(solution)/shard_map/ppermute | solution.py:144
  26.9 7.1 %collective-permute-done.1 = bf16[2,98,896]{2,1,0:T(8,128)(2,1)S(1)} collective-permute-done((bf16[2,98,896]{2,1,0:T(8,128)(2,1)S(1)}, bf16[2,98,896]{2,1,0:T(8,128)(2,1)S(1)}, u32[]{:S(2)}, u32[]{:S(2)}) %collective-permute-start.1) | collective-permute-done | bytes 351264 | tf_op jit(solution)/shard_map/ppermute | solution.py:144
  34.0 1.6 %collective-permute-done.3 = bf16[2,98,896]{2,1,0:T(8,128)(2,1)S(1)} collective-permute-done((bf16[2,98,896]{2,1,0:T(8,128)(2,1)S(1)}, bf16[2,98,896]{2,1,0:T(8,128)(2,1)S(1)}, u32[]{:S(2)}, u32[]{:S(2)}) %collective-permute-start.3) | collective-permute-done | bytes 351264 | tf_op jit(solution)/shard_map/ppermute | solution.py:144
  35.6 1.4 %pad_maximum_fusion = bf16[4,2,98,896]{3,2,1,0:T(8,128)(2,1)} fusion(bf16[1,2,98,896]{3,2,1,0:T(8,128)(2,1)S(1)} %bitcast.80, bf16[1,2,98,896]{3,2,1,0:T(8,128)(2,1)S(1)} %bitcast.78, bf16[1,2,98,896]{3,2,1,0:T(8,128)(2,1)S(1)} %bitcast.79, bf16[1,2,98,896]{3,2,1,0:T(8,128)(2,1)S(1)} %get-tuple-element.31), kind=kLoop, calls=%fused_computation.4 | loop fusion | flops 2107392 | bytes 2809856 | tf_op jit(solution)/shard_map/stack | solution.py:145
  36.9 2.2 %gather_fusion = bf16[8,98,896]{2,1,0:T(8,128)(2,1)S(1)} fusion(bf16[8,98,896]{2,1,0:T(8,128)(2,1)} %bitcast.75, s32[1024]{0:T(1024)S(1)} %pad_clamp_fusion.1), kind=kCustom, calls=%fused_computation | custom fusion | bytes 2809888 | tf_op jit(solution)/shard_map/jit(_take)/gather | solution.py:150
  39.3 2.3 %fusion.42 = (f32[7]{0:T(128)S(1)}, f32[7,4097]{1,0:T(8,128)S(1)}) fusion(bf16[1,1,128]{2,1,0:T(2,128)(2,1)S(1)} %get-tuple-element.44, bf16[1,4096,128]{2,1,0:T(8,128)(2,1)} %param.19, bf16[896]{0:T(1024)(128)(2,1)S(1)} %fusion.21, pred[4097]{0:T(1024)(128)(4,1)S(1)} %add_reduce_fusion), kind=kOutput, calls=%fused_computation.96 | convolution fusion | flops 9525518 | bytes 1169465 | tf_op jit(solution)/shard_map/vmap()/dot_general | solution.py:16
  42.7 0.7 reduce.10
  44.1 4.7 %all-to-all-start = ((bf16[8,2,448]{2,1,0:T(2,128)(2,1)}), bf16[8,2,448]{2,1,0:T(2,128)(2,1)S(1)}, u32[]{:S(2)}, u32[]{:S(2)}) async-start(bf16[8,2,448]{2,1,0:T(2,128)(2,1)} %reshape.432), calls=%async_computation | async-start | bytes 32768 | tf_op jit(solution)/shard_map/all_to_all | solution.py:217
  48.8 15.7 %shard_map.149 = (bf16[8,99,896]{2,1,0:T(8,128)(2,1)}, f32[3,256,7]{2,1,0:T(8,128)}) custom-call(s32[4]{0:T(128)} %pad_add_fusion.info_ref, bf16[8,98,896]{2,1,0:T(8,128)(2,1)} %copy-done.1, bf16[3,1024,128]{2,1,0:T(8,128)(2,1)} %k_ref.1, bf16[3,1024,128]{2,1,0:T(8,128)(2,1)} %v_ref.1, bf16[3,32,128]{2,1,0:T(8,128)(2,1)} %sk_ref.1, bf16[3,32,128]{2,1,0:T(8,128)(2,1)} %sv_ref.1), custom_call_target="tpu_custom_call" | custom-call | tf_op jit(solution)/shard_map/pallas_call | solution.py:81
  64.5 1.2 %copy.28 = f32[1,3,8,32,7]{3,2,4,1,0:T(8,128)S(1)} copy(f32[1,3,8,32,7]{4,3,2,1,0:T(8,128)} %bitcast.77) | data formatting | bytes 43008 | tf_op jit(solution)/shard_map/reshape | solution.py:256
  67.7 6.1 %all-to-all-start.1 = ((bf16[8,99,896]{2,1,0:T(8,128)(2,1)}), bf16[8,99,896]{2,1,0:T(8,128)(2,1)S(1)}, u32[]{:S(2)}, u32[]{:S(2)}) async-start(bf16[8,99,896]{2,1,0:T(8,128)(2,1)} %constant_dynamic-update-slice_fusion), calls=%async_computation.1 | async-start | bytes 2981888 | tf_op jit(solution)/shard_map/all_to_all | solution.py:273
  76.2 10.7 %all-reduce.2 = bf16[8,448]{1,0:T(8,128)(2,1)S(1)} all-reduce(f32[8,448]{1,0:T(8,128)S(1)} %fusion.17), channel_id=2, replica_groups=mesh['seq'=8,'tp'=4] {'tp'}, use_global_device_ids=true, to_apply=%region_3.5.clone | all-reduce | flops 3584 | bytes 21504
  87.5 20.1 %all-to-all-done.1.o_ref = bf16[8,99,896]{2,1,0:T(8,128)(2,1)S(1)} async-done(((bf16[8,99,896]{2,1,0:T(8,128)(2,1)}), bf16[8,99,896]{2,1,0:T(8,128)(2,1)S(1)}, u32[]{:S(2)}, u32[]{:S(2)}) %all-to-all-start.1) | async-done | bytes 1419296 | tf_op jit(solution)/shard_map/all_to_all | solution.py:273
  107.7 1.1 reshape.382
  108.7 0.8 fusion.8.lse_ref
  109.6 3.0 %shard_map.150 = bf16[3,32,896]{2,1,0:T(8,128)(2,1)} custom-call(bf16[8,99,896]{2,1,0:T(8,128)(2,1)} %copy-done.2, f32[8,3,32,7]{3,2,1,0:T(8,128)} %fusion.8.lse_ref), custom_call_target="tpu_custom_call" | custom-call | tf_op jit(solution)/shard_map/pallas_call | solution.py:125
  (50 shorter events, 7.0 us)
Async XLA Ops:
  0.6 75.2 %copy-start = (bf16[896,448]{0,1:T(8,128)(2,1)S(1)}, bf16[896,448]{0,1:T(8,128)(2,1)}, u32[]{:S(2)}) copy-start(bf16[896,448]{0,1:T(8,128)(2,1)} %param.23) | copy-start | bytes 2408452
  0.6 18.3 %copy-start.5 = (s32[3]{0:T(128)S(1)}, s32[3]{0:T(128)}, u32[]{:S(2)}) copy-start(s32[3]{0:T(128)} %param.29) | copy-start | bytes 40
  2.4 12.8 %collective-permute-start = (bf16[98,896]{1,0:T(8,128)(2,1)S(1)}, bf16[98,896]{1,0:T(8,128)(2,1)S(1)}, u32[]{:S(2)}, u32[]{:S(2)}) collective-permute-start(bf16[98,896]{1,0:T(8,128)(2,1)S(1)} %get-tuple-element.34), channel_id=1, source_target_pairs={{0,16},{4,20},{8,24},{12,28},{16,0},{20,4},{24,8},{28,12},{1,17},{... | collective-permute-start | bytes 526856 | tf_op jit(solution)/shard_map/ppermute | solution.py:139
  15.2 11.7 %collective-permute-start.2 = (bf16[2,98,896]{2,1,0:T(8,128)(2,1)S(1)}, bf16[2,98,896]{2,1,0:T(8,128)(2,1)S(1)}, u32[]{:S(2)}, u32[]{:S(2)}) collective-permute-start(bf16[2,98,896]{2,1,0:T(8,128)(2,1)S(1)} %get-tuple-element.32), channel_id=1, source_target_pairs={{0,8},{4,12},{8,0},{12,4},{16,24},{20,28},{24,16},{28,20},{1,9},{5... | collective-permute-start | bytes 1053704 | tf_op jit(solution)/shard_map/ppermute | solution.py:144
  16.0 17.9 %collective-permute-start.1 = (bf16[2,98,896]{2,1,0:T(8,128)(2,1)S(1)}, bf16[2,98,896]{2,1,0:T(8,128)(2,1)S(1)}, u32[]{:S(2)}, u32[]{:S(2)}) collective-permute-start(bf16[2,98,896]{2,1,0:T(8,128)(2,1)S(1)} %get-tuple-element.32), channel_id=1, source_target_pairs={{0,4},{4,8},{8,12},{12,0},{16,20},{20,24},{24,28},{28,16},{1,5},{5... | collective-permute-start | bytes 1053704 | tf_op jit(solution)/shard_map/ppermute | solution.py:144
  17.5 18.0 %collective-permute-start.3 = (bf16[2,98,896]{2,1,0:T(8,128)(2,1)S(1)}, bf16[2,98,896]{2,1,0:T(8,128)(2,1)S(1)}, u32[]{:S(2)}, u32[]{:S(2)}) collective-permute-start(bf16[2,98,896]{2,1,0:T(8,128)(2,1)S(1)} %get-tuple-element.32), channel_id=1, source_target_pairs={{0,12},{4,0},{8,4},{12,8},{16,28},{20,16},{24,20},{28,24},{1,13},{... | collective-permute-start | bytes 1053704 | tf_op jit(solution)/shard_map/ppermute | solution.py:144
  39.1 3.0 %copy-start.1 = (bf16[8,98,896]{2,1,0:T(8,128)(2,1)}, bf16[8,98,896]{2,1,0:T(8,128)(2,1)S(1)}, u32[]{:S(2)}) copy-start(bf16[8,98,896]{2,1,0:T(8,128)(2,1)S(1)} %gather_fusion) | copy-start | bytes 4214788
  39.1 2.7 %copy-start.4 = (bf16[1,4096,128]{2,1,0:T(8,128)(2,1)S(1)}, bf16[1,4096,128]{2,1,0:T(8,128)(2,1)}, u32[]{:S(2)}) copy-start(bf16[1,4096,128]{2,1,0:T(8,128)(2,1)} %param.20) | copy-start | bytes 3145732
  44.1 23.6 %all-to-all-start = ((bf16[8,2,448]{2,1,0:T(2,128)(2,1)}), bf16[8,2,448]{2,1,0:T(2,128)(2,1)S(1)}, u32[]{:S(2)}, u32[]{:S(2)}) async-start(bf16[8,2,448]{2,1,0:T(2,128)(2,1)} %reshape.432), calls=%async_computation | async-start | bytes 32768 | tf_op jit(solution)/shard_map/all_to_all | solution.py:217
  67.7 6.1 %copy-start.6 = (u32[32]{0:T(128)S(1)}, u32[32]{0:T(128)}, u32[]{:S(2)}) copy-start(u32[32]{0:T(128)} %constant.192) | copy-start | bytes 388
  67.7 7.4 %copy-start.3 = (s32[8]{0:T(128)S(1)}, s32[8]{0:T(128)}, u32[]{:S(2)}) copy-start(s32[8]{0:T(128)} %param.22) | copy-start | bytes 100
  67.7 39.9 %all-to-all-start.1 = ((bf16[8,99,896]{2,1,0:T(8,128)(2,1)}), bf16[8,99,896]{2,1,0:T(8,128)(2,1)S(1)}, u32[]{:S(2)}, u32[]{:S(2)}) async-start(bf16[8,99,896]{2,1,0:T(8,128)(2,1)} %constant_dynamic-update-slice_fusion), calls=%async_computation.1 | async-start | bytes 2981888 | tf_op jit(solution)/shard_map/all_to_all | solution.py:273
  107.6 2.0 %copy-start.2 = (bf16[8,99,896]{2,1,0:T(8,128)(2,1)}, bf16[8,99,896]{2,1,0:T(8,128)(2,1)S(1)}, u32[]{:S(2)}) copy-start(bf16[8,99,896]{2,1,0:T(8,128)(2,1)S(1)} %all-to-all-done.1.o_ref) | copy-start | bytes 4257796

commit v13 on v12

--- a/solution.py
+++ b/solution.py
@@ -23,9 +23,27 @@
 
 
 def _prefill_kernel(
-    info_ref, q_ref, k_ref, v_ref, sk_ref, sv_ref, o_ref, lse_ref, *, group_size, head_size, local_tok
+    info_ref, order_ref, q_hbm, k_ref, v_ref, sk_ref, sv_ref, o_ref, lse_ref, q_ref, sems,
+    *, group_size, head_size, local_tok
 ):
     c = pl.program_id(0)
+    stretch_count, src_count, tok_block, _ = q_ref.shape
+
+    def query_copy(stretch, src):
+        return pltpu.make_async_copy(
+            q_hbm.at[order_ref[src], pl.ds(stretch * tok_block, tok_block)],
+            q_ref.at[stretch, src],
+            sems.at[stretch, src],
+        )
+
+    @pl.when(c == 0)
+    def _():
+        for stretch in range(stretch_count):
+            for src in range(src_count):
+                query_copy(stretch, src).start()
+
+    for src in range(src_count):
+        query_copy(c, src).wait()
     limit = info_ref[c]
     key_offset = info_ref[info_ref.shape[0] - 1]
     keys = k_ref[0]
@@ -33,7 +51,6 @@
     own_keys = sk_ref[0]
     own_values = sv_ref[0]
     factor = 1.0 / math.sqrt(head_size)
-    src_count, tok_block, _ = q_ref.shape
     tokens = src_count * tok_block
     col = lax.broadcasted_iota(jnp.int32, (1, keys.shape[0]), 1)
     visible = col < limit
@@ -43,7 +60,7 @@
     causal = key_token <= query_token
     dims = (((1,), (1,)), ((), ()))
     for h in range(group_size):
-        q = q_ref[:, :, h * head_size : (h + 1) * head_size].reshape(tokens, head_size)
+        q = q_ref[c, :, :, h * head_size : (h + 1) * head_size].reshape(tokens, head_size)
         s = lax.dot_general(q, keys, dims, preferred_element_type=jnp.float32) * factor
         s = jnp.where(visible, s, NEG_FILL)
         s_own = lax.dot_general(q, own_keys, dims, preferred_element_type=jnp.float32) * factor
@@ -69,9 +86,11 @@
 
 
 def prefill_partial(
-    info, queries, keys, values, own_keys, own_values, group_size, tok_block, local_tok, out_rows
+    info, order, queries, keys, values, own_keys, own_values, group_size, tok_block, local_tok,
+    out_rows,
 ):
-    src_count, _, qw = queries.shape
+    src_count = order.shape[0]
+    qw = queries.shape[2]
     n, p, hd = keys.shape
     own = own_keys.shape[1]
     tokens = src_count * tok_block
@@ -81,25 +100,29 @@
     return pl.pallas_call(
         kern,
         grid_spec=pltpu.PrefetchScalarGridSpec(
-            num_scalar_prefetch=1,
+            num_scalar_prefetch=2,
             grid=(n,),
             in_specs=[
-                pl.BlockSpec((src_count, tok_block, qw), lambda c, info: (0, c, 0)),
-                pl.BlockSpec((1, p, hd), lambda c, info: (c, 0, 0)),
-                pl.BlockSpec((1, p, hd), lambda c, info: (c, 0, 0)),
-                pl.BlockSpec((1, own, hd), lambda c, info: (c, 0, 0)),
-                pl.BlockSpec((1, own, hd), lambda c, info: (c, 0, 0)),
+                pl.BlockSpec(memory_space=pl.ANY),
+                pl.BlockSpec((1, p, hd), lambda c, info, order: (c, 0, 0)),
+                pl.BlockSpec((1, p, hd), lambda c, info, order: (c, 0, 0)),
+                pl.BlockSpec((1, own, hd), lambda c, info, order: (c, 0, 0)),
+                pl.BlockSpec((1, own, hd), lambda c, info, order: (c, 0, 0)),
             ],
             out_specs=[
-                pl.BlockSpec((src_count, tok_block, qw), lambda c, info: (0, c, 0)),
-                pl.BlockSpec((1, tokens, group_size), lambda c, info: (c, 0, 0)),
+                pl.BlockSpec((src_count, tok_block, qw), lambda c, info, order: (0, c, 0)),
+                pl.BlockSpec((1, tokens, group_size), lambda c, info, order: (c, 0, 0)),
+            ],
+            scratch_shapes=[
+                pltpu.VMEM((n, src_count, tok_block, qw), jnp.bfloat16),
+                pltpu.SemaphoreType.DMA((n, src_count)),
             ],
         ),
         out_shape=[
             jax.ShapeDtypeStruct((src_count, out_rows, qw), jnp.bfloat16),
             jax.ShapeDtypeStruct((n, tokens, group_size), jnp.float32),
         ],
-    )(info, queries, keys, values, own_keys, own_values)
+    )(info, order, queries, keys, values, own_keys, own_values)
 
 
 def _combine_kernel(o_ref, lse_ref, out_ref, *, group_size, head_size):
@@ -132,9 +155,10 @@
 
 def broadcast_over_seq(pack, seq_rank, seq_count):
     if seq_count > 16 or seq_count % 2:
-        return lax.all_to_all(
+        every = lax.all_to_all(
             jnp.broadcast_to(pack[None], (seq_count,) + pack.shape), "seq", 0, 0, tiled=True
         )
+        return every, jnp.arange(seq_count, dtype=jnp.int32)
     half = seq_count // 2
     partner = lax.ppermute(pack, "seq", [(i, (i + half) % seq_count) for i in range(seq_count)])
     pair = jnp.stack([pack, partner])
@@ -147,7 +171,7 @@
     far = (sources // half) != (seq_rank // half)
     near = jnp.where(far, (sources + half) % seq_count, sources)
     shift_of = (seq_rank % half - near % half) % half
-    return jnp.take(every, shift_of * 2 + far.astype(jnp.int32), axis=0, mode="clip")
+    return every, (shift_of * 2 + far.astype(jnp.int32)).astype(jnp.int32)
 
 
 def body(
@@ -181,11 +205,10 @@
     pack = jnp.concatenate(
         [stretch_query.reshape(stretch_rows, query_width), new_query, decode_kv], axis=0
     )
-    gathered = broadcast_over_seq(pack, seq_rank, seq_count)
-    every_query = gathered[:, stretch_rows : stretch_rows + local_dec, :].reshape(
-        total_dec, query_width
-    )
-    every_kv = gathered[:, stretch_rows + local_dec :, :].reshape(total_dec, query_width)
+    every, order = broadcast_over_seq(pack, seq_rank, seq_count)
+    decode_rows = jnp.take(every[:, stretch_rows:, :], order, axis=0)
+    every_query = decode_rows[:, :local_dec, :].reshape(total_dec, query_width)
+    every_kv = decode_rows[:, local_dec:, :].reshape(total_dec, query_width)
     every_key = every_kv[:, :key_width]
     every_value = every_kv[:, key_width : 2 * key_width]
     slot_ids = seq_rank * local_dec + jnp.arange(local_dec, dtype=jnp.int32)
@@ -232,19 +255,19 @@
     info = jnp.concatenate([limits, (seq_rank * local_tok).astype(jnp.int32)[None]])
     if direct:
         payload, part_lse = prefill_partial(
-            info, gathered, prior_keys, prior_values, stretch_key, stretch_value, group_size,
+            info, order, every, prior_keys, prior_values, stretch_key, stretch_value, group_size,
             local_tok, local_tok, out_rows + stat_rows,
         )
     else:
         token_count = seq_count * local_tok
         queries_all = (
-            gathered[:, :stretch_rows, :]
+            jnp.take(every, order, axis=0)[:, :stretch_rows, :]
             .reshape(seq_count, stretch_count, local_tok, query_width)
             .transpose(1, 0, 2, 3)
             .reshape(1, stretch_rows * seq_count, query_width)
         )
         flat_out, part_lse = prefill_partial(
-            info, queries_all, prior_keys, prior_values, stretch_key, stretch_value, group_size,
+            info, jnp.zeros((1,), jnp.int32), queries_all, prior_keys, prior_values, stretch_key, stretch_value, group_size,
             token_count, token_count, stretch_rows * seq_count,
         )
         payload = jnp.pad(

time: 113 us -> 110 us (0.973)
  matrix products: 2.98 us -> 1.13 us
  waiting for transfers between devices: 40.7 us -> 39.4 us
  local copies, waits for them, and re-layouts: 9.57 us -> 8.34 us
    dot_general x1, matrix products: 2.33 us -> 0.49 us  [partial_attend(): jnp.dot(queries, keys.T, preferred_element_type=jnp.float32) * factor]
    gather x1, local copies, waits for them, and re-layouts: 2.19 us -> 0.61 us  [body(): decode_rows = jnp.take(every[:, stretch_rows:, :], order, axis=0)]
    ppermute x1, waiting for transfers between devices: 6.7 us -> 5.37 us  [broadcast_over_seq(): lax.ppermute(pack, 'seq', [(i, (i + half) % seq_count) for i in range(seq...]
  transfers between devices with their start and end apart: 6 -> 6, of which waited for: 5 -> 5; matrix products, arithmetic and copies ran while one was open for 7% -> 8% of each run, Pallas kernels for 14% -> 15%
where the time goes in v13:
time: 110 us
  waiting for transfers between devices  39.4 us (36%)
  Pallas kernels  19.8 us (18%)
  starting transfers between devices  18.6 us (17%)
  blocking collectives  10.7 us (10%)
  local copies, waits for them, and re-layouts  8.34 us (8%)
  other arithmetic  7.39 us (7%)
  between operations  4.13 us (4%)
  matrix products  1.13 us (1%)
    all_to_all x1, waiting for transfers between devices, body(): received = lax.all_to_all(payload, 'seq', 0, 0, tiled=True)  20.1 us
    pallas_call x1, Pallas kernels, prefill_partial(): pl.pallas_call(kern, grid_spec=pltpu.PrefetchScalarGridSpec(num_scalar_pr...  16.8 us
    ppermute x3, waiting for transfers between devices, broadcast_over_seq(): pieces.append(lax.ppermute(pair, 'seq', perm))  13.9 us
    unnamed x1, blocking collectives  10.7 us
    all_to_all x1, starting transfers between devices, body(): received = lax.all_to_all(payload, 'seq', 0, 0, tiled=True)  6.12 us
    ppermute x1, waiting for transfers between devices, broadcast_over_seq(): lax.ppermute(pack, 'seq', [(i, (i + half) % seq_count) for i in range(seq...  5.37 us
    all_to_all x1, starting transfers between devices, body(): lax.all_to_all(jnp.broadcast_to(home_out[None], (seq_count,) + home_out.s...  4.66 us
    ppermute x1, starting transfers between devices, broadcast_over_seq(): lax.ppermute(pack, 'seq', [(i, (i + half) % seq_count) for i in range(seq...  4.1 us
  transfers between devices with their start and end apart: 6, of which 5 were waited for; matrix products, arithmetic and copies ran while one was open for 8% of the time, Pallas kernels for 15%

profile of v13, /device:TPU:0, one launch (start us, length us, event | category | flops | bytes accessed | tf_op | source)
XLA Modules:
  0.0 109.6 jit_solution(2410099273852627960)
XLA Ops:
  0.7 0.8 fusion.22
  1.4 1.0 fusion.44
  2.4 4.1 %collective-permute-start = (bf16[98,896]{1,0:T(8,128)(2,1)S(1)}, bf16[98,896]{1,0:T(8,128)(2,1)S(1)}, u32[]{:S(2)}, u32[]{:S(2)}) collective-permute-start(bf16[98,896]{1,0:T(8,128)(2,1)S(1)} %get-tuple-element.34), channel_id=1, source_target_pairs={{0,16},{4,20},{8,24},{12,28},{16,0},{20,4},{24,8},{28,12},{1,17},{... | collective-permute-start | bytes 526856 | tf_op jit(solution)/shard_map/ppermute | solution.py:163
  7.2 0.7 subtract_clamp_fusion
  8.5 1.3 %compare_select_fusion.4 = (s32[8]{0:T(128)S(1)}, s32[]{:T(128)}) fusion(s32[8]{0:T(128)} %param.22, s32[]{:T(128)S(6)} %axis_index.15), kind=kLoop, calls=%fused_computation.55 | loop fusion | flops 47 | bytes 72 | tf_op jit(solution)/shard_map/jit(_take)/jit(_where)/select_n | solution.py:243
  9.8 5.4 %collective-permute-done = bf16[98,896]{1,0:T(8,128)(2,1)S(1)} collective-permute-done((bf16[98,896]{1,0:T(8,128)(2,1)S(1)}, bf16[98,896]{1,0:T(8,128)(2,1)S(1)}, u32[]{:S(2)}, u32[]{:S(2)}) %collective-permute-start) | collective-permute-done | bytes 175648 | tf_op jit(solution)/shard_map/ppermute | solution.py:163
  15.2 0.8 collective-permute-start.2
  16.0 1.5 %collective-permute-start.1 = (bf16[2,98,896]{2,1,0:T(8,128)(2,1)S(1)}, bf16[2,98,896]{2,1,0:T(8,128)(2,1)S(1)}, u32[]{:S(2)}, u32[]{:S(2)}) collective-permute-start(bf16[2,98,896]{2,1,0:T(8,128)(2,1)S(1)} %get-tuple-element.32), channel_id=1, source_target_pairs={{0,4},{4,8},{8,12},{12,0},{16,20},{20,24},{24,28},{28,16},{1,5},{5... | collective-permute-start | bytes 1053704 | tf_op jit(solution)/shard_map/ppermute | solution.py:168
  17.5 1.4 %collective-permute-start.3 = (bf16[2,98,896]{2,1,0:T(8,128)(2,1)S(1)}, bf16[2,98,896]{2,1,0:T(8,128)(2,1)S(1)}, u32[]{:S(2)}, u32[]{:S(2)}) collective-permute-start(bf16[2,98,896]{2,1,0:T(8,128)(2,1)S(1)} %get-tuple-element.32), channel_id=1, source_target_pairs={{0,12},{4,0},{8,4},{12,8},{16,28},{20,16},{24,20},{28,24},{1,13},{... | collective-permute-start | bytes 1053704 | tf_op jit(solution)/shard_map/ppermute | solution.py:168
  21.6 5.3 %collective-permute-done.2 = bf16[2,98,896]{2,1,0:T(8,128)(2,1)S(1)} collective-permute-done((bf16[2,98,896]{2,1,0:T(8,128)(2,1)S(1)}, bf16[2,98,896]{2,1,0:T(8,128)(2,1)S(1)}, u32[]{:S(2)}, u32[]{:S(2)}) %collective-permute-start.2) | collective-permute-done | bytes 351264 | tf_op jit(solution)/shard_map/ppermute | solution.py:168
  26.9 7.1 %collective-permute-done.1 = bf16[2,98,896]{2,1,0:T(8,128)(2,1)S(1)} collective-permute-done((bf16[2,98,896]{2,1,0:T(8,128)(2,1)S(1)}, bf16[2,98,896]{2,1,0:T(8,128)(2,1)S(1)}, u32[]{:S(2)}, u32[]{:S(2)}) %collective-permute-start.1) | collective-permute-done | bytes 351264 | tf_op jit(solution)/shard_map/ppermute | solution.py:168
  34.0 1.6 %collective-permute-done.3 = bf16[2,98,896]{2,1,0:T(8,128)(2,1)S(1)} collective-permute-done((bf16[2,98,896]{2,1,0:T(8,128)(2,1)S(1)}, bf16[2,98,896]{2,1,0:T(8,128)(2,1)S(1)}, u32[]{:S(2)}, u32[]{:S(2)}) %collective-permute-start.3) | collective-permute-done | bytes 351264 | tf_op jit(solution)/shard_map/ppermute | solution.py:168
  38.6 0.7 reduce.10
  39.4 0.7 reshape.446
  40.0 4.7 %all-to-all-start = ((bf16[8,2,448]{2,1,0:T(2,128)(2,1)}), bf16[8,2,448]{2,1,0:T(2,128)(2,1)S(1)}, u32[]{:S(2)}, u32[]{:S(2)}) async-start(bf16[8,2,448]{2,1,0:T(2,128)(2,1)} %reshape.446), calls=%async_computation | async-start | bytes 32768 | tf_op jit(solution)/shard_map/all_to_all | solution.py:240
  44.7 16.8 %shard_map.149 = (bf16[8,99,896]{2,1,0:T(8,128)(2,1)}, f32[3,256,7]{2,1,0:T(8,128)}) custom-call(s32[4]{0:T(128)} %pad_add_fusion.info_ref, s32[8]{0:T(128)} %get-tuple-element.30.order_ref, bf16[8,98,896]{2,1,0:T(8,128)(2,1)} %bitcast.76, bf16[3,1024,128]{2,1,0:T(8,128)(2,1)} %k_ref.1, bf16[3,1024,128]{2,1,0:T(8,128)(2,1)} %v_ref.1, ...), custom_call_target="tpu_custom_call" | custom-call | tf_op jit(solution)/shard_map/pallas_call | solution.py:100
  61.5 1.2 %copy.28 = f32[1,3,8,32,7]{3,2,4,1,0:T(8,128)S(1)} copy(f32[1,3,8,32,7]{4,3,2,1,0:T(8,128)} %bitcast.78) | data formatting | bytes 43008 | tf_op jit(solution)/shard_map/reshape | solution.py:279
  64.0 0.7 constant_dynamic-update-slice_fusion
  64.7 6.1 %all-to-all-start.1 = ((bf16[8,99,896]{2,1,0:T(8,128)(2,1)}), bf16[8,99,896]{2,1,0:T(8,128)(2,1)S(1)}, u32[]{:S(2)}, u32[]{:S(2)}) async-start(bf16[8,99,896]{2,1,0:T(8,128)(2,1)} %constant_dynamic-update-slice_fusion), calls=%async_computation.1 | async-start | bytes 2981888 | tf_op jit(solution)/shard_map/all_to_all | solution.py:296
  73.1 10.7 %all-reduce.2 = bf16[8,448]{1,0:T(8,128)(2,1)S(1)} all-reduce(f32[8,448]{1,0:T(8,128)S(1)} %fusion.17), channel_id=2, replica_groups=mesh['seq'=8,'tp'=4] {'tp'}, use_global_device_ids=true, to_apply=%region_3.5.clone | all-reduce | flops 3584 | bytes 21504
  84.5 20.1 %all-to-all-done.1.o_ref = bf16[8,99,896]{2,1,0:T(8,128)(2,1)S(1)} async-done(((bf16[8,99,896]{2,1,0:T(8,128)(2,1)}), bf16[8,99,896]{2,1,0:T(8,128)(2,1)S(1)}, u32[]{:S(2)}, u32[]{:S(2)}) %all-to-all-start.1) | async-done | bytes 1419296 | tf_op jit(solution)/shard_map/all_to_all | solution.py:296
  104.7 1.1 reshape.396
  105.7 0.8 fusion.8.lse_ref
  106.6 3.0 %shard_map.150 = bf16[3,32,896]{2,1,0:T(8,128)(2,1)} custom-call(bf16[8,99,896]{2,1,0:T(8,128)(2,1)} %copy-done.1, f32[8,3,32,7]{3,2,1,0:T(8,128)} %fusion.8.lse_ref), custom_call_target="tpu_custom_call" | custom-call | tf_op jit(solution)/shard_map/pallas_call | solution.py:148
  (53 shorter events, 8.0 us)
Async XLA Ops:
  0.6 72.2 %copy-start = (bf16[896,448]{0,1:T(8,128)(2,1)S(1)}, bf16[896,448]{0,1:T(8,128)(2,1)}, u32[]{:S(2)}) copy-start(bf16[896,448]{0,1:T(8,128)(2,1)} %param.23) | copy-start | bytes 2408452
  0.6 20.3 %copy-start.3 = (s32[8]{0:T(128)S(1)}, s32[8]{0:T(128)}, u32[]{:S(2)}) copy-start(s32[8]{0:T(128)} %param.22) | copy-start | bytes 100
  2.4 12.8 %collective-permute-start = (bf16[98,896]{1,0:T(8,128)(2,1)S(1)}, bf16[98,896]{1,0:T(8,128)(2,1)S(1)}, u32[]{:S(2)}, u32[]{:S(2)}) collective-permute-start(bf16[98,896]{1,0:T(8,128)(2,1)S(1)} %get-tuple-element.34), channel_id=1, source_target_pairs={{0,16},{4,20},{8,24},{12,28},{16,0},{20,4},{24,8},{28,12},{1,17},{... | collective-permute-start | bytes 526856 | tf_op jit(solution)/shard_map/ppermute | solution.py:163
  15.2 11.7 %collective-permute-start.2 = (bf16[2,98,896]{2,1,0:T(8,128)(2,1)S(1)}, bf16[2,98,896]{2,1,0:T(8,128)(2,1)S(1)}, u32[]{:S(2)}, u32[]{:S(2)}) collective-permute-start(bf16[2,98,896]{2,1,0:T(8,128)(2,1)S(1)} %get-tuple-element.32), channel_id=1, source_target_pairs={{0,8},{4,12},{8,0},{12,4},{16,24},{20,28},{24,16},{28,20},{1,9},{5... | collective-permute-start | bytes 1053704 | tf_op jit(solution)/shard_map/ppermute | solution.py:168
  16.0 17.9 %collective-permute-start.1 = (bf16[2,98,896]{2,1,0:T(8,128)(2,1)S(1)}, bf16[2,98,896]{2,1,0:T(8,128)(2,1)S(1)}, u32[]{:S(2)}, u32[]{:S(2)}) collective-permute-start(bf16[2,98,896]{2,1,0:T(8,128)(2,1)S(1)} %get-tuple-element.32), channel_id=1, source_target_pairs={{0,4},{4,8},{8,12},{12,0},{16,20},{20,24},{24,28},{28,16},{1,5},{5... | collective-permute-start | bytes 1053704 | tf_op jit(solution)/shard_map/ppermute | solution.py:168
  17.5 18.0 %collective-permute-start.3 = (bf16[2,98,896]{2,1,0:T(8,128)(2,1)S(1)}, bf16[2,98,896]{2,1,0:T(8,128)(2,1)S(1)}, u32[]{:S(2)}, u32[]{:S(2)}) collective-permute-start(bf16[2,98,896]{2,1,0:T(8,128)(2,1)S(1)} %get-tuple-element.32), channel_id=1, source_target_pairs={{0,12},{4,0},{8,4},{12,8},{16,28},{20,16},{24,20},{28,24},{1,13},{... | collective-permute-start | bytes 1053704 | tf_op jit(solution)/shard_map/ppermute | solution.py:168
  35.6 1.4 %copy-start.4 = (bf16[1,4096,128]{2,1,0:T(8,128)(2,1)S(1)}, bf16[1,4096,128]{2,1,0:T(8,128)(2,1)}, u32[]{:S(2)}) copy-start(bf16[1,4096,128]{2,1,0:T(8,128)(2,1)} %param.19) | copy-start | bytes 3145732
  35.8 2.3 %copy-start.2 = (bf16[4,2,98,896]{3,2,1,0:T(8,128)(2,1)}, bf16[4,2,98,896]{3,2,1,0:T(8,128)(2,1)S(1)}, u32[]{:S(2)}) copy-start(bf16[4,2,98,896]{3,2,1,0:T(8,128)(2,1)S(1)} %pad_maximum_fusion) | copy-start | bytes 4214788
  36.5 1.3 %copy-start.5 = (bf16[1,4096,128]{2,1,0:T(8,128)(2,1)S(1)}, bf16[1,4096,128]{2,1,0:T(8,128)(2,1)}, u32[]{:S(2)}) copy-start(bf16[1,4096,128]{2,1,0:T(8,128)(2,1)} %param.20) | copy-start | bytes 3145732
  40.0 24.7 %all-to-all-start = ((bf16[8,2,448]{2,1,0:T(2,128)(2,1)}), bf16[8,2,448]{2,1,0:T(2,128)(2,1)S(1)}, u32[]{:S(2)}, u32[]{:S(2)}) async-start(bf16[8,2,448]{2,1,0:T(2,128)(2,1)} %reshape.446), calls=%async_computation | async-start | bytes 32768 | tf_op jit(solution)/shard_map/all_to_all | solution.py:240
  64.7 6.1 %copy-start.6 = (u32[32]{0:T(128)S(1)}, u32[32]{0:T(128)}, u32[]{:S(2)}) copy-start(u32[32]{0:T(128)} %constant.214) | copy-start | bytes 388
  64.7 39.9 %all-to-all-start.1 = ((bf16[8,99,896]{2,1,0:T(8,128)(2,1)}), bf16[8,99,896]{2,1,0:T(8,128)(2,1)S(1)}, u32[]{:S(2)}, u32[]{:S(2)}) async-start(bf16[8,99,896]{2,1,0:T(8,128)(2,1)} %constant_dynamic-update-slice_fusion), calls=%async_computation.1 | async-start | bytes 2981888 | tf_op jit(solution)/shard_map/all_to_all | solution.py:296
  104.6 2.0 %copy-start.1 = (bf16[8,99,896]{2,1,0:T(8,128)(2,1)}, bf16[8,99,896]{2,1,0:T(8,128)(2,1)S(1)}, u32[]{:S(2)}) copy-start(bf16[8,99,896]{2,1,0:T(8,128)(2,1)S(1)} %all-to-all-done.1.o_ref) | copy-start | bytes 4257796

commit v14 on v13

--- a/solution.py
+++ b/solution.py
@@ -161,17 +161,23 @@
         return every, jnp.arange(seq_count, dtype=jnp.int32)
     half = seq_count // 2
     partner = lax.ppermute(pack, "seq", [(i, (i + half) % seq_count) for i in range(seq_count)])
-    pair = jnp.stack([pack, partner])
-    pieces = [pair]
-    for shift in range(1, half):
-        perm = [(i, (i // half) * half + (i % half + shift) % half) for i in range(seq_count)]
-        pieces.append(lax.ppermute(pair, "seq", perm))
-    every = jnp.stack(pieces).reshape((2 * half,) + pack.shape)
+    perms = [
+        [(i, (i // half) * half + (i % half + shift) % half) for i in range(seq_count)]
+        for shift in range(1, half)
+    ]
+    near_pieces = [lax.ppermute(pack, "seq", perm) for perm in perms]
+    far_pieces = [lax.ppermute(partner, "seq", perm) for perm in perms]
+    every = jnp.stack([pack, partner] + near_pieces + far_pieces)
     sources = jnp.arange(seq_count, dtype=jnp.int32)
     far = (sources // half) != (seq_rank // half)
     near = jnp.where(far, (sources + half) % seq_count, sources)
     shift_of = (seq_rank % half - near % half) % half
-    return every, (shift_of * 2 + far.astype(jnp.int32)).astype(jnp.int32)
+    order = jnp.where(
+        far,
+        jnp.where(shift_of == 0, 1, half + shift_of),
+        jnp.where(shift_of == 0, 0, 1 + shift_of),
+    )
+    return every, order.astype(jnp.int32)
 
 
 def body(

time: 110 us -> 106 us (0.964)
  waiting for transfers between devices: 39.4 us -> 27.6 us
  starting transfers between devices: 18.6 us -> 23.2 us
  matrix products: 1.13 us -> 3.58 us
    ppermute x3 -> x6, waiting for transfers between devices: 13.9 us -> 6.79 us  [the longest x3 6.78 us: broadcast_over_seq(): far_pieces = [lax.ppermute(partner, 'seq', perm) for perm in perms]]
    ppermute x1, waiting for transfers between devices: 5.37 us -> 0.01 us  [broadcast_over_seq(): lax.ppermute(pack, 'seq', [(i, (i + half) % seq_count) for i in range(seq...]
    ppermute x3 -> x6, starting transfers between devices: 3.71 us -> 7.98 us  [the longest x3 4.5 us: broadcast_over_seq(): near_pieces = [lax.ppermute(pack, 'seq', perm) for perm in perms]]
    another operation x4 -> x1, other arithmetic: 1.3 us -> 0.04 us  [the longest x1 0.96 us: broadcast_over_seq(): pair = jnp.stack([pack, partner])]
    dot_general x1, matrix products: 0.49 us -> 1.72 us  [partial_attend(): jnp.dot(queries, keys.T, preferred_element_type=jnp.float32) * factor]
    dot_general x1, matrix products: 0.31 us -> 1.53 us  [partial_attend(): jnp.dot(weights.astype(jnp.bfloat16), values, preferred_element_type=jnp....]
  transfers between devices with their start and end apart: 6 -> 9, of which waited for: 5 -> 3; matrix products, arithmetic and copies ran while one was open for 8% -> 9% of each run, Pallas kernels for 15% -> 16%
where the time goes in v14:
time: 106 us; the launch traced here: 105 us
  waiting for transfers between devices  27.6 us (26%)
  starting transfers between devices  23.2 us (22%)
  Pallas kernels  19.8 us (19%)
  blocking collectives  10.7 us (10%)
  local copies, waits for them, and re-layouts  8.17 us (8%)
  other arithmetic  8.04 us (8%)
  between operations  4.15 us (4%)
  matrix products  3.58 us (3%)
    all_to_all x1, waiting for transfers between devices, body(): received = lax.all_to_all(payload, 'seq', 0, 0, tiled=True)  20.8 us
    pallas_call x1, Pallas kernels, prefill_partial(): pl.pallas_call(kern, grid_spec=pltpu.PrefetchScalarGridSpec(num_scalar_pr...  16.8 us
    unnamed x1, blocking collectives  10.7 us
    ppermute x3, waiting for transfers between devices, broadcast_over_seq(): far_pieces = [lax.ppermute(partner, 'seq', perm) for perm in perms]  6.78 us
    all_to_all x1, starting transfers between devices, body(): received = lax.all_to_all(payload, 'seq', 0, 0, tiled=True)  6.13 us
    all_to_all x1, starting transfers between devices, body(): lax.all_to_all(jnp.broadcast_to(home_out[None], (seq_count,) + home_out.s...  4.95 us
    ppermute x3, starting transfers between devices, broadcast_over_seq(): near_pieces = [lax.ppermute(pack, 'seq', perm) for perm in perms]  4.5 us
    ppermute x1, starting transfers between devices, broadcast_over_seq(): lax.ppermute(pack, 'seq', [(i, (i + half) % seq_count) for i in range(seq...  4.1 us
  transfers between devices with their start and end apart: 9, of which 3 were waited for; matrix products, arithmetic and copies ran while one was open for 9% of the time, Pallas kernels for 16%

profile of v14, /device:TPU:0, one launch (start us, length us, event | category | flops | bytes accessed | tf_op | source)
XLA Modules:
  0.0 105.3 jit_solution(238697874602583252)
XLA Ops:
  0.6 0.8 fusion.22
  1.4 1.0 pad_maximum_fusion
  2.4 4.1 %collective-permute-start = (bf16[98,896]{1,0:T(8,128)(2,1)S(1)}, bf16[98,896]{1,0:T(8,128)(2,1)S(1)}, u32[]{:S(2)}, u32[]{:S(2)}) collective-permute-start(bf16[98,896]{1,0:T(8,128)(2,1)S(1)} %pad_maximum_fusion), channel_id=1, source_target_pairs={{0,16},{4,20},{8,24},{12,28},{16,0},{20,4},{24,8},{28,12},{1,17},{... | collective-permute-start | bytes 526856 | tf_op jit(solution)/shard_map/ppermute | solution.py:163
  6.5 1.5 %collective-permute-start.1 = (bf16[98,896]{1,0:T(8,128)(2,1)S(1)}, bf16[98,896]{1,0:T(8,128)(2,1)S(1)}, u32[]{:S(2)}, u32[]{:S(2)}) collective-permute-start(bf16[98,896]{1,0:T(8,128)(2,1)S(1)} %pad_maximum_fusion), channel_id=1, source_target_pairs={{0,4},{4,8},{8,12},{12,0},{16,20},{20,24},{24,28},{28,16},{1,5},{5... | collective-permute-start | bytes 526856 | tf_op jit(solution)/shard_map/ppermute | solution.py:168
  8.0 1.6 %collective-permute-start.2 = (bf16[98,896]{1,0:T(8,128)(2,1)S(1)}, bf16[98,896]{1,0:T(8,128)(2,1)S(1)}, u32[]{:S(2)}, u32[]{:S(2)}) collective-permute-start(bf16[98,896]{1,0:T(8,128)(2,1)S(1)} %pad_maximum_fusion), channel_id=1, source_target_pairs={{0,8},{4,12},{8,0},{12,4},{16,24},{20,28},{24,16},{28,20},{1,9},{5... | collective-permute-start | bytes 526856 | tf_op jit(solution)/shard_map/ppermute | solution.py:168
  9.6 1.4 %collective-permute-start.3 = (bf16[98,896]{1,0:T(8,128)(2,1)S(1)}, bf16[98,896]{1,0:T(8,128)(2,1)S(1)}, u32[]{:S(2)}, u32[]{:S(2)}) collective-permute-start(bf16[98,896]{1,0:T(8,128)(2,1)S(1)} %pad_maximum_fusion), channel_id=1, source_target_pairs={{0,12},{4,0},{8,4},{12,8},{16,28},{20,16},{24,20},{28,24},{1,13},{... | collective-permute-start | bytes 526856 | tf_op jit(solution)/shard_map/ppermute | solution.py:168
  11.6 1.3 %compare_select_fusion.4 = (s32[8]{0:T(128)S(1)}, s32[]{:T(128)}) fusion(s32[8]{0:T(128)} %param.22, s32[]{:T(128)S(6)} %axis_index.15), kind=kLoop, calls=%fused_computation.61 | loop fusion | flops 47 | bytes 72 | tf_op jit(solution)/shard_map/jit(_take)/jit(_where)/select_n | solution.py:249
  16.9 1.0 bitcast_dynamic-update-slice_fusion.7
  19.1 2.4 %collective-permute-start.6 = (bf16[98,896]{1,0:T(8,128)(2,1)S(1)}, bf16[98,896]{1,0:T(8,128)(2,1)S(1)}, u32[]{:S(2)}, u32[]{:S(2)}) collective-permute-start(bf16[98,896]{1,0:T(8,128)(2,1)S(1)} %collective-permute-done), channel_id=1, source_target_pairs={{0,12},{4,0},{8,4},{12,8},{16,28},{20,16},{24,20},{28,24},{1,13},{... | collective-permute-start | bytes 526856 | tf_op jit(solution)/shard_map/ppermute | solution.py:169
  21.5 4.9 %collective-permute-done.4 = bf16[98,896]{1,0:T(8,128)(2,1)S(1)} collective-permute-done((bf16[98,896]{1,0:T(8,128)(2,1)S(1)}, bf16[98,896]{1,0:T(8,128)(2,1)S(1)}, u32[]{:S(2)}, u32[]{:S(2)}) %collective-permute-start.4) | collective-permute-done | bytes 175648 | tf_op jit(solution)/shard_map/ppermute | solution.py:169
  26.5 1.9 %collective-permute-done.6 = bf16[98,896]{1,0:T(8,128)(2,1)S(1)} collective-permute-done((bf16[98,896]{1,0:T(8,128)(2,1)S(1)}, bf16[98,896]{1,0:T(8,128)(2,1)S(1)}, u32[]{:S(2)}, u32[]{:S(2)}) %collective-permute-start.6) | collective-permute-done | bytes 175648 | tf_op jit(solution)/shard_map/ppermute | solution.py:169
  29.3 1.7 %fusion.42 = (f32[7]{0:T(128)S(1)}, f32[7,4097]{1,0:T(8,128)S(1)}) fusion(bf16[1,1,128]{2,1,0:T(2,128)(2,1)S(1)} %get-tuple-element.42, bf16[1,4096,128]{2,1,0:T(8,128)(2,1)} %param.19, bf16[896]{0:T(1024)(128)(2,1)S(1)} %fusion.21, pred[4097]{0:T(1024)(128)(4,1)S(1)} %add_reduce_fusion), kind=kOutput, calls=%fused_computation.125 | convolution fusion | flops 9525518 | bytes 1169465 | tf_op jit(solution)/shard_map/vmap()/dot_general | solution.py:16
  31.2 1.5 %fusion.2 = bf16[896]{0:T(1024)(128)(2,1)S(1)} fusion(bf16[1,1,128]{2,1,0:T(2,128)(2,1)S(1)} %get-tuple-element.43, bf16[1,4096,128]{2,1,0:T(8,128)(2,1)} %param.20, f32[7,4097]{1,0:T(8,128)S(1)} %get-tuple-element.41, f32[7]{0:T(128)S(1)} %get-tuple-element.40, pred[4097]{0:T(1024)(128)(4,1)S(1)} %add_reduce_fusion, f32[7]{0:T(128)S(1)} %fusion.10), kind=kOutput, calls=%fused_computation.6 | convolution fusion | flops 9527317 | bytes 1169493 | tf_op jit(solution)/shard_map/vmap()/dot_general | solution.py:21
  33.3 0.7 reduce.10
  34.0 0.7 reshape.451
  34.7 5.0 %all-to-all-start = ((bf16[8,2,448]{2,1,0:T(2,128)(2,1)}), bf16[8,2,448]{2,1,0:T(2,128)(2,1)S(1)}, u32[]{:S(2)}, u32[]{:S(2)}) async-start(bf16[8,2,448]{2,1,0:T(2,128)(2,1)} %reshape.451), calls=%async_computation | async-start | bytes 32768 | tf_op jit(solution)/shard_map/all_to_all | solution.py:246
  39.7 16.8 %shard_map.149 = (bf16[8,99,896]{2,1,0:T(8,128)(2,1)}, f32[3,256,7]{2,1,0:T(8,128)}) custom-call(s32[4]{0:T(128)} %pad_add_fusion.info_ref, s32[8]{0:T(128)} %get-tuple-element.30.order_ref, bf16[8,98,896]{2,1,0:T(8,128)(2,1)} %copy-done.2, bf16[3,1024,128]{2,1,0:T(8,128)(2,1)} %k_ref.1, bf16[3,1024,128]{2,1,0:T(8,128)(2,1)} %v_ref.1, ...), custom_call_target="tpu_custom_call" | custom-call | tf_op jit(solution)/shard_map/pallas_call | solution.py:100
  56.5 1.2 %copy.28 = f32[1,3,8,32,7]{3,2,4,1,0:T(8,128)S(1)} copy(f32[1,3,8,32,7]{4,3,2,1,0:T(8,128)} %bitcast.85) | data formatting | bytes 43008 | tf_op jit(solution)/shard_map/reshape | solution.py:285
  59.7 6.1 %all-to-all-start.1 = ((bf16[8,99,896]{2,1,0:T(8,128)(2,1)}), bf16[8,99,896]{2,1,0:T(8,128)(2,1)S(1)}, u32[]{:S(2)}, u32[]{:S(2)}) async-start(bf16[8,99,896]{2,1,0:T(8,128)(2,1)} %constant_dynamic-update-slice_fusion), calls=%async_computation.1 | async-start | bytes 2981888 | tf_op jit(solution)/shard_map/all_to_all | solution.py:302
  68.1 10.7 %all-reduce.2 = bf16[8,448]{1,0:T(8,128)(2,1)S(1)} all-reduce(f32[8,448]{1,0:T(8,128)S(1)} %fusion.17), channel_id=2, replica_groups=mesh['seq'=8,'tp'=4] {'tp'}, use_global_device_ids=true, to_apply=%region_3.5.clone | all-reduce | flops 3584 | bytes 21504
  79.5 20.8 %all-to-all-done.1.o_ref = bf16[8,99,896]{2,1,0:T(8,128)(2,1)S(1)} async-done(((bf16[8,99,896]{2,1,0:T(8,128)(2,1)}), bf16[8,99,896]{2,1,0:T(8,128)(2,1)S(1)}, u32[]{:S(2)}, u32[]{:S(2)}) %all-to-all-start.1) | async-done | bytes 1419296 | tf_op jit(solution)/shard_map/all_to_all | solution.py:302
  100.3 1.1 reshape.401
  101.4 0.8 fusion.8.lse_ref
  102.2 3.0 %shard_map.150 = bf16[3,32,896]{2,1,0:T(8,128)(2,1)} custom-call(bf16[8,99,896]{2,1,0:T(8,128)(2,1)} %copy-done.1, f32[8,3,32,7]{3,2,1,0:T(8,128)} %fusion.8.lse_ref), custom_call_target="tpu_custom_call" | custom-call | tf_op jit(solution)/shard_map/pallas_call | solution.py:148
  (61 shorter events, 9.2 us)
Async XLA Ops:
  0.6 67.2 %copy-start = (bf16[896,448]{0,1:T(8,128)(2,1)S(1)}, bf16[896,448]{0,1:T(8,128)(2,1)}, u32[]{:S(2)}) copy-start(bf16[896,448]{0,1:T(8,128)(2,1)} %param.23) | copy-start | bytes 2408452
  2.4 15.5 %collective-permute-start = (bf16[98,896]{1,0:T(8,128)(2,1)S(1)}, bf16[98,896]{1,0:T(8,128)(2,1)S(1)}, u32[]{:S(2)}, u32[]{:S(2)}) collective-permute-start(bf16[98,896]{1,0:T(8,128)(2,1)S(1)} %pad_maximum_fusion), channel_id=1, source_target_pairs={{0,16},{4,20},{8,24},{12,28},{16,0},{20,4},{24,8},{28,12},{1,17},{... | collective-permute-start | bytes 526856 | tf_op jit(solution)/shard_map/ppermute | solution.py:163
  6.5 12.6 %collective-permute-start.1 = (bf16[98,896]{1,0:T(8,128)(2,1)S(1)}, bf16[98,896]{1,0:T(8,128)(2,1)S(1)}, u32[]{:S(2)}, u32[]{:S(2)}) collective-permute-start(bf16[98,896]{1,0:T(8,128)(2,1)S(1)} %pad_maximum_fusion), channel_id=1, source_target_pairs={{0,4},{4,8},{8,12},{12,0},{16,20},{20,24},{24,28},{28,16},{1,5},{5... | collective-permute-start | bytes 526856 | tf_op jit(solution)/shard_map/ppermute | solution.py:168
  8.0 13.5 %collective-permute-start.2 = (bf16[98,896]{1,0:T(8,128)(2,1)S(1)}, bf16[98,896]{1,0:T(8,128)(2,1)S(1)}, u32[]{:S(2)}, u32[]{:S(2)}) collective-permute-start(bf16[98,896]{1,0:T(8,128)(2,1)S(1)} %pad_maximum_fusion), channel_id=1, source_target_pairs={{0,8},{4,12},{8,0},{12,4},{16,24},{20,28},{24,16},{28,20},{1,9},{5... | collective-permute-start | bytes 526856 | tf_op jit(solution)/shard_map/ppermute | solution.py:168
  9.6 11.9 %collective-permute-start.3 = (bf16[98,896]{1,0:T(8,128)(2,1)S(1)}, bf16[98,896]{1,0:T(8,128)(2,1)S(1)}, u32[]{:S(2)}, u32[]{:S(2)}) collective-permute-start(bf16[98,896]{1,0:T(8,128)(2,1)S(1)} %pad_maximum_fusion), channel_id=1, source_target_pairs={{0,12},{4,0},{8,4},{12,8},{16,28},{20,16},{24,20},{28,24},{1,13},{... | collective-permute-start | bytes 526856 | tf_op jit(solution)/shard_map/ppermute | solution.py:168
  17.9 8.5 %collective-permute-start.4 = (bf16[98,896]{1,0:T(8,128)(2,1)S(1)}, bf16[98,896]{1,0:T(8,128)(2,1)S(1)}, u32[]{:S(2)}, u32[]{:S(2)}) collective-permute-start(bf16[98,896]{1,0:T(8,128)(2,1)S(1)} %collective-permute-done), channel_id=1, source_target_pairs={{0,4},{4,8},{8,12},{12,0},{16,20},{20,24},{24,28},{28,16},{1,5},{5... | collective-permute-start | bytes 526856 | tf_op jit(solution)/shard_map/ppermute | solution.py:169
  18.6 7.9 %collective-permute-start.5 = (bf16[98,896]{1,0:T(8,128)(2,1)S(1)}, bf16[98,896]{1,0:T(8,128)(2,1)S(1)}, u32[]{:S(2)}, u32[]{:S(2)}) collective-permute-start(bf16[98,896]{1,0:T(8,128)(2,1)S(1)} %collective-permute-done), channel_id=1, source_target_pairs={{0,8},{4,12},{8,0},{12,4},{16,24},{20,28},{24,16},{28,20},{1,9},{5... | collective-permute-start | bytes 526856 | tf_op jit(solution)/shard_map/ppermute | solution.py:169
  19.1 9.3 %collective-permute-start.6 = (bf16[98,896]{1,0:T(8,128)(2,1)S(1)}, bf16[98,896]{1,0:T(8,128)(2,1)S(1)}, u32[]{:S(2)}, u32[]{:S(2)}) collective-permute-start(bf16[98,896]{1,0:T(8,128)(2,1)S(1)} %collective-permute-done), channel_id=1, source_target_pairs={{0,12},{4,0},{8,4},{12,8},{16,28},{20,16},{24,20},{28,24},{1,13},{... | collective-permute-start | bytes 526856 | tf_op jit(solution)/shard_map/ppermute | solution.py:169
  28.4 4.4 %copy-start.2 = (bf16[8,98,896]{2,1,0:T(8,128)(2,1)}, bf16[8,98,896]{2,1,0:T(8,128)(2,1)S(1)}, u32[]{:S(2)}) copy-start(bf16[8,98,896]{2,1,0:T(8,128)(2,1)S(1)} %bitcast_dynamic-update-slice_fusion.q_hbm) | copy-start | bytes 4214788
  34.7 25.0 %all-to-all-start = ((bf16[8,2,448]{2,1,0:T(2,128)(2,1)}), bf16[8,2,448]{2,1,0:T(2,128)(2,1)S(1)}, u32[]{:S(2)}, u32[]{:S(2)}) async-start(bf16[8,2,448]{2,1,0:T(2,128)(2,1)} %reshape.451), calls=%async_computation | async-start | bytes 32768 | tf_op jit(solution)/shard_map/all_to_all | solution.py:246
  59.7 6.1 %copy-start.4 = (u32[32]{0:T(128)S(1)}, u32[32]{0:T(128)}, u32[]{:S(2)}) copy-start(u32[32]{0:T(128)} %constant.216) | copy-start | bytes 388
  59.7 7.4 %copy-start.3 = (s32[8]{0:T(128)S(1)}, s32[8]{0:T(128)}, u32[]{:S(2)}) copy-start(s32[8]{0:T(128)} %param.22) | copy-start | bytes 100
  59.7 40.6 %all-to-all-start.1 = ((bf16[8,99,896]{2,1,0:T(8,128)(2,1)}), bf16[8,99,896]{2,1,0:T(8,128)(2,1)S(1)}, u32[]{:S(2)}, u32[]{:S(2)}) async-start(bf16[8,99,896]{2,1,0:T(8,128)(2,1)} %constant_dynamic-update-slice_fusion), calls=%async_computation.1 | async-start | bytes 2981888 | tf_op jit(solution)/shard_map/all_to_all | solution.py:302
  100.3 2.0 %copy-start.1 = (bf16[8,99,896]{2,1,0:T(8,128)(2,1)}, bf16[8,99,896]{2,1,0:T(8,128)(2,1)S(1)}, u32[]{:S(2)}) copy-start(bf16[8,99,896]{2,1,0:T(8,128)(2,1)S(1)} %all-to-all-done.1.o_ref) | copy-start | bytes 4257796

commit v15 on v14

--- a/solution.py
+++ b/solution.py
@@ -180,6 +180,35 @@
     return every, order.astype(jnp.int32)
 
 
+def exchange_over_seq(payload, seq_rank, seq_count):
+    if seq_count > 16 or seq_count % 2:
+        return lax.all_to_all(payload, "seq", 0, 0, tiled=True)
+    half = seq_count // 2
+    mine = lax.dynamic_index_in_dim(payload, seq_rank, 0, keepdims=False)
+    partner_of = (seq_rank + half) % seq_count
+    direct = lax.ppermute(
+        lax.dynamic_index_in_dim(payload, partner_of, 0, keepdims=False),
+        "seq",
+        [(i, (i + half) % seq_count) for i in range(seq_count)],
+    )
+    near_pieces, far_pieces = [], []
+    for shift in range(1, half):
+        perm = [(i, (i // half) * half + (i % half + shift) % half) for i in range(seq_count)]
+        target = (seq_rank // half) * half + (seq_rank % half + shift) % half
+        pair = jnp.stack(
+            [
+                lax.dynamic_index_in_dim(payload, target, 0, keepdims=False),
+                lax.dynamic_index_in_dim(payload, (target + half) % seq_count, 0, keepdims=False),
+            ]
+        )
+        got = lax.ppermute(pair, "seq", perm)
+        near_pieces.append(got[0])
+        far_pieces.append(
+            lax.ppermute(got[1], "seq", [(i, (i + half) % seq_count) for i in range(seq_count)])
+        )
+    return jnp.stack([mine, direct] + near_pieces + far_pieces)
+
+
 def body(
     new_query,
     new_key,
@@ -299,7 +328,7 @@
         (0, out_rows, 0),
     )
 
-    received = lax.all_to_all(payload, "seq", 0, 0, tiled=True)
+    received = exchange_over_seq(payload, seq_rank, seq_count)
     got_stats = (
         received[:, out_rows:, :]
         .reshape(seq_count, stat_rows * query_width)[:, :stat_count]

time: 106 us -> 120 us (1.13)
  waiting for transfers between devices: 27.6 us -> 32.2 us
  local copies, waits for them, and re-layouts: 8.17 us -> 12.3 us
  starting transfers between devices: 23.2 us -> 26.3 us
  other arithmetic: 8.04 us -> 10.9 us
    ppermute x0 -> x7, waiting for transfers between devices: none -> 25.6 us  [the longest x3 21 us: exchange_over_seq(): lax.ppermute(got[1], 'seq', [(i, (i + half) % seq_count) for i in range(s...]
    all_to_all x1 -> x0, waiting for transfers between devices: 20.8 us -> none  [body(): received = lax.all_to_all(payload, 'seq', 0, 0, tiled=True)]
    ppermute x0 -> x7, starting transfers between devices: none -> 10.9 us  [the longest x3 4.57 us: exchange_over_seq(): lax.ppermute(got[1], 'seq', [(i, (i + half) % seq_count) for i in range(s...]
    all_to_all x1 -> x0, starting transfers between devices: 6.13 us -> none  [body(): received = lax.all_to_all(payload, 'seq', 0, 0, tiled=True)]
    another operation x1 -> x4, other arithmetic: 0.04 us -> 2.4 us  [the longest x3 2.36 us: exchange_over_seq(): jnp.stack([lax.dynamic_index_in_dim(payload, target, 0, keepdims=False),...]
    dynamic_slice x0 -> x1, local copies, waits for them, and re-layouts: none -> 2.24 us  [exchange_over_seq(): lax.dynamic_index_in_dim(payload, target, 0, keepdims=False)]
    all_to_all x1, starting transfers between devices: 4.95 us -> 3.34 us  [body(): lax.all_to_all(jnp.broadcast_to(home_out[None], (seq_count,) + home_out.s...]
  transfers between devices with their start and end apart: 9 -> 15, of which waited for: 3 -> 7; matrix products, arithmetic and copies ran while one was open for 9% -> 14% of each run, Pallas kernels for 16% -> 14%
where the time goes in v15:
time: 120 us; the launch traced here: 119 us
  waiting for transfers between devices  32.2 us (27%)
  starting transfers between devices  26.3 us (22%)
  Pallas kernels  19.8 us (16%)
  local copies, waits for them, and re-layouts  12.3 us (10%)
  other arithmetic  10.9 us (9%)
  blocking collectives  10.2 us (8%)
  between operations  4.17 us (3%)
  matrix products  3.58 us (3%)
    ppermute x3, waiting for transfers between devices, exchange_over_seq(): lax.ppermute(got[1], 'seq', [(i, (i + half) % seq_count) for i in range(s...  21 us
    pallas_call x1, Pallas kernels, prefill_partial(): pl.pallas_call(kern, grid_spec=pltpu.PrefetchScalarGridSpec(num_scalar_pr...  16.8 us
    unnamed x1, blocking collectives  10.2 us
    ppermute x3, waiting for transfers between devices, broadcast_over_seq(): far_pieces = [lax.ppermute(partner, 'seq', perm) for perm in perms]  6.56 us
    ppermute x3, starting transfers between devices, exchange_over_seq(): lax.ppermute(got[1], 'seq', [(i, (i + half) % seq_count) for i in range(s...  4.57 us
    ppermute x3, starting transfers between devices, broadcast_over_seq(): near_pieces = [lax.ppermute(pack, 'seq', perm) for perm in perms]  4.5 us
    ppermute x1, starting transfers between devices, broadcast_over_seq(): lax.ppermute(pack, 'seq', [(i, (i + half) % seq_count) for i in range(seq...  4.1 us
    ppermute x3, starting transfers between devices, exchange_over_seq(): got = lax.ppermute(pair, 'seq', perm)  3.94 us
  transfers between devices with their start and end apart: 15, of which 7 were waited for; matrix products, arithmetic and copies ran while one was open for 14% of the time, Pallas kernels for 14%

profile of v15, /device:TPU:0, one launch (start us, length us, event | category | flops | bytes accessed | tf_op | source)
XLA Modules:
  0.0 119.4 jit_solution(452856755002312904)
XLA Ops:
  2.4 4.1 %collective-permute-start = (bf16[98,896]{1,0:T(8,128)(2,1)S(1)}, bf16[98,896]{1,0:T(8,128)(2,1)S(1)}, u32[]{:S(2)}, u32[]{:S(2)}) collective-permute-start(bf16[98,896]{1,0:T(8,128)(2,1)S(1)} %pad_maximum_fusion.3), channel_id=1, source_target_pairs={{0,16},{4,20},{8,24},{12,28},{16,0},{20,4},{24,8},{28,12},{1,17},{... | collective-permute-start | bytes 526856 | tf_op jit(solution)/shard_map/ppermute | solution.py:163
  6.5 1.5 %collective-permute-start.1 = (bf16[98,896]{1,0:T(8,128)(2,1)S(1)}, bf16[98,896]{1,0:T(8,128)(2,1)S(1)}, u32[]{:S(2)}, u32[]{:S(2)}) collective-permute-start(bf16[98,896]{1,0:T(8,128)(2,1)S(1)} %pad_maximum_fusion.3), channel_id=1, source_target_pairs={{0,4},{4,8},{8,12},{12,0},{16,20},{20,24},{24,28},{28,16},{1,5},{5... | collective-permute-start | bytes 526856 | tf_op jit(solution)/shard_map/ppermute | solution.py:168
  8.0 1.6 %collective-permute-start.2 = (bf16[98,896]{1,0:T(8,128)(2,1)S(1)}, bf16[98,896]{1,0:T(8,128)(2,1)S(1)}, u32[]{:S(2)}, u32[]{:S(2)}) collective-permute-start(bf16[98,896]{1,0:T(8,128)(2,1)S(1)} %pad_maximum_fusion.3), channel_id=1, source_target_pairs={{0,8},{4,12},{8,0},{12,4},{16,24},{20,28},{24,16},{28,20},{1,9},{5... | collective-permute-start | bytes 526856 | tf_op jit(solution)/shard_map/ppermute | solution.py:168
  9.6 1.4 %collective-permute-start.3 = (bf16[98,896]{1,0:T(8,128)(2,1)S(1)}, bf16[98,896]{1,0:T(8,128)(2,1)S(1)}, u32[]{:S(2)}, u32[]{:S(2)}) collective-permute-start(bf16[98,896]{1,0:T(8,128)(2,1)S(1)} %pad_maximum_fusion.3), channel_id=1, source_target_pairs={{0,12},{4,0},{8,4},{12,8},{16,28},{20,16},{24,20},{28,24},{1,13},{... | collective-permute-start | bytes 526856 | tf_op jit(solution)/shard_map/ppermute | solution.py:168
  21.4 2.4 %collective-permute-start.6 = (bf16[98,896]{1,0:T(8,128)(2,1)S(1)}, bf16[98,896]{1,0:T(8,128)(2,1)S(1)}, u32[]{:S(2)}, u32[]{:S(2)}) collective-permute-start(bf16[98,896]{1,0:T(8,128)(2,1)S(1)} %collective-permute-done), channel_id=1, source_target_pairs={{0,12},{4,0},{8,4},{12,8},{16,28},{20,16},{24,20},{28,24},{1,13},{... | collective-permute-start | bytes 526856 | tf_op jit(solution)/shard_map/ppermute | solution.py:169
  23.9 4.7 %collective-permute-done.4 = bf16[98,896]{1,0:T(8,128)(2,1)S(1)} collective-permute-done((bf16[98,896]{1,0:T(8,128)(2,1)S(1)}, bf16[98,896]{1,0:T(8,128)(2,1)S(1)}, u32[]{:S(2)}, u32[]{:S(2)}) %collective-permute-start.4) | collective-permute-done | bytes 175648 | tf_op jit(solution)/shard_map/ppermute | solution.py:169
  28.6 1.9 %collective-permute-done.6 = bf16[98,896]{1,0:T(8,128)(2,1)S(1)} collective-permute-done((bf16[98,896]{1,0:T(8,128)(2,1)S(1)}, bf16[98,896]{1,0:T(8,128)(2,1)S(1)}, u32[]{:S(2)}, u32[]{:S(2)}) %collective-permute-start.6) | collective-permute-done | bytes 175648 | tf_op jit(solution)/shard_map/ppermute | solution.py:169
  31.4 1.7 %fusion.42 = (f32[7]{0:T(128)S(1)}, f32[7,4097]{1,0:T(8,128)S(1)}) fusion(bf16[1,1,128]{2,1,0:T(2,128)(2,1)S(1)} %get-tuple-element.56, bf16[1,4096,128]{2,1,0:T(8,128)(2,1)} %param.19, bf16[896]{0:T(1024)(128)(2,1)S(1)} %fusion.21, pred[4097]{0:T(1024)(128)(4,1)S(1)} %add_reduce_fusion), kind=kOutput, calls=%fused_computation.146 | convolution fusion | flops 9525518 | bytes 1169465 | tf_op jit(solution)/shard_map/vmap()/dot_general | solution.py:16
  33.4 1.5 %fusion.2 = bf16[896]{0:T(1024)(128)(2,1)S(1)} fusion(bf16[1,1,128]{2,1,0:T(2,128)(2,1)S(1)} %get-tuple-element.57, bf16[1,4096,128]{2,1,0:T(8,128)(2,1)} %param.20, f32[7,4097]{1,0:T(8,128)S(1)} %get-tuple-element.55, f32[7]{0:T(128)S(1)} %get-tuple-element.54, pred[4097]{0:T(1024)(128)(4,1)S(1)} %add_reduce_fusion, f32[7]{0:T(128)S(1)} %fusion.10), kind=kOutput, calls=%fused_computation.6 | convolution fusion | flops 9527317 | bytes 1169493 | tf_op jit(solution)/shard_map/vmap()/dot_general | solution.py:21
  36.9 3.3 %all-to-all-start = ((bf16[8,2,448]{2,1,0:T(2,128)(2,1)}), bf16[8,2,448]{2,1,0:T(2,128)(2,1)S(1)}, u32[]{:S(2)}, u32[]{:S(2)}) async-start(bf16[8,2,448]{2,1,0:T(2,128)(2,1)} %reshape.451), calls=%async_computation | async-start | bytes 32768 | tf_op jit(solution)/shard_map/all_to_all | solution.py:275
  40.2 16.8 %shard_map.149 = (bf16[8,99,896]{2,1,0:T(8,128)(2,1)}, f32[3,256,7]{2,1,0:T(8,128)}) custom-call(s32[4]{0:T(128)} %pad_add_fusion.info_ref, s32[8]{0:T(128)} %get-tuple-element.30.order_ref, bf16[8,98,896]{2,1,0:T(8,128)(2,1)} %copy-done.2, bf16[3,1024,128]{2,1,0:T(8,128)(2,1)} %k_ref.1, bf16[3,1024,128]{2,1,0:T(8,128)(2,1)} %v_ref.1, ...), custom_call_target="tpu_custom_call" | custom-call | tf_op jit(solution)/shard_map/pallas_call | solution.py:100
  60.2 2.2 %constant_dynamic-slice_fusion.3 = (bf16[1,99,896]{2,1,0:T(8,128)(2,1)S(1)}, bf16[1,99,896]{2,1,0:T(8,128)(2,1)S(1)}, bf16[1,99,896]{2,1,0:T(8,128)(2,1)S(1)}, b...) fusion(bf16[8,99,896]{2,1,0:T(8,128)(2,1)} %constant_dynamic-up, ...), kind=kLoop, calls=%fused_computation.77 | loop fusion | bytes 2901280 | tf_op jit(solution)/shard_map/jit(dynamic_index_in_dim)/dynamic_slice | solution.py:200
  63.2 2.8 %collective-permute-start.10 = (bf16[2,99,896]{2,1,0:T(8,128)(2,1)}, bf16[2,99,896]{2,1,0:T(8,128)(2,1)S(1)}, u32[]{:S(2)}, u32[]{:S(2)}) collective-permute-start(bf16[2,99,896]{2,1,0:T(8,128)(2,1)} %pad_maximum_fusion.2), channel_id=1, source_target_pairs={{0,12},{4,0},{8,4},{12,8},{16,28},{20,16},{24,20},{28,24},{1,13},{... | collective-permute-start | bytes 1064456 | tf_op jit(solution)/shard_map/ppermute | solution.py:204
  68.8 2.4 %collective-permute-start.7 = (bf16[99,896]{1,0:T(8,128)(2,1)}, bf16[99,896]{1,0:T(8,128)(2,1)S(1)}, u32[]{:S(2)}, u32[]{:S(2)}) collective-permute-start(bf16[99,896]{1,0:T(8,128)(2,1)} %get-tuple-element.37), channel_id=1, source_target_pairs={{0,16},{4,20},{8,24},{12,28},{16,0},{20,4},{24,8},{28,12},{1,17},{... | collective-permute-start | bytes 532232 | tf_op jit(solution)/shard_map/ppermute | solution.py:189
  72.2 10.2 %all-reduce.2 = bf16[8,448]{1,0:T(8,128)(2,1)S(1)} all-reduce(f32[8,448]{1,0:T(8,128)S(1)} %fusion.17), channel_id=2, replica_groups=mesh['seq'=8,'tp'=4] {'tp'}, use_global_device_ids=true, to_apply=%region_3.5.clone | all-reduce | flops 3584 | bytes 21504
  82.9 2.7 %collective-permute-done.7 = bf16[99,896]{1,0:T(8,128)(2,1)S(1)} collective-permute-done((bf16[99,896]{1,0:T(8,128)(2,1)}, bf16[99,896]{1,0:T(8,128)(2,1)S(1)}, u32[]{:S(2)}, u32[]{:S(2)}) %collective-permute-start.7) | collective-permute-done | bytes 177440 | tf_op jit(solution)/shard_map/ppermute | solution.py:189
  85.7 1.8 %collective-permute-done.8 = bf16[2,99,896]{2,1,0:T(8,128)(2,1)} collective-permute-done((bf16[2,99,896]{2,1,0:T(8,128)(2,1)}, bf16[2,99,896]{2,1,0:T(8,128)(2,1)}, u32[]{:S(2)}, u32[]{:S(2)}) %collective-permute-start.8) | collective-permute-done | bytes 354848 | tf_op jit(solution)/shard_map/ppermute | solution.py:204
  88.6 1.5 %collective-permute-start.11 = (bf16[99,896]{1,0:T(8,128)(2,1)S(1)}, bf16[99,896]{1,0:T(8,128)(2,1)S(1)}, u32[]{:S(2)}, u32[]{:S(2)}) collective-permute-start(bf16[99,896]{1,0:T(8,128)(2,1)S(1)} %get-tuple-element.43), channel_id=1, source_target_pairs={{0,16},{4,20},{8,24},{12,28},{16,0},{20,4},{24,8},{28,12},{1,17},{... | collective-permute-start | bytes 532232 | tf_op jit(solution)/shard_map/ppermute | solution.py:207
  90.1 1.5 %collective-permute-start.12 = (bf16[99,896]{1,0:T(8,128)(2,1)S(1)}, bf16[99,896]{1,0:T(8,128)(2,1)S(1)}, u32[]{:S(2)}, u32[]{:S(2)}) collective-permute-start(bf16[99,896]{1,0:T(8,128)(2,1)S(1)} %get-tuple-element.41), channel_id=1, source_target_pairs={{0,16},{4,20},{8,24},{12,28},{16,0},{20,4},{24,8},{28,12},{1,17},{... | collective-permute-start | bytes 532232 | tf_op jit(solution)/shard_map/ppermute | solution.py:207
  91.7 1.5 %collective-permute-start.13 = (bf16[99,896]{1,0:T(8,128)(2,1)S(1)}, bf16[99,896]{1,0:T(8,128)(2,1)S(1)}, u32[]{:S(2)}, u32[]{:S(2)}) collective-permute-start(bf16[99,896]{1,0:T(8,128)(2,1)S(1)} %get-tuple-element.39), channel_id=1, source_target_pairs={{0,16},{4,20},{8,24},{12,28},{16,0},{20,4},{24,8},{28,12},{1,17},{... | collective-permute-start | bytes 532232 | tf_op jit(solution)/shard_map/ppermute | solution.py:207
  93.2 14.3 %collective-permute-done.11 = bf16[99,896]{1,0:T(8,128)(2,1)S(1)} collective-permute-done((bf16[99,896]{1,0:T(8,128)(2,1)S(1)}, bf16[99,896]{1,0:T(8,128)(2,1)S(1)}, u32[]{:S(2)}, u32[]{:S(2)}) %collective-permute-start.11) | collective-permute-done | bytes 177440 | tf_op jit(solution)/shard_map/ppermute | solution.py:207
  107.5 4.0 %collective-permute-done.12 = bf16[99,896]{1,0:T(8,128)(2,1)S(1)} collective-permute-done((bf16[99,896]{1,0:T(8,128)(2,1)S(1)}, bf16[99,896]{1,0:T(8,128)(2,1)S(1)}, u32[]{:S(2)}, u32[]{:S(2)}) %collective-permute-start.12) | collective-permute-done | bytes 177440 | tf_op jit(solution)/shard_map/ppermute | solution.py:207
  111.5 2.8 %collective-permute-done.13 = bf16[99,896]{1,0:T(8,128)(2,1)S(1)} collective-permute-done((bf16[99,896]{1,0:T(8,128)(2,1)S(1)}, bf16[99,896]{1,0:T(8,128)(2,1)S(1)}, u32[]{:S(2)}, u32[]{:S(2)}) %collective-permute-start.13) | collective-permute-done | bytes 177440 | tf_op jit(solution)/shard_map/ppermute | solution.py:207
  116.3 3.0 %shard_map.150 = bf16[3,32,896]{2,1,0:T(8,128)(2,1)} custom-call(bf16[8,99,896]{2,1,0:T(8,128)(2,1)} %copy-done.1, f32[8,3,32,7]{3,2,1,0:T(8,128)} %fusion.8.lse_ref), custom_call_target="tpu_custom_call" | custom-call | tf_op jit(solution)/shard_map/pallas_call | solution.py:148
  (80 shorter events, 23.5 us)
Async XLA Ops:
  0.6 71.2 %copy-start = (bf16[896,448]{0,1:T(8,128)(2,1)S(1)}, bf16[896,448]{0,1:T(8,128)(2,1)}, u32[]{:S(2)}) copy-start(bf16[896,448]{0,1:T(8,128)(2,1)} %param.23) | copy-start | bytes 2408452
  2.4 18.0 %collective-permute-start = (bf16[98,896]{1,0:T(8,128)(2,1)S(1)}, bf16[98,896]{1,0:T(8,128)(2,1)S(1)}, u32[]{:S(2)}, u32[]{:S(2)}) collective-permute-start(bf16[98,896]{1,0:T(8,128)(2,1)S(1)} %pad_maximum_fusion.3), channel_id=1, source_target_pairs={{0,16},{4,20},{8,24},{12,28},{16,0},{20,4},{24,8},{28,12},{1,17},{... | collective-permute-start | bytes 526856 | tf_op jit(solution)/shard_map/ppermute | solution.py:163
  6.5 15.0 %collective-permute-start.1 = (bf16[98,896]{1,0:T(8,128)(2,1)S(1)}, bf16[98,896]{1,0:T(8,128)(2,1)S(1)}, u32[]{:S(2)}, u32[]{:S(2)}) collective-permute-start(bf16[98,896]{1,0:T(8,128)(2,1)S(1)} %pad_maximum_fusion.3), channel_id=1, source_target_pairs={{0,4},{4,8},{8,12},{12,0},{16,20},{20,24},{24,28},{28,16},{1,5},{5... | collective-permute-start | bytes 526856 | tf_op jit(solution)/shard_map/ppermute | solution.py:168
  8.0 15.8 %collective-permute-start.2 = (bf16[98,896]{1,0:T(8,128)(2,1)S(1)}, bf16[98,896]{1,0:T(8,128)(2,1)S(1)}, u32[]{:S(2)}, u32[]{:S(2)}) collective-permute-start(bf16[98,896]{1,0:T(8,128)(2,1)S(1)} %pad_maximum_fusion.3), channel_id=1, source_target_pairs={{0,8},{4,12},{8,0},{12,4},{16,24},{20,28},{24,16},{28,20},{1,9},{5... | collective-permute-start | bytes 526856 | tf_op jit(solution)/shard_map/ppermute | solution.py:168
  9.6 14.3 %collective-permute-start.3 = (bf16[98,896]{1,0:T(8,128)(2,1)S(1)}, bf16[98,896]{1,0:T(8,128)(2,1)S(1)}, u32[]{:S(2)}, u32[]{:S(2)}) collective-permute-start(bf16[98,896]{1,0:T(8,128)(2,1)S(1)} %pad_maximum_fusion.3), channel_id=1, source_target_pairs={{0,12},{4,0},{8,4},{12,8},{16,28},{20,16},{24,20},{28,24},{1,13},{... | collective-permute-start | bytes 526856 | tf_op jit(solution)/shard_map/ppermute | solution.py:168
  20.3 8.2 %collective-permute-start.4 = (bf16[98,896]{1,0:T(8,128)(2,1)S(1)}, bf16[98,896]{1,0:T(8,128)(2,1)S(1)}, u32[]{:S(2)}, u32[]{:S(2)}) collective-permute-start(bf16[98,896]{1,0:T(8,128)(2,1)S(1)} %collective-permute-done), channel_id=1, source_target_pairs={{0,4},{4,8},{8,12},{12,0},{16,20},{20,24},{24,28},{28,16},{1,5},{5... | collective-permute-start | bytes 526856 | tf_op jit(solution)/shard_map/ppermute | solution.py:169
  20.9 7.7 %collective-permute-start.5 = (bf16[98,896]{1,0:T(8,128)(2,1)S(1)}, bf16[98,896]{1,0:T(8,128)(2,1)S(1)}, u32[]{:S(2)}, u32[]{:S(2)}) collective-permute-start(bf16[98,896]{1,0:T(8,128)(2,1)S(1)} %collective-permute-done), channel_id=1, source_target_pairs={{0,8},{4,12},{8,0},{12,4},{16,24},{20,28},{24,16},{28,20},{1,9},{5... | collective-permute-start | bytes 526856 | tf_op jit(solution)/shard_map/ppermute | solution.py:169
  21.4 9.1 %collective-permute-start.6 = (bf16[98,896]{1,0:T(8,128)(2,1)S(1)}, bf16[98,896]{1,0:T(8,128)(2,1)S(1)}, u32[]{:S(2)}, u32[]{:S(2)}) collective-permute-start(bf16[98,896]{1,0:T(8,128)(2,1)S(1)} %collective-permute-done), channel_id=1, source_target_pairs={{0,12},{4,0},{8,4},{12,8},{16,28},{20,16},{24,20},{28,24},{1,13},{... | collective-permute-start | bytes 526856 | tf_op jit(solution)/shard_map/ppermute | solution.py:169
  30.5 4.4 %copy-start.2 = (bf16[8,98,896]{2,1,0:T(8,128)(2,1)}, bf16[8,98,896]{2,1,0:T(8,128)(2,1)S(1)}, u32[]{:S(2)}) copy-start(bf16[8,98,896]{2,1,0:T(8,128)(2,1)S(1)} %bitcast_dynamic-update-slice_fusion.4.q_hbm) | copy-start | bytes 4214788
  36.9 34.3 %all-to-all-start = ((bf16[8,2,448]{2,1,0:T(2,128)(2,1)}), bf16[8,2,448]{2,1,0:T(2,128)(2,1)S(1)}, u32[]{:S(2)}, u32[]{:S(2)}) async-start(bf16[8,2,448]{2,1,0:T(2,128)(2,1)} %reshape.451), calls=%async_computation | async-start | bytes 32768 | tf_op jit(solution)/shard_map/all_to_all | solution.py:275
  63.2 28.4 %collective-permute-start.10 = (bf16[2,99,896]{2,1,0:T(8,128)(2,1)}, bf16[2,99,896]{2,1,0:T(8,128)(2,1)S(1)}, u32[]{:S(2)}, u32[]{:S(2)}) collective-permute-start(bf16[2,99,896]{2,1,0:T(8,128)(2,1)} %pad_maximum_fusion.2), channel_id=1, source_target_pairs={{0,12},{4,0},{8,4},{12,8},{16,28},{20,16},{24,20},{28,24},{1,13},{... | collective-permute-start | bytes 1064456 | tf_op jit(solution)/shard_map/ppermute | solution.py:204
  66.9 23.2 %collective-permute-start.9 = (bf16[2,99,896]{2,1,0:T(8,128)(2,1)}, bf16[2,99,896]{2,1,0:T(8,128)(2,1)S(1)}, u32[]{:S(2)}, u32[]{:S(2)}) collective-permute-start(bf16[2,99,896]{2,1,0:T(8,128)(2,1)} %pad_maximum_fusion.1), channel_id=1, source_target_pairs={{0,8},{4,12},{8,0},{12,4},{16,24},{20,28},{24,16},{28,20},{1,9},{5... | collective-permute-start | bytes 1064456 | tf_op jit(solution)/shard_map/ppermute | solution.py:204
  68.2 19.3 %collective-permute-start.8 = (bf16[2,99,896]{2,1,0:T(8,128)(2,1)}, bf16[2,99,896]{2,1,0:T(8,128)(2,1)}, u32[]{:S(2)}, u32[]{:S(2)}) collective-permute-start(bf16[2,99,896]{2,1,0:T(8,128)(2,1)} %pad_maximum_fusion), channel_id=1, source_target_pairs={{0,4},{4,8},{8,12},{12,0},{16,20},{20,24},{24,28},{28,16},{1,5},{5... | collective-permute-start | bytes 1064456 | tf_op jit(solution)/shard_map/ppermute | solution.py:204
  68.8 16.9 %collective-permute-start.7 = (bf16[99,896]{1,0:T(8,128)(2,1)}, bf16[99,896]{1,0:T(8,128)(2,1)S(1)}, u32[]{:S(2)}, u32[]{:S(2)}) collective-permute-start(bf16[99,896]{1,0:T(8,128)(2,1)} %get-tuple-element.37), channel_id=1, source_target_pairs={{0,16},{4,20},{8,24},{12,28},{16,0},{20,4},{24,8},{28,12},{1,17},{... | collective-permute-start | bytes 532232 | tf_op jit(solution)/shard_map/ppermute | solution.py:189
  88.6 18.9 %collective-permute-start.11 = (bf16[99,896]{1,0:T(8,128)(2,1)S(1)}, bf16[99,896]{1,0:T(8,128)(2,1)S(1)}, u32[]{:S(2)}, u32[]{:S(2)}) collective-permute-start(bf16[99,896]{1,0:T(8,128)(2,1)S(1)} %get-tuple-element.43), channel_id=1, source_target_pairs={{0,16},{4,20},{8,24},{12,28},{16,0},{20,4},{24,8},{28,12},{1,17},{... | collective-permute-start | bytes 532232 | tf_op jit(solution)/shard_map/ppermute | solution.py:207
  90.1 21.4 %collective-permute-start.12 = (bf16[99,896]{1,0:T(8,128)(2,1)S(1)}, bf16[99,896]{1,0:T(8,128)(2,1)S(1)}, u32[]{:S(2)}, u32[]{:S(2)}) collective-permute-start(bf16[99,896]{1,0:T(8,128)(2,1)S(1)} %get-tuple-element.41), channel_id=1, source_target_pairs={{0,16},{4,20},{8,24},{12,28},{16,0},{20,4},{24,8},{28,12},{1,17},{... | collective-permute-start | bytes 532232 | tf_op jit(solution)/shard_map/ppermute | solution.py:207
  91.7 22.6 %collective-permute-start.13 = (bf16[99,896]{1,0:T(8,128)(2,1)S(1)}, bf16[99,896]{1,0:T(8,128)(2,1)S(1)}, u32[]{:S(2)}, u32[]{:S(2)}) collective-permute-start(bf16[99,896]{1,0:T(8,128)(2,1)S(1)} %get-tuple-element.39), channel_id=1, source_target_pairs={{0,16},{4,20},{8,24},{12,28},{16,0},{20,4},{24,8},{28,12},{1,17},{... | collective-permute-start | bytes 532232 | tf_op jit(solution)/shard_map/ppermute | solution.py:207
  114.3 2.0 %copy-start.1 = (bf16[8,99,896]{2,1,0:T(8,128)(2,1)}, bf16[8,99,896]{2,1,0:T(8,128)(2,1)S(1)}, u32[]{:S(2)}) copy-start(bf16[8,99,896]{2,1,0:T(8,128)(2,1)S(1)} %bitcast_dynamic-update-slice_fusion.o_ref) | copy-start | bytes 4257796

commit v16 on v14

--- a/solution.py
+++ b/solution.py
@@ -82,7 +82,7 @@
         o_ref[:, :, h * head_size : (h + 1) * head_size] = (
             (num / safe).astype(o_ref.dtype).reshape(src_count, tok_block, head_size)
         )
-        lse_ref[0, :, h : h + 1] = m + jnp.log(safe)
+        lse_ref[:, 0, :, h : h + 1] = (m + jnp.log(safe)).reshape(src_count, tok_block, 1)
 
 
 def prefill_partial(
@@ -111,7 +111,9 @@
             ],
             out_specs=[
                 pl.BlockSpec((src_count, tok_block, qw), lambda c, info, order: (0, c, 0)),
-                pl.BlockSpec((1, tokens, group_size), lambda c, info, order: (c, 0, 0)),
+                pl.BlockSpec(
+                    (src_count, 1, tok_block, group_size), lambda c, info, order: (0, c, 0, 0)
+                ),
             ],
             scratch_shapes=[
                 pltpu.VMEM((n, src_count, tok_block, qw), jnp.bfloat16),
@@ -120,7 +122,7 @@
         ),
         out_shape=[
             jax.ShapeDtypeStruct((src_count, out_rows, qw), jnp.bfloat16),
-            jax.ShapeDtypeStruct((n, tokens, group_size), jnp.float32),
+            jax.ShapeDtypeStruct((src_count, n, tok_block, group_size), jnp.float32),
         ],
     )(info, order, queries, keys, values, own_keys, own_values)
 
@@ -282,16 +284,15 @@
             .reshape(seq_count, out_rows, query_width),
             ((0, 0), (0, stat_rows), (0, 0)),
         )
-    part_lse = part_lse.reshape(stretch_count, seq_count, local_tok, group_size)
+    if not direct:
+        part_lse = part_lse.reshape(stretch_count, seq_count, local_tok, group_size).transpose(
+            1, 0, 2, 3
+        )
     lse_hi = lax.reduce_precision(part_lse, exponent_bits=8, mantissa_bits=7)
     lse_rest = part_lse - lse_hi
     lse_mid = lax.reduce_precision(lse_rest, exponent_bits=8, mantissa_bits=7)
     lse_lo = lse_rest - lse_mid
-    stats = (
-        jnp.stack([lse_hi, lse_mid, lse_lo])
-        .transpose(2, 0, 1, 3, 4)
-        .reshape(seq_count, stat_count)
-    )
+    stats = jnp.stack([lse_hi, lse_mid, lse_lo], axis=1).reshape(seq_count, stat_count)
     stats = jnp.pad(stats, ((0, 0), (0, stat_rows * query_width - stat_count)))
     payload = lax.dynamic_update_slice(
         payload,

time: 106 us -> 105 us (level)
  local copies, waits for them, and re-layouts: 8.17 us -> 6.44 us
  other arithmetic: 8.04 us -> 9.22 us
    reshape x2 -> x1, local copies, waits for them, and re-layouts: 1.85 us -> 0.64 us  [body(): jnp.stack([lse_hi, lse_mid, lse_lo], axis=1).reshape(seq_count, stat_count)]
    another operation x1 -> x2, other arithmetic: 0.04 us -> 1.25 us  [body(): jnp.stack([lse_hi, lse_mid, lse_lo], axis=1).reshape(seq_count, stat_count)]
where the time goes in v16:
time: 105 us
  waiting for transfers between devices  27.6 us (26%)
  starting transfers between devices  23.2 us (22%)
  Pallas kernels  19.8 us (19%)
  blocking collectives  10.7 us (10%)
  other arithmetic  9.22 us (9%)
  local copies, waits for them, and re-layouts  6.44 us (6%)
  between operations  4.16 us (4%)
  matrix products  3.58 us (3%)
    all_to_all x1, waiting for transfers between devices, body(): received = lax.all_to_all(payload, 'seq', 0, 0, tiled=True)  20.8 us
    pallas_call x1, Pallas kernels, prefill_partial(): pl.pallas_call(kern, grid_spec=pltpu.PrefetchScalarGridSpec(num_scalar_pr...  16.8 us
    unnamed x1, blocking collectives  10.7 us
    ppermute x3, waiting for transfers between devices, broadcast_over_seq(): far_pieces = [lax.ppermute(partner, 'seq', perm) for perm in perms]  6.78 us
    all_to_all x1, starting transfers between devices, body(): received = lax.all_to_all(payload, 'seq', 0, 0, tiled=True)  6.13 us
    all_to_all x1, starting transfers between devices, body(): lax.all_to_all(jnp.broadcast_to(home_out[None], (seq_count,) + home_out.s...  4.95 us
    ppermute x3, starting transfers between devices, broadcast_over_seq(): near_pieces = [lax.ppermute(pack, 'seq', perm) for perm in perms]  4.5 us
    ppermute x1, starting transfers between devices, broadcast_over_seq(): lax.ppermute(pack, 'seq', [(i, (i + half) % seq_count) for i in range(seq...  4.1 us
  transfers between devices with their start and end apart: 9, of which 3 were waited for; matrix products, arithmetic and copies ran while one was open for 9% of the time, Pallas kernels for 16%

profile of v16, /device:TPU:0, one launch (start us, length us, event | category | flops | bytes accessed | tf_op | source)
XLA Modules:
  0.0 104.7 jit_solution(6574527417646045131)
XLA Ops:
  0.6 0.8 fusion.25
  1.4 1.0 pad_maximum_fusion.1
  2.4 4.1 %collective-permute-start = (bf16[98,896]{1,0:T(8,128)(2,1)S(1)}, bf16[98,896]{1,0:T(8,128)(2,1)S(1)}, u32[]{:S(2)}, u32[]{:S(2)}) collective-permute-start(bf16[98,896]{1,0:T(8,128)(2,1)S(1)} %pad_maximum_fusion.1), channel_id=1, source_target_pairs={{0,16},{4,20},{8,24},{12,28},{16,0},{20,4},{24,8},{28,12},{1,17},{... | collective-permute-start | bytes 526856 | tf_op jit(solution)/shard_map/ppermute | solution.py:165
  6.5 1.5 %collective-permute-start.1 = (bf16[98,896]{1,0:T(8,128)(2,1)S(1)}, bf16[98,896]{1,0:T(8,128)(2,1)S(1)}, u32[]{:S(2)}, u32[]{:S(2)}) collective-permute-start(bf16[98,896]{1,0:T(8,128)(2,1)S(1)} %pad_maximum_fusion.1), channel_id=1, source_target_pairs={{0,4},{4,8},{8,12},{12,0},{16,20},{20,24},{24,28},{28,16},{1,5},{5... | collective-permute-start | bytes 526856 | tf_op jit(solution)/shard_map/ppermute | solution.py:170
  8.0 1.6 %collective-permute-start.2 = (bf16[98,896]{1,0:T(8,128)(2,1)S(1)}, bf16[98,896]{1,0:T(8,128)(2,1)S(1)}, u32[]{:S(2)}, u32[]{:S(2)}) collective-permute-start(bf16[98,896]{1,0:T(8,128)(2,1)S(1)} %pad_maximum_fusion.1), channel_id=1, source_target_pairs={{0,8},{4,12},{8,0},{12,4},{16,24},{20,28},{24,16},{28,20},{1,9},{5... | collective-permute-start | bytes 526856 | tf_op jit(solution)/shard_map/ppermute | solution.py:170
  9.6 1.4 %collective-permute-start.3 = (bf16[98,896]{1,0:T(8,128)(2,1)S(1)}, bf16[98,896]{1,0:T(8,128)(2,1)S(1)}, u32[]{:S(2)}, u32[]{:S(2)}) collective-permute-start(bf16[98,896]{1,0:T(8,128)(2,1)S(1)} %pad_maximum_fusion.1), channel_id=1, source_target_pairs={{0,12},{4,0},{8,4},{12,8},{16,28},{20,16},{24,20},{28,24},{1,13},{... | collective-permute-start | bytes 526856 | tf_op jit(solution)/shard_map/ppermute | solution.py:170
  11.6 1.3 %compare_select_fusion.4 = (s32[8]{0:T(128)S(1)}, s32[]{:T(128)}) fusion(s32[8]{0:T(128)} %param.22, s32[]{:T(128)S(6)} %axis_index.15), kind=kLoop, calls=%fused_computation.64 | loop fusion | flops 47 | bytes 72 | tf_op jit(solution)/shard_map/jit(_take)/jit(_where)/select_n | solution.py:251
  16.9 1.0 bitcast_dynamic-update-slice_fusion.7
  19.1 2.4 %collective-permute-start.6 = (bf16[98,896]{1,0:T(8,128)(2,1)S(1)}, bf16[98,896]{1,0:T(8,128)(2,1)S(1)}, u32[]{:S(2)}, u32[]{:S(2)}) collective-permute-start(bf16[98,896]{1,0:T(8,128)(2,1)S(1)} %collective-permute-done), channel_id=1, source_target_pairs={{0,12},{4,0},{8,4},{12,8},{16,28},{20,16},{24,20},{28,24},{1,13},{... | collective-permute-start | bytes 526856 | tf_op jit(solution)/shard_map/ppermute | solution.py:171
  21.5 4.9 %collective-permute-done.4 = bf16[98,896]{1,0:T(8,128)(2,1)S(1)} collective-permute-done((bf16[98,896]{1,0:T(8,128)(2,1)S(1)}, bf16[98,896]{1,0:T(8,128)(2,1)S(1)}, u32[]{:S(2)}, u32[]{:S(2)}) %collective-permute-start.4) | collective-permute-done | bytes 175648 | tf_op jit(solution)/shard_map/ppermute | solution.py:171
  26.5 1.9 %collective-permute-done.6 = bf16[98,896]{1,0:T(8,128)(2,1)S(1)} collective-permute-done((bf16[98,896]{1,0:T(8,128)(2,1)S(1)}, bf16[98,896]{1,0:T(8,128)(2,1)S(1)}, u32[]{:S(2)}, u32[]{:S(2)}) %collective-permute-start.6) | collective-permute-done | bytes 175648 | tf_op jit(solution)/shard_map/ppermute | solution.py:171
  29.3 1.7 %fusion.45 = (f32[7]{0:T(128)S(1)}, f32[7,4097]{1,0:T(8,128)S(1)}) fusion(bf16[1,1,128]{2,1,0:T(2,128)(2,1)S(1)} %get-tuple-element.42, bf16[1,4096,128]{2,1,0:T(8,128)(2,1)} %param.19, bf16[896]{0:T(1024)(128)(2,1)S(1)} %fusion.24, pred[4097]{0:T(1024)(128)(4,1)S(1)} %add_reduce_fusion), kind=kOutput, calls=%fused_computation.128 | convolution fusion | flops 9525518 | bytes 1169465 | tf_op jit(solution)/shard_map/vmap()/dot_general | solution.py:16
  31.2 1.5 %fusion.2 = bf16[896]{0:T(1024)(128)(2,1)S(1)} fusion(bf16[1,1,128]{2,1,0:T(2,128)(2,1)S(1)} %get-tuple-element.43, bf16[1,4096,128]{2,1,0:T(8,128)(2,1)} %param.20, f32[7,4097]{1,0:T(8,128)S(1)} %get-tuple-element.41, f32[7]{0:T(128)S(1)} %get-tuple-element.40, pred[4097]{0:T(1024)(128)(4,1)S(1)} %add_reduce_fusion, f32[7]{0:T(128)S(1)} %fusion.14), kind=kOutput, calls=%fused_computation.6 | convolution fusion | flops 9527317 | bytes 1169493 | tf_op jit(solution)/shard_map/vmap()/dot_general | solution.py:21
  33.3 0.7 reduce.10
  34.0 0.7 reshape.411
  34.7 5.0 %all-to-all-start = ((bf16[8,2,448]{2,1,0:T(2,128)(2,1)}), bf16[8,2,448]{2,1,0:T(2,128)(2,1)S(1)}, u32[]{:S(2)}, u32[]{:S(2)}) async-start(bf16[8,2,448]{2,1,0:T(2,128)(2,1)} %reshape.411), calls=%async_computation | async-start | bytes 32768 | tf_op jit(solution)/shard_map/all_to_all | solution.py:248
  39.7 16.8 %shard_map.149 = (bf16[8,99,896]{2,1,0:T(8,128)(2,1)}, f32[8,3,32,7]{3,2,1,0:T(8,128)}) custom-call(s32[4]{0:T(128)} %pad_add_fusion.info_ref, s32[8]{0:T(128)} %get-tuple-element.30.order_ref, bf16[8,98,896]{2,1,0:T(8,128)(2,1)} %copy-done.2, bf16[3,1024,128]{2,1,0:T(8,128)(2,1)} %k_ref.1, bf16[3,1024,128]{2,1,0:T(8,128)(2,1)} %v_ref.1, ...), custom_call_target="tpu_custom_call" | custom-call | tf_op jit(solution)/shard_map/pallas_call | solution.py:100
  56.5 1.1 %fusion.12 = (bf16[8,1,3,32,7]{4,3,2,0,1:T(8,128)(2,1)S(1)}, bf16[8,1,3,32,7]{4,3,2,0,1:T(8,128)(2,1)S(1)}, bf16[8,1,3,32,7]{4,3,2,0,1:T(8,128)(2,1)S(1)}) fusion(f32[8,3,32,7]{3,2,1,0:T(8,128)} %get-tuple-element.6), kind=kLoop, calls=%fused_computation.26 | loop fusion | flops 37632 | bytes 53760 | tf_op jit(solution)/shard_map/stack | solution.py:295
  59.1 6.1 %all-to-all-start.1 = ((bf16[8,99,896]{2,1,0:T(8,128)(2,1)}), bf16[8,99,896]{2,1,0:T(8,128)(2,1)S(1)}, u32[]{:S(2)}, u32[]{:S(2)}) async-start(bf16[8,99,896]{2,1,0:T(8,128)(2,1)} %constant_dynamic-update-slice_fusion), calls=%async_computation.1 | async-start | bytes 2981888 | tf_op jit(solution)/shard_map/all_to_all | solution.py:303
  67.6 10.7 %all-reduce.2 = bf16[8,448]{1,0:T(8,128)(2,1)S(1)} all-reduce(f32[8,448]{1,0:T(8,128)S(1)} %fusion.20), channel_id=2, replica_groups=mesh['seq'=8,'tp'=4] {'tp'}, use_global_device_ids=true, to_apply=%region_3.5.clone | all-reduce | flops 3584 | bytes 21504
  78.9 20.8 %all-to-all-done.1.o_ref = bf16[8,99,896]{2,1,0:T(8,128)(2,1)S(1)} async-done(((bf16[8,99,896]{2,1,0:T(8,128)(2,1)}), bf16[8,99,896]{2,1,0:T(8,128)(2,1)S(1)}, u32[]{:S(2)}, u32[]{:S(2)}) %all-to-all-start.1) | async-done | bytes 1419296 | tf_op jit(solution)/shard_map/all_to_all | solution.py:303
  99.8 1.1 %reshape.361 = f32[8,3,3,32,7]{4,3,2,1,0:T(8,128)S(1)} reshape(f32[8,2016]{1,0:T(8,128)S(1)} %slice_convert_fusion) | data formatting | bytes 129024 | tf_op jit(solution)/shard_map/reshape | solution.py:308
  100.8 0.8 fusion.9.lse_ref
  101.7 3.0 %shard_map.150 = bf16[3,32,896]{2,1,0:T(8,128)(2,1)} custom-call(bf16[8,99,896]{2,1,0:T(8,128)(2,1)} %copy-done.1, f32[8,3,32,7]{3,2,1,0:T(8,128)} %fusion.9.lse_ref), custom_call_target="tpu_custom_call" | custom-call | tf_op jit(solution)/shard_map/pallas_call | solution.py:150
  (60 shorter events, 8.8 us)
Async XLA Ops:
  0.6 66.6 %copy-start = (bf16[896,448]{0,1:T(8,128)(2,1)S(1)}, bf16[896,448]{0,1:T(8,128)(2,1)}, u32[]{:S(2)}) copy-start(bf16[896,448]{0,1:T(8,128)(2,1)} %param.23) | copy-start | bytes 2408452
  2.4 15.5 %collective-permute-start = (bf16[98,896]{1,0:T(8,128)(2,1)S(1)}, bf16[98,896]{1,0:T(8,128)(2,1)S(1)}, u32[]{:S(2)}, u32[]{:S(2)}) collective-permute-start(bf16[98,896]{1,0:T(8,128)(2,1)S(1)} %pad_maximum_fusion.1), channel_id=1, source_target_pairs={{0,16},{4,20},{8,24},{12,28},{16,0},{20,4},{24,8},{28,12},{1,17},{... | collective-permute-start | bytes 526856 | tf_op jit(solution)/shard_map/ppermute | solution.py:165
  6.5 12.6 %collective-permute-start.1 = (bf16[98,896]{1,0:T(8,128)(2,1)S(1)}, bf16[98,896]{1,0:T(8,128)(2,1)S(1)}, u32[]{:S(2)}, u32[]{:S(2)}) collective-permute-start(bf16[98,896]{1,0:T(8,128)(2,1)S(1)} %pad_maximum_fusion.1), channel_id=1, source_target_pairs={{0,4},{4,8},{8,12},{12,0},{16,20},{20,24},{24,28},{28,16},{1,5},{5... | collective-permute-start | bytes 526856 | tf_op jit(solution)/shard_map/ppermute | solution.py:170
  8.0 13.5 %collective-permute-start.2 = (bf16[98,896]{1,0:T(8,128)(2,1)S(1)}, bf16[98,896]{1,0:T(8,128)(2,1)S(1)}, u32[]{:S(2)}, u32[]{:S(2)}) collective-permute-start(bf16[98,896]{1,0:T(8,128)(2,1)S(1)} %pad_maximum_fusion.1), channel_id=1, source_target_pairs={{0,8},{4,12},{8,0},{12,4},{16,24},{20,28},{24,16},{28,20},{1,9},{5... | collective-permute-start | bytes 526856 | tf_op jit(solution)/shard_map/ppermute | solution.py:170
  9.6 11.9 %collective-permute-start.3 = (bf16[98,896]{1,0:T(8,128)(2,1)S(1)}, bf16[98,896]{1,0:T(8,128)(2,1)S(1)}, u32[]{:S(2)}, u32[]{:S(2)}) collective-permute-start(bf16[98,896]{1,0:T(8,128)(2,1)S(1)} %pad_maximum_fusion.1), channel_id=1, source_target_pairs={{0,12},{4,0},{8,4},{12,8},{16,28},{20,16},{24,20},{28,24},{1,13},{... | collective-permute-start | bytes 526856 | tf_op jit(solution)/shard_map/ppermute | solution.py:170
  17.9 8.5 %collective-permute-start.4 = (bf16[98,896]{1,0:T(8,128)(2,1)S(1)}, bf16[98,896]{1,0:T(8,128)(2,1)S(1)}, u32[]{:S(2)}, u32[]{:S(2)}) collective-permute-start(bf16[98,896]{1,0:T(8,128)(2,1)S(1)} %collective-permute-done), channel_id=1, source_target_pairs={{0,4},{4,8},{8,12},{12,0},{16,20},{20,24},{24,28},{28,16},{1,5},{5... | collective-permute-start | bytes 526856 | tf_op jit(solution)/shard_map/ppermute | solution.py:171
  18.6 7.9 %collective-permute-start.5 = (bf16[98,896]{1,0:T(8,128)(2,1)S(1)}, bf16[98,896]{1,0:T(8,128)(2,1)S(1)}, u32[]{:S(2)}, u32[]{:S(2)}) collective-permute-start(bf16[98,896]{1,0:T(8,128)(2,1)S(1)} %collective-permute-done), channel_id=1, source_target_pairs={{0,8},{4,12},{8,0},{12,4},{16,24},{20,28},{24,16},{28,20},{1,9},{5... | collective-permute-start | bytes 526856 | tf_op jit(solution)/shard_map/ppermute | solution.py:171
  19.1 9.3 %collective-permute-start.6 = (bf16[98,896]{1,0:T(8,128)(2,1)S(1)}, bf16[98,896]{1,0:T(8,128)(2,1)S(1)}, u32[]{:S(2)}, u32[]{:S(2)}) collective-permute-start(bf16[98,896]{1,0:T(8,128)(2,1)S(1)} %collective-permute-done), channel_id=1, source_target_pairs={{0,12},{4,0},{8,4},{12,8},{16,28},{20,16},{24,20},{28,24},{1,13},{... | collective-permute-start | bytes 526856 | tf_op jit(solution)/shard_map/ppermute | solution.py:171
  28.4 4.4 %copy-start.2 = (bf16[8,98,896]{2,1,0:T(8,128)(2,1)}, bf16[8,98,896]{2,1,0:T(8,128)(2,1)S(1)}, u32[]{:S(2)}) copy-start(bf16[8,98,896]{2,1,0:T(8,128)(2,1)S(1)} %bitcast_dynamic-update-slice_fusion.q_hbm) | copy-start | bytes 4214788
  34.7 24.4 %all-to-all-start = ((bf16[8,2,448]{2,1,0:T(2,128)(2,1)}), bf16[8,2,448]{2,1,0:T(2,128)(2,1)S(1)}, u32[]{:S(2)}, u32[]{:S(2)}) async-start(bf16[8,2,448]{2,1,0:T(2,128)(2,1)} %reshape.411), calls=%async_computation | async-start | bytes 32768 | tf_op jit(solution)/shard_map/all_to_all | solution.py:248
  59.1 6.1 %copy-start.4 = (u32[32]{0:T(128)S(1)}, u32[32]{0:T(128)}, u32[]{:S(2)}) copy-start(u32[32]{0:T(128)} %constant.216) | copy-start | bytes 388
  59.1 7.4 %copy-start.3 = (s32[8]{0:T(128)S(1)}, s32[8]{0:T(128)}, u32[]{:S(2)}) copy-start(s32[8]{0:T(128)} %param.22) | copy-start | bytes 100
  59.1 40.6 %all-to-all-start.1 = ((bf16[8,99,896]{2,1,0:T(8,128)(2,1)}), bf16[8,99,896]{2,1,0:T(8,128)(2,1)S(1)}, u32[]{:S(2)}, u32[]{:S(2)}) async-start(bf16[8,99,896]{2,1,0:T(8,128)(2,1)} %constant_dynamic-update-slice_fusion), calls=%async_computation.1 | async-start | bytes 2981888 | tf_op jit(solution)/shard_map/all_to_all | solution.py:303
  99.7 2.0 %copy-start.1 = (bf16[8,99,896]{2,1,0:T(8,128)(2,1)}, bf16[8,99,896]{2,1,0:T(8,128)(2,1)S(1)}, u32[]{:S(2)}) copy-start(bf16[8,99,896]{2,1,0:T(8,128)(2,1)S(1)} %all-to-all-done.1.o_ref) | copy-start | bytes 4257796

commit v17 on v16

--- a/solution.py
+++ b/solution.py
@@ -130,7 +130,8 @@
 def _combine_kernel(o_ref, lse_ref, out_ref, *, group_size, head_size):
     stretch_count, local_tok, _ = out_ref.shape
     for c in range(stretch_count):
-        lse = lse_ref[:, c]
+        parts = [lse_ref[:, p, c].astype(jnp.float32) for p in range(3)]
+        lse = (parts[0] + parts[1]) + parts[2]
         top = jnp.max(lse, axis=0, keepdims=True)
         weights = jnp.exp(lse - top)
         total = jnp.sum(weights, axis=0)
@@ -145,7 +146,7 @@
 
 
 def combine_partials(received, lse, group_size, head_size):
-    _, stretch_count, local_tok, _ = lse.shape
+    _, _, stretch_count, local_tok, _ = lse.shape
     kern = functools.partial(_combine_kernel, group_size=group_size, head_size=head_size)
     return pl.pallas_call(
         kern,
@@ -304,11 +305,9 @@
     got_stats = (
         received[:, out_rows:, :]
         .reshape(seq_count, stat_rows * query_width)[:, :stat_count]
-        .astype(jnp.float32)
         .reshape(seq_count, 3, stretch_count, local_tok, group_size)
     )
-    got_lse = (got_stats[:, 0] + got_stats[:, 1]) + got_stats[:, 2]
-    stretch_out = combine_partials(received, got_lse, group_size, head_size)
+    stretch_out = combine_partials(received, got_stats, group_size, head_size)
     return (decode_mixed, stretch_out)
 
 

time: 105 us -> 105 us (level)
  no operation moved by 1% of the time
where the time goes in v17:
time: 105 us
  waiting for transfers between devices  27.6 us (26%)
  starting transfers between devices  23.2 us (22%)
  Pallas kernels  19.9 us (19%)
  blocking collectives  10.7 us (10%)
  other arithmetic  8.37 us (8%)
  local copies, waits for them, and re-layouts  7.34 us (7%)
  between operations  4.15 us (4%)
  matrix products  3.58 us (3%)
    all_to_all x1, waiting for transfers between devices, body(): received = lax.all_to_all(payload, 'seq', 0, 0, tiled=True)  20.8 us
    pallas_call x1, Pallas kernels, prefill_partial(): pl.pallas_call(kern, grid_spec=pltpu.PrefetchScalarGridSpec(num_scalar_pr...  16.8 us
    unnamed x1, blocking collectives  10.7 us
    ppermute x3, waiting for transfers between devices, broadcast_over_seq(): far_pieces = [lax.ppermute(partner, 'seq', perm) for perm in perms]  6.78 us
    all_to_all x1, starting transfers between devices, body(): received = lax.all_to_all(payload, 'seq', 0, 0, tiled=True)  6.14 us
    all_to_all x1, starting transfers between devices, body(): lax.all_to_all(jnp.broadcast_to(home_out[None], (seq_count,) + home_out.s...  4.95 us
    ppermute x3, starting transfers between devices, broadcast_over_seq(): near_pieces = [lax.ppermute(pack, 'seq', perm) for perm in perms]  4.5 us
    ppermute x1, starting transfers between devices, broadcast_over_seq(): lax.ppermute(pack, 'seq', [(i, (i + half) % seq_count) for i in range(seq...  4.1 us
  transfers between devices with their start and end apart: 9, of which 3 were waited for; matrix products, arithmetic and copies ran while one was open for 9% of the time, Pallas kernels for 16%

profile of v17, /device:TPU:0, one launch (start us, length us, event | category | flops | bytes accessed | tf_op | source)
XLA Modules:
  0.0 104.9 jit_solution(9016082697542035278)
XLA Ops:
  0.6 0.8 fusion.22
  1.4 1.0 pad_maximum_fusion.1
  2.4 4.1 %collective-permute-start = (bf16[98,896]{1,0:T(8,128)(2,1)S(1)}, bf16[98,896]{1,0:T(8,128)(2,1)S(1)}, u32[]{:S(2)}, u32[]{:S(2)}) collective-permute-start(bf16[98,896]{1,0:T(8,128)(2,1)S(1)} %pad_maximum_fusion.1), channel_id=1, source_target_pairs={{0,16},{4,20},{8,24},{12,28},{16,0},{20,4},{24,8},{28,12},{1,17},{... | collective-permute-start | bytes 526856 | tf_op jit(solution)/shard_map/ppermute | solution.py:166
  6.5 1.5 %collective-permute-start.1 = (bf16[98,896]{1,0:T(8,128)(2,1)S(1)}, bf16[98,896]{1,0:T(8,128)(2,1)S(1)}, u32[]{:S(2)}, u32[]{:S(2)}) collective-permute-start(bf16[98,896]{1,0:T(8,128)(2,1)S(1)} %pad_maximum_fusion.1), channel_id=1, source_target_pairs={{0,4},{4,8},{8,12},{12,0},{16,20},{20,24},{24,28},{28,16},{1,5},{5... | collective-permute-start | bytes 526856 | tf_op jit(solution)/shard_map/ppermute | solution.py:171
  8.0 1.6 %collective-permute-start.2 = (bf16[98,896]{1,0:T(8,128)(2,1)S(1)}, bf16[98,896]{1,0:T(8,128)(2,1)S(1)}, u32[]{:S(2)}, u32[]{:S(2)}) collective-permute-start(bf16[98,896]{1,0:T(8,128)(2,1)S(1)} %pad_maximum_fusion.1), channel_id=1, source_target_pairs={{0,8},{4,12},{8,0},{12,4},{16,24},{20,28},{24,16},{28,20},{1,9},{5... | collective-permute-start | bytes 526856 | tf_op jit(solution)/shard_map/ppermute | solution.py:171
  9.6 1.4 %collective-permute-start.3 = (bf16[98,896]{1,0:T(8,128)(2,1)S(1)}, bf16[98,896]{1,0:T(8,128)(2,1)S(1)}, u32[]{:S(2)}, u32[]{:S(2)}) collective-permute-start(bf16[98,896]{1,0:T(8,128)(2,1)S(1)} %pad_maximum_fusion.1), channel_id=1, source_target_pairs={{0,12},{4,0},{8,4},{12,8},{16,28},{20,16},{24,20},{28,24},{1,13},{... | collective-permute-start | bytes 526856 | tf_op jit(solution)/shard_map/ppermute | solution.py:171
  11.6 1.3 %compare_select_fusion.4 = (s32[8]{0:T(128)S(1)}, s32[]{:T(128)}) fusion(s32[8]{0:T(128)} %param.22, s32[]{:T(128)S(6)} %axis_index.15), kind=kLoop, calls=%fused_computation.57 | loop fusion | flops 47 | bytes 72 | tf_op jit(solution)/shard_map/jit(_take)/jit(_where)/select_n | solution.py:252
  16.9 1.0 bitcast_dynamic-update-slice_fusion.7
  19.1 2.4 %collective-permute-start.6 = (bf16[98,896]{1,0:T(8,128)(2,1)S(1)}, bf16[98,896]{1,0:T(8,128)(2,1)S(1)}, u32[]{:S(2)}, u32[]{:S(2)}) collective-permute-start(bf16[98,896]{1,0:T(8,128)(2,1)S(1)} %collective-permute-done), channel_id=1, source_target_pairs={{0,12},{4,0},{8,4},{12,8},{16,28},{20,16},{24,20},{28,24},{1,13},{... | collective-permute-start | bytes 526856 | tf_op jit(solution)/shard_map/ppermute | solution.py:172
  21.5 4.9 %collective-permute-done.4 = bf16[98,896]{1,0:T(8,128)(2,1)S(1)} collective-permute-done((bf16[98,896]{1,0:T(8,128)(2,1)S(1)}, bf16[98,896]{1,0:T(8,128)(2,1)S(1)}, u32[]{:S(2)}, u32[]{:S(2)}) %collective-permute-start.4) | collective-permute-done | bytes 175648 | tf_op jit(solution)/shard_map/ppermute | solution.py:172
  26.5 1.9 %collective-permute-done.6 = bf16[98,896]{1,0:T(8,128)(2,1)S(1)} collective-permute-done((bf16[98,896]{1,0:T(8,128)(2,1)S(1)}, bf16[98,896]{1,0:T(8,128)(2,1)S(1)}, u32[]{:S(2)}, u32[]{:S(2)}) %collective-permute-start.6) | collective-permute-done | bytes 175648 | tf_op jit(solution)/shard_map/ppermute | solution.py:172
  29.3 1.7 %fusion.42 = (f32[7]{0:T(128)S(1)}, f32[7,4097]{1,0:T(8,128)S(1)}) fusion(bf16[1,1,128]{2,1,0:T(2,128)(2,1)S(1)} %get-tuple-element.42, bf16[1,4096,128]{2,1,0:T(8,128)(2,1)} %param.19, bf16[896]{0:T(1024)(128)(2,1)S(1)} %fusion.21, pred[4097]{0:T(1024)(128)(4,1)S(1)} %add_reduce_fusion), kind=kOutput, calls=%fused_computation.121 | convolution fusion | flops 9525518 | bytes 1169465 | tf_op jit(solution)/shard_map/vmap()/dot_general | solution.py:16
  31.2 1.5 %fusion.2 = bf16[896]{0:T(1024)(128)(2,1)S(1)} fusion(bf16[1,1,128]{2,1,0:T(2,128)(2,1)S(1)} %get-tuple-element.43, bf16[1,4096,128]{2,1,0:T(8,128)(2,1)} %param.20, f32[7,4097]{1,0:T(8,128)S(1)} %get-tuple-element.41, f32[7]{0:T(128)S(1)} %get-tuple-element.40, pred[4097]{0:T(1024)(128)(4,1)S(1)} %add_reduce_fusion, f32[7]{0:T(128)S(1)} %fusion.11), kind=kOutput, calls=%fused_computation.6 | convolution fusion | flops 9527317 | bytes 1169493 | tf_op jit(solution)/shard_map/vmap()/dot_general | solution.py:21
  33.3 0.7 reduce.10
  34.0 0.7 reshape.402
  34.7 5.0 %all-to-all-start = ((bf16[8,2,448]{2,1,0:T(2,128)(2,1)}), bf16[8,2,448]{2,1,0:T(2,128)(2,1)S(1)}, u32[]{:S(2)}, u32[]{:S(2)}) async-start(bf16[8,2,448]{2,1,0:T(2,128)(2,1)} %reshape.402), calls=%async_computation | async-start | bytes 32768 | tf_op jit(solution)/shard_map/all_to_all | solution.py:249
  39.7 16.8 %shard_map.149 = (bf16[8,99,896]{2,1,0:T(8,128)(2,1)}, f32[8,3,32,7]{3,2,1,0:T(8,128)}) custom-call(s32[4]{0:T(128)} %pad_add_fusion.info_ref, s32[8]{0:T(128)} %get-tuple-element.30.order_ref, bf16[8,98,896]{2,1,0:T(8,128)(2,1)} %copy-done.2, bf16[3,1024,128]{2,1,0:T(8,128)(2,1)} %k_ref.1, bf16[3,1024,128]{2,1,0:T(8,128)(2,1)} %v_ref.1, ...), custom_call_target="tpu_custom_call" | custom-call | tf_op jit(solution)/shard_map/pallas_call | solution.py:100
  56.5 1.1 %fusion.9 = (bf16[8,1,3,32,7]{4,3,2,0,1:T(8,128)(2,1)S(1)}, bf16[8,1,3,32,7]{4,3,2,0,1:T(8,128)(2,1)S(1)}, bf16[8,1,3,32,7]{4,3,2,0,1:T(8,128)(2,1)S(1)}) fusion(f32[8,3,32,7]{3,2,1,0:T(8,128)} %get-tuple-element.6), kind=kLoop, calls=%fused_computation.20 | loop fusion | flops 37632 | bytes 53760 | tf_op jit(solution)/shard_map/stack | solution.py:296
  58.5 0.7 constant_dynamic-update-slice_fusion
  59.2 6.1 %all-to-all-start.1 = ((bf16[8,99,896]{2,1,0:T(8,128)(2,1)}), bf16[8,99,896]{2,1,0:T(8,128)(2,1)S(1)}, u32[]{:S(2)}, u32[]{:S(2)}) async-start(bf16[8,99,896]{2,1,0:T(8,128)(2,1)} %constant_dynamic-update-slice_fusion), calls=%async_computation.1 | async-start | bytes 2981888 | tf_op jit(solution)/shard_map/all_to_all | solution.py:304
  67.7 10.7 %all-reduce.2 = bf16[8,448]{1,0:T(8,128)(2,1)S(1)} all-reduce(f32[8,448]{1,0:T(8,128)S(1)} %fusion.17), channel_id=2, replica_groups=mesh['seq'=8,'tp'=4] {'tp'}, use_global_device_ids=true, to_apply=%region_3.5.clone | all-reduce | flops 3584 | bytes 21504
  79.0 20.8 %all-to-all-done.1.o_ref = bf16[8,99,896]{2,1,0:T(8,128)(2,1)S(1)} async-done(((bf16[8,99,896]{2,1,0:T(8,128)(2,1)}), bf16[8,99,896]{2,1,0:T(8,128)(2,1)S(1)}, u32[]{:S(2)}, u32[]{:S(2)}) %all-to-all-start.1) | async-done | bytes 1419296 | tf_op jit(solution)/shard_map/all_to_all | solution.py:304
  99.9 1.9 %reshape.313.lse_ref = bf16[8,3,3,32,7]{4,3,2,1,0:T(8,128)(2,1)} reshape(bf16[8,2016]{1,0:T(8,128)(2,1)S(1)} %slice.52) | data formatting | bytes 64512 | tf_op jit(solution)/shard_map/reshape | solution.py:308
  101.8 3.1 %shard_map.150 = bf16[3,32,896]{2,1,0:T(8,128)(2,1)} custom-call(bf16[8,99,896]{2,1,0:T(8,128)(2,1)} %copy-done.1, bf16[8,3,3,32,7]{4,3,2,1,0:T(8,128)(2,1)} %reshape.313.lse_ref), custom_call_target="tpu_custom_call" | custom-call | tf_op jit(solution)/shard_map/pallas_call | solution.py:151
  (59 shorter events, 8.1 us)
Async XLA Ops:
  0.6 66.7 %copy-start = (bf16[896,448]{0,1:T(8,128)(2,1)S(1)}, bf16[896,448]{0,1:T(8,128)(2,1)}, u32[]{:S(2)}) copy-start(bf16[896,448]{0,1:T(8,128)(2,1)} %param.23) | copy-start | bytes 2408452
  2.4 15.5 %collective-permute-start = (bf16[98,896]{1,0:T(8,128)(2,1)S(1)}, bf16[98,896]{1,0:T(8,128)(2,1)S(1)}, u32[]{:S(2)}, u32[]{:S(2)}) collective-permute-start(bf16[98,896]{1,0:T(8,128)(2,1)S(1)} %pad_maximum_fusion.1), channel_id=1, source_target_pairs={{0,16},{4,20},{8,24},{12,28},{16,0},{20,4},{24,8},{28,12},{1,17},{... | collective-permute-start | bytes 526856 | tf_op jit(solution)/shard_map/ppermute | solution.py:166
  6.5 12.6 %collective-permute-start.1 = (bf16[98,896]{1,0:T(8,128)(2,1)S(1)}, bf16[98,896]{1,0:T(8,128)(2,1)S(1)}, u32[]{:S(2)}, u32[]{:S(2)}) collective-permute-start(bf16[98,896]{1,0:T(8,128)(2,1)S(1)} %pad_maximum_fusion.1), channel_id=1, source_target_pairs={{0,4},{4,8},{8,12},{12,0},{16,20},{20,24},{24,28},{28,16},{1,5},{5... | collective-permute-start | bytes 526856 | tf_op jit(solution)/shard_map/ppermute | solution.py:171
  8.0 13.5 %collective-permute-start.2 = (bf16[98,896]{1,0:T(8,128)(2,1)S(1)}, bf16[98,896]{1,0:T(8,128)(2,1)S(1)}, u32[]{:S(2)}, u32[]{:S(2)}) collective-permute-start(bf16[98,896]{1,0:T(8,128)(2,1)S(1)} %pad_maximum_fusion.1), channel_id=1, source_target_pairs={{0,8},{4,12},{8,0},{12,4},{16,24},{20,28},{24,16},{28,20},{1,9},{5... | collective-permute-start | bytes 526856 | tf_op jit(solution)/shard_map/ppermute | solution.py:171
  9.6 11.9 %collective-permute-start.3 = (bf16[98,896]{1,0:T(8,128)(2,1)S(1)}, bf16[98,896]{1,0:T(8,128)(2,1)S(1)}, u32[]{:S(2)}, u32[]{:S(2)}) collective-permute-start(bf16[98,896]{1,0:T(8,128)(2,1)S(1)} %pad_maximum_fusion.1), channel_id=1, source_target_pairs={{0,12},{4,0},{8,4},{12,8},{16,28},{20,16},{24,20},{28,24},{1,13},{... | collective-permute-start | bytes 526856 | tf_op jit(solution)/shard_map/ppermute | solution.py:171
  17.9 8.5 %collective-permute-start.4 = (bf16[98,896]{1,0:T(8,128)(2,1)S(1)}, bf16[98,896]{1,0:T(8,128)(2,1)S(1)}, u32[]{:S(2)}, u32[]{:S(2)}) collective-permute-start(bf16[98,896]{1,0:T(8,128)(2,1)S(1)} %collective-permute-done), channel_id=1, source_target_pairs={{0,4},{4,8},{8,12},{12,0},{16,20},{20,24},{24,28},{28,16},{1,5},{5... | collective-permute-start | bytes 526856 | tf_op jit(solution)/shard_map/ppermute | solution.py:172
  18.6 7.9 %collective-permute-start.5 = (bf16[98,896]{1,0:T(8,128)(2,1)S(1)}, bf16[98,896]{1,0:T(8,128)(2,1)S(1)}, u32[]{:S(2)}, u32[]{:S(2)}) collective-permute-start(bf16[98,896]{1,0:T(8,128)(2,1)S(1)} %collective-permute-done), channel_id=1, source_target_pairs={{0,8},{4,12},{8,0},{12,4},{16,24},{20,28},{24,16},{28,20},{1,9},{5... | collective-permute-start | bytes 526856 | tf_op jit(solution)/shard_map/ppermute | solution.py:172
  19.1 9.3 %collective-permute-start.6 = (bf16[98,896]{1,0:T(8,128)(2,1)S(1)}, bf16[98,896]{1,0:T(8,128)(2,1)S(1)}, u32[]{:S(2)}, u32[]{:S(2)}) collective-permute-start(bf16[98,896]{1,0:T(8,128)(2,1)S(1)} %collective-permute-done), channel_id=1, source_target_pairs={{0,12},{4,0},{8,4},{12,8},{16,28},{20,16},{24,20},{28,24},{1,13},{... | collective-permute-start | bytes 526856 | tf_op jit(solution)/shard_map/ppermute | solution.py:172
  28.4 4.4 %copy-start.2 = (bf16[8,98,896]{2,1,0:T(8,128)(2,1)}, bf16[8,98,896]{2,1,0:T(8,128)(2,1)S(1)}, u32[]{:S(2)}) copy-start(bf16[8,98,896]{2,1,0:T(8,128)(2,1)S(1)} %bitcast_dynamic-update-slice_fusion.q_hbm) | copy-start | bytes 4214788
  34.7 24.5 %all-to-all-start = ((bf16[8,2,448]{2,1,0:T(2,128)(2,1)}), bf16[8,2,448]{2,1,0:T(2,128)(2,1)S(1)}, u32[]{:S(2)}, u32[]{:S(2)}) async-start(bf16[8,2,448]{2,1,0:T(2,128)(2,1)} %reshape.402), calls=%async_computation | async-start | bytes 32768 | tf_op jit(solution)/shard_map/all_to_all | solution.py:249
  59.2 6.1 %copy-start.4 = (u32[32]{0:T(128)S(1)}, u32[32]{0:T(128)}, u32[]{:S(2)}) copy-start(u32[32]{0:T(128)} %constant.216) | copy-start | bytes 388
  59.2 7.4 %copy-start.3 = (s32[8]{0:T(128)S(1)}, s32[8]{0:T(128)}, u32[]{:S(2)}) copy-start(s32[8]{0:T(128)} %param.22) | copy-start | bytes 100
  59.2 40.6 %all-to-all-start.1 = ((bf16[8,99,896]{2,1,0:T(8,128)(2,1)}), bf16[8,99,896]{2,1,0:T(8,128)(2,1)S(1)}, u32[]{:S(2)}, u32[]{:S(2)}) async-start(bf16[8,99,896]{2,1,0:T(8,128)(2,1)} %constant_dynamic-update-slice_fusion), calls=%async_computation.1 | async-start | bytes 2981888 | tf_op jit(solution)/shard_map/all_to_all | solution.py:304
  99.8 2.0 %copy-start.1 = (bf16[8,99,896]{2,1,0:T(8,128)(2,1)}, bf16[8,99,896]{2,1,0:T(8,128)(2,1)S(1)}, u32[]{:S(2)}) copy-start(bf16[8,99,896]{2,1,0:T(8,128)(2,1)S(1)} %all-to-all-done.1.o_ref) | copy-start | bytes 4257796

commit v18 on v16

--- a/solution.py
+++ b/solution.py
@@ -231,16 +231,24 @@
     cache_pos = jnp.arange(cache_span, dtype=jnp.int32)
 
     def decode_slot(query_row, own_key, own_value, cached_keys, cached_values, length):
-        key_all = jnp.concatenate([cached_keys, own_key[None, :]], axis=0)
-        value_all = jnp.concatenate([cached_values, own_value[None, :]], axis=0)
-        visible = jnp.concatenate([cache_pos < length, jnp.ones((1,), dtype=jnp.bool_)])
-        visible = jnp.broadcast_to(visible[None, :], (group_size, cache_span + 1))
-        row_top, weight_sum, numerator = partial_attend(
-            query_row.reshape(group_size, head_size), key_all, value_all, visible
-        )
-        return (
-            (numerator / weight_sum[:, None]).astype(jnp.bfloat16).reshape(group_size * head_size)
-        )
+        factor = 1.0 / math.sqrt(head_size)
+        queries = query_row.reshape(group_size, head_size)
+        visible = (cache_pos < length)[None, :]
+        scores = jnp.dot(queries, cached_keys.T, preferred_element_type=jnp.float32) * factor
+        scores = jnp.where(visible, scores, NEG_FILL)
+        own_score = (
+            jnp.dot(queries, own_key[:, None], preferred_element_type=jnp.float32) * factor
+        )
+        row_top = jnp.maximum(jnp.max(scores, axis=1, keepdims=True), own_score)
+        weights = jnp.where(visible, jnp.exp(scores - row_top), 0.0)
+        own_weight = jnp.exp(own_score - row_top)
+        weight_sum = jnp.sum(weights, axis=1, keepdims=True) + own_weight
+        numerator = jnp.dot(
+            weights.astype(jnp.bfloat16), cached_values, preferred_element_type=jnp.float32
+        ) + lax.reduce_precision(own_weight, exponent_bits=8, mantissa_bits=7) * own_value.astype(
+            jnp.float32
+        )
+        return (numerator / weight_sum).astype(jnp.bfloat16).reshape(group_size * head_size)
 
     home_out = jax.vmap(decode_slot)(
         home_query, home_key, home_value, cache_keys, cache_values, cache_length

time: 105 us -> 105 us (level)
  matrix products: 3.58 us -> 1.25 us
  local copies, waits for them, and re-layouts: 6.44 us -> 7.56 us
  other arithmetic: 9.22 us -> 10.3 us
    dot_general x2 -> x3, matrix products: 3.25 us -> 0.92 us  [the longest x1 0.49 us: decode_slot(): jnp.dot(queries, cached_keys.T, preferred_element_type=jnp.float32) * factor]
    add x1, other arithmetic: 0.84 us -> 2.1 us  [body(): got_lse = got_stats[:, 0] + got_stats[:, 1] + got_stats[:, 2]]
where the time goes in v18:
time: 105 us
  waiting for transfers between devices  27.6 us (26%)
  starting transfers between devices  23.4 us (22%)
  Pallas kernels  19.8 us (19%)
  blocking collectives  10.7 us (10%)
  other arithmetic  10.3 us (10%)
  local copies, waits for them, and re-layouts  7.56 us (7%)
  between operations  4.18 us (4%)
  matrix products  1.25 us (1%)
    all_to_all x1, waiting for transfers between devices, body(): received = lax.all_to_all(payload, 'seq', 0, 0, tiled=True)  20.8 us
    pallas_call x1, Pallas kernels, prefill_partial(): pl.pallas_call(kern, grid_spec=pltpu.PrefetchScalarGridSpec(num_scalar_pr...  16.8 us
    unnamed x1, blocking collectives  10.7 us
    ppermute x3, waiting for transfers between devices, broadcast_over_seq(): far_pieces = [lax.ppermute(partner, 'seq', perm) for perm in perms]  6.79 us
    all_to_all x1, starting transfers between devices, body(): received = lax.all_to_all(payload, 'seq', 0, 0, tiled=True)  6.15 us
    all_to_all x1, starting transfers between devices, body(): lax.all_to_all(jnp.broadcast_to(home_out[None], (seq_count,) + home_out.s...  5.17 us
    ppermute x3, starting transfers between devices, broadcast_over_seq(): near_pieces = [lax.ppermute(pack, 'seq', perm) for perm in perms]  4.5 us
    ppermute x1, starting transfers between devices, broadcast_over_seq(): lax.ppermute(pack, 'seq', [(i, (i + half) % seq_count) for i in range(seq...  4.1 us
  transfers between devices with their start and end apart: 9, of which 3 were waited for; matrix products, arithmetic and copies ran while one was open for 9% of the time, Pallas kernels for 16%

profile of v18, /device:TPU:0, one launch (start us, length us, event | category | flops | bytes accessed | tf_op | source)
XLA Modules:
  0.0 104.8 jit_solution(12726735022492619439)
XLA Ops:
  0.6 0.8 fusion.25
  1.4 1.0 pad_maximum_fusion.1
  2.4 4.1 %collective-permute-start = (bf16[98,896]{1,0:T(8,128)(2,1)S(1)}, bf16[98,896]{1,0:T(8,128)(2,1)S(1)}, u32[]{:S(2)}, u32[]{:S(2)}) collective-permute-start(bf16[98,896]{1,0:T(8,128)(2,1)S(1)} %pad_maximum_fusion.1), channel_id=1, source_target_pairs={{0,16},{4,20},{8,24},{12,28},{16,0},{20,4},{24,8},{28,12},{1,17},{... | collective-permute-start | bytes 526856 | tf_op jit(solution)/shard_map/ppermute | solution.py:165
  6.5 1.5 %collective-permute-start.1 = (bf16[98,896]{1,0:T(8,128)(2,1)S(1)}, bf16[98,896]{1,0:T(8,128)(2,1)S(1)}, u32[]{:S(2)}, u32[]{:S(2)}) collective-permute-start(bf16[98,896]{1,0:T(8,128)(2,1)S(1)} %pad_maximum_fusion.1), channel_id=1, source_target_pairs={{0,4},{4,8},{8,12},{12,0},{16,20},{20,24},{24,28},{28,16},{1,5},{5... | collective-permute-start | bytes 526856 | tf_op jit(solution)/shard_map/ppermute | solution.py:170
  8.0 1.6 %collective-permute-start.2 = (bf16[98,896]{1,0:T(8,128)(2,1)S(1)}, bf16[98,896]{1,0:T(8,128)(2,1)S(1)}, u32[]{:S(2)}, u32[]{:S(2)}) collective-permute-start(bf16[98,896]{1,0:T(8,128)(2,1)S(1)} %pad_maximum_fusion.1), channel_id=1, source_target_pairs={{0,8},{4,12},{8,0},{12,4},{16,24},{20,28},{24,16},{28,20},{1,9},{5... | collective-permute-start | bytes 526856 | tf_op jit(solution)/shard_map/ppermute | solution.py:170
  9.6 1.4 %collective-permute-start.3 = (bf16[98,896]{1,0:T(8,128)(2,1)S(1)}, bf16[98,896]{1,0:T(8,128)(2,1)S(1)}, u32[]{:S(2)}, u32[]{:S(2)}) collective-permute-start(bf16[98,896]{1,0:T(8,128)(2,1)S(1)} %pad_maximum_fusion.1), channel_id=1, source_target_pairs={{0,12},{4,0},{8,4},{12,8},{16,28},{20,16},{24,20},{28,24},{1,13},{... | collective-permute-start | bytes 526856 | tf_op jit(solution)/shard_map/ppermute | solution.py:170
  11.6 1.3 %compare_select_fusion.4 = (s32[8]{0:T(128)S(1)}, s32[]{:T(128)}) fusion(s32[8]{0:T(128)} %param.22, s32[]{:T(128)S(6)} %axis_index.15), kind=kLoop, calls=%fused_computation.62 | loop fusion | flops 47 | bytes 72 | tf_op jit(solution)/shard_map/jit(_take)/jit(_where)/select_n | solution.py:259
  15.5 0.7 subtract_clamp_fusion
  16.7 1.0 bitcast_dynamic-update-slice_fusion.7
  17.7 0.7 collective-permute-start.4
  18.8 2.4 %collective-permute-start.6 = (bf16[98,896]{1,0:T(8,128)(2,1)S(1)}, bf16[98,896]{1,0:T(8,128)(2,1)S(1)}, u32[]{:S(2)}, u32[]{:S(2)}) collective-permute-start(bf16[98,896]{1,0:T(8,128)(2,1)S(1)} %collective-permute-done), channel_id=1, source_target_pairs={{0,12},{4,0},{8,4},{12,8},{16,28},{20,16},{24,20},{28,24},{1,13},{... | collective-permute-start | bytes 526856 | tf_op jit(solution)/shard_map/ppermute | solution.py:171
  21.3 5.0 %collective-permute-done.4 = bf16[98,896]{1,0:T(8,128)(2,1)S(1)} collective-permute-done((bf16[98,896]{1,0:T(8,128)(2,1)S(1)}, bf16[98,896]{1,0:T(8,128)(2,1)S(1)}, u32[]{:S(2)}, u32[]{:S(2)}) %collective-permute-start.4) | collective-permute-done | bytes 175648 | tf_op jit(solution)/shard_map/ppermute | solution.py:171
  26.3 1.8 %collective-permute-done.6 = bf16[98,896]{1,0:T(8,128)(2,1)S(1)} collective-permute-done((bf16[98,896]{1,0:T(8,128)(2,1)S(1)}, bf16[98,896]{1,0:T(8,128)(2,1)S(1)}, u32[]{:S(2)}, u32[]{:S(2)}) %collective-permute-start.6) | collective-permute-done | bytes 175648 | tf_op jit(solution)/shard_map/ppermute | solution.py:171
  30.9 0.7 reduce.8
  31.6 0.7 reshape.439
  32.3 5.2 %all-to-all-start = ((bf16[8,2,448]{2,1,0:T(2,128)(2,1)}), bf16[8,2,448]{2,1,0:T(2,128)(2,1)S(1)}, u32[]{:S(2)}, u32[]{:S(2)}) async-start(bf16[8,2,448]{2,1,0:T(2,128)(2,1)} %reshape.439), calls=%async_computation | async-start | bytes 32768 | tf_op jit(solution)/shard_map/all_to_all | solution.py:256
  37.5 16.8 %shard_map.149 = (bf16[8,99,896]{2,1,0:T(8,128)(2,1)}, f32[8,3,32,7]{3,2,1,0:T(8,128)}) custom-call(s32[4]{0:T(128)} %pad_add_fusion.info_ref, s32[8]{0:T(128)} %get-tuple-element.32.order_ref, bf16[8,98,896]{2,1,0:T(8,128)(2,1)} %copy-done.2, bf16[3,1024,128]{2,1,0:T(8,128)(2,1)} %k_ref.1, bf16[3,1024,128]{2,1,0:T(8,128)(2,1)} %v_ref.1, ...), custom_call_target="tpu_custom_call" | custom-call | tf_op jit(solution)/shard_map/pallas_call | solution.py:100
  54.3 1.1 %fusion.12 = (bf16[8,1,3,32,7]{4,3,2,0,1:T(8,128)(2,1)S(1)}, bf16[8,1,3,32,7]{4,3,2,0,1:T(8,128)(2,1)S(1)}, bf16[8,1,3,32,7]{4,3,2,0,1:T(8,128)(2,1)S(1)}) fusion(f32[8,3,32,7]{3,2,1,0:T(8,128)} %get-tuple-element.6), kind=kLoop, calls=%fused_computation.25 | loop fusion | flops 37632 | bytes 53760 | tf_op jit(solution)/shard_map/stack | solution.py:303
  57.0 6.1 %all-to-all-start.1 = ((bf16[8,99,896]{2,1,0:T(8,128)(2,1)}), bf16[8,99,896]{2,1,0:T(8,128)(2,1)S(1)}, u32[]{:S(2)}, u32[]{:S(2)}) async-start(bf16[8,99,896]{2,1,0:T(8,128)(2,1)} %constant_dynamic-update-slice_fusion), calls=%async_computation.1 | async-start | bytes 2981888 | tf_op jit(solution)/shard_map/all_to_all | solution.py:311
  65.4 10.7 %all-reduce.2 = bf16[8,448]{1,0:T(8,128)(2,1)S(1)} all-reduce(f32[8,448]{1,0:T(8,128)S(1)} %fusion.20), channel_id=2, replica_groups=mesh['seq'=8,'tp'=4] {'tp'}, use_global_device_ids=true, to_apply=%region_3.5.clone | all-reduce | flops 3584 | bytes 21504
  76.7 20.8 %all-to-all-done.1.o_ref = bf16[8,99,896]{2,1,0:T(8,128)(2,1)S(1)} async-done(((bf16[8,99,896]{2,1,0:T(8,128)(2,1)}), bf16[8,99,896]{2,1,0:T(8,128)(2,1)S(1)}, u32[]{:S(2)}, u32[]{:S(2)}) %all-to-all-start.1) | async-done | bytes 1419296 | tf_op jit(solution)/shard_map/all_to_all | solution.py:311
  97.6 2.1 %reshape.388 = f32[8,3,3,32,7]{4,3,2,1,0:T(8,128)} reshape(f32[8,2016]{1,0:T(8,128)S(1)} %slice_convert_fusion) | data formatting | bytes 129024 | tf_op jit(solution)/shard_map/reshape | solution.py:316
  99.7 2.1 %fusion.9.lse_ref = f32[8,3,32,7]{3,2,1,0:T(8,128)} fusion(f32[8,3,3,32,7]{4,3,2,1,0:T(8,128)} %reshape.388), kind=kLoop, calls=%fused_computation.20 | loop fusion | flops 10752 | bytes 86016 | tf_op jit(solution)/shard_map/add | solution.py:318
  101.8 3.0 %shard_map.150 = bf16[3,32,896]{2,1,0:T(8,128)(2,1)} custom-call(bf16[8,99,896]{2,1,0:T(8,128)(2,1)} %copy-done.1, f32[8,3,32,7]{3,2,1,0:T(8,128)} %fusion.9.lse_ref), custom_call_target="tpu_custom_call" | custom-call | tf_op jit(solution)/shard_map/pallas_call | solution.py:150
  (65 shorter events, 8.2 us)
Async XLA Ops:
  0.6 28.4 %copy-start = (bf16[1,4096,128]{2,1,0:T(8,128)(2,1)S(1)}, bf16[1,4096,128]{2,1,0:T(8,128)(2,1)}, u32[]{:S(2)}) copy-start(bf16[1,4096,128]{2,1,0:T(8,128)(2,1)} %param.19) | copy-start | bytes 3145732
  2.4 15.3 %collective-permute-start = (bf16[98,896]{1,0:T(8,128)(2,1)S(1)}, bf16[98,896]{1,0:T(8,128)(2,1)S(1)}, u32[]{:S(2)}, u32[]{:S(2)}) collective-permute-start(bf16[98,896]{1,0:T(8,128)(2,1)S(1)} %pad_maximum_fusion.1), channel_id=1, source_target_pairs={{0,16},{4,20},{8,24},{12,28},{16,0},{20,4},{24,8},{28,12},{1,17},{... | collective-permute-start | bytes 526856 | tf_op jit(solution)/shard_map/ppermute | solution.py:165
  6.5 12.4 %collective-permute-start.1 = (bf16[98,896]{1,0:T(8,128)(2,1)S(1)}, bf16[98,896]{1,0:T(8,128)(2,1)S(1)}, u32[]{:S(2)}, u32[]{:S(2)}) collective-permute-start(bf16[98,896]{1,0:T(8,128)(2,1)S(1)} %pad_maximum_fusion.1), channel_id=1, source_target_pairs={{0,4},{4,8},{8,12},{12,0},{16,20},{20,24},{24,28},{28,16},{1,5},{5... | collective-permute-start | bytes 526856 | tf_op jit(solution)/shard_map/ppermute | solution.py:170
  8.0 13.2 %collective-permute-start.2 = (bf16[98,896]{1,0:T(8,128)(2,1)S(1)}, bf16[98,896]{1,0:T(8,128)(2,1)S(1)}, u32[]{:S(2)}, u32[]{:S(2)}) collective-permute-start(bf16[98,896]{1,0:T(8,128)(2,1)S(1)} %pad_maximum_fusion.1), channel_id=1, source_target_pairs={{0,8},{4,12},{8,0},{12,4},{16,24},{20,28},{24,16},{28,20},{1,9},{5... | collective-permute-start | bytes 526856 | tf_op jit(solution)/shard_map/ppermute | solution.py:170
  9.6 11.7 %collective-permute-start.3 = (bf16[98,896]{1,0:T(8,128)(2,1)S(1)}, bf16[98,896]{1,0:T(8,128)(2,1)S(1)}, u32[]{:S(2)}, u32[]{:S(2)}) collective-permute-start(bf16[98,896]{1,0:T(8,128)(2,1)S(1)} %pad_maximum_fusion.1), channel_id=1, source_target_pairs={{0,12},{4,0},{8,4},{12,8},{16,28},{20,16},{24,20},{28,24},{1,13},{... | collective-permute-start | bytes 526856 | tf_op jit(solution)/shard_map/ppermute | solution.py:170
  17.7 8.6 %collective-permute-start.4 = (bf16[98,896]{1,0:T(8,128)(2,1)S(1)}, bf16[98,896]{1,0:T(8,128)(2,1)S(1)}, u32[]{:S(2)}, u32[]{:S(2)}) collective-permute-start(bf16[98,896]{1,0:T(8,128)(2,1)S(1)} %collective-permute-done), channel_id=1, source_target_pairs={{0,4},{4,8},{8,12},{12,0},{16,20},{20,24},{24,28},{28,16},{1,5},{5... | collective-permute-start | bytes 526856 | tf_op jit(solution)/shard_map/ppermute | solution.py:171
  18.4 7.9 %collective-permute-start.5 = (bf16[98,896]{1,0:T(8,128)(2,1)S(1)}, bf16[98,896]{1,0:T(8,128)(2,1)S(1)}, u32[]{:S(2)}, u32[]{:S(2)}) collective-permute-start(bf16[98,896]{1,0:T(8,128)(2,1)S(1)} %collective-permute-done), channel_id=1, source_target_pairs={{0,8},{4,12},{8,0},{12,4},{16,24},{20,28},{24,16},{28,20},{1,9},{5... | collective-permute-start | bytes 526856 | tf_op jit(solution)/shard_map/ppermute | solution.py:171
  18.8 9.3 %collective-permute-start.6 = (bf16[98,896]{1,0:T(8,128)(2,1)S(1)}, bf16[98,896]{1,0:T(8,128)(2,1)S(1)}, u32[]{:S(2)}, u32[]{:S(2)}) collective-permute-start(bf16[98,896]{1,0:T(8,128)(2,1)S(1)} %collective-permute-done), channel_id=1, source_target_pairs={{0,12},{4,0},{8,4},{12,8},{16,28},{20,16},{24,20},{28,24},{1,13},{... | collective-permute-start | bytes 526856 | tf_op jit(solution)/shard_map/ppermute | solution.py:171
  28.2 4.2 %copy-start.2 = (bf16[8,98,896]{2,1,0:T(8,128)(2,1)}, bf16[8,98,896]{2,1,0:T(8,128)(2,1)S(1)}, u32[]{:S(2)}) copy-start(bf16[8,98,896]{2,1,0:T(8,128)(2,1)S(1)} %bitcast_dynamic-update-slice_fusion.q_hbm) | copy-start | bytes 4214788
  28.8 1.2 %copy-start.3 = (bf16[1,4096,128]{2,1,0:T(8,128)(2,1)S(1)}, bf16[1,4096,128]{2,1,0:T(8,128)(2,1)}, u32[]{:S(2)}) copy-start(bf16[1,4096,128]{2,1,0:T(8,128)(2,1)} %param.20) | copy-start | bytes 3145732
  32.3 24.6 %all-to-all-start = ((bf16[8,2,448]{2,1,0:T(2,128)(2,1)}), bf16[8,2,448]{2,1,0:T(2,128)(2,1)S(1)}, u32[]{:S(2)}, u32[]{:S(2)}) async-start(bf16[8,2,448]{2,1,0:T(2,128)(2,1)} %reshape.439), calls=%async_computation | async-start | bytes 32768 | tf_op jit(solution)/shard_map/all_to_all | solution.py:256
  57.0 6.2 %copy-start.6 = (u32[32]{0:T(128)S(1)}, u32[32]{0:T(128)}, u32[]{:S(2)}) copy-start(u32[32]{0:T(128)} %constant.215) | copy-start | bytes 388
  57.0 7.4 %copy-start.5 = (s32[8]{0:T(128)S(1)}, s32[8]{0:T(128)}, u32[]{:S(2)}) copy-start(s32[8]{0:T(128)} %param.22) | copy-start | bytes 100
  57.0 8.1 %copy-start.4 = (bf16[896,448]{0,1:T(8,128)(2,1)S(1)}, bf16[896,448]{0,1:T(8,128)(2,1)}, u32[]{:S(2)}) copy-start(bf16[896,448]{0,1:T(8,128)(2,1)} %param.23) | copy-start | bytes 2408452
  57.0 40.6 %all-to-all-start.1 = ((bf16[8,99,896]{2,1,0:T(8,128)(2,1)}), bf16[8,99,896]{2,1,0:T(8,128)(2,1)S(1)}, u32[]{:S(2)}, u32[]{:S(2)}) async-start(bf16[8,99,896]{2,1,0:T(8,128)(2,1)} %constant_dynamic-update-slice_fusion), calls=%async_computation.1 | async-start | bytes 2981888 | tf_op jit(solution)/shard_map/all_to_all | solution.py:311
  97.5 4.2 %copy-start.1 = (bf16[8,99,896]{2,1,0:T(8,128)(2,1)}, bf16[8,99,896]{2,1,0:T(8,128)(2,1)S(1)}, u32[]{:S(2)}) copy-start(bf16[8,99,896]{2,1,0:T(8,128)(2,1)S(1)} %all-to-all-done.1.o_ref) | copy-start | bytes 4257796

commit v19 on v16

--- a/solution.py
+++ b/solution.py
@@ -145,13 +145,23 @@
 
 
 def combine_partials(received, lse, group_size, head_size):
-    _, stretch_count, local_tok, _ = lse.shape
+    src_count, stretch_count, local_tok, _ = lse.shape
     kern = functools.partial(_combine_kernel, group_size=group_size, head_size=head_size)
+    out_shape = jax.ShapeDtypeStruct(
+        (stretch_count, local_tok, group_size * head_size), jnp.bfloat16
+    )
+    if local_tok % 16:
+        return pl.pallas_call(kern, out_shape=out_shape)(received, lse)
+    width = received.shape[2]
     return pl.pallas_call(
         kern,
-        out_shape=jax.ShapeDtypeStruct(
-            (stretch_count, local_tok, group_size * head_size), jnp.bfloat16
-        ),
+        grid=(stretch_count,),
+        in_specs=[
+            pl.BlockSpec((src_count, local_tok, width), lambda c: (0, c, 0)),
+            pl.BlockSpec((src_count, 1, local_tok, group_size), lambda c: (0, c, 0, 0)),
+        ],
+        out_specs=pl.BlockSpec((1, local_tok, width), lambda c: (c, 0, 0)),
+        out_shape=out_shape,
     )(received, lse)
 
 

time: 105 us -> 106 us (level)
  no operation moved by 1% of the time
where the time goes in v19:
time: 106 us; the launch traced here: 105 us
  waiting for transfers between devices  27.6 us (26%)
  starting transfers between devices  23.2 us (22%)
  Pallas kernels  20.3 us (19%)
  blocking collectives  10.7 us (10%)
  other arithmetic  9.22 us (9%)
  local copies, waits for them, and re-layouts  6.44 us (6%)
  between operations  4.16 us (4%)
  matrix products  3.58 us (3%)
    all_to_all x1, waiting for transfers between devices, body(): received = lax.all_to_all(payload, 'seq', 0, 0, tiled=True)  20.8 us
    pallas_call x1, Pallas kernels, prefill_partial(): pl.pallas_call(kern, grid_spec=pltpu.PrefetchScalarGridSpec(num_scalar_pr...  16.8 us
    unnamed x1, blocking collectives  10.7 us
    ppermute x3, waiting for transfers between devices, broadcast_over_seq(): far_pieces = [lax.ppermute(partner, 'seq', perm) for perm in perms]  6.78 us
    all_to_all x1, starting transfers between devices, body(): received = lax.all_to_all(payload, 'seq', 0, 0, tiled=True)  6.13 us
    all_to_all x1, starting transfers between devices, body(): lax.all_to_all(jnp.broadcast_to(home_out[None], (seq_count,) + home_out.s...  4.95 us
    ppermute x3, starting transfers between devices, broadcast_over_seq(): near_pieces = [lax.ppermute(pack, 'seq', perm) for perm in perms]  4.5 us
    ppermute x1, starting transfers between devices, broadcast_over_seq(): lax.ppermute(pack, 'seq', [(i, (i + half) % seq_count) for i in range(seq...  4.1 us
  transfers between devices with their start and end apart: 9, of which 3 were waited for; matrix products, arithmetic and copies ran while one was open for 9% of the time, Pallas kernels for 16%

profile of v19, /device:TPU:0, one launch (start us, length us, event | category | flops | bytes accessed | tf_op | source)
XLA Modules:
  0.0 105.2 jit_solution(1561738276820297374)
XLA Ops:
  0.6 0.8 fusion.25
  1.4 1.0 pad_maximum_fusion.1
  2.4 4.1 %collective-permute-start = (bf16[98,896]{1,0:T(8,128)(2,1)S(1)}, bf16[98,896]{1,0:T(8,128)(2,1)S(1)}, u32[]{:S(2)}, u32[]{:S(2)}) collective-permute-start(bf16[98,896]{1,0:T(8,128)(2,1)S(1)} %pad_maximum_fusion.1), channel_id=1, source_target_pairs={{0,16},{4,20},{8,24},{12,28},{16,0},{20,4},{24,8},{28,12},{1,17},{... | collective-permute-start | bytes 526856 | tf_op jit(solution)/shard_map/ppermute | solution.py:175
  6.5 1.5 %collective-permute-start.1 = (bf16[98,896]{1,0:T(8,128)(2,1)S(1)}, bf16[98,896]{1,0:T(8,128)(2,1)S(1)}, u32[]{:S(2)}, u32[]{:S(2)}) collective-permute-start(bf16[98,896]{1,0:T(8,128)(2,1)S(1)} %pad_maximum_fusion.1), channel_id=1, source_target_pairs={{0,4},{4,8},{8,12},{12,0},{16,20},{20,24},{24,28},{28,16},{1,5},{5... | collective-permute-start | bytes 526856 | tf_op jit(solution)/shard_map/ppermute | solution.py:180
  8.0 1.6 %collective-permute-start.2 = (bf16[98,896]{1,0:T(8,128)(2,1)S(1)}, bf16[98,896]{1,0:T(8,128)(2,1)S(1)}, u32[]{:S(2)}, u32[]{:S(2)}) collective-permute-start(bf16[98,896]{1,0:T(8,128)(2,1)S(1)} %pad_maximum_fusion.1), channel_id=1, source_target_pairs={{0,8},{4,12},{8,0},{12,4},{16,24},{20,28},{24,16},{28,20},{1,9},{5... | collective-permute-start | bytes 526856 | tf_op jit(solution)/shard_map/ppermute | solution.py:180
  9.6 1.4 %collective-permute-start.3 = (bf16[98,896]{1,0:T(8,128)(2,1)S(1)}, bf16[98,896]{1,0:T(8,128)(2,1)S(1)}, u32[]{:S(2)}, u32[]{:S(2)}) collective-permute-start(bf16[98,896]{1,0:T(8,128)(2,1)S(1)} %pad_maximum_fusion.1), channel_id=1, source_target_pairs={{0,12},{4,0},{8,4},{12,8},{16,28},{20,16},{24,20},{28,24},{1,13},{... | collective-permute-start | bytes 526856 | tf_op jit(solution)/shard_map/ppermute | solution.py:180
  11.6 1.3 %compare_select_fusion.4 = (s32[8]{0:T(128)S(1)}, s32[]{:T(128)}) fusion(s32[8]{0:T(128)} %param.22, s32[]{:T(128)S(6)} %axis_index.15), kind=kLoop, calls=%fused_computation.64 | loop fusion | flops 47 | bytes 72 | tf_op jit(solution)/shard_map/jit(_take)/jit(_where)/select_n | solution.py:261
  16.9 1.0 bitcast_dynamic-update-slice_fusion.7
  19.1 2.4 %collective-permute-start.6 = (bf16[98,896]{1,0:T(8,128)(2,1)S(1)}, bf16[98,896]{1,0:T(8,128)(2,1)S(1)}, u32[]{:S(2)}, u32[]{:S(2)}) collective-permute-start(bf16[98,896]{1,0:T(8,128)(2,1)S(1)} %collective-permute-done), channel_id=1, source_target_pairs={{0,12},{4,0},{8,4},{12,8},{16,28},{20,16},{24,20},{28,24},{1,13},{... | collective-permute-start | bytes 526856 | tf_op jit(solution)/shard_map/ppermute | solution.py:181
  21.5 4.9 %collective-permute-done.4 = bf16[98,896]{1,0:T(8,128)(2,1)S(1)} collective-permute-done((bf16[98,896]{1,0:T(8,128)(2,1)S(1)}, bf16[98,896]{1,0:T(8,128)(2,1)S(1)}, u32[]{:S(2)}, u32[]{:S(2)}) %collective-permute-start.4) | collective-permute-done | bytes 175648 | tf_op jit(solution)/shard_map/ppermute | solution.py:181
  26.5 1.9 %collective-permute-done.6 = bf16[98,896]{1,0:T(8,128)(2,1)S(1)} collective-permute-done((bf16[98,896]{1,0:T(8,128)(2,1)S(1)}, bf16[98,896]{1,0:T(8,128)(2,1)S(1)}, u32[]{:S(2)}, u32[]{:S(2)}) %collective-permute-start.6) | collective-permute-done | bytes 175648 | tf_op jit(solution)/shard_map/ppermute | solution.py:181
  29.3 1.7 %fusion.45 = (f32[7]{0:T(128)S(1)}, f32[7,4097]{1,0:T(8,128)S(1)}) fusion(bf16[1,1,128]{2,1,0:T(2,128)(2,1)S(1)} %get-tuple-element.42, bf16[1,4096,128]{2,1,0:T(8,128)(2,1)} %param.19, bf16[896]{0:T(1024)(128)(2,1)S(1)} %fusion.24, pred[4097]{0:T(1024)(128)(4,1)S(1)} %add_reduce_fusion), kind=kOutput, calls=%fused_computation.128 | convolution fusion | flops 9525518 | bytes 1169465 | tf_op jit(solution)/shard_map/vmap()/dot_general | solution.py:16
  31.2 1.5 %fusion.2 = bf16[896]{0:T(1024)(128)(2,1)S(1)} fusion(bf16[1,1,128]{2,1,0:T(2,128)(2,1)S(1)} %get-tuple-element.43, bf16[1,4096,128]{2,1,0:T(8,128)(2,1)} %param.20, f32[7,4097]{1,0:T(8,128)S(1)} %get-tuple-element.41, f32[7]{0:T(128)S(1)} %get-tuple-element.40, pred[4097]{0:T(1024)(128)(4,1)S(1)} %add_reduce_fusion, f32[7]{0:T(128)S(1)} %fusion.14), kind=kOutput, calls=%fused_computation.6 | convolution fusion | flops 9527317 | bytes 1169493 | tf_op jit(solution)/shard_map/vmap()/dot_general | solution.py:21
  33.3 0.7 reduce.10
  34.0 0.7 reshape.411
  34.7 5.0 %all-to-all-start = ((bf16[8,2,448]{2,1,0:T(2,128)(2,1)}), bf16[8,2,448]{2,1,0:T(2,128)(2,1)S(1)}, u32[]{:S(2)}, u32[]{:S(2)}) async-start(bf16[8,2,448]{2,1,0:T(2,128)(2,1)} %reshape.411), calls=%async_computation | async-start | bytes 32768 | tf_op jit(solution)/shard_map/all_to_all | solution.py:258
  39.7 16.8 %shard_map.149 = (bf16[8,99,896]{2,1,0:T(8,128)(2,1)}, f32[8,3,32,7]{3,2,1,0:T(8,128)}) custom-call(s32[4]{0:T(128)} %pad_add_fusion.info_ref, s32[8]{0:T(128)} %get-tuple-element.30.order_ref, bf16[8,98,896]{2,1,0:T(8,128)(2,1)} %copy-done.2, bf16[3,1024,128]{2,1,0:T(8,128)(2,1)} %k_ref.1, bf16[3,1024,128]{2,1,0:T(8,128)(2,1)} %v_ref.1, ...), custom_call_target="tpu_custom_call" | custom-call | tf_op jit(solution)/shard_map/pallas_call | solution.py:100
  56.5 1.1 %fusion.12 = (bf16[8,1,3,32,7]{4,3,2,0,1:T(8,128)(2,1)S(1)}, bf16[8,1,3,32,7]{4,3,2,0,1:T(8,128)(2,1)S(1)}, bf16[8,1,3,32,7]{4,3,2,0,1:T(8,128)(2,1)S(1)}) fusion(f32[8,3,32,7]{3,2,1,0:T(8,128)} %get-tuple-element.6), kind=kLoop, calls=%fused_computation.26 | loop fusion | flops 37632 | bytes 53760 | tf_op jit(solution)/shard_map/stack | solution.py:305
  59.1 6.1 %all-to-all-start.1 = ((bf16[8,99,896]{2,1,0:T(8,128)(2,1)}), bf16[8,99,896]{2,1,0:T(8,128)(2,1)S(1)}, u32[]{:S(2)}, u32[]{:S(2)}) async-start(bf16[8,99,896]{2,1,0:T(8,128)(2,1)} %constant_dynamic-update-slice_fusion), calls=%async_computation.1 | async-start | bytes 2981888 | tf_op jit(solution)/shard_map/all_to_all | solution.py:313
  67.6 10.7 %all-reduce.2 = bf16[8,448]{1,0:T(8,128)(2,1)S(1)} all-reduce(f32[8,448]{1,0:T(8,128)S(1)} %fusion.20), channel_id=2, replica_groups=mesh['seq'=8,'tp'=4] {'tp'}, use_global_device_ids=true, to_apply=%region_3.5.clone | all-reduce | flops 3584 | bytes 21504
  78.9 20.8 %all-to-all-done.1.o_ref = bf16[8,99,896]{2,1,0:T(8,128)(2,1)S(1)} async-done(((bf16[8,99,896]{2,1,0:T(8,128)(2,1)}), bf16[8,99,896]{2,1,0:T(8,128)(2,1)S(1)}, u32[]{:S(2)}, u32[]{:S(2)}) %all-to-all-start.1) | async-done | bytes 1419296 | tf_op jit(solution)/shard_map/all_to_all | solution.py:313
  99.8 1.1 %reshape.361 = f32[8,3,3,32,7]{4,3,2,1,0:T(8,128)S(1)} reshape(f32[8,2016]{1,0:T(8,128)S(1)} %slice_convert_fusion) | data formatting | bytes 129024 | tf_op jit(solution)/shard_map/reshape | solution.py:318
  100.8 0.8 fusion.9.lse_ref
  101.7 3.5 %shard_map.150 = bf16[3,32,896]{2,1,0:T(8,128)(2,1)} custom-call(bf16[8,99,896]{2,1,0:T(8,128)(2,1)} %copy-done.1, f32[8,3,32,7]{3,2,1,0:T(8,128)} %fusion.9.lse_ref), custom_call_target="tpu_custom_call" | custom-call | tf_op jit(solution)/shard_map/pallas_call | solution.py:156
  (60 shorter events, 8.8 us)
Async XLA Ops:
  0.6 66.6 %copy-start = (bf16[896,448]{0,1:T(8,128)(2,1)S(1)}, bf16[896,448]{0,1:T(8,128)(2,1)}, u32[]{:S(2)}) copy-start(bf16[896,448]{0,1:T(8,128)(2,1)} %param.23) | copy-start | bytes 2408452
  2.4 15.5 %collective-permute-start = (bf16[98,896]{1,0:T(8,128)(2,1)S(1)}, bf16[98,896]{1,0:T(8,128)(2,1)S(1)}, u32[]{:S(2)}, u32[]{:S(2)}) collective-permute-start(bf16[98,896]{1,0:T(8,128)(2,1)S(1)} %pad_maximum_fusion.1), channel_id=1, source_target_pairs={{0,16},{4,20},{8,24},{12,28},{16,0},{20,4},{24,8},{28,12},{1,17},{... | collective-permute-start | bytes 526856 | tf_op jit(solution)/shard_map/ppermute | solution.py:175
  6.5 12.6 %collective-permute-start.1 = (bf16[98,896]{1,0:T(8,128)(2,1)S(1)}, bf16[98,896]{1,0:T(8,128)(2,1)S(1)}, u32[]{:S(2)}, u32[]{:S(2)}) collective-permute-start(bf16[98,896]{1,0:T(8,128)(2,1)S(1)} %pad_maximum_fusion.1), channel_id=1, source_target_pairs={{0,4},{4,8},{8,12},{12,0},{16,20},{20,24},{24,28},{28,16},{1,5},{5... | collective-permute-start | bytes 526856 | tf_op jit(solution)/shard_map/ppermute | solution.py:180
  8.0 13.5 %collective-permute-start.2 = (bf16[98,896]{1,0:T(8,128)(2,1)S(1)}, bf16[98,896]{1,0:T(8,128)(2,1)S(1)}, u32[]{:S(2)}, u32[]{:S(2)}) collective-permute-start(bf16[98,896]{1,0:T(8,128)(2,1)S(1)} %pad_maximum_fusion.1), channel_id=1, source_target_pairs={{0,8},{4,12},{8,0},{12,4},{16,24},{20,28},{24,16},{28,20},{1,9},{5... | collective-permute-start | bytes 526856 | tf_op jit(solution)/shard_map/ppermute | solution.py:180
  9.6 11.9 %collective-permute-start.3 = (bf16[98,896]{1,0:T(8,128)(2,1)S(1)}, bf16[98,896]{1,0:T(8,128)(2,1)S(1)}, u32[]{:S(2)}, u32[]{:S(2)}) collective-permute-start(bf16[98,896]{1,0:T(8,128)(2,1)S(1)} %pad_maximum_fusion.1), channel_id=1, source_target_pairs={{0,12},{4,0},{8,4},{12,8},{16,28},{20,16},{24,20},{28,24},{1,13},{... | collective-permute-start | bytes 526856 | tf_op jit(solution)/shard_map/ppermute | solution.py:180
  17.9 8.5 %collective-permute-start.4 = (bf16[98,896]{1,0:T(8,128)(2,1)S(1)}, bf16[98,896]{1,0:T(8,128)(2,1)S(1)}, u32[]{:S(2)}, u32[]{:S(2)}) collective-permute-start(bf16[98,896]{1,0:T(8,128)(2,1)S(1)} %collective-permute-done), channel_id=1, source_target_pairs={{0,4},{4,8},{8,12},{12,0},{16,20},{20,24},{24,28},{28,16},{1,5},{5... | collective-permute-start | bytes 526856 | tf_op jit(solution)/shard_map/ppermute | solution.py:181
  18.6 7.9 %collective-permute-start.5 = (bf16[98,896]{1,0:T(8,128)(2,1)S(1)}, bf16[98,896]{1,0:T(8,128)(2,1)S(1)}, u32[]{:S(2)}, u32[]{:S(2)}) collective-permute-start(bf16[98,896]{1,0:T(8,128)(2,1)S(1)} %collective-permute-done), channel_id=1, source_target_pairs={{0,8},{4,12},{8,0},{12,4},{16,24},{20,28},{24,16},{28,20},{1,9},{5... | collective-permute-start | bytes 526856 | tf_op jit(solution)/shard_map/ppermute | solution.py:181
  19.1 9.3 %collective-permute-start.6 = (bf16[98,896]{1,0:T(8,128)(2,1)S(1)}, bf16[98,896]{1,0:T(8,128)(2,1)S(1)}, u32[]{:S(2)}, u32[]{:S(2)}) collective-permute-start(bf16[98,896]{1,0:T(8,128)(2,1)S(1)} %collective-permute-done), channel_id=1, source_target_pairs={{0,12},{4,0},{8,4},{12,8},{16,28},{20,16},{24,20},{28,24},{1,13},{... | collective-permute-start | bytes 526856 | tf_op jit(solution)/shard_map/ppermute | solution.py:181
  28.4 4.4 %copy-start.2 = (bf16[8,98,896]{2,1,0:T(8,128)(2,1)}, bf16[8,98,896]{2,1,0:T(8,128)(2,1)S(1)}, u32[]{:S(2)}) copy-start(bf16[8,98,896]{2,1,0:T(8,128)(2,1)S(1)} %bitcast_dynamic-update-slice_fusion.q_hbm) | copy-start | bytes 4214788
  34.7 24.4 %all-to-all-start = ((bf16[8,2,448]{2,1,0:T(2,128)(2,1)}), bf16[8,2,448]{2,1,0:T(2,128)(2,1)S(1)}, u32[]{:S(2)}, u32[]{:S(2)}) async-start(bf16[8,2,448]{2,1,0:T(2,128)(2,1)} %reshape.411), calls=%async_computation | async-start | bytes 32768 | tf_op jit(solution)/shard_map/all_to_all | solution.py:258
  59.1 6.1 %copy-start.4 = (u32[32]{0:T(128)S(1)}, u32[32]{0:T(128)}, u32[]{:S(2)}) copy-start(u32[32]{0:T(128)} %constant.216) | copy-start | bytes 388
  59.1 7.4 %copy-start.3 = (s32[8]{0:T(128)S(1)}, s32[8]{0:T(128)}, u32[]{:S(2)}) copy-start(s32[8]{0:T(128)} %param.22) | copy-start | bytes 100
  59.1 40.6 %all-to-all-start.1 = ((bf16[8,99,896]{2,1,0:T(8,128)(2,1)}), bf16[8,99,896]{2,1,0:T(8,128)(2,1)S(1)}, u32[]{:S(2)}, u32[]{:S(2)}) async-start(bf16[8,99,896]{2,1,0:T(8,128)(2,1)} %constant_dynamic-update-slice_fusion), calls=%async_computation.1 | async-start | bytes 2981888 | tf_op jit(solution)/shard_map/all_to_all | solution.py:313
  99.7 2.0 %copy-start.1 = (bf16[8,99,896]{2,1,0:T(8,128)(2,1)}, bf16[8,99,896]{2,1,0:T(8,128)(2,1)S(1)}, u32[]{:S(2)}) copy-start(bf16[8,99,896]{2,1,0:T(8,128)(2,1)S(1)} %all-to-all-done.1.o_ref) | copy-start | bytes 4257796

commit v20 on v16

--- a/solution.py
+++ b/solution.py
@@ -38,12 +38,17 @@
 
     @pl.when(c == 0)
     def _():
-        for stretch in range(stretch_count):
+        for src in range(src_count):
+            query_copy(0, src).start()
+
+    for src in range(src_count):
+        query_copy(c, src).wait()
+
+    @pl.when(c == 0)
+    def _():
+        for stretch in range(1, stretch_count):
             for src in range(src_count):
                 query_copy(stretch, src).start()
-
-    for src in range(src_count):
-        query_copy(c, src).wait()
     limit = info_ref[c]
     key_offset = info_ref[info_ref.shape[0] - 1]
     keys = k_ref[0]

time: 105 us -> 105 us (level)
  no operation moved by 1% of the time
where the time goes in v20:
time: 105 us
  waiting for transfers between devices  27.6 us (26%)
  starting transfers between devices  23.2 us (22%)
  Pallas kernels  19.8 us (19%)
  blocking collectives  10.7 us (10%)
  other arithmetic  9.22 us (9%)
  local copies, waits for them, and re-layouts  6.44 us (6%)
  between operations  4.16 us (4%)
  matrix products  3.58 us (3%)
    all_to_all x1, waiting for transfers between devices, body(): received = lax.all_to_all(payload, 'seq', 0, 0, tiled=True)  20.8 us
    pallas_call x1, Pallas kernels, prefill_partial(): pl.pallas_call(kern, grid_spec=pltpu.PrefetchScalarGridSpec(num_scalar_pr...  16.8 us
    unnamed x1, blocking collectives  10.7 us
    ppermute x3, waiting for transfers between devices, broadcast_over_seq(): far_pieces = [lax.ppermute(partner, 'seq', perm) for perm in perms]  6.78 us
    all_to_all x1, starting transfers between devices, body(): received = lax.all_to_all(payload, 'seq', 0, 0, tiled=True)  6.13 us
    all_to_all x1, starting transfers between devices, body(): lax.all_to_all(jnp.broadcast_to(home_out[None], (seq_count,) + home_out.s...  4.95 us
    ppermute x3, starting transfers between devices, broadcast_over_seq(): near_pieces = [lax.ppermute(pack, 'seq', perm) for perm in perms]  4.5 us
    ppermute x1, starting transfers between devices, broadcast_over_seq(): lax.ppermute(pack, 'seq', [(i, (i + half) % seq_count) for i in range(seq...  4.1 us
  transfers between devices with their start and end apart: 9, of which 3 were waited for; matrix products, arithmetic and copies ran while one was open for 9% of the time, Pallas kernels for 16%

profile of v20, /device:TPU:0, one launch (start us, length us, event | category | flops | bytes accessed | tf_op | source)
XLA Modules:
  0.0 104.7 jit_solution(1044773623311561024)
XLA Ops:
  0.6 0.8 fusion.25
  1.4 1.0 pad_maximum_fusion.1
  2.4 4.1 %collective-permute-start = (bf16[98,896]{1,0:T(8,128)(2,1)S(1)}, bf16[98,896]{1,0:T(8,128)(2,1)S(1)}, u32[]{:S(2)}, u32[]{:S(2)}) collective-permute-start(bf16[98,896]{1,0:T(8,128)(2,1)S(1)} %pad_maximum_fusion.1), channel_id=1, source_target_pairs={{0,16},{4,20},{8,24},{12,28},{16,0},{20,4},{24,8},{28,12},{1,17},{... | collective-permute-start | bytes 526856 | tf_op jit(solution)/shard_map/ppermute | solution.py:170
  6.5 1.5 %collective-permute-start.1 = (bf16[98,896]{1,0:T(8,128)(2,1)S(1)}, bf16[98,896]{1,0:T(8,128)(2,1)S(1)}, u32[]{:S(2)}, u32[]{:S(2)}) collective-permute-start(bf16[98,896]{1,0:T(8,128)(2,1)S(1)} %pad_maximum_fusion.1), channel_id=1, source_target_pairs={{0,4},{4,8},{8,12},{12,0},{16,20},{20,24},{24,28},{28,16},{1,5},{5... | collective-permute-start | bytes 526856 | tf_op jit(solution)/shard_map/ppermute | solution.py:175
  8.0 1.6 %collective-permute-start.2 = (bf16[98,896]{1,0:T(8,128)(2,1)S(1)}, bf16[98,896]{1,0:T(8,128)(2,1)S(1)}, u32[]{:S(2)}, u32[]{:S(2)}) collective-permute-start(bf16[98,896]{1,0:T(8,128)(2,1)S(1)} %pad_maximum_fusion.1), channel_id=1, source_target_pairs={{0,8},{4,12},{8,0},{12,4},{16,24},{20,28},{24,16},{28,20},{1,9},{5... | collective-permute-start | bytes 526856 | tf_op jit(solution)/shard_map/ppermute | solution.py:175
  9.6 1.4 %collective-permute-start.3 = (bf16[98,896]{1,0:T(8,128)(2,1)S(1)}, bf16[98,896]{1,0:T(8,128)(2,1)S(1)}, u32[]{:S(2)}, u32[]{:S(2)}) collective-permute-start(bf16[98,896]{1,0:T(8,128)(2,1)S(1)} %pad_maximum_fusion.1), channel_id=1, source_target_pairs={{0,12},{4,0},{8,4},{12,8},{16,28},{20,16},{24,20},{28,24},{1,13},{... | collective-permute-start | bytes 526856 | tf_op jit(solution)/shard_map/ppermute | solution.py:175
  11.6 1.3 %compare_select_fusion.4 = (s32[8]{0:T(128)S(1)}, s32[]{:T(128)}) fusion(s32[8]{0:T(128)} %param.22, s32[]{:T(128)S(6)} %axis_index.15), kind=kLoop, calls=%fused_computation.64 | loop fusion | flops 47 | bytes 72 | tf_op jit(solution)/shard_map/jit(_take)/jit(_where)/select_n | solution.py:256
  16.9 1.0 bitcast_dynamic-update-slice_fusion.7
  19.1 2.4 %collective-permute-start.6 = (bf16[98,896]{1,0:T(8,128)(2,1)S(1)}, bf16[98,896]{1,0:T(8,128)(2,1)S(1)}, u32[]{:S(2)}, u32[]{:S(2)}) collective-permute-start(bf16[98,896]{1,0:T(8,128)(2,1)S(1)} %collective-permute-done), channel_id=1, source_target_pairs={{0,12},{4,0},{8,4},{12,8},{16,28},{20,16},{24,20},{28,24},{1,13},{... | collective-permute-start | bytes 526856 | tf_op jit(solution)/shard_map/ppermute | solution.py:176
  21.5 4.9 %collective-permute-done.4 = bf16[98,896]{1,0:T(8,128)(2,1)S(1)} collective-permute-done((bf16[98,896]{1,0:T(8,128)(2,1)S(1)}, bf16[98,896]{1,0:T(8,128)(2,1)S(1)}, u32[]{:S(2)}, u32[]{:S(2)}) %collective-permute-start.4) | collective-permute-done | bytes 175648 | tf_op jit(solution)/shard_map/ppermute | solution.py:176
  26.5 1.9 %collective-permute-done.6 = bf16[98,896]{1,0:T(8,128)(2,1)S(1)} collective-permute-done((bf16[98,896]{1,0:T(8,128)(2,1)S(1)}, bf16[98,896]{1,0:T(8,128)(2,1)S(1)}, u32[]{:S(2)}, u32[]{:S(2)}) %collective-permute-start.6) | collective-permute-done | bytes 175648 | tf_op jit(solution)/shard_map/ppermute | solution.py:176
  29.3 1.7 %fusion.45 = (f32[7]{0:T(128)S(1)}, f32[7,4097]{1,0:T(8,128)S(1)}) fusion(bf16[1,1,128]{2,1,0:T(2,128)(2,1)S(1)} %get-tuple-element.42, bf16[1,4096,128]{2,1,0:T(8,128)(2,1)} %param.19, bf16[896]{0:T(1024)(128)(2,1)S(1)} %fusion.24, pred[4097]{0:T(1024)(128)(4,1)S(1)} %add_reduce_fusion), kind=kOutput, calls=%fused_computation.128 | convolution fusion | flops 9525518 | bytes 1169465 | tf_op jit(solution)/shard_map/vmap()/dot_general | solution.py:16
  31.2 1.5 %fusion.2 = bf16[896]{0:T(1024)(128)(2,1)S(1)} fusion(bf16[1,1,128]{2,1,0:T(2,128)(2,1)S(1)} %get-tuple-element.43, bf16[1,4096,128]{2,1,0:T(8,128)(2,1)} %param.20, f32[7,4097]{1,0:T(8,128)S(1)} %get-tuple-element.41, f32[7]{0:T(128)S(1)} %get-tuple-element.40, pred[4097]{0:T(1024)(128)(4,1)S(1)} %add_reduce_fusion, f32[7]{0:T(128)S(1)} %fusion.14), kind=kOutput, calls=%fused_computation.6 | convolution fusion | flops 9527317 | bytes 1169493 | tf_op jit(solution)/shard_map/vmap()/dot_general | solution.py:21
  33.3 0.7 reduce.10
  34.0 0.7 reshape.411
  34.7 5.0 %all-to-all-start = ((bf16[8,2,448]{2,1,0:T(2,128)(2,1)}), bf16[8,2,448]{2,1,0:T(2,128)(2,1)S(1)}, u32[]{:S(2)}, u32[]{:S(2)}) async-start(bf16[8,2,448]{2,1,0:T(2,128)(2,1)} %reshape.411), calls=%async_computation | async-start | bytes 32768 | tf_op jit(solution)/shard_map/all_to_all | solution.py:253
  39.7 16.8 %shard_map.149 = (bf16[8,99,896]{2,1,0:T(8,128)(2,1)}, f32[8,3,32,7]{3,2,1,0:T(8,128)}) custom-call(s32[4]{0:T(128)} %pad_add_fusion.info_ref, s32[8]{0:T(128)} %get-tuple-element.30.order_ref, bf16[8,98,896]{2,1,0:T(8,128)(2,1)} %copy-done.2, bf16[3,1024,128]{2,1,0:T(8,128)(2,1)} %k_ref.1, bf16[3,1024,128]{2,1,0:T(8,128)(2,1)} %v_ref.1, ...), custom_call_target="tpu_custom_call" | custom-call | tf_op jit(solution)/shard_map/pallas_call | solution.py:105
  56.5 1.1 %fusion.12 = (bf16[8,1,3,32,7]{4,3,2,0,1:T(8,128)(2,1)S(1)}, bf16[8,1,3,32,7]{4,3,2,0,1:T(8,128)(2,1)S(1)}, bf16[8,1,3,32,7]{4,3,2,0,1:T(8,128)(2,1)S(1)}) fusion(f32[8,3,32,7]{3,2,1,0:T(8,128)} %get-tuple-element.6), kind=kLoop, calls=%fused_computation.26 | loop fusion | flops 37632 | bytes 53760 | tf_op jit(solution)/shard_map/stack | solution.py:300
  59.2 6.1 %all-to-all-start.1 = ((bf16[8,99,896]{2,1,0:T(8,128)(2,1)}), bf16[8,99,896]{2,1,0:T(8,128)(2,1)S(1)}, u32[]{:S(2)}, u32[]{:S(2)}) async-start(bf16[8,99,896]{2,1,0:T(8,128)(2,1)} %constant_dynamic-update-slice_fusion), calls=%async_computation.1 | async-start | bytes 2981888 | tf_op jit(solution)/shard_map/all_to_all | solution.py:308
  67.6 10.7 %all-reduce.2 = bf16[8,448]{1,0:T(8,128)(2,1)S(1)} all-reduce(f32[8,448]{1,0:T(8,128)S(1)} %fusion.20), channel_id=2, replica_groups=mesh['seq'=8,'tp'=4] {'tp'}, use_global_device_ids=true, to_apply=%region_3.5.clone | all-reduce | flops 3584 | bytes 21504
  78.9 20.8 %all-to-all-done.1.o_ref = bf16[8,99,896]{2,1,0:T(8,128)(2,1)S(1)} async-done(((bf16[8,99,896]{2,1,0:T(8,128)(2,1)}), bf16[8,99,896]{2,1,0:T(8,128)(2,1)S(1)}, u32[]{:S(2)}, u32[]{:S(2)}) %all-to-all-start.1) | async-done | bytes 1419296 | tf_op jit(solution)/shard_map/all_to_all | solution.py:308
  99.8 1.1 %reshape.361 = f32[8,3,3,32,7]{4,3,2,1,0:T(8,128)S(1)} reshape(f32[8,2016]{1,0:T(8,128)S(1)} %slice_convert_fusion) | data formatting | bytes 129024 | tf_op jit(solution)/shard_map/reshape | solution.py:313
  100.9 0.8 fusion.9.lse_ref
  101.7 3.0 %shard_map.150 = bf16[3,32,896]{2,1,0:T(8,128)(2,1)} custom-call(bf16[8,99,896]{2,1,0:T(8,128)(2,1)} %copy-done.1, f32[8,3,32,7]{3,2,1,0:T(8,128)} %fusion.9.lse_ref), custom_call_target="tpu_custom_call" | custom-call | tf_op jit(solution)/shard_map/pallas_call | solution.py:155
  (60 shorter events, 8.8 us)
Async XLA Ops:
  0.6 66.7 %copy-start = (bf16[896,448]{0,1:T(8,128)(2,1)S(1)}, bf16[896,448]{0,1:T(8,128)(2,1)}, u32[]{:S(2)}) copy-start(bf16[896,448]{0,1:T(8,128)(2,1)} %param.23) | copy-start | bytes 2408452
  2.4 15.5 %collective-permute-start = (bf16[98,896]{1,0:T(8,128)(2,1)S(1)}, bf16[98,896]{1,0:T(8,128)(2,1)S(1)}, u32[]{:S(2)}, u32[]{:S(2)}) collective-permute-start(bf16[98,896]{1,0:T(8,128)(2,1)S(1)} %pad_maximum_fusion.1), channel_id=1, source_target_pairs={{0,16},{4,20},{8,24},{12,28},{16,0},{20,4},{24,8},{28,12},{1,17},{... | collective-permute-start | bytes 526856 | tf_op jit(solution)/shard_map/ppermute | solution.py:170
  6.5 12.6 %collective-permute-start.1 = (bf16[98,896]{1,0:T(8,128)(2,1)S(1)}, bf16[98,896]{1,0:T(8,128)(2,1)S(1)}, u32[]{:S(2)}, u32[]{:S(2)}) collective-permute-start(bf16[98,896]{1,0:T(8,128)(2,1)S(1)} %pad_maximum_fusion.1), channel_id=1, source_target_pairs={{0,4},{4,8},{8,12},{12,0},{16,20},{20,24},{24,28},{28,16},{1,5},{5... | collective-permute-start | bytes 526856 | tf_op jit(solution)/shard_map/ppermute | solution.py:175
  8.0 13.5 %collective-permute-start.2 = (bf16[98,896]{1,0:T(8,128)(2,1)S(1)}, bf16[98,896]{1,0:T(8,128)(2,1)S(1)}, u32[]{:S(2)}, u32[]{:S(2)}) collective-permute-start(bf16[98,896]{1,0:T(8,128)(2,1)S(1)} %pad_maximum_fusion.1), channel_id=1, source_target_pairs={{0,8},{4,12},{8,0},{12,4},{16,24},{20,28},{24,16},{28,20},{1,9},{5... | collective-permute-start | bytes 526856 | tf_op jit(solution)/shard_map/ppermute | solution.py:175
  9.6 11.9 %collective-permute-start.3 = (bf16[98,896]{1,0:T(8,128)(2,1)S(1)}, bf16[98,896]{1,0:T(8,128)(2,1)S(1)}, u32[]{:S(2)}, u32[]{:S(2)}) collective-permute-start(bf16[98,896]{1,0:T(8,128)(2,1)S(1)} %pad_maximum_fusion.1), channel_id=1, source_target_pairs={{0,12},{4,0},{8,4},{12,8},{16,28},{20,16},{24,20},{28,24},{1,13},{... | collective-permute-start | bytes 526856 | tf_op jit(solution)/shard_map/ppermute | solution.py:175
  17.9 8.5 %collective-permute-start.4 = (bf16[98,896]{1,0:T(8,128)(2,1)S(1)}, bf16[98,896]{1,0:T(8,128)(2,1)S(1)}, u32[]{:S(2)}, u32[]{:S(2)}) collective-permute-start(bf16[98,896]{1,0:T(8,128)(2,1)S(1)} %collective-permute-done), channel_id=1, source_target_pairs={{0,4},{4,8},{8,12},{12,0},{16,20},{20,24},{24,28},{28,16},{1,5},{5... | collective-permute-start | bytes 526856 | tf_op jit(solution)/shard_map/ppermute | solution.py:176
  18.6 7.9 %collective-permute-start.5 = (bf16[98,896]{1,0:T(8,128)(2,1)S(1)}, bf16[98,896]{1,0:T(8,128)(2,1)S(1)}, u32[]{:S(2)}, u32[]{:S(2)}) collective-permute-start(bf16[98,896]{1,0:T(8,128)(2,1)S(1)} %collective-permute-done), channel_id=1, source_target_pairs={{0,8},{4,12},{8,0},{12,4},{16,24},{20,28},{24,16},{28,20},{1,9},{5... | collective-permute-start | bytes 526856 | tf_op jit(solution)/shard_map/ppermute | solution.py:176
  19.1 9.3 %collective-permute-start.6 = (bf16[98,896]{1,0:T(8,128)(2,1)S(1)}, bf16[98,896]{1,0:T(8,128)(2,1)S(1)}, u32[]{:S(2)}, u32[]{:S(2)}) collective-permute-start(bf16[98,896]{1,0:T(8,128)(2,1)S(1)} %collective-permute-done), channel_id=1, source_target_pairs={{0,12},{4,0},{8,4},{12,8},{16,28},{20,16},{24,20},{28,24},{1,13},{... | collective-permute-start | bytes 526856 | tf_op jit(solution)/shard_map/ppermute | solution.py:176
  28.4 4.4 %copy-start.2 = (bf16[8,98,896]{2,1,0:T(8,128)(2,1)}, bf16[8,98,896]{2,1,0:T(8,128)(2,1)S(1)}, u32[]{:S(2)}) copy-start(bf16[8,98,896]{2,1,0:T(8,128)(2,1)S(1)} %bitcast_dynamic-update-slice_fusion.q_hbm) | copy-start | bytes 4214788
  34.7 24.4 %all-to-all-start = ((bf16[8,2,448]{2,1,0:T(2,128)(2,1)}), bf16[8,2,448]{2,1,0:T(2,128)(2,1)S(1)}, u32[]{:S(2)}, u32[]{:S(2)}) async-start(bf16[8,2,448]{2,1,0:T(2,128)(2,1)} %reshape.411), calls=%async_computation | async-start | bytes 32768 | tf_op jit(solution)/shard_map/all_to_all | solution.py:253
  59.2 6.1 %copy-start.4 = (u32[32]{0:T(128)S(1)}, u32[32]{0:T(128)}, u32[]{:S(2)}) copy-start(u32[32]{0:T(128)} %constant.216) | copy-start | bytes 388
  59.2 7.4 %copy-start.3 = (s32[8]{0:T(128)S(1)}, s32[8]{0:T(128)}, u32[]{:S(2)}) copy-start(s32[8]{0:T(128)} %param.22) | copy-start | bytes 100
  59.2 40.6 %all-to-all-start.1 = ((bf16[8,99,896]{2,1,0:T(8,128)(2,1)}), bf16[8,99,896]{2,1,0:T(8,128)(2,1)S(1)}, u32[]{:S(2)}, u32[]{:S(2)}) async-start(bf16[8,99,896]{2,1,0:T(8,128)(2,1)} %constant_dynamic-update-slice_fusion), calls=%async_computation.1 | async-start | bytes 2981888 | tf_op jit(solution)/shard_map/all_to_all | solution.py:308
  99.8 2.0 %copy-start.1 = (bf16[8,99,896]{2,1,0:T(8,128)(2,1)}, bf16[8,99,896]{2,1,0:T(8,128)(2,1)S(1)}, u32[]{:S(2)}) copy-start(bf16[8,99,896]{2,1,0:T(8,128)(2,1)S(1)} %all-to-all-done.1.o_ref) | copy-start | bytes 4257796
